TPU v7x, 512 devices: a whole 4x8x8 slice. The times are simulated.
512 devices in a mesh: win: 8 (over y), lon: 32 (over x, z_lo, core), lat: 2 (over z_hi).
Axes of the slice: x: 4, y: 8, z: 8 (z_hi: 2, z_lo: 4; z = z_hi * 4 + z_lo), core: 2. Of those that a mesh axis runs over, the one named last changes fastest.
Arguments:
- dual_state: float32 [8, 16, 2, 16384], P('win', None, 'lat', 'lon'), may hold values from -6 to 6
- dual_obs: float32 [8, 16, 2, 16384], P('win', None, 'lat', 'lon'), may hold values from -6 to 6
- increment: float32 [8, 16, 2, 16384], P('win', None, 'lat', 'lon'), may hold values from -6 to 6
- resid_dual: float32 [8, 16, 2, 16384], P('win', None, 'lat', 'lon'), may hold values from -6 to 6
- resid_obs: float32 [8, 16, 2, 16384], P('win', None, 'lat', 'lon'), may hold values from -6 to 6
- resid_incr: float32 [8, 16, 2, 16384], P('win', None, 'lat', 'lon'), may hold values from -6 to 6
- search_dual: float32 [8, 16, 2, 16384], P('win', None, 'lat', 'lon'), may hold values from -6 to 6
- search_obs: float32 [8, 16, 2, 16384], P('win', None, 'lat', 'lon'), may hold values from -6 to 6
- search_incr: float32 [8, 16, 2, 16384], P('win', None, 'lat', 'lon'), may hold values from -6 to 6
- ensemble: bfloat16 [8, 64, 16, 2, 16384], P('win', None, None, 'lat', 'lon'), may hold values from -12 to 12
- tangent_coefs: float32 [8, 5, 16, 2, 16384], P('win', None, None, 'lat', 'lon'), may hold values from -0.25 to 0.25
- obs_weight: float32 [8, 16, 2, 16384], P('win', None, 'lat', 'lon'), may hold values from 0.25 to 2
- obs_var: float32 [8, 16, 2, 16384], P('win', None, 'lat', 'lon'), may hold values from 0.5 to 2
- loc_cols: int32 [32, 5], P('lon'), may hold values from 0 to 31, as said below
- loc_vals: bfloat16 [32, 5, 512, 512], P('lon'), may hold values from -0.125 to 0.125
Outputs:
- next_dual: float32 [8, 16, 2, 16384], P('win', None, 'lat', 'lon')
- next_obs: float32 [8, 16, 2, 16384], P('win', None, 'lat', 'lon')
- next_incr: float32 [8, 16, 2, 16384], P('win', None, 'lat', 'lon')
- next_res_dual: float32 [8, 16, 2, 16384], P('win', None, 'lat', 'lon')
- next_res_obs: float32 [8, 16, 2, 16384], P('win', None, 'lat', 'lon')
- next_res_incr: float32 [8, 16, 2, 16384], P('win', None, 'lat', 'lon')
Inputs may be any that keep to these rules, and one draw needn't show every extreme that they name: `loc_cols`: row block i names 5 distinct column blocks, block i itself among them, each within 3 blocks of i around the longitude loop.
All inputs are finite; a program needn't handle non-finite values.
Results may differ from a plain program's by a relative error of at most 0.0017.
Values may be sent and summed in bfloat16 or wider, within the bound.
No kernel may reach another device: no remote copies, remote signals or barrier semaphores. Data moves between devices by JAX's collectives and lax.ppermute only.
A program may use at most 64 MiB of HBM per device.

v0:
```python
import jax
import jax.numpy as jnp
from jax import lax
from jax.sharding import PartitionSpec as P

REACH = 3


def extended_2(array, sides, width, wrap):
    for axis, dim in sides:
        peers, length = (lax.axis_size(axis), array.shape[dim])
        up = [(i, (i + 1) % peers) for i in range(peers if wrap else peers - 1)]
        down = [(j, i) for i, j in up]
        last = lax.slice_in_dim(array, length - width, length, axis=dim)
        leading = lax.slice_in_dim(array, 0, width, axis=dim)
        before = lax.ppermute(last, axis, up)
        after = lax.ppermute(leading, axis, down)
        array = jnp.concatenate([before, array, after], axis=dim)
    return array


def passed_along(block, axis, distance):
    devices = range(lax.axis_size(axis))
    route = [((i - distance) % len(devices), i) for i in devices]
    return lax.ppermute(block, axis, route)


def shifted(value, axis, steps):
    count = lax.axis_size(axis)
    leading, last = (max(0, -steps), min(count, count - steps))
    return lax.ppermute(value, axis, [(source, source + steps) for source in range(leading, last)])


def lon_rim(field, width):
    return extended_2(field, (("lon", 3),), width, True)


def lat_rim(field):
    return extended_2(field, (("lat", 2),), 1, False)


def forward_step(extended, coeff):
    inner = coeff[:, :, 1:-1, 1:-1]
    return (
        (0.5 + inner[0]) * extended[:, 1:-1, 1:-1]
        + inner[1] * extended[:, 1:-1, 2:]
        + inner[2] * extended[:, 1:-1, :-2]
        + inner[3] * extended[:, 2:, 1:-1]
        + inner[4] * extended[:, :-2, 1:-1]
    )


def adjoint_step(extended, coeff):
    scaled = coeff * extended[None]
    return (
        (0.5 + coeff[0, :, 1:-1, 1:-1]) * extended[:, 1:-1, 1:-1]
        + scaled[1, :, 1:-1, :-2]
        + scaled[2, :, 1:-1, 2:]
        + scaled[3, :, :-2, 1:-1]
        + scaled[4, :, 2:, 1:-1]
    )


def propagate(field, coeff_wide, stepper):
    coeff_one = coeff_wide[..., 1:-1]
    first = stepper(lat_rim(lon_rim(field, 1))[0], coeff_one)
    return stepper(lat_rim(lon_rim(first[None], 1))[0], coeff_one)


def localize(members, search, loc_cols, loc_vals):
    count_members = members.shape[0]
    block = members.shape[-1]
    products = (members * search[None]).astype(jnp.bfloat16)
    flat = products.reshape(-1, block)
    bands = lax.axis_size("lon")
    here = lax.axis_index("lon")
    columns = loc_cols[0]
    tiles = loc_vals[0]

    def weight_for(offset):
        target = (here + offset + bands) % bands
        match = (columns == target).astype(jnp.bfloat16)
        return jnp.einsum("j,jpq->pq", match, tiles, preferred_element_type=jnp.float32).astype(
            jnp.bfloat16
        )

    total = jnp.dot(flat, weight_for(0), preferred_element_type=jnp.float32)
    east_side = flat
    west_side = flat
    for distance in range(1, REACH + 1):
        east_side = passed_along(east_side, "lon", -1)
        total = total + jnp.dot(east_side, weight_for(distance), preferred_element_type=jnp.float32)
        west_side = passed_along(west_side, "lon", 1)
        total = total + jnp.dot(
            west_side, weight_for(-distance), preferred_element_type=jnp.float32
        )
    spread = total.reshape(products.shape)
    return jnp.sum(members * spread, axis=0) / (count_members - 1)


def local(
    dual_state,
    dual_obs,
    increment,
    resid_dual,
    resid_obs,
    resid_incr,
    search_dual,
    search_obs,
    search_incr,
    ensemble,
    tangent_coefs,
    obs_weight,
    obs_var,
    loc_cols,
    loc_vals,
):
    coeff_wide = lat_rim(lon_rim(tangent_coefs[0], 2))
    forward_image = propagate(search_incr, coeff_wide, forward_step)
    backward_image = propagate(search_dual, coeff_wide, adjoint_step)
    earlier = shifted(forward_image[None].astype(jnp.bfloat16), "win", 1).astype(jnp.float32)
    following = shifted(backward_image[None].astype(jnp.bfloat16), "win", -1).astype(jnp.float32)
    covar = localize(ensemble[0], search_dual[0], loc_cols, loc_vals)[None]
    image_dual = covar + search_incr - earlier
    image_obs = obs_var * search_obs + obs_weight * search_incr
    image_incr = search_dual - following + obs_weight * search_obs
    resid_local = (
        jnp.sum(resid_dual * resid_dual)
        + jnp.sum(resid_obs * resid_obs)
        + jnp.sum(resid_incr * resid_incr)
    )
    search_local = (
        jnp.sum(search_dual * search_dual)
        + jnp.sum(search_obs * search_obs)
        + jnp.sum(search_incr * search_incr)
    )
    resid_sq, search_sq = lax.psum((resid_local, search_local), ("win", "lon", "lat"))
    alpha = resid_sq / (search_sq + 1e-06)
    return (
        dual_state + alpha * search_dual,
        dual_obs + alpha * search_obs,
        increment + alpha * search_incr,
        resid_dual - alpha * image_dual,
        resid_obs - alpha * image_obs,
        resid_incr - alpha * image_incr,
    )


def solution(mesh):
    placed = (
        P("win", None, "lat", "lon"),
        P("win", None, "lat", "lon"),
        P("win", None, "lat", "lon"),
        P("win", None, "lat", "lon"),
        P("win", None, "lat", "lon"),
        P("win", None, "lat", "lon"),
        P("win", None, "lat", "lon"),
        P("win", None, "lat", "lon"),
        P("win", None, "lat", "lon"),
        P("win", None, None, "lat", "lon"),
        P("win", None, None, "lat", "lon"),
        P("win", None, "lat", "lon"),
        P("win", None, "lat", "lon"),
        P("lon", None),
        P("lon", None, None, None),
    )
    return jax.shard_map(
        local,
        mesh=mesh,
        in_specs=placed,
        out_specs=(
            P("win", None, "lat", "lon"),
            P("win", None, "lat", "lon"),
            P("win", None, "lat", "lon"),
            P("win", None, "lat", "lon"),
            P("win", None, "lat", "lon"),
            P("win", None, "lat", "lon"),
        ),
        check_vma=False,
    )
```

profile of v0, /device:TPU:1, one launch (start us, length us, event | category | flops | bytes accessed | tf_op | source)
XLA Modules:
  0.0 300.7 jit_solution(16440169841457526612)
XLA Ops:
  0.7 1.6 multiply_reduce_fusion
  2.3 1.4 multiply_reduce_fusion.3
  3.7 1.4 multiply_reduce_fusion.1
  7.1 1.5 multiply_reduce_fusion.4
  10.5 106.1 %all-reduce = (f32[]{:T(128)}, f32[]{:T(128)}) all-reduce(f32[]{:T(128)S(6)} %add.184, f32[]{:T(128)S(6)} %add.186), channel_id=1, replica_groups=mesh['win'=8,'lon'=32,'lat'=2] {'win','lon','lat'}, use_global_device_ids=true, to_apply=%region_3.4 | all-reduce | flops 2 | bytes 16 | tf_op jit(solution)/shard_map/psum | solution.py:137
  118.0 0.8 fusion.75
  118.7 2.5 fusion.14
  121.2 2.6 collective-permute-start
  123.9 3.0 collective-permute-start.15
  126.8 1.9 collective-permute-start.16
  128.9 3.6 %collective-permute-start.19 = (f32[5,16,1,2]{3,1,2,0:T(8,128)S(1)}, f32[5,16,1,2]{3,1,2,0:T(8,128)S(1)}, u32[]{:S(2)}, u32[]{:S(2)}) collective-permute-start(f32[5,16,1,2]{3,1,2,0:T(8,128)S(1)} %get-tuple-element.14), channel_id=1, source_target_pairs={{0,2},{2,4},{4,6},{6,8},{8,10},{10,12},{12,14},{14,16},{16,18},{18... | collective-permute-start | bytes 1928 | tf_op jit(solution)/shard_map/ppermute | solution.py:16
  132.5 5.0 %collective-permute-start.20 = (f32[5,16,1,2]{3,1,2,0:T(8,128)S(1)}, f32[5,16,1,2]{3,1,2,0:T(8,128)S(1)}, u32[]{:S(2)}, u32[]{:S(2)}) collective-permute-start(f32[5,16,1,2]{3,1,2,0:T(8,128)S(1)} %get-tuple-element.15), channel_id=1, source_target_pairs={{2,0},{4,2},{6,4},{8,6},{10,8},{12,10},{14,12},{16,14},{18,16},{20... | collective-permute-start | bytes 1928 | tf_op jit(solution)/shard_map/ppermute | solution.py:17
  137.6 2.9 fusion.2
  140.6 2.9 fusion.6
  143.5 3.0 fusion.4
  146.5 2.9 fusion.10
  149.4 3.0 fusion.8
  152.4 3.2 %fusion.12 = bf16[1,512,512]{2,0,1:T(2,128)(2,1)} fusion(bf16[5,512,512]{2,1,0:T(8,128)(2,1)S(1)} %bitcast.198, s32[1,5]{1,0:T(1,128)S(1)} %copy-done.19, s32[]{:T(128)S(6)} %select_n.31), kind=kOutput, calls=%fused_computation.12 | convolution fusion | flops 2621445 | bytes 3145752 | tf_op jit(solution)/shard_map/j,jpq->pq/dot_general | solution.py:83
  155.6 2.0 fusion
  157.8 1.9 collective-permute-start.6
  159.7 7.5 %collective-permute-start.7 = (f32[1,16,1,1]{3,1,2,0:T(8,128)S(1)}, f32[1,16,1,1]{3,1,2,0:T(8,128)S(1)}, u32[]{:S(2)}, u32[]{:S(2)}) collective-permute-start(f32[1,16,1,1]{3,1,2,0:T(8,128)S(1)} %get-tuple-element.39), channel_id=1, source_target_pairs={{2,0},{4,2},{6,4},{8,6},{10,8},{12,10},{14,12},{16,14},{18,16},{20... | collective-permute-start | bytes 200 | tf_op jit(solution)/shard_map/ppermute | solution.py:17
  167.4 5.7 %collective-permute-start.17 = (f32[1,16,1,514]{3,1,2,0:T(8,128)S(1)}, f32[1,16,1,514]{3,1,2,0:T(8,128)S(1)}, u32[]{:S(2)}, u32[]{:S(2)}) collective-permute-start(f32[1,16,1,514]{3,1,2,0:T(8,128)S(1)} %pad_maximum_fusion.7), channel_id=1, source_target_pairs={{0,1},{2,3},{4,5},{6,7},{8,9},{10,11},{12,13},{14,15},{16,17},{18,... | collective-permute-start | bytes 98696 | tf_op jit(solution)/shard_map/ppermute | solution.py:16
  173.1 1.3 collective-permute-start.18
  174.5 7.9 %collective-permute-start.8 = (f32[1,16,1,514]{3,1,2,0:T(8,128)S(1)}, f32[1,16,1,514]{3,1,2,0:T(8,128)S(1)}, u32[]{:S(2)}, u32[]{:S(2)}) collective-permute-start(f32[1,16,1,514]{3,1,2,0:T(8,128)S(1)} %pad_maximum_fusion.5), channel_id=1, source_target_pairs={{0,1},{2,3},{4,5},{6,7},{8,9},{10,11},{12,13},{14,15},{16,17},{18,... | collective-permute-start | bytes 98696 | tf_op jit(solution)/shard_map/ppermute | solution.py:16
  182.4 1.3 collective-permute-start.9
  183.8 7.9 %collective-permute-start.21 = (f32[5,16,1,516]{3,1,2,0:T(8,128)S(1)}, f32[5,16,1,516]{3,1,2,0:T(8,128)S(1)}, u32[]{:S(2)}, u32[]{:S(2)}) collective-permute-start(f32[5,16,1,516]{3,1,2,0:T(8,128)S(1)} %pad_maximum_fusion.4), channel_id=1, source_target_pairs={{0,1},{2,3},{4,5},{6,7},{8,9},{10,11},{12,13},{14,15},{16,17},{18,... | collective-permute-start | bytes 495368 | tf_op jit(solution)/shard_map/ppermute | solution.py:16
  191.8 1.3 collective-permute-start.22
  193.1 1.9 collective-permute-start.1
  195.2 1.8 collective-permute-done.21
  197.0 5.3 %collective-permute-done.22 = f32[5,16,1,516]{3,1,2,0:T(8,128)S(1)} collective-permute-done((f32[5,16,1,516]{3,1,2,0:T(8,128)S(1)}, f32[5,16,1,516]{3,1,2,0:T(8,128)S(1)}, u32[]{:S(2)}, u32[]{:S(2)}) %collective-permute-start.22) | collective-permute-done | bytes 165152 | tf_op jit(solution)/shard_map/ppermute | solution.py:17
  202.3 0.2 broadcast_multiply_fusion.1
  202.8 4.9 %collective-permute-start.10 = (f32[1,16,1,1]{3,1,2,0:T(8,128)S(1)}, f32[1,16,1,1]{3,1,2,0:T(8,128)S(1)}, u32[]{:S(2)}, u32[]{:S(2)}) collective-permute-start(f32[1,16,1,1]{3,1,2,0:T(8,128)S(1)} %get-tuple-element.36), channel_id=1, source_target_pairs={{0,2},{2,4},{4,6},{6,8},{8,10},{10,12},{12,14},{14,16},{16,18},{18... | collective-permute-start | bytes 200 | tf_op jit(solution)/shard_map/ppermute | solution.py:16
  207.7 9.2 %collective-permute-start.11 = (f32[1,16,1,1]{3,1,2,0:T(8,128)S(1)}, f32[1,16,1,1]{3,1,2,0:T(8,128)S(1)}, u32[]{:S(2)}, u32[]{:S(2)}) collective-permute-start(f32[1,16,1,1]{3,1,2,0:T(8,128)S(1)} %get-tuple-element.37), channel_id=1, source_target_pairs={{2,0},{4,2},{6,4},{8,6},{10,8},{12,10},{14,12},{16,14},{18,16},{20... | collective-permute-start | bytes 200 | tf_op jit(solution)/shard_map/ppermute | solution.py:17
  217.0 1.9 collective-permute-start.23
  218.9 7.5 %collective-permute-start.24 = (f32[1,16,1,1]{3,1,2,0:T(8,128)S(1)}, f32[1,16,1,1]{3,1,2,0:T(8,128)S(1)}, u32[]{:S(2)}, u32[]{:S(2)}) collective-permute-start(f32[1,16,1,1]{3,1,2,0:T(8,128)S(1)} %get-tuple-element.24), channel_id=1, source_target_pairs={{2,0},{4,2},{6,4},{8,6},{10,8},{12,10},{14,12},{16,14},{18,16},{20... | collective-permute-start | bytes 200 | tf_op jit(solution)/shard_map/ppermute | solution.py:17
  226.6 4.7 %collective-permute-start.12 = (f32[1,16,1,514]{3,1,2,0:T(8,128)S(1)}, f32[1,16,1,514]{3,1,2,0:T(8,128)S(1)}, u32[]{:S(2)}, u32[]{:S(2)}) collective-permute-start(f32[1,16,1,514]{3,1,2,0:T(8,128)S(1)} %pad_maximum_fusion.6), channel_id=1, source_target_pairs={{0,1},{2,3},{4,5},{6,7},{8,9},{10,11},{12,13},{14,15},{16,17},{18,... | collective-permute-start | bytes 98696 | tf_op jit(solution)/shard_map/ppermute | solution.py:16
  231.3 1.3 collective-permute-start.13
  232.6 7.9 %collective-permute-start.25 = (f32[1,16,1,514]{3,1,2,0:T(8,128)S(1)}, f32[1,16,1,514]{3,1,2,0:T(8,128)S(1)}, u32[]{:S(2)}, u32[]{:S(2)}) collective-permute-start(f32[1,16,1,514]{3,1,2,0:T(8,128)S(1)} %pad_maximum_fusion.8), channel_id=1, source_target_pairs={{0,1},{2,3},{4,5},{6,7},{8,9},{10,11},{12,13},{14,15},{16,17},{18,... | collective-permute-start | bytes 98696 | tf_op jit(solution)/shard_map/ppermute | solution.py:16
  240.5 1.3 collective-permute-start.26
  241.9 4.9 %collective-permute-start.2 = (bf16[1024,512]{1,0:T(8,128)(2,1)}, bf16[1024,512]{1,0:T(8,128)(2,1)S(1)}, u32[]{:S(2)}, u32[]{:S(2)}) collective-permute-start(bf16[1024,512]{1,0:T(8,128)(2,1)} %collective-permute-done), channel_id=1, source_target_pairs={{2,0},{4,2},{6,4},{8,6},{10,8},{12,10},{14,12},{16,14},{18,16},{20... | collective-permute-start | bytes 3145736 | tf_op jit(solution)/shard_map/ppermute | solution.py:25
  246.8 2.5 collective-permute-done.26
  249.4 0.2 broadcast_multiply_fusion
  249.7 1.9 collective-permute-start.3
  251.8 1.4 collective-permute-start.27
  253.3 1.9 fusion.16
  255.2 0.6 copy.47
  255.9 0.6 copy.48
  256.5 0.6 copy.50
  257.2 0.6 copy.46
  257.8 4.0 %collective-permute-start.14 = (bf16[1,16,1,512]{3,1,2,0:T(8,128)(2,1)S(1)}, bf16[1,16,1,512]{3,1,2,0:T(8,128)(2,1)S(1)}, u32[]{:S(2)}, u32[]{:S(2)}) collective-permute-start(bf16[1,16,1,512]{3,1,2,0:T(8,128)(2,1)S(1)} %get-tuple-element.22), channel_id=1, source_target_pairs={{0,64},{64,128},{128,192},{192,256},{256,320},{320,384},{384,448},... | collective-permute-start | bytes 49160 | tf_op jit(solution)/shard_map/ppermute | solution.py:31
  261.8 0.7 multiply_subtract_fusion
  262.5 7.3 %collective-permute-done.2 = bf16[1024,512]{1,0:T(8,128)(2,1)S(1)} collective-permute-done((bf16[1024,512]{1,0:T(8,128)(2,1)}, bf16[1024,512]{1,0:T(8,128)(2,1)S(1)}, u32[]{:S(2)}, u32[]{:S(2)}) %collective-permute-start.2) | collective-permute-done | bytes 1048608 | tf_op jit(solution)/shard_map/ppermute | solution.py:25
  269.8 1.9 collective-permute-start.4
  271.7 1.9 fusion.17
  273.7 3.8 %collective-permute-start.5 = (bf16[1024,512]{1,0:T(8,128)(2,1)S(1)}, bf16[1024,512]{1,0:T(8,128)(2,1)S(1)}, u32[]{:S(2)}, u32[]{:S(2)}) collective-permute-start(bf16[1024,512]{1,0:T(8,128)(2,1)S(1)} %collective-permute-done.3), channel_id=1, source_target_pairs={{62,0},{0,2},{2,4},{4,6},{6,8},{8,10},{10,12},{12,14},{14,16},{16,... | collective-permute-start | bytes 3145736 | tf_op jit(solution)/shard_map/ppermute | solution.py:25
  277.5 0.7 fusion.18
  278.2 0.7 fusion.19
  278.9 0.5 copy-done.4
  279.4 0.7 fusion.20
  280.1 17.3 %collective-permute-done.4 = bf16[1024,512]{1,0:T(8,128)(2,1)S(1)} collective-permute-done((bf16[1024,512]{1,0:T(8,128)(2,1)S(1)}, bf16[1024,512]{1,0:T(8,128)(2,1)S(1)}, u32[]{:S(2)}, u32[]{:S(2)}) %collective-permute-start.4) | collective-permute-done | bytes 1048608 | tf_op jit(solution)/shard_map/ppermute | solution.py:25
  297.4 0.7 fusion.21
  298.2 1.0 add_add_fusion
  299.4 0.4 fusion.15
  300.0 0.6 copy.49
  (83 shorter events, 2.1 us)
Async XLA Ops:
  0.6 137.0 %copy-start = (bf16[1,5,512,512]{3,2,1,0:T(8,128)(2,1)S(1)}, bf16[1,5,512,512]{3,2,1,0:T(8,128)(2,1)}, u32[]{:S(2)}) copy-start(bf16[1,5,512,512]{3,2,1,0:T(8,128)(2,1)} %param.29) | copy-start | bytes 7864324
  0.6 128.1 %copy-start.8 = (f32[1,5,16,1,512]{4,3,2,1,0:T(1,128)S(1)}, f32[1,5,16,1,512]{4,3,2,1,0:T(1,128)}, u32[]{:S(2)}) copy-start(f32[1,5,16,1,512]{4,3,2,1,0:T(1,128)} %param.25) | copy-start | bytes 491524
  0.7 137.0 %copy-start.19 = (s32[1,5]{1,0:T(1,128)S(1)}, s32[1,5]{1,0:T(1,128)}, u32[]{:S(2)}) copy-start(s32[1,5]{1,0:T(1,128)} %param.28) | copy-start | bytes 64
  121.2 120.7 %collective-permute-start = (bf16[1024,512]{1,0:T(8,128)(2,1)}, bf16[1024,512]{1,0:T(8,128)(2,1)}, u32[]{:S(2)}, u32[]{:S(2)}) collective-permute-start(bf16[1024,512]{1,0:T(8,128)(2,1)} %fusion.14), channel_id=1, source_target_pairs={{2,0},{4,2},{6,4},{8,6},{10,8},{12,10},{14,12},{16,14},{18,16},{20... | collective-permute-start | bytes 3145736 | tf_op jit(solution)/shard_map/ppermute | solution.py:25
  123.9 33.9 %collective-permute-start.15 = (f32[1,16,1,1]{3,1,2,0:T(8,128)S(1)}, f32[1,16,1,1]{3,1,2,0:T(8,128)S(1)}, u32[]{:S(2)}, u32[]{:S(2)}) collective-permute-start(f32[1,16,1,1]{3,1,2,0:T(8,128)S(1)} %get-tuple-element.27), channel_id=1, source_target_pairs={{0,2},{2,4},{4,6},{6,8},{8,10},{10,12},{12,14},{14,16},{16,18},{18... | collective-permute-start | bytes 200 | tf_op jit(solution)/shard_map/ppermute | solution.py:16
  126.8 32.9 %collective-permute-start.16 = (f32[1,16,1,1]{3,1,2,0:T(8,128)S(1)}, f32[1,16,1,1]{3,1,2,0:T(8,128)S(1)}, u32[]{:S(2)}, u32[]{:S(2)}) collective-permute-start(f32[1,16,1,1]{3,1,2,0:T(8,128)S(1)} %get-tuple-element.28), channel_id=1, source_target_pairs={{2,0},{4,2},{6,4},{8,6},{10,8},{12,10},{14,12},{16,14},{18,16},{20... | collective-permute-start | bytes 200 | tf_op jit(solution)/shard_map/ppermute | solution.py:17
  128.9 45.6 %collective-permute-start.19 = (f32[5,16,1,2]{3,1,2,0:T(8,128)S(1)}, f32[5,16,1,2]{3,1,2,0:T(8,128)S(1)}, u32[]{:S(2)}, u32[]{:S(2)}) collective-permute-start(f32[5,16,1,2]{3,1,2,0:T(8,128)S(1)} %get-tuple-element.14), channel_id=1, source_target_pairs={{0,2},{2,4},{4,6},{6,8},{8,10},{10,12},{12,14},{14,16},{16,18},{18... | collective-permute-start | bytes 1928 | tf_op jit(solution)/shard_map/ppermute | solution.py:16
  132.5 49.9 %collective-permute-start.20 = (f32[5,16,1,2]{3,1,2,0:T(8,128)S(1)}, f32[5,16,1,2]{3,1,2,0:T(8,128)S(1)}, u32[]{:S(2)}, u32[]{:S(2)}) collective-permute-start(f32[5,16,1,2]{3,1,2,0:T(8,128)S(1)} %get-tuple-element.15), channel_id=1, source_target_pairs={{2,0},{4,2},{6,4},{8,6},{10,8},{12,10},{14,12},{16,14},{18,16},{20... | collective-permute-start | bytes 1928 | tf_op jit(solution)/shard_map/ppermute | solution.py:17
  155.6 2.0 copy-start.10
  155.6 2.0 copy-start.11
  155.6 2.0 copy-start.14
  155.6 2.0 copy-start.15
  155.6 2.0 copy-start.16
  155.6 2.0 copy-start.17
  155.6 2.0 copy-start.18
  157.8 9.6 %collective-permute-start.6 = (f32[1,16,1,1]{3,1,2,0:T(8,128)S(1)}, f32[1,16,1,1]{3,1,2,0:T(8,128)S(1)}, u32[]{:S(2)}, u32[]{:S(2)}) collective-permute-start(f32[1,16,1,1]{3,1,2,0:T(8,128)S(1)} %get-tuple-element.38), channel_id=1, source_target_pairs={{0,2},{2,4},{4,6},{6,8},{8,10},{10,12},{12,14},{14,16},{16,18},{18... | collective-permute-start | bytes 200 | tf_op jit(solution)/shard_map/ppermute | solution.py:16
  159.7 13.4 %collective-permute-start.7 = (f32[1,16,1,1]{3,1,2,0:T(8,128)S(1)}, f32[1,16,1,1]{3,1,2,0:T(8,128)S(1)}, u32[]{:S(2)}, u32[]{:S(2)}) collective-permute-start(f32[1,16,1,1]{3,1,2,0:T(8,128)S(1)} %get-tuple-element.39), channel_id=1, source_target_pairs={{2,0},{4,2},{6,4},{8,6},{10,8},{12,10},{14,12},{16,14},{18,16},{20... | collective-permute-start | bytes 200 | tf_op jit(solution)/shard_map/ppermute | solution.py:17
  167.4 16.5 %collective-permute-start.17 = (f32[1,16,1,514]{3,1,2,0:T(8,128)S(1)}, f32[1,16,1,514]{3,1,2,0:T(8,128)S(1)}, u32[]{:S(2)}, u32[]{:S(2)}) collective-permute-start(f32[1,16,1,514]{3,1,2,0:T(8,128)S(1)} %pad_maximum_fusion.7), channel_id=1, source_target_pairs={{0,1},{2,3},{4,5},{6,7},{8,9},{10,11},{12,13},{14,15},{16,17},{18,... | collective-permute-start | bytes 98696 | tf_op jit(solution)/shard_map/ppermute | solution.py:16
  173.1 18.7 %collective-permute-start.18 = (f32[1,16,1,514]{3,1,2,0:T(8,128)S(1)}, f32[1,16,1,514]{3,1,2,0:T(8,128)S(1)}, u32[]{:S(2)}, u32[]{:S(2)}) collective-permute-start(f32[1,16,1,514]{3,1,2,0:T(8,128)S(1)} %pad_maximum_fusion.7), channel_id=1, source_target_pairs={{1,0},{3,2},{5,4},{7,6},{9,8},{11,10},{13,12},{15,14},{17,16},{19,... | collective-permute-start | bytes 98696 | tf_op jit(solution)/shard_map/ppermute | solution.py:17
  174.5 18.7 %collective-permute-start.8 = (f32[1,16,1,514]{3,1,2,0:T(8,128)S(1)}, f32[1,16,1,514]{3,1,2,0:T(8,128)S(1)}, u32[]{:S(2)}, u32[]{:S(2)}) collective-permute-start(f32[1,16,1,514]{3,1,2,0:T(8,128)S(1)} %pad_maximum_fusion.5), channel_id=1, source_target_pairs={{0,1},{2,3},{4,5},{6,7},{8,9},{10,11},{12,13},{14,15},{16,17},{18,... | collective-permute-start | bytes 98696 | tf_op jit(solution)/shard_map/ppermute | solution.py:16
  182.4 12.7 %collective-permute-start.9 = (f32[1,16,1,514]{3,1,2,0:T(8,128)S(1)}, f32[1,16,1,514]{3,1,2,0:T(8,128)S(1)}, u32[]{:S(2)}, u32[]{:S(2)}) collective-permute-start(f32[1,16,1,514]{3,1,2,0:T(8,128)S(1)} %pad_maximum_fusion.5), channel_id=1, source_target_pairs={{1,0},{3,2},{5,4},{7,6},{9,8},{11,10},{13,12},{15,14},{17,16},{19,... | collective-permute-start | bytes 98696 | tf_op jit(solution)/shard_map/ppermute | solution.py:17
  183.8 13.2 %collective-permute-start.21 = (f32[5,16,1,516]{3,1,2,0:T(8,128)S(1)}, f32[5,16,1,516]{3,1,2,0:T(8,128)S(1)}, u32[]{:S(2)}, u32[]{:S(2)}) collective-permute-start(f32[5,16,1,516]{3,1,2,0:T(8,128)S(1)} %pad_maximum_fusion.4), channel_id=1, source_target_pairs={{0,1},{2,3},{4,5},{6,7},{8,9},{10,11},{12,13},{14,15},{16,17},{18,... | collective-permute-start | bytes 495368 | tf_op jit(solution)/shard_map/ppermute | solution.py:16
  191.8 10.6 %collective-permute-start.22 = (f32[5,16,1,516]{3,1,2,0:T(8,128)S(1)}, f32[5,16,1,516]{3,1,2,0:T(8,128)S(1)}, u32[]{:S(2)}, u32[]{:S(2)}) collective-permute-start(f32[5,16,1,516]{3,1,2,0:T(8,128)S(1)} %pad_maximum_fusion.4), channel_id=1, source_target_pairs={{1,0},{3,2},{5,4},{7,6},{9,8},{11,10},{13,12},{15,14},{17,16},{19,... | collective-permute-start | bytes 495368 | tf_op jit(solution)/shard_map/ppermute | solution.py:17
  193.1 56.5 %collective-permute-start.1 = (bf16[1024,512]{1,0:T(8,128)(2,1)}, bf16[1024,512]{1,0:T(8,128)(2,1)S(1)}, u32[]{:S(2)}, u32[]{:S(2)}) collective-permute-start(bf16[1024,512]{1,0:T(8,128)(2,1)} %fusion.14), channel_id=1, source_target_pairs={{62,0},{0,2},{2,4},{4,6},{6,8},{8,10},{10,12},{12,14},{14,16},{16,... | collective-permute-start | bytes 3145736 | tf_op jit(solution)/shard_map/ppermute | solution.py:25
  195.2 58.1 %copy-start.7 = (bf16[1,512,512]{2,0,1:T(2,128)(2,1)S(1)}, bf16[1,512,512]{2,0,1:T(2,128)(2,1)}, u32[]{:S(2)}) copy-start(bf16[1,512,512]{2,0,1:T(2,128)(2,1)} %fusion.12) | copy-start | bytes 1572868
  202.8 16.1 %collective-permute-start.10 = (f32[1,16,1,1]{3,1,2,0:T(8,128)S(1)}, f32[1,16,1,1]{3,1,2,0:T(8,128)S(1)}, u32[]{:S(2)}, u32[]{:S(2)}) collective-permute-start(f32[1,16,1,1]{3,1,2,0:T(8,128)S(1)} %get-tuple-element.36), channel_id=1, source_target_pairs={{0,2},{2,4},{4,6},{6,8},{8,10},{10,12},{12,14},{14,16},{16,18},{18... | collective-permute-start | bytes 200 | tf_op jit(solution)/shard_map/ppermute | solution.py:16
  207.7 18.8 %collective-permute-start.11 = (f32[1,16,1,1]{3,1,2,0:T(8,128)S(1)}, f32[1,16,1,1]{3,1,2,0:T(8,128)S(1)}, u32[]{:S(2)}, u32[]{:S(2)}) collective-permute-start(f32[1,16,1,1]{3,1,2,0:T(8,128)S(1)} %get-tuple-element.37), channel_id=1, source_target_pairs={{2,0},{4,2},{6,4},{8,6},{10,8},{12,10},{14,12},{16,14},{18,16},{20... | collective-permute-start | bytes 200 | tf_op jit(solution)/shard_map/ppermute | solution.py:17
  217.0 14.3 %collective-permute-start.23 = (f32[1,16,1,1]{3,1,2,0:T(8,128)S(1)}, f32[1,16,1,1]{3,1,2,0:T(8,128)S(1)}, u32[]{:S(2)}, u32[]{:S(2)}) collective-permute-start(f32[1,16,1,1]{3,1,2,0:T(8,128)S(1)} %get-tuple-element.23), channel_id=1, source_target_pairs={{0,2},{2,4},{4,6},{6,8},{8,10},{10,12},{12,14},{14,16},{16,18},{18... | collective-permute-start | bytes 200 | tf_op jit(solution)/shard_map/ppermute | solution.py:16
  218.9 13.6 %collective-permute-start.24 = (f32[1,16,1,1]{3,1,2,0:T(8,128)S(1)}, f32[1,16,1,1]{3,1,2,0:T(8,128)S(1)}, u32[]{:S(2)}, u32[]{:S(2)}) collective-permute-start(f32[1,16,1,1]{3,1,2,0:T(8,128)S(1)} %get-tuple-element.24), channel_id=1, source_target_pairs={{2,0},{4,2},{6,4},{8,6},{10,8},{12,10},{14,12},{16,14},{18,16},{20... | collective-permute-start | bytes 200 | tf_op jit(solution)/shard_map/ppermute | solution.py:17
  226.6 14.0 %collective-permute-start.12 = (f32[1,16,1,514]{3,1,2,0:T(8,128)S(1)}, f32[1,16,1,514]{3,1,2,0:T(8,128)S(1)}, u32[]{:S(2)}, u32[]{:S(2)}) collective-permute-start(f32[1,16,1,514]{3,1,2,0:T(8,128)S(1)} %pad_maximum_fusion.6), channel_id=1, source_target_pairs={{0,1},{2,3},{4,5},{6,7},{8,9},{10,11},{12,13},{14,15},{16,17},{18,... | collective-permute-start | bytes 98696 | tf_op jit(solution)/shard_map/ppermute | solution.py:16
  231.3 10.6 %collective-permute-start.13 = (f32[1,16,1,514]{3,1,2,0:T(8,128)S(1)}, f32[1,16,1,514]{3,1,2,0:T(8,128)S(1)}, u32[]{:S(2)}, u32[]{:S(2)}) collective-permute-start(f32[1,16,1,514]{3,1,2,0:T(8,128)S(1)} %pad_maximum_fusion.6), channel_id=1, source_target_pairs={{1,0},{3,2},{5,4},{7,6},{9,8},{11,10},{13,12},{15,14},{17,16},{19,... | collective-permute-start | bytes 98696 | tf_op jit(solution)/shard_map/ppermute | solution.py:17
  232.6 14.2 %collective-permute-start.25 = (f32[1,16,1,514]{3,1,2,0:T(8,128)S(1)}, f32[1,16,1,514]{3,1,2,0:T(8,128)S(1)}, u32[]{:S(2)}, u32[]{:S(2)}) collective-permute-start(f32[1,16,1,514]{3,1,2,0:T(8,128)S(1)} %pad_maximum_fusion.8), channel_id=1, source_target_pairs={{0,1},{2,3},{4,5},{6,7},{8,9},{10,11},{12,13},{14,15},{16,17},{18,... | collective-permute-start | bytes 98696 | tf_op jit(solution)/shard_map/ppermute | solution.py:16
  240.5 8.8 %collective-permute-start.26 = (f32[1,16,1,514]{3,1,2,0:T(8,128)S(1)}, f32[1,16,1,514]{3,1,2,0:T(8,128)S(1)}, u32[]{:S(2)}, u32[]{:S(2)}) collective-permute-start(f32[1,16,1,514]{3,1,2,0:T(8,128)S(1)} %pad_maximum_fusion.8), channel_id=1, source_target_pairs={{1,0},{3,2},{5,4},{7,6},{9,8},{11,10},{13,12},{15,14},{17,16},{19,... | collective-permute-start | bytes 98696 | tf_op jit(solution)/shard_map/ppermute | solution.py:17
  241.9 27.9 %collective-permute-start.2 = (bf16[1024,512]{1,0:T(8,128)(2,1)}, bf16[1024,512]{1,0:T(8,128)(2,1)S(1)}, u32[]{:S(2)}, u32[]{:S(2)}) collective-permute-start(bf16[1024,512]{1,0:T(8,128)(2,1)} %collective-permute-done), channel_id=1, source_target_pairs={{2,0},{4,2},{6,4},{8,6},{10,8},{12,10},{14,12},{16,14},{18,16},{20... | collective-permute-start | bytes 3145736 | tf_op jit(solution)/shard_map/ppermute | solution.py:25
  249.7 24.0 %collective-permute-start.3 = (bf16[1024,512]{1,0:T(8,128)(2,1)S(1)}, bf16[1024,512]{1,0:T(8,128)(2,1)S(1)}, u32[]{:S(2)}, u32[]{:S(2)}) collective-permute-start(bf16[1024,512]{1,0:T(8,128)(2,1)S(1)} %collective-permute-done.1), channel_id=1, source_target_pairs={{62,0},{0,2},{2,4},{4,6},{6,8},{8,10},{10,12},{12,14},{14,16},{16,... | collective-permute-start | bytes 3145736 | tf_op jit(solution)/shard_map/ppermute | solution.py:25
  251.8 10.0 %copy-start.9 = (f32[1,16,1,512]{3,2,1,0:T(1,128)S(1)}, f32[1,16,1,512]{3,2,1,0:T(1,128)}, u32[]{:S(2)}) copy-start(f32[1,16,1,512]{3,2,1,0:T(1,128)} %param.21) | copy-start | bytes 98308
  251.8 10.0 %copy-start.12 = (f32[1,16,1,512]{3,2,1,0:T(1,128)S(1)}, f32[1,16,1,512]{3,2,1,0:T(1,128)}, u32[]{:S(2)}) copy-start(f32[1,16,1,512]{3,2,1,0:T(1,128)} %param.20) | copy-start | bytes 98308
  251.8 19.9 %copy-start.5 = (bf16[1,512,512]{2,0,1:T(2,128)(2,1)S(1)}, bf16[1,512,512]{2,0,1:T(2,128)(2,1)}, u32[]{:S(2)}) copy-start(bf16[1,512,512]{2,0,1:T(2,128)(2,1)} %fusion.10) | copy-start | bytes 1572868
  251.8 10.0 %collective-permute-start.27 = (bf16[1,16,1,512]{3,2,1,0:T(2,128)(2,1)S(1)}, bf16[1,16,1,512]{3,2,1,0:T(2,128)(2,1)S(1)}, u32[]{:S(2)}, u32[]{:S(2)}) collective-permute-start(bf16[1,16,1,512]{3,2,1,0:T(2,128)(2,1)S(1)} %convert_element_type.106), channel_id=1, source_target_pairs={{64,0},{128,64},{192,128},{256,192},{320,256},{384,320},{448,384},... | collective-permute-start | bytes 49160 | tf_op jit(solution)/shard_map/ppermute | solution.py:31
  255.2 22.3 %copy-start.6 = (bf16[1,512,512]{2,0,1:T(2,128)(2,1)S(1)}, bf16[1,512,512]{2,0,1:T(2,128)(2,1)}, u32[]{:S(2)}) copy-start(bf16[1,512,512]{2,0,1:T(2,128)(2,1)} %fusion.8) | copy-start | bytes 1572868
  257.8 42.0 %collective-permute-start.14 = (bf16[1,16,1,512]{3,1,2,0:T(8,128)(2,1)S(1)}, bf16[1,16,1,512]{3,1,2,0:T(8,128)(2,1)S(1)}, u32[]{:S(2)}, u32[]{:S(2)}) collective-permute-start(bf16[1,16,1,512]{3,1,2,0:T(8,128)(2,1)S(1)} %get-tuple-element.22), channel_id=1, source_target_pairs={{0,64},{64,128},{128,192},{192,256},{256,320},{320,384},{384,448},... | collective-permute-start | bytes 49160 | tf_op jit(solution)/shard_map/ppermute | solution.py:31
  269.8 27.6 %collective-permute-start.4 = (bf16[1024,512]{1,0:T(8,128)(2,1)S(1)}, bf16[1024,512]{1,0:T(8,128)(2,1)S(1)}, u32[]{:S(2)}, u32[]{:S(2)}) collective-permute-start(bf16[1024,512]{1,0:T(8,128)(2,1)S(1)} %collective-permute-done.2), channel_id=1, source_target_pairs={{2,0},{4,2},{6,4},{8,6},{10,8},{12,10},{14,12},{16,14},{18,16},{20... | collective-permute-start | bytes 3145736 | tf_op jit(solution)/shard_map/ppermute | solution.py:25
  273.7 4.5 %copy-start.3 = (bf16[1,512,512]{2,0,1:T(2,128)(2,1)S(1)}, bf16[1,512,512]{2,0,1:T(2,128)(2,1)}, u32[]{:S(2)}) copy-start(bf16[1,512,512]{2,0,1:T(2,128)(2,1)} %fusion.6) | copy-start | bytes 1572868
  273.7 24.5 %collective-permute-start.5 = (bf16[1024,512]{1,0:T(8,128)(2,1)S(1)}, bf16[1024,512]{1,0:T(8,128)(2,1)S(1)}, u32[]{:S(2)}, u32[]{:S(2)}) collective-permute-start(bf16[1024,512]{1,0:T(8,128)(2,1)S(1)} %collective-permute-done.3), channel_id=1, source_target_pairs={{62,0},{0,2},{2,4},{4,6},{6,8},{8,10},{10,12},{12,14},{14,16},{16,... | collective-permute-start | bytes 3145736 | tf_op jit(solution)/shard_map/ppermute | solution.py:25
  278.2 1.2 copy-start.4
  279.4 18.0 %copy-start.2 = (bf16[1,512,512]{2,0,1:T(2,128)(2,1)S(1)}, bf16[1,512,512]{2,0,1:T(2,128)(2,1)}, u32[]{:S(2)}) copy-start(bf16[1,512,512]{2,0,1:T(2,128)(2,1)} %fusion.2) | copy-start | bytes 1572868
  298.2 1.2 copy-start.1
  299.2 0.8 copy-start.13
where the time goes:
time: 302 us; the launch traced here: 301 us
  starting transfers between devices  109 us (36%)
  blocking collectives  106 us (35%)
  waiting for transfers between devices  34.3 us (11%)
  matrix products  27.6 us (9%)
  other arithmetic  11.9 us (4%)
  between operations  6.65 us (2%)
  local copies, waits for them, and re-layouts  4.67 us (2%)
    psum x1, blocking collectives, local(): lax.psum((resid_local, search_local), ('win', 'lon', 'lat'))  106 us
    ppermute x10, starting transfers between devices, extended_2(): before = lax.ppermute(last, axis, up)  49.4 us
    ppermute x10, starting transfers between devices, extended_2(): after = lax.ppermute(leading, axis, down)  37.7 us
    ppermute x6, waiting for transfers between devices, passed_along(): return lax.ppermute(block, axis, route)  24.6 us
    dot_general x7, matrix products, weight_for(): jnp.einsum('j,jpq->pq', match, tiles, preferred_element_type=jnp.float32)  19.9 us
    ppermute x6, starting transfers between devices, passed_along(): return lax.ppermute(block, axis, route)  17 us
    ppermute x10, waiting for transfers between devices, extended_2(): after = lax.ppermute(leading, axis, down)  7.86 us
  transfers between devices with their start and end apart: 28, of which 5 were waited for; matrix products, arithmetic and copies ran while one was open for 11% of the time, Pallas kernels for 0%

commit v1 on v0

v1 whole, which is shorter than its diff:
```python
import jax
import jax.numpy as jnp
from jax import lax
from jax.sharding import PartitionSpec as P

REACH = 3


def from_offset(value, axis, distance):
    count = lax.axis_size(axis)
    return lax.ppermute(value, axis, [((i + distance) % count, i) for i in range(count)])


def shifted(value, axis, steps):
    count = lax.axis_size(axis)
    leading, last = (max(0, -steps), min(count, count - steps))
    return lax.ppermute(value, axis, [(source, source + steps) for source in range(leading, last)])


def lon_extended(packed, width):
    left = from_offset(packed[..., -width:], "lon", -1)
    right = from_offset(packed[..., :width], "lon", 1)
    return jnp.concatenate([left, packed, right], axis=-1)


def lat_partner(value):
    return lax.ppermute(value, "lat", [(0, 1), (1, 0)])


def forward_pair(f_a, f_b, c_a, cn_a):
    return (
        (0.5 + c_a[0, :, 1:-1]) * f_a[:, 1:-1]
        + c_a[1, :, 1:-1] * f_a[:, 2:]
        + c_a[2, :, 1:-1] * f_a[:, :-2]
        + cn_a[:, 1:-1] * f_b[:, 1:-1]
    )


def adjoint_pair(f_a, f_b, c_a, ca_a):
    return (
        (0.5 + c_a[0, :, 1:-1]) * f_a[:, 1:-1]
        + (c_a[1] * f_a)[:, :-2]
        + (c_a[2] * f_a)[:, 2:]
        + ca_a[:, 1:-1] * f_b[:, 1:-1]
    )


def propagate_both(own, other, first_row):
    u_a, w_a, c_a = own[0], own[1], own[2:]
    u_b, w_b, c_b = other[0], other[1], other[2:]
    cn_a = jnp.where(first_row, c_a[3], c_a[4])
    cn_b = jnp.where(first_row, c_b[4], c_b[3])
    ca_a = jnp.where(first_row, c_b[4], c_b[3])
    ca_b = jnp.where(first_row, c_a[3], c_a[4])
    s_a = forward_pair(u_a, u_b, c_a, cn_a)
    s_b = forward_pair(u_b, u_a, c_b, cn_b)
    moved = forward_pair(s_a, s_b, c_a[:, :, 1:-1], cn_a[:, 1:-1])
    t_a = adjoint_pair(w_a, w_b, c_a, ca_a)
    t_b = adjoint_pair(w_b, w_a, c_b, ca_b)
    backed = adjoint_pair(t_a, t_b, c_a[:, :, 1:-1], ca_a[:, 1:-1])
    return moved, backed


def localize(members, search, loc_cols, loc_vals):
    count_members = members.shape[0]
    block = members.shape[-1]
    products = (members.astype(jnp.float32) * search[None]).astype(jnp.bfloat16)
    flat = products.reshape(-1, block)
    bands = lax.axis_size("lon")
    here = lax.axis_index("lon")
    columns = loc_cols[0]
    tiles = loc_vals[0]
    offsets = [0]
    for distance in range(1, REACH + 1):
        offsets += [distance, -distance]
    sources = {0: flat}
    for offset in offsets[1:]:
        sources[offset] = from_offset(flat, "lon", offset)

    def weight_for(offset):
        target = (here + offset + bands) % bands
        match = columns == target
        picked = tiles[jnp.argmax(match)]
        return jnp.where(jnp.any(match), picked, jnp.zeros_like(picked))

    total = jnp.dot(flat, weight_for(0), preferred_element_type=jnp.float32)
    for offset in offsets[1:]:
        total = total + jnp.dot(sources[offset], weight_for(offset), preferred_element_type=jnp.float32)
    spread = total.reshape(products.shape)
    return jnp.sum(members.astype(jnp.float32) * spread, axis=0) / (count_members - 1)


def local(
    dual_state,
    dual_obs,
    increment,
    resid_dual,
    resid_obs,
    resid_incr,
    search_dual,
    search_obs,
    search_incr,
    ensemble,
    tangent_coefs,
    obs_weight,
    obs_var,
    loc_cols,
    loc_vals,
):
    resid_local = (
        jnp.sum(resid_dual * resid_dual)
        + jnp.sum(resid_obs * resid_obs)
        + jnp.sum(resid_incr * resid_incr)
    )
    search_local = (
        jnp.sum(search_dual * search_dual)
        + jnp.sum(search_obs * search_obs)
        + jnp.sum(search_incr * search_incr)
    )
    sums = lax.psum(lax.psum(lax.psum(jnp.stack([resid_local, search_local]), "lat"), "lon"), "win")
    alpha = sums[0] / (sums[1] + 1e-06)

    packed = jnp.concatenate(
        [search_incr[0, :, 0][None], search_dual[0, :, 0][None], tangent_coefs[0, :, :, 0]], axis=0
    )
    own = lon_extended(packed, 2)
    other = lat_partner(own)
    first_row = lax.axis_index("lat") == 0
    moved, backed = propagate_both(own, other, first_row)
    earlier = shifted(moved, "win", 1)[None, :, None]
    following = shifted(backed, "win", -1)[None, :, None]

    covar = localize(ensemble[0, :, :, 0], search_dual[0, :, 0], loc_cols, loc_vals)[None, :, None]
    image_dual = covar + search_incr - earlier
    image_obs = obs_var * search_obs + obs_weight * search_incr
    image_incr = search_dual - following + obs_weight * search_obs
    return (
        dual_state + alpha * search_dual,
        dual_obs + alpha * search_obs,
        increment + alpha * search_incr,
        resid_dual - alpha * image_dual,
        resid_obs - alpha * image_obs,
        resid_incr - alpha * image_incr,
    )


def solution(mesh):
    field = P("win", None, "lat", "lon")
    stacked = P("win", None, None, "lat", "lon")
    placed = (
        field, field, field, field, field, field, field, field, field,
        stacked, stacked, field, field,
        P("lon", None),
        P("lon", None, None, None),
    )
    return jax.shard_map(
        local,
        mesh=mesh,
        in_specs=placed,
        out_specs=(field,) * 6,
        check_vma=False,
    )
```

time: 302 us -> 275 us (0.911)
  the two profiles are of different devices: /device:TPU:1 before, /device:TPU:2 now
where the time goes in v1:
time: 275 us; the launch traced here: 274 us
  blocking collectives  89 us (32%)
  waiting for transfers between devices  86.3 us (31%)
  starting transfers between devices  39.8 us (14%)
  between operations  19.8 us (7%)
  other arithmetic  19.5 us (7%)
  matrix products  14.7 us (5%)
  local copies, waits for them, and re-layouts  4.86 us (2%)
    psum x1, blocking collectives, local(): lax.psum(lax.psum(jnp.stack([resid_local, search_local]), 'lat'), 'lon')  59.5 us
    ppermute x8, waiting for transfers between devices, from_offset(): lax.ppermute(value, axis, [((i + distance) % count, i) for i in range(cou...  50.5 us
    ppermute x1, waiting for transfers between devices, lat_partner(): return lax.ppermute(value, 'lat', [(0, 1), (1, 0)])  31.5 us
    ppermute x8, starting transfers between devices, from_offset(): lax.ppermute(value, axis, [((i + distance) % count, i) for i in range(cou...  28.6 us
    psum x1, blocking collectives, local(): lax.psum(lax.psum(lax.psum(jnp.stack([resid_local, search_local]), 'lat')...  17.6 us
    dot_general x6, matrix products, localize(): jnp.dot(sources[offset], weight_for(offset), preferred_element_type=jnp.f...  12 us
    psum x1, blocking collectives, local(): lax.psum(jnp.stack([resid_local, search_local]), 'lat')  11.9 us
    ppermute x1, starting transfers between devices, lat_partner(): return lax.ppermute(value, 'lat', [(0, 1), (1, 0)])  7.85 us
  transfers between devices with their start and end apart: 11, of which 4 were waited for; matrix products, arithmetic and copies ran while one was open for 10% of the time, Pallas kernels for 0%

profile of v1, /device:TPU:2, one launch (start us, length us, event | category | flops | bytes accessed | tf_op | source)
XLA Modules:
  0.0 273.9 jit_solution(9785465574743663310)
XLA Ops:
  0.7 1.5 multiply_reduce_fusion.3
  2.2 1.4 multiply_reduce_fusion
  3.6 1.4 multiply_reduce_fusion.4
  7.0 1.5 multiply_reduce_fusion.1
  10.4 0.1 pad_maximum_fusion.4
  10.5 11.9 %psum.21 = f32[2]{0:T(128)S(1)} all-reduce(f32[2]{0:T(128)S(1)} %pad_maximum_fusion.4), channel_id=1, replica_groups=mesh['win'=8,'lon'=32,'lat'=2] {'lat'}, use_global_device_ids=true, to_apply=%region_6.0 | all-reduce | flops 2 | bytes 16 | tf_op jit(solution)/shard_map/psum | solution.py:120
  22.4 59.5 %psum.22 = f32[2]{0:T(128)S(1)} all-reduce(f32[2]{0:T(128)S(1)} %psum.21), channel_id=1, replica_groups=mesh['win'=8,'lon'=32,'lat'=2] {'lon'}, use_global_device_ids=true, to_apply=%region_7.0 | all-reduce | flops 2 | bytes 16 | tf_op jit(solution)/shard_map/psum | solution.py:120
  81.9 17.6 %psum.23 = f32[2]{0:T(128)S(1)} all-reduce(f32[2]{0:T(128)S(1)} %psum.22), channel_id=1, replica_groups=mesh['win'=8,'lon'=32,'lat'=2] {'win'}, use_global_device_ids=true, to_apply=%region_8.0 | all-reduce | flops 2 | bytes 16 | tf_op jit(solution)/shard_map/psum | solution.py:120
  99.5 0.6 fusion.92
  101.4 0.8 copy_bitcast_fusion.4
  102.2 2.4 fusion
  104.6 1.9 collective-permute-start.2
  106.5 1.9 collective-permute-start.1
  108.5 6.3 %collective-permute-start = (bf16[1024,512]{1,0:T(8,128)(2,1)}, bf16[1024,512]{1,0:T(8,128)(2,1)}, u32[]{:S(2)}, u32[]{:S(2)}) collective-permute-start(bf16[1024,512]{1,0:T(8,128)(2,1)} %fusion), channel_id=1, source_target_pairs={{2,0},{4,2},{6,4},{8,6},{10,8},{12,10},{14,12},{16,14},{18,16},{20... | collective-permute-start | bytes 3145736 | tf_op jit(solution)/shard_map/ppermute | solution.py:11
  114.9 0.7 pad_maximum_fusion.3
  115.6 1.9 collective-permute-start.6
  117.5 6.3 %collective-permute-start.7 = (f32[7,16,2]{2,1,0:T(8,128)}, f32[7,16,2]{2,1,0:T(8,128)}, u32[]{:S(2)}, u32[]{:S(2)}) collective-permute-start(f32[7,16,2]{2,1,0:T(8,128)} %get-tuple-element.51), channel_id=1, source_target_pairs={{2,0},{4,2},{6,4},{8,6},{10,8},{12,10},{14,12},{16,14},{18,16},{20... | collective-permute-start | bytes 2696 | tf_op jit(solution)/shard_map/ppermute | solution.py:11
  123.9 0.7 bitcast_reduce_fusion.3
  126.0 0.7 bitcast_reduce_fusion.4
  127.8 0.7 bitcast_reduce_fusion.5
  129.8 0.7 bitcast_reduce_fusion.6
  131.7 1.2 fusion.1
  133.0 0.7 bitcast_reduce_fusion.1
  133.6 0.7 bitcast_reduce_fusion.2
  134.3 0.8 compare_reduce_fusion
  135.1 0.7 bitcast_reduce_fusion
  137.1 2.7 fusion.17
  143.1 0.6 copy.38
  147.6 6.4 %collective-permute-start.4 = (bf16[1024,512]{1,0:T(8,128)(2,1)}, bf16[1024,512]{1,0:T(8,128)(2,1)S(1)}, u32[]{:S(2)}, u32[]{:S(2)}) collective-permute-start(bf16[1024,512]{1,0:T(8,128)(2,1)} %fusion), channel_id=1, source_target_pairs={{6,0},{8,2},{10,4},{12,6},{14,8},{16,10},{18,12},{20,14},{22,16},{... | collective-permute-start | bytes 3145736 | tf_op jit(solution)/shard_map/ppermute | solution.py:11
  154.0 1.0 pad_maximum_fusion
  155.1 7.8 %collective-permute-start.8 = (f32[7,16,516]{2,1,0:T(8,128)S(1)}, f32[7,16,516]{2,1,0:T(8,128)S(1)}, u32[]{:S(2)}, u32[]{:S(2)}) collective-permute-start(f32[7,16,516]{2,1,0:T(8,128)S(1)} %pad_maximum_fusion), channel_id=1, source_target_pairs={{0,1},{1,0},{2,3},{3,2},{4,5},{5,4},{6,7},{7,6},{8,9},{9,8},{10,11... | collective-permute-start | bytes 693512 | tf_op jit(solution)/shard_map/ppermute | solution.py:27
  162.9 0.1 slice.250
  163.0 0.1 slice.281
  163.1 0.1 slice_bitcast_fusion.10
  163.2 31.5 %collective-permute-done.8 = f32[7,16,516]{2,1,0:T(8,128)S(1)} collective-permute-done((f32[7,16,516]{2,1,0:T(8,128)S(1)}, f32[7,16,516]{2,1,0:T(8,128)S(1)}, u32[]{:S(2)}, u32[]{:S(2)}) %collective-permute-start.8) | collective-permute-done | bytes 231200 | tf_op jit(solution)/shard_map/ppermute | solution.py:27
  194.7 0.2 fusion.48
  194.9 0.1 fusion.91
  195.0 0.1 fusion.51
  195.1 0.1 slice.271
  195.2 0.1 slice.259
  195.3 0.1 slice.300
  195.3 0.2 fusion.59
  195.5 1.3 collective-permute-start.10
  196.8 0.2 fusion.66
  197.0 4.3 %collective-permute-done.10 = f32[16,512]{1,0:T(8,128)S(1)} collective-permute-done((f32[16,512]{1,0:T(8,128)S(1)}, f32[16,512]{1,0:T(8,128)S(1)}, u32[]{:S(2)}, u32[]{:S(2)}) %collective-permute-start.10) | collective-permute-done | bytes 32800 | tf_op jit(solution)/shard_map/ppermute | solution.py:17
  201.3 1.9 collective-permute-start.3
  203.3 0.7 multiply_subtract_fusion
  204.0 1.9 collective-permute-start.5
  205.9 2.6 fusion.11
  208.5 2.0 collective-permute-start.9
  210.5 2.6 fusion.13
  213.1 2.5 fusion.15
  215.6 1.4 fusion.7
  217.0 19.1 %collective-permute-done.3 = bf16[1024,512]{1,0:T(8,128)(2,1)S(1)} collective-permute-done((bf16[1024,512]{1,0:T(8,128)(2,1)}, bf16[1024,512]{1,0:T(8,128)(2,1)S(1)}, u32[]{:S(2)}, u32[]{:S(2)}) %collective-permute-start.3) | collective-permute-done | bytes 1048608 | tf_op jit(solution)/shard_map/ppermute | solution.py:11
  236.1 1.4 fusion.9
  237.5 31.4 %collective-permute-done.5 = bf16[1024,512]{1,0:T(8,128)(2,1)S(1)} collective-permute-done((bf16[1024,512]{1,0:T(8,128)(2,1)}, bf16[1024,512]{1,0:T(8,128)(2,1)S(1)}, u32[]{:S(2)}, u32[]{:S(2)}) %collective-permute-start.5) | collective-permute-done | bytes 1048608 | tf_op jit(solution)/shard_map/ppermute | solution.py:11
  268.8 1.6 add_add_fusion
  270.5 0.4 fusion.2
  270.9 0.3 copy-done.6
  271.3 0.0 copy-done.12
  271.4 0.6 copy.39
  272.0 0.6 copy.40
  272.6 0.6 copy.41
  273.3 0.6 copy.42
  (39 shorter events, 0.2 us)
Async XLA Ops:
  0.6 114.2 %copy-start.3 = (f32[1,16,1,512]{3,2,1,0:T(1,128)S(1)}, f32[1,16,1,512]{3,2,1,0:T(1,128)}, u32[]{:S(2)}) copy-start(f32[1,16,1,512]{3,2,1,0:T(1,128)} %param.23) | copy-start | bytes 98308
  0.6 131.1 %copy-start = (bf16[1,64,16,1,512]{4,2,3,1,0:T(8,128)(2,1)S(1)}, bf16[1,64,16,1,512]{4,2,3,1,0:T(8,128)(2,1)}, u32[]{:S(2)}) copy-start(bf16[1,64,16,1,512]{4,2,3,1,0:T(8,128)(2,1)} %param.24) | copy-start | bytes 3145732
  0.7 114.2 %copy-start.2 = (f32[1,5,16,1,512]{4,3,2,1,0:T(1,128)S(1)}, f32[1,5,16,1,512]{4,3,2,1,0:T(1,128)}, u32[]{:S(2)}) copy-start(f32[1,5,16,1,512]{4,3,2,1,0:T(1,128)} %param.25) | copy-start | bytes 491524
  0.7 123.2 %copy-start.13 = (s32[1,5]{1,0:T(1,128)S(1)}, s32[1,5]{1,0:T(1,128)}, u32[]{:S(2)}) copy-start(s32[1,5]{1,0:T(1,128)} %param.28) | copy-start | bytes 64
  104.6 99.4 %collective-permute-start.2 = (bf16[1024,512]{1,0:T(8,128)(2,1)}, bf16[1024,512]{1,0:T(8,128)(2,1)}, u32[]{:S(2)}, u32[]{:S(2)}) collective-permute-start(bf16[1024,512]{1,0:T(8,128)(2,1)} %fusion), channel_id=1, source_target_pairs={{4,0},{6,2},{8,4},{10,6},{12,8},{14,10},{16,12},{18,14},{20,16},{2... | collective-permute-start | bytes 3145736 | tf_op jit(solution)/shard_map/ppermute | solution.py:11
  106.5 102.0 %collective-permute-start.1 = (bf16[1024,512]{1,0:T(8,128)(2,1)}, bf16[1024,512]{1,0:T(8,128)(2,1)}, u32[]{:S(2)}, u32[]{:S(2)}) collective-permute-start(bf16[1024,512]{1,0:T(8,128)(2,1)} %fusion), channel_id=1, source_target_pairs={{62,0},{0,2},{2,4},{4,6},{6,8},{8,10},{10,12},{12,14},{14,16},{16,... | collective-permute-start | bytes 3145736 | tf_op jit(solution)/shard_map/ppermute | solution.py:11
  108.5 104.7 %collective-permute-start = (bf16[1024,512]{1,0:T(8,128)(2,1)}, bf16[1024,512]{1,0:T(8,128)(2,1)}, u32[]{:S(2)}, u32[]{:S(2)}) collective-permute-start(bf16[1024,512]{1,0:T(8,128)(2,1)} %fusion), channel_id=1, source_target_pairs={{2,0},{4,2},{6,4},{8,6},{10,8},{12,10},{14,12},{16,14},{18,16},{20... | collective-permute-start | bytes 3145736 | tf_op jit(solution)/shard_map/ppermute | solution.py:11
  115.6 32.1 %collective-permute-start.6 = (f32[7,16,2]{2,1,0:T(8,128)}, f32[7,16,2]{2,1,0:T(8,128)}, u32[]{:S(2)}, u32[]{:S(2)}) collective-permute-start(f32[7,16,2]{2,1,0:T(8,128)} %get-tuple-element.50), channel_id=1, source_target_pairs={{62,0},{0,2},{2,4},{4,6},{6,8},{8,10},{10,12},{12,14},{14,16},{16,... | collective-permute-start | bytes 2696 | tf_op jit(solution)/shard_map/ppermute | solution.py:11
  117.5 36.5 %collective-permute-start.7 = (f32[7,16,2]{2,1,0:T(8,128)}, f32[7,16,2]{2,1,0:T(8,128)}, u32[]{:S(2)}, u32[]{:S(2)}) collective-permute-start(f32[7,16,2]{2,1,0:T(8,128)} %get-tuple-element.51), channel_id=1, source_target_pairs={{2,0},{4,2},{6,4},{8,6},{10,8},{12,10},{14,12},{16,14},{18,16},{20... | collective-permute-start | bytes 2696 | tf_op jit(solution)/shard_map/ppermute | solution.py:11
  147.6 68.0 %collective-permute-start.4 = (bf16[1024,512]{1,0:T(8,128)(2,1)}, bf16[1024,512]{1,0:T(8,128)(2,1)S(1)}, u32[]{:S(2)}, u32[]{:S(2)}) collective-permute-start(bf16[1024,512]{1,0:T(8,128)(2,1)} %fusion), channel_id=1, source_target_pairs={{6,0},{8,2},{10,4},{12,6},{14,8},{16,10},{18,12},{20,14},{22,16},{... | collective-permute-start | bytes 3145736 | tf_op jit(solution)/shard_map/ppermute | solution.py:11
  155.0 48.3 %copy-start.4 = (f32[1,16,1,512]{3,2,1,0:T(1,128)S(1)}, f32[1,16,1,512]{3,2,1,0:T(1,128)}, u32[]{:S(2)}) copy-start(f32[1,16,1,512]{3,2,1,0:T(1,128)} %param.21) | copy-start | bytes 98308
  155.0 48.3 %copy-start.5 = (f32[1,16,1,512]{3,2,1,0:T(1,128)S(1)}, f32[1,16,1,512]{3,2,1,0:T(1,128)}, u32[]{:S(2)}) copy-start(f32[1,16,1,512]{3,2,1,0:T(1,128)} %param.22) | copy-start | bytes 98308
  155.0 48.3 %copy-start.8 = (f32[1,16,1,512]{3,2,1,0:T(1,128)S(1)}, f32[1,16,1,512]{3,2,1,0:T(1,128)}, u32[]{:S(2)}) copy-start(f32[1,16,1,512]{3,2,1,0:T(1,128)} %param.26) | copy-start | bytes 98308
  155.0 48.3 %copy-start.9 = (f32[1,16,1,512]{3,2,1,0:T(1,128)S(1)}, f32[1,16,1,512]{3,2,1,0:T(1,128)}, u32[]{:S(2)}) copy-start(f32[1,16,1,512]{3,2,1,0:T(1,128)} %param.20) | copy-start | bytes 98308
  155.1 50.9 %copy-start.1 = (bf16[1,5,512,512]{3,2,1,0:T(8,128)(2,1)S(1)}, bf16[1,5,512,512]{3,2,1,0:T(8,128)(2,1)}, u32[]{:S(2)}) copy-start(bf16[1,5,512,512]{3,2,1,0:T(8,128)(2,1)} %param.29) | copy-start | bytes 7864324
  155.1 39.6 %collective-permute-start.8 = (f32[7,16,516]{2,1,0:T(8,128)S(1)}, f32[7,16,516]{2,1,0:T(8,128)S(1)}, u32[]{:S(2)}, u32[]{:S(2)}) collective-permute-start(f32[7,16,516]{2,1,0:T(8,128)S(1)} %pad_maximum_fusion), channel_id=1, source_target_pairs={{0,1},{1,0},{2,3},{3,2},{4,5},{5,4},{6,7},{7,6},{8,9},{9,8},{10,11... | collective-permute-start | bytes 693512 | tf_op jit(solution)/shard_map/ppermute | solution.py:27
  195.5 5.8 %collective-permute-start.10 = (f32[16,512]{1,0:T(8,128)S(1)}, f32[16,512]{1,0:T(8,128)S(1)}, u32[]{:S(2)}, u32[]{:S(2)}) collective-permute-start(f32[16,512]{1,0:T(8,128)S(1)} %fusion.59), channel_id=1, source_target_pairs={{64,0},{128,64},{192,128},{256,192},{320,256},{384,320},{448,384},... | collective-permute-start | bytes 98312 | tf_op jit(solution)/shard_map/ppermute | solution.py:17
  201.3 34.8 %collective-permute-start.3 = (bf16[1024,512]{1,0:T(8,128)(2,1)}, bf16[1024,512]{1,0:T(8,128)(2,1)S(1)}, u32[]{:S(2)}, u32[]{:S(2)}) collective-permute-start(bf16[1024,512]{1,0:T(8,128)(2,1)} %fusion), channel_id=1, source_target_pairs={{60,0},{62,2},{0,4},{2,6},{4,8},{6,10},{8,12},{10,14},{12,16},{14,... | collective-permute-start | bytes 3145736 | tf_op jit(solution)/shard_map/ppermute | solution.py:11
  204.0 64.9 %collective-permute-start.5 = (bf16[1024,512]{1,0:T(8,128)(2,1)}, bf16[1024,512]{1,0:T(8,128)(2,1)S(1)}, u32[]{:S(2)}, u32[]{:S(2)}) collective-permute-start(bf16[1024,512]{1,0:T(8,128)(2,1)} %fusion), channel_id=1, source_target_pairs={{58,0},{60,2},{62,4},{0,6},{2,8},{4,10},{6,12},{8,14},{10,16},{12,... | collective-permute-start | bytes 3145736 | tf_op jit(solution)/shard_map/ppermute | solution.py:11
  208.5 62.4 %collective-permute-start.9 = (f32[16,512]{1,0:T(8,128)S(1)}, f32[16,512]{1,0:T(8,128)S(1)}, u32[]{:S(2)}, u32[]{:S(2)}) collective-permute-start(f32[16,512]{1,0:T(8,128)S(1)} %fusion.66), channel_id=1, source_target_pairs={{0,64},{64,128},{128,192},{192,256},{256,320},{320,384},{384,448},... | collective-permute-start | bytes 98312 | tf_op jit(solution)/shard_map/ppermute | solution.py:17
  270.5 0.8 copy-start.6
  270.5 0.8 copy-start.7
  270.5 0.8 copy-start.10
  270.5 0.8 copy-start.11
  270.5 0.8 copy-start.12

commit v2 on v1

--- a/solution.py
+++ b/solution.py
@@ -117,7 +117,8 @@
         + jnp.sum(search_obs * search_obs)
         + jnp.sum(search_incr * search_incr)
     )
-    sums = lax.psum(lax.psum(lax.psum(jnp.stack([resid_local, search_local]), "lat"), "lon"), "win")
+    wide = jnp.broadcast_to(jnp.stack([resid_local, search_local])[:, None], (2, 8192))
+    sums = lax.psum(wide, ("win", "lon", "lat"))[:, 0]
     alpha = sums[0] / (sums[1] + 1e-06)
 
     packed = jnp.concatenate(

time: 275 us -> 462 us (1.68)
  the two profiles are of different devices: /device:TPU:2 before, /device:TPU:8 now
where the time goes in v2:
time: 462 us; the launch traced here: 461 us
  waiting for transfers between devices  350 us (76%)
  starting transfers between devices  40 us (9%)
  between operations  32.7 us (7%)
  other arithmetic  20 us (4%)
  matrix products  9.73 us (2%)
  local copies, waits for them, and re-layouts  8.71 us (2%)
    psum x1, waiting for transfers between devices, local(): sums = lax.psum(wide, ('win', 'lon', 'lat'))[:, 0]  237 us
    ppermute x8, waiting for transfers between devices, from_offset(): lax.ppermute(value, axis, [((i + distance) % count, i) for i in range(cou...  76.8 us
    ppermute x1, waiting for transfers between devices, lat_partner(): return lax.ppermute(value, 'lat', [(0, 1), (1, 0)])  32.2 us
    ppermute x8, starting transfers between devices, from_offset(): lax.ppermute(value, axis, [((i + distance) % count, i) for i in range(cou...  28 us
    another operation x7, other arithmetic, weight_for(): picked = tiles[jnp.argmax(match)]  9.35 us
  transfers between devices with their start and end apart: 12, of which 6 were waited for; matrix products, arithmetic and copies ran while one was open for 6% of the time, Pallas kernels for 0%

profile of v2, /device:TPU:8, one launch (start us, length us, event | category | flops | bytes accessed | tf_op | source)
XLA Modules:
  0.0 461.0 jit_solution(7638493862482164467)
XLA Ops:
  7.2 1.5 multiply_reduce_fusion.3
  8.7 1.4 multiply_reduce_fusion
  10.2 1.4 multiply_reduce_fusion.4
  13.6 1.5 multiply_reduce_fusion.1
  17.0 0.1 pad_maximum_fusion.4
  17.0 0.7 broadcast_in_dim.6
  17.8 1.4 bitcast_reduce_fusion.3
  19.2 1.3 bitcast_reduce_fusion.4
  20.5 1.3 bitcast_reduce_fusion.5
  21.9 1.3 bitcast_reduce_fusion.1
  23.2 1.3 bitcast_reduce_fusion.2
  24.5 1.3 bitcast_reduce_fusion.6
  25.8 1.4 bitcast_reduce_fusion
  27.2 0.8 fusion.90
  28.0 1.5 compare_reduce_fusion
  38.1 0.9 copy.88
  39.1 0.8 copy.89
  44.2 237.0 %all-reduce.2.cloned.1.call-done = f32[2,8192]{1,0:T(2,128)} async-done(((f32[2,8192]{1,0:T(2,128)}), f32[2,8192]{1,0:T(2,128)}) %all-reduce.2.cloned.1.call-update) | async-done | bytes 65552 | tf_op jit(solution)/shard_map/psum | solution.py:121
  281.2 1.3 fusion.91
  283.8 0.8 copy_bitcast_fusion.4
  284.6 0.2 fusion
  284.8 2.5 collective-permute-start.2
  287.3 2.2 collective-permute-start.1
  289.5 7.2 %collective-permute-start = (bf16[1024,512]{1,0:T(8,128)(2,1)S(1)}, bf16[1024,512]{1,0:T(8,128)(2,1)S(1)}, u32[]{:S(2)}, u32[]{:S(2)}) collective-permute-start(bf16[1024,512]{1,0:T(8,128)(2,1)S(1)} %fusion), channel_id=1, source_target_pairs={{2,0},{4,2},{6,4},{8,6},{10,8},{12,10},{14,12},{16,14},{18,16},{20... | collective-permute-start | bytes 3145736 | tf_op jit(solution)/shard_map/ppermute | solution.py:11
  296.8 0.3 fusion.1
  297.0 0.1 pad_maximum_fusion.3
  297.1 1.9 collective-permute-start.6
  299.0 7.5 %collective-permute-start.7 = (f32[7,16,2]{2,1,0:T(8,128)S(1)}, f32[7,16,2]{2,1,0:T(8,128)S(1)}, u32[]{:S(2)}, u32[]{:S(2)}) collective-permute-start(f32[7,16,2]{2,1,0:T(8,128)S(1)} %get-tuple-element.51), channel_id=1, source_target_pairs={{2,0},{4,2},{6,4},{8,6},{10,8},{12,10},{14,12},{16,14},{18,16},{20... | collective-permute-start | bytes 2696 | tf_op jit(solution)/shard_map/ppermute | solution.py:11
  306.6 1.4 fusion.17
  308.0 0.6 copy.38
  308.6 25.5 %collective-permute-done.6 = f32[7,16,2]{2,1,0:T(8,128)S(1)} collective-permute-done((f32[7,16,2]{2,1,0:T(8,128)S(1)}, f32[7,16,2]{2,1,0:T(8,128)S(1)}, u32[]{:S(2)}, u32[]{:S(2)}) %collective-permute-start.6) | collective-permute-done | bytes 928 | tf_op jit(solution)/shard_map/ppermute | solution.py:11
  334.1 2.8 collective-permute-start.4
  336.9 0.2 pad_maximum_fusion
  337.1 7.8 %collective-permute-start.8 = (f32[7,16,516]{2,1,0:T(8,128)S(1)}, f32[7,16,516]{2,1,0:T(8,128)S(1)}, u32[]{:S(2)}, u32[]{:S(2)}) collective-permute-start(f32[7,16,516]{2,1,0:T(8,128)S(1)} %pad_maximum_fusion), channel_id=1, source_target_pairs={{0,1},{1,0},{2,3},{3,2},{4,5},{5,4},{6,7},{7,6},{8,9},{9,8},{10,11... | collective-permute-start | bytes 693512 | tf_op jit(solution)/shard_map/ppermute | solution.py:27
  345.0 0.1 slice.257
  345.2 0.1 slice_bitcast_fusion.10
  345.3 32.2 %collective-permute-done.8 = f32[7,16,516]{2,1,0:T(8,128)S(1)} collective-permute-done((f32[7,16,516]{2,1,0:T(8,128)S(1)}, f32[7,16,516]{2,1,0:T(8,128)S(1)}, u32[]{:S(2)}, u32[]{:S(2)}) %collective-permute-start.8) | collective-permute-done | bytes 231200 | tf_op jit(solution)/shard_map/ppermute | solution.py:27
  377.5 0.2 fusion.48
  377.7 0.1 fusion.92
  377.8 0.1 fusion.51
  378.0 0.1 slice.266
  378.0 0.1 slice.307
  378.1 0.2 fusion.59
  378.3 1.9 collective-permute-start.10
  380.2 0.2 fusion.66
  380.4 3.7 collective-permute-done.10
  384.1 1.9 collective-permute-start.3
  386.1 0.7 multiply_subtract_fusion
  386.8 1.9 collective-permute-start.5
  388.7 1.4 fusion.11
  390.1 2.2 collective-permute-start.9
  392.3 1.3 fusion.13
  393.6 1.4 fusion.15
  395.0 1.3 fusion.7
  396.4 19.6 %collective-permute-done.3 = bf16[1024,512]{1,0:T(8,128)(2,1)S(1)} collective-permute-done((bf16[1024,512]{1,0:T(8,128)(2,1)S(1)}, bf16[1024,512]{1,0:T(8,128)(2,1)S(1)}, u32[]{:S(2)}, u32[]{:S(2)}) %collective-permute-start.3) | collective-permute-done | bytes 1048608 | tf_op jit(solution)/shard_map/ppermute | solution.py:11
  416.0 1.4 fusion.9
  417.4 31.6 %collective-permute-done.5 = bf16[1024,512]{1,0:T(8,128)(2,1)S(1)} collective-permute-done((bf16[1024,512]{1,0:T(8,128)(2,1)S(1)}, bf16[1024,512]{1,0:T(8,128)(2,1)S(1)}, u32[]{:S(2)}, u32[]{:S(2)}) %collective-permute-start.5) | collective-permute-done | bytes 1048608 | tf_op jit(solution)/shard_map/ppermute | solution.py:11
  449.0 1.6 add_add_fusion
  450.7 0.4 fusion.2
  451.1 0.3 copy-done.2
  451.5 0.6 copy.39
  452.2 0.6 copy.40
  452.8 0.6 copy.41
  453.5 0.6 copy.42
  (36 shorter events, 0.4 us)
Async XLA Ops:
  7.2 277.4 %copy-start = (bf16[1,64,16,1,512]{4,2,3,1,0:T(8,128)(2,1)S(1)}, bf16[1,64,16,1,512]{4,2,3,1,0:T(8,128)(2,1)}, u32[]{:S(2)}) copy-start(bf16[1,64,16,1,512]{4,2,3,1,0:T(8,128)(2,1)} %param.24) | copy-start | bytes 3145732
  7.2 274.0 %all-reduce.2.cloned.1.call-start = ((), (), s32[]{:S(2)}) async-start(), calls=%async_computation | async-start | bytes 131072 | tf_op jit(solution)/shard_map/psum | solution.py:121
  284.6 22.0 %copy-start.1 = (bf16[1,5,512,512]{3,2,1,0:T(8,128)(2,1)S(1)}, bf16[1,5,512,512]{3,2,1,0:T(8,128)(2,1)}, u32[]{:S(2)}) copy-start(bf16[1,5,512,512]{3,2,1,0:T(8,128)(2,1)} %param.29) | copy-start | bytes 7864324
  284.8 102.0 %collective-permute-start.2 = (bf16[1024,512]{1,0:T(8,128)(2,1)S(1)}, bf16[1024,512]{1,0:T(8,128)(2,1)S(1)}, u32[]{:S(2)}, u32[]{:S(2)}) collective-permute-start(bf16[1024,512]{1,0:T(8,128)(2,1)S(1)} %fusion), channel_id=1, source_target_pairs={{4,0},{6,2},{8,4},{10,6},{12,8},{14,10},{16,12},{18,14},{20,16},{2... | collective-permute-start | bytes 3145736 | tf_op jit(solution)/shard_map/ppermute | solution.py:11
  287.3 102.8 %collective-permute-start.1 = (bf16[1024,512]{1,0:T(8,128)(2,1)S(1)}, bf16[1024,512]{1,0:T(8,128)(2,1)S(1)}, u32[]{:S(2)}, u32[]{:S(2)}) collective-permute-start(bf16[1024,512]{1,0:T(8,128)(2,1)S(1)} %fusion), channel_id=1, source_target_pairs={{62,0},{0,2},{2,4},{4,6},{6,8},{8,10},{10,12},{12,14},{14,16},{16,... | collective-permute-start | bytes 3145736 | tf_op jit(solution)/shard_map/ppermute | solution.py:11
  289.5 104.1 %collective-permute-start = (bf16[1024,512]{1,0:T(8,128)(2,1)S(1)}, bf16[1024,512]{1,0:T(8,128)(2,1)S(1)}, u32[]{:S(2)}, u32[]{:S(2)}) collective-permute-start(bf16[1024,512]{1,0:T(8,128)(2,1)S(1)} %fusion), channel_id=1, source_target_pairs={{2,0},{4,2},{6,4},{8,6},{10,8},{12,10},{14,12},{16,14},{18,16},{20... | collective-permute-start | bytes 3145736 | tf_op jit(solution)/shard_map/ppermute | solution.py:11
  297.1 37.0 %collective-permute-start.6 = (f32[7,16,2]{2,1,0:T(8,128)S(1)}, f32[7,16,2]{2,1,0:T(8,128)S(1)}, u32[]{:S(2)}, u32[]{:S(2)}) collective-permute-start(f32[7,16,2]{2,1,0:T(8,128)S(1)} %get-tuple-element.50), channel_id=1, source_target_pairs={{62,0},{0,2},{2,4},{4,6},{6,8},{8,10},{10,12},{12,14},{14,16},{16,... | collective-permute-start | bytes 2696 | tf_op jit(solution)/shard_map/ppermute | solution.py:11
  299.0 37.9 %collective-permute-start.7 = (f32[7,16,2]{2,1,0:T(8,128)S(1)}, f32[7,16,2]{2,1,0:T(8,128)S(1)}, u32[]{:S(2)}, u32[]{:S(2)}) collective-permute-start(f32[7,16,2]{2,1,0:T(8,128)S(1)} %get-tuple-element.51), channel_id=1, source_target_pairs={{2,0},{4,2},{6,4},{8,6},{10,8},{12,10},{14,12},{16,14},{18,16},{20... | collective-permute-start | bytes 2696 | tf_op jit(solution)/shard_map/ppermute | solution.py:11
  334.1 60.9 %collective-permute-start.4 = (bf16[1024,512]{1,0:T(8,128)(2,1)S(1)}, bf16[1024,512]{1,0:T(8,128)(2,1)S(1)}, u32[]{:S(2)}, u32[]{:S(2)}) collective-permute-start(bf16[1024,512]{1,0:T(8,128)(2,1)S(1)} %fusion), channel_id=1, source_target_pairs={{6,0},{8,2},{10,4},{12,6},{14,8},{16,10},{18,12},{20,14},{22,16},{... | collective-permute-start | bytes 3145736 | tf_op jit(solution)/shard_map/ppermute | solution.py:11
  337.1 48.9 %copy-start.3 = (f32[1,16,1,512]{3,2,1,0:T(1,128)S(1)}, f32[1,16,1,512]{3,2,1,0:T(1,128)}, u32[]{:S(2)}) copy-start(f32[1,16,1,512]{3,2,1,0:T(1,128)} %param.21) | copy-start | bytes 98308
  337.1 48.9 %copy-start.4 = (f32[1,16,1,512]{3,2,1,0:T(1,128)S(1)}, f32[1,16,1,512]{3,2,1,0:T(1,128)}, u32[]{:S(2)}) copy-start(f32[1,16,1,512]{3,2,1,0:T(1,128)} %param.22) | copy-start | bytes 98308
  337.1 48.9 %copy-start.7 = (f32[1,16,1,512]{3,2,1,0:T(1,128)S(1)}, f32[1,16,1,512]{3,2,1,0:T(1,128)}, u32[]{:S(2)}) copy-start(f32[1,16,1,512]{3,2,1,0:T(1,128)} %param.26) | copy-start | bytes 98308
  337.1 48.9 %copy-start.8 = (f32[1,16,1,512]{3,2,1,0:T(1,128)S(1)}, f32[1,16,1,512]{3,2,1,0:T(1,128)}, u32[]{:S(2)}) copy-start(f32[1,16,1,512]{3,2,1,0:T(1,128)} %param.20) | copy-start | bytes 98308
  337.1 40.3 %collective-permute-start.8 = (f32[7,16,516]{2,1,0:T(8,128)S(1)}, f32[7,16,516]{2,1,0:T(8,128)S(1)}, u32[]{:S(2)}, u32[]{:S(2)}) collective-permute-start(f32[7,16,516]{2,1,0:T(8,128)S(1)} %pad_maximum_fusion), channel_id=1, source_target_pairs={{0,1},{1,0},{2,3},{3,2},{4,5},{5,4},{6,7},{7,6},{8,9},{9,8},{10,11... | collective-permute-start | bytes 693512 | tf_op jit(solution)/shard_map/ppermute | solution.py:27
  378.3 5.8 %collective-permute-start.10 = (f32[16,512]{1,0:T(8,128)S(1)}, f32[16,512]{1,0:T(8,128)S(1)}, u32[]{:S(2)}, u32[]{:S(2)}) collective-permute-start(f32[16,512]{1,0:T(8,128)S(1)} %fusion.59), channel_id=1, source_target_pairs={{64,0},{128,64},{192,128},{256,192},{320,256},{384,320},{448,384},... | collective-permute-start | bytes 98312 | tf_op jit(solution)/shard_map/ppermute | solution.py:17
  384.1 31.9 %collective-permute-start.3 = (bf16[1024,512]{1,0:T(8,128)(2,1)S(1)}, bf16[1024,512]{1,0:T(8,128)(2,1)S(1)}, u32[]{:S(2)}, u32[]{:S(2)}) collective-permute-start(bf16[1024,512]{1,0:T(8,128)(2,1)S(1)} %fusion), channel_id=1, source_target_pairs={{60,0},{62,2},{0,4},{2,6},{4,8},{6,10},{8,12},{10,14},{12,16},{14,... | collective-permute-start | bytes 3145736 | tf_op jit(solution)/shard_map/ppermute | solution.py:11
  386.8 62.2 %collective-permute-start.5 = (bf16[1024,512]{1,0:T(8,128)(2,1)S(1)}, bf16[1024,512]{1,0:T(8,128)(2,1)S(1)}, u32[]{:S(2)}, u32[]{:S(2)}) collective-permute-start(bf16[1024,512]{1,0:T(8,128)(2,1)S(1)} %fusion), channel_id=1, source_target_pairs={{58,0},{60,2},{62,4},{0,6},{2,8},{4,10},{6,12},{8,14},{10,16},{12,... | collective-permute-start | bytes 3145736 | tf_op jit(solution)/shard_map/ppermute | solution.py:11
  390.1 61.0 %collective-permute-start.9 = (f32[16,512]{1,0:T(8,128)S(1)}, f32[16,512]{1,0:T(8,128)S(1)}, u32[]{:S(2)}, u32[]{:S(2)}) collective-permute-start(f32[16,512]{1,0:T(8,128)S(1)} %fusion.66), channel_id=1, source_target_pairs={{0,64},{64,128},{128,192},{192,256},{256,320},{320,384},{384,448},... | collective-permute-start | bytes 98312 | tf_op jit(solution)/shard_map/ppermute | solution.py:17
  450.6 0.8 copy-start.2
  450.7 0.8 copy-start.5
  450.7 0.8 copy-start.6
  450.7 0.8 copy-start.9
  450.7 0.8 copy-start.10
  450.7 0.8 copy-start.11
Sparse Core Ops, SparseCore 0:
  17.9 263.2 all-reduce.1

commit v3 on v1

--- a/solution.py
+++ b/solution.py
@@ -15,6 +15,16 @@
     count = lax.axis_size(axis)
     leading, last = (max(0, -steps), min(count, count - steps))
     return lax.ppermute(value, axis, [(source, source + steps) for source in range(leading, last)])
+
+
+def butterfly_sum(value, axes):
+    for axis in axes:
+        count = lax.axis_size(axis)
+        step = 1
+        while step < count:
+            value = value + lax.ppermute(value, axis, [(i, i ^ step) for i in range(count)])
+            step *= 2
+    return value
 
 
 def lon_extended(packed, width):
@@ -117,7 +127,7 @@
         + jnp.sum(search_obs * search_obs)
         + jnp.sum(search_incr * search_incr)
     )
-    sums = lax.psum(lax.psum(lax.psum(jnp.stack([resid_local, search_local]), "lat"), "lon"), "win")
+    sums = butterfly_sum(jnp.stack([resid_local, search_local]), ("lon", "lat", "win"))
     alpha = sums[0] / (sums[1] + 1e-06)
 
     packed = jnp.concatenate(

time: 275 us -> 262 us (0.953)
  the two profiles are of different devices: /device:TPU:2 before, /device:TPU:24 now
where the time goes in v3:
time: 262 us; the launch traced here: 261 us
  waiting for transfers between devices  117 us (45%)
  starting transfers between devices  86 us (33%)
  other arithmetic  21.6 us (8%)
  between operations  19.6 us (7%)
  matrix products  9.68 us (4%)
  local copies, waits for them, and re-layouts  7.32 us (3%)
    ppermute x8, waiting for transfers between devices, from_offset(): lax.ppermute(value, axis, [((i + distance) % count, i) for i in range(cou...  63.1 us
    ppermute x9, starting transfers between devices, butterfly_sum(): lax.ppermute(value, axis, [(i, i ^ step) for i in range(count)])  40.2 us
    ppermute x8, starting transfers between devices, from_offset(): lax.ppermute(value, axis, [((i + distance) % count, i) for i in range(cou...  32.1 us
    ppermute x1, waiting for transfers between devices, lat_partner(): return lax.ppermute(value, 'lat', [(0, 1), (1, 0)])  29.9 us
    ppermute x9, waiting for transfers between devices, butterfly_sum(): lax.ppermute(value, axis, [(i, i ^ step) for i in range(count)])  19.3 us
    another operation x7, other arithmetic, weight_for(): picked = tiles[jnp.argmax(match)]  9.35 us
    dot_general x6, matrix products, localize(): jnp.dot(sources[offset], weight_for(offset), preferred_element_type=jnp.f...  8.31 us
    ppermute x1, starting transfers between devices, lat_partner(): return lax.ppermute(value, 'lat', [(0, 1), (1, 0)])  7.96 us
  transfers between devices with their start and end apart: 20, of which 14 were waited for; matrix products, arithmetic and copies ran while one was open for 10% of the time, Pallas kernels for 0%

profile of v3, /device:TPU:24, one launch (start us, length us, event | category | flops | bytes accessed | tf_op | source)
XLA Modules:
  0.0 260.9 jit_solution(732020691589441184)
XLA Ops:
  0.6 1.5 multiply_reduce_fusion.3
  2.2 1.4 multiply_reduce_fusion
  3.6 1.4 multiply_reduce_fusion.4
  7.0 1.5 multiply_reduce_fusion.1
  10.5 1.9 collective-permute-start
  12.4 1.3 bitcast_reduce_fusion.3
  14.9 1.4 bitcast_reduce_fusion.4
  17.7 1.4 bitcast_reduce_fusion.5
  20.4 1.3 bitcast_reduce_fusion.1
  23.0 1.3 bitcast_reduce_fusion.2
  25.6 1.3 bitcast_reduce_fusion.6
  28.0 1.4 compare_reduce_fusion
  29.5 1.4 bitcast_reduce_fusion
  32.1 0.8 copy.89
  32.9 0.9 copy.88
  33.8 0.8 fusion.90
  39.1 4.3 %collective-permute-start.1 = (f32[2]{0:T(128)S(1)}, f32[2]{0:T(128)S(1)}, u32[]{:S(2)}, u32[]{:S(2)}) collective-permute-start(f32[2]{0:T(128)S(1)} %fusion.100), channel_id=1, source_target_pairs={{0,4},{2,6},{4,0},{6,2},{8,12},{10,14},{12,8},{14,10},{16,20},{18,... | collective-permute-start | bytes 32 | tf_op jit(solution)/shard_map/ppermute | solution.py:25
  43.3 1.5 collective-permute-done.1
  44.9 6.1 %collective-permute-start.2 = (f32[2]{0:T(128)S(1)}, f32[2]{0:T(128)S(1)}, u32[]{:S(2)}, u32[]{:S(2)}) collective-permute-start(f32[2]{0:T(128)S(1)} %fusion.101), channel_id=1, source_target_pairs={{0,8},{2,10},{4,12},{6,14},{8,0},{10,2},{12,4},{14,6},{16,24},{18,... | collective-permute-start | bytes 32 | tf_op jit(solution)/shard_map/ppermute | solution.py:25
  51.0 1.5 collective-permute-done.2
  52.5 3.4 %collective-permute-start.3 = (f32[2]{0:T(128)S(1)}, f32[2]{0:T(128)S(1)}, u32[]{:S(2)}, u32[]{:S(2)}) collective-permute-start(f32[2]{0:T(128)S(1)} %add.242), channel_id=1, source_target_pairs={{0,16},{2,18},{4,20},{6,22},{8,24},{10,26},{12,28},{14,30},{16,0},... | collective-permute-start | bytes 32 | tf_op jit(solution)/shard_map/ppermute | solution.py:25
  55.9 2.0 collective-permute-done.3
  57.9 4.9 %collective-permute-start.4 = (f32[2]{0:T(128)S(1)}, f32[2]{0:T(128)S(1)}, u32[]{:S(2)}, u32[]{:S(2)}) collective-permute-start(f32[2]{0:T(128)S(1)} %add.243), channel_id=1, source_target_pairs={{0,32},{2,34},{4,36},{6,38},{8,40},{10,42},{12,44},{14,46},{16,48}... | collective-permute-start | bytes 32 | tf_op jit(solution)/shard_map/ppermute | solution.py:25
  62.9 2.0 collective-permute-done.4
  64.9 9.3 %collective-permute-start.5 = (f32[2]{0:T(128)S(1)}, f32[2]{0:T(128)S(1)}, u32[]{:S(2)}, u32[]{:S(2)}) collective-permute-start(f32[2]{0:T(128)S(1)} %add.244), channel_id=1, source_target_pairs={{0,1},{1,0},{2,3},{3,2},{4,5},{5,4},{6,7},{7,6},{8,9},{9,8},{10,11... | collective-permute-start | bytes 32 | tf_op jit(solution)/shard_map/ppermute | solution.py:25
  74.2 1.5 collective-permute-done.5
  75.7 2.3 collective-permute-start.6
  78.0 3.1 %collective-permute-done.6 = f32[2]{0:T(128)S(1)} collective-permute-done((f32[2]{0:T(128)S(1)}, f32[2]{0:T(128)S(1)}, u32[]{:S(2)}, u32[]{:S(2)}) %collective-permute-start.6) | collective-permute-done | bytes 40 | tf_op jit(solution)/shard_map/ppermute | solution.py:25
  81.1 3.0 %collective-permute-start.7 = (f32[2]{0:T(128)S(1)}, f32[2]{0:T(128)S(1)}, u32[]{:S(2)}, u32[]{:S(2)}) collective-permute-start(f32[2]{0:T(128)S(1)} %add.246), channel_id=1, source_target_pairs={{0,128},{64,192},{128,0},{192,64},{256,384},{320,448},{384,256},{4... | collective-permute-start | bytes 32 | tf_op jit(solution)/shard_map/ppermute | solution.py:25
  84.1 3.4 %collective-permute-done.7 = f32[2]{0:T(128)S(1)} collective-permute-done((f32[2]{0:T(128)S(1)}, f32[2]{0:T(128)S(1)}, u32[]{:S(2)}, u32[]{:S(2)}) %collective-permute-start.7) | collective-permute-done | bytes 40 | tf_op jit(solution)/shard_map/ppermute | solution.py:25
  87.4 5.0 %collective-permute-start.8 = (f32[2]{0:T(128)S(1)}, f32[2]{0:T(128)S(1)}, u32[]{:S(2)}, u32[]{:S(2)}) collective-permute-start(f32[2]{0:T(128)S(1)} %add.247), channel_id=1, source_target_pairs={{0,256},{64,320},{128,384},{192,448},{256,0},{320,64},{384,128},{4... | collective-permute-start | bytes 32 | tf_op jit(solution)/shard_map/ppermute | solution.py:25
  92.5 4.3 %collective-permute-done.8 = f32[2]{0:T(128)S(1)} collective-permute-done((f32[2]{0:T(128)S(1)}, f32[2]{0:T(128)S(1)}, u32[]{:S(2)}, u32[]{:S(2)}) %collective-permute-start.8) | collective-permute-done | bytes 40 | tf_op jit(solution)/shard_map/ppermute | solution.py:25
  98.6 0.8 copy_bitcast_fusion.4
  99.4 1.6 fusion
  101.0 7.4 %collective-permute-start.11 = (bf16[1024,512]{1,0:T(8,128)(2,1)S(1)}, bf16[1024,512]{1,0:T(8,128)(2,1)S(1)}, u32[]{:S(2)}, u32[]{:S(2)}) collective-permute-start(bf16[1024,512]{1,0:T(8,128)(2,1)S(1)} %fusion), channel_id=1, source_target_pairs={{4,0},{6,2},{8,4},{10,6},{12,8},{14,10},{16,12},{18,14},{20,16},{2... | collective-permute-start | bytes 3145736 | tf_op jit(solution)/shard_map/ppermute | solution.py:11
  108.4 1.9 collective-permute-start.10
  110.4 7.5 %collective-permute-start.9 = (bf16[1024,512]{1,0:T(8,128)(2,1)S(1)}, bf16[1024,512]{1,0:T(8,128)(2,1)S(1)}, u32[]{:S(2)}, u32[]{:S(2)}) collective-permute-start(bf16[1024,512]{1,0:T(8,128)(2,1)S(1)} %fusion), channel_id=1, source_target_pairs={{2,0},{4,2},{6,4},{8,6},{10,8},{12,10},{14,12},{16,14},{18,16},{20... | collective-permute-start | bytes 3145736 | tf_op jit(solution)/shard_map/ppermute | solution.py:11
  118.3 1.9 collective-permute-start.15
  120.2 7.5 %collective-permute-start.16 = (f32[7,16,2]{2,1,0:T(8,128)S(1)}, f32[7,16,2]{2,1,0:T(8,128)S(1)}, u32[]{:S(2)}, u32[]{:S(2)}) collective-permute-start(f32[7,16,2]{2,1,0:T(8,128)S(1)} %get-tuple-element.51), channel_id=1, source_target_pairs={{2,0},{4,2},{6,4},{8,6},{10,8},{12,10},{14,12},{16,14},{18,16},{20... | collective-permute-start | bytes 2696 | tf_op jit(solution)/shard_map/ppermute | solution.py:11
  127.8 1.4 fusion.17
  129.1 0.6 copy.38
  129.8 11.2 %collective-permute-done.15 = f32[7,16,2]{2,1,0:T(8,128)S(1)} collective-permute-done((f32[7,16,2]{2,1,0:T(8,128)S(1)}, f32[7,16,2]{2,1,0:T(8,128)S(1)}, u32[]{:S(2)}, u32[]{:S(2)}) %collective-permute-start.15) | collective-permute-done | bytes 928 | tf_op jit(solution)/shard_map/ppermute | solution.py:11
  141.0 1.9 collective-permute-start.13
  142.9 6.0 %collective-permute-done.16 = f32[7,16,2]{2,1,0:T(8,128)S(1)} collective-permute-done((f32[7,16,2]{2,1,0:T(8,128)S(1)}, f32[7,16,2]{2,1,0:T(8,128)S(1)}, u32[]{:S(2)}, u32[]{:S(2)}) %collective-permute-start.16) | collective-permute-done | bytes 928 | tf_op jit(solution)/shard_map/ppermute | solution.py:11
  149.1 8.0 %collective-permute-start.17 = (f32[7,16,516]{2,1,0:T(8,128)S(1)}, f32[7,16,516]{2,1,0:T(8,128)S(1)}, u32[]{:S(2)}, u32[]{:S(2)}) collective-permute-start(f32[7,16,516]{2,1,0:T(8,128)S(1)} %pad_maximum_fusion), channel_id=1, source_target_pairs={{0,1},{1,0},{2,3},{3,2},{4,5},{5,4},{6,7},{7,6},{8,9},{9,8},{10,11... | collective-permute-start | bytes 693512 | tf_op jit(solution)/shard_map/ppermute | solution.py:37
  157.3 29.9 %collective-permute-done.17 = f32[7,16,516]{2,1,0:T(8,128)S(1)} collective-permute-done((f32[7,16,516]{2,1,0:T(8,128)S(1)}, f32[7,16,516]{2,1,0:T(8,128)S(1)}, u32[]{:S(2)}, u32[]{:S(2)}) %collective-permute-start.17) | collective-permute-done | bytes 231200 | tf_op jit(solution)/shard_map/ppermute | solution.py:37
  188.0 2.4 collective-permute-start.19
  190.6 4.5 %collective-permute-done.19 = f32[16,512]{1,0:T(8,128)S(1)} collective-permute-done((f32[16,512]{1,0:T(8,128)S(1)}, f32[16,512]{1,0:T(8,128)S(1)}, u32[]{:S(2)}, u32[]{:S(2)}) %collective-permute-start.19) | collective-permute-done | bytes 32800 | tf_op jit(solution)/shard_map/ppermute | solution.py:17
  195.0 1.9 collective-permute-start.12
  197.0 0.7 multiply_subtract_fusion
  197.7 1.9 collective-permute-start.14
  199.6 1.3 fusion.11
  200.9 3.5 %collective-permute-start.18 = (f32[16,512]{1,0:T(8,128)S(1)}, f32[16,512]{1,0:T(8,128)S(1)}, u32[]{:S(2)}, u32[]{:S(2)}) collective-permute-start(f32[16,512]{1,0:T(8,128)S(1)} %fusion.66), channel_id=1, source_target_pairs={{0,64},{64,128},{128,192},{192,256},{256,320},{320,384},{384,448},... | collective-permute-start | bytes 98312 | tf_op jit(solution)/shard_map/ppermute | solution.py:17
  204.4 1.3 fusion.13
  205.8 1.3 fusion.15
  207.1 1.3 fusion.7
  208.4 18.6 %collective-permute-done.12 = bf16[1024,512]{1,0:T(8,128)(2,1)S(1)} collective-permute-done((bf16[1024,512]{1,0:T(8,128)(2,1)S(1)}, bf16[1024,512]{1,0:T(8,128)(2,1)S(1)}, u32[]{:S(2)}, u32[]{:S(2)}) %collective-permute-start.12) | collective-permute-done | bytes 1048608 | tf_op jit(solution)/shard_map/ppermute | solution.py:11
  227.0 1.4 fusion.9
  228.4 27.3 %collective-permute-done.14 = bf16[1024,512]{1,0:T(8,128)(2,1)S(1)} collective-permute-done((bf16[1024,512]{1,0:T(8,128)(2,1)S(1)}, bf16[1024,512]{1,0:T(8,128)(2,1)S(1)}, u32[]{:S(2)}, u32[]{:S(2)}) %collective-permute-start.14) | collective-permute-done | bytes 1048608 | tf_op jit(solution)/shard_map/ppermute | solution.py:11
  255.7 1.6 add_add_fusion
  258.3 0.6 copy.39
  258.9 0.6 copy.40
  259.6 0.6 copy.41
  260.2 0.6 copy.42
  (59 shorter events, 3.4 us)
Async XLA Ops:
  0.6 117.3 %copy-start = (bf16[1,64,16,1,512]{4,2,3,1,0:T(8,128)(2,1)S(1)}, bf16[1,64,16,1,512]{4,2,3,1,0:T(8,128)(2,1)}, u32[]{:S(2)}) copy-start(bf16[1,64,16,1,512]{4,2,3,1,0:T(8,128)(2,1)} %param.24) | copy-start | bytes 3145732
  10.5 28.5 %collective-permute-start = (f32[2]{0:T(128)S(1)}, f32[2]{0:T(128)S(1)}, u32[]{:S(2)}, u32[]{:S(2)}) collective-permute-start(f32[2]{0:T(128)S(1)} %pad_maximum_fusion.4), channel_id=1, source_target_pairs={{0,2},{2,0},{4,6},{6,4},{8,10},{10,8},{12,14},{14,12},{16,18},{18,... | collective-permute-start | bytes 32 | tf_op jit(solution)/shard_map/ppermute | solution.py:25
  39.1 5.8 %collective-permute-start.1 = (f32[2]{0:T(128)S(1)}, f32[2]{0:T(128)S(1)}, u32[]{:S(2)}, u32[]{:S(2)}) collective-permute-start(f32[2]{0:T(128)S(1)} %fusion.100), channel_id=1, source_target_pairs={{0,4},{2,6},{4,0},{6,2},{8,12},{10,14},{12,8},{14,10},{16,20},{18,... | collective-permute-start | bytes 32 | tf_op jit(solution)/shard_map/ppermute | solution.py:25
  44.9 7.6 %collective-permute-start.2 = (f32[2]{0:T(128)S(1)}, f32[2]{0:T(128)S(1)}, u32[]{:S(2)}, u32[]{:S(2)}) collective-permute-start(f32[2]{0:T(128)S(1)} %fusion.101), channel_id=1, source_target_pairs={{0,8},{2,10},{4,12},{6,14},{8,0},{10,2},{12,4},{14,6},{16,24},{18,... | collective-permute-start | bytes 32 | tf_op jit(solution)/shard_map/ppermute | solution.py:25
  52.5 5.4 %collective-permute-start.3 = (f32[2]{0:T(128)S(1)}, f32[2]{0:T(128)S(1)}, u32[]{:S(2)}, u32[]{:S(2)}) collective-permute-start(f32[2]{0:T(128)S(1)} %add.242), channel_id=1, source_target_pairs={{0,16},{2,18},{4,20},{6,22},{8,24},{10,26},{12,28},{14,30},{16,0},... | collective-permute-start | bytes 32 | tf_op jit(solution)/shard_map/ppermute | solution.py:25
  57.9 6.9 %collective-permute-start.4 = (f32[2]{0:T(128)S(1)}, f32[2]{0:T(128)S(1)}, u32[]{:S(2)}, u32[]{:S(2)}) collective-permute-start(f32[2]{0:T(128)S(1)} %add.243), channel_id=1, source_target_pairs={{0,32},{2,34},{4,36},{6,38},{8,40},{10,42},{12,44},{14,46},{16,48}... | collective-permute-start | bytes 32 | tf_op jit(solution)/shard_map/ppermute | solution.py:25
  64.9 10.8 %collective-permute-start.5 = (f32[2]{0:T(128)S(1)}, f32[2]{0:T(128)S(1)}, u32[]{:S(2)}, u32[]{:S(2)}) collective-permute-start(f32[2]{0:T(128)S(1)} %add.244), channel_id=1, source_target_pairs={{0,1},{1,0},{2,3},{3,2},{4,5},{5,4},{6,7},{7,6},{8,9},{9,8},{10,11... | collective-permute-start | bytes 32 | tf_op jit(solution)/shard_map/ppermute | solution.py:25
  75.7 5.4 %collective-permute-start.6 = (f32[2]{0:T(128)S(1)}, f32[2]{0:T(128)S(1)}, u32[]{:S(2)}, u32[]{:S(2)}) collective-permute-start(f32[2]{0:T(128)S(1)} %add.245), channel_id=1, source_target_pairs={{0,64},{64,0},{128,192},{192,128},{256,320},{320,256},{384,448},{4... | collective-permute-start | bytes 32 | tf_op jit(solution)/shard_map/ppermute | solution.py:25
  81.1 6.3 %collective-permute-start.7 = (f32[2]{0:T(128)S(1)}, f32[2]{0:T(128)S(1)}, u32[]{:S(2)}, u32[]{:S(2)}) collective-permute-start(f32[2]{0:T(128)S(1)} %add.246), channel_id=1, source_target_pairs={{0,128},{64,192},{128,0},{192,64},{256,384},{320,448},{384,256},{4... | collective-permute-start | bytes 32 | tf_op jit(solution)/shard_map/ppermute | solution.py:25
  87.4 9.3 %collective-permute-start.8 = (f32[2]{0:T(128)S(1)}, f32[2]{0:T(128)S(1)}, u32[]{:S(2)}, u32[]{:S(2)}) collective-permute-start(f32[2]{0:T(128)S(1)} %add.247), channel_id=1, source_target_pairs={{0,256},{64,320},{128,384},{192,448},{256,0},{320,64},{384,128},{4... | collective-permute-start | bytes 32 | tf_op jit(solution)/shard_map/ppermute | solution.py:25
  99.4 28.3 %copy-start.1 = (bf16[1,5,512,512]{3,2,1,0:T(8,128)(2,1)S(1)}, bf16[1,5,512,512]{3,2,1,0:T(8,128)(2,1)}, u32[]{:S(2)}) copy-start(bf16[1,5,512,512]{3,2,1,0:T(8,128)(2,1)} %param.29) | copy-start | bytes 7864324
  101.0 96.7 %collective-permute-start.11 = (bf16[1024,512]{1,0:T(8,128)(2,1)S(1)}, bf16[1024,512]{1,0:T(8,128)(2,1)S(1)}, u32[]{:S(2)}, u32[]{:S(2)}) collective-permute-start(bf16[1024,512]{1,0:T(8,128)(2,1)S(1)} %fusion), channel_id=1, source_target_pairs={{4,0},{6,2},{8,4},{10,6},{12,8},{14,10},{16,12},{18,14},{20,16},{2... | collective-permute-start | bytes 3145736 | tf_op jit(solution)/shard_map/ppermute | solution.py:11
  108.4 92.5 %collective-permute-start.10 = (bf16[1024,512]{1,0:T(8,128)(2,1)S(1)}, bf16[1024,512]{1,0:T(8,128)(2,1)S(1)}, u32[]{:S(2)}, u32[]{:S(2)}) collective-permute-start(bf16[1024,512]{1,0:T(8,128)(2,1)S(1)} %fusion), channel_id=1, source_target_pairs={{62,0},{0,2},{2,4},{4,6},{6,8},{8,10},{10,12},{12,14},{14,16},{16,... | collective-permute-start | bytes 3145736 | tf_op jit(solution)/shard_map/ppermute | solution.py:11
  110.4 95.4 %collective-permute-start.9 = (bf16[1024,512]{1,0:T(8,128)(2,1)S(1)}, bf16[1024,512]{1,0:T(8,128)(2,1)S(1)}, u32[]{:S(2)}, u32[]{:S(2)}) collective-permute-start(bf16[1024,512]{1,0:T(8,128)(2,1)S(1)} %fusion), channel_id=1, source_target_pairs={{2,0},{4,2},{6,4},{8,6},{10,8},{12,10},{14,12},{16,14},{18,16},{20... | collective-permute-start | bytes 3145736 | tf_op jit(solution)/shard_map/ppermute | solution.py:11
  118.3 22.7 %collective-permute-start.15 = (f32[7,16,2]{2,1,0:T(8,128)S(1)}, f32[7,16,2]{2,1,0:T(8,128)S(1)}, u32[]{:S(2)}, u32[]{:S(2)}) collective-permute-start(f32[7,16,2]{2,1,0:T(8,128)S(1)} %get-tuple-element.50), channel_id=1, source_target_pairs={{62,0},{0,2},{2,4},{4,6},{6,8},{8,10},{10,12},{12,14},{14,16},{16,... | collective-permute-start | bytes 2696 | tf_op jit(solution)/shard_map/ppermute | solution.py:11
  120.2 28.7 %collective-permute-start.16 = (f32[7,16,2]{2,1,0:T(8,128)S(1)}, f32[7,16,2]{2,1,0:T(8,128)S(1)}, u32[]{:S(2)}, u32[]{:S(2)}) collective-permute-start(f32[7,16,2]{2,1,0:T(8,128)S(1)} %get-tuple-element.51), channel_id=1, source_target_pairs={{2,0},{4,2},{6,4},{8,6},{10,8},{12,10},{14,12},{16,14},{18,16},{20... | collective-permute-start | bytes 2696 | tf_op jit(solution)/shard_map/ppermute | solution.py:11
  141.0 66.1 %collective-permute-start.13 = (bf16[1024,512]{1,0:T(8,128)(2,1)S(1)}, bf16[1024,512]{1,0:T(8,128)(2,1)S(1)}, u32[]{:S(2)}, u32[]{:S(2)}) collective-permute-start(bf16[1024,512]{1,0:T(8,128)(2,1)S(1)} %fusion), channel_id=1, source_target_pairs={{6,0},{8,2},{10,4},{12,6},{14,8},{16,10},{18,12},{20,14},{22,16},{... | collective-permute-start | bytes 3145736 | tf_op jit(solution)/shard_map/ppermute | solution.py:11
  149.0 47.9 %copy-start.3 = (f32[1,16,1,512]{3,2,1,0:T(1,128)S(1)}, f32[1,16,1,512]{3,2,1,0:T(1,128)}, u32[]{:S(2)}) copy-start(f32[1,16,1,512]{3,2,1,0:T(1,128)} %param.21) | copy-start | bytes 98308
  149.0 47.9 %copy-start.4 = (f32[1,16,1,512]{3,2,1,0:T(1,128)S(1)}, f32[1,16,1,512]{3,2,1,0:T(1,128)}, u32[]{:S(2)}) copy-start(f32[1,16,1,512]{3,2,1,0:T(1,128)} %param.22) | copy-start | bytes 98308
  149.0 47.9 %copy-start.7 = (f32[1,16,1,512]{3,2,1,0:T(1,128)S(1)}, f32[1,16,1,512]{3,2,1,0:T(1,128)}, u32[]{:S(2)}) copy-start(f32[1,16,1,512]{3,2,1,0:T(1,128)} %param.26) | copy-start | bytes 98308
  149.1 47.9 %copy-start.8 = (f32[1,16,1,512]{3,2,1,0:T(1,128)S(1)}, f32[1,16,1,512]{3,2,1,0:T(1,128)}, u32[]{:S(2)}) copy-start(f32[1,16,1,512]{3,2,1,0:T(1,128)} %param.20) | copy-start | bytes 98308
  149.1 38.1 %collective-permute-start.17 = (f32[7,16,516]{2,1,0:T(8,128)S(1)}, f32[7,16,516]{2,1,0:T(8,128)S(1)}, u32[]{:S(2)}, u32[]{:S(2)}) collective-permute-start(f32[7,16,516]{2,1,0:T(8,128)S(1)} %pad_maximum_fusion), channel_id=1, source_target_pairs={{0,1},{1,0},{2,3},{3,2},{4,5},{5,4},{6,7},{7,6},{8,9},{9,8},{10,11... | collective-permute-start | bytes 693512 | tf_op jit(solution)/shard_map/ppermute | solution.py:37
  188.0 7.0 %collective-permute-start.19 = (f32[16,512]{1,0:T(8,128)S(1)}, f32[16,512]{1,0:T(8,128)S(1)}, u32[]{:S(2)}, u32[]{:S(2)}) collective-permute-start(f32[16,512]{1,0:T(8,128)S(1)} %fusion.59), channel_id=1, source_target_pairs={{64,0},{128,64},{192,128},{256,192},{320,256},{384,320},{448,384},... | collective-permute-start | bytes 98312 | tf_op jit(solution)/shard_map/ppermute | solution.py:17
  195.0 32.0 %collective-permute-start.12 = (bf16[1024,512]{1,0:T(8,128)(2,1)S(1)}, bf16[1024,512]{1,0:T(8,128)(2,1)S(1)}, u32[]{:S(2)}, u32[]{:S(2)}) collective-permute-start(bf16[1024,512]{1,0:T(8,128)(2,1)S(1)} %fusion), channel_id=1, source_target_pairs={{60,0},{62,2},{0,4},{2,6},{4,8},{6,10},{8,12},{10,14},{12,16},{14,... | collective-permute-start | bytes 3145736 | tf_op jit(solution)/shard_map/ppermute | solution.py:11
  197.7 58.1 %collective-permute-start.14 = (bf16[1024,512]{1,0:T(8,128)(2,1)S(1)}, bf16[1024,512]{1,0:T(8,128)(2,1)S(1)}, u32[]{:S(2)}, u32[]{:S(2)}) collective-permute-start(bf16[1024,512]{1,0:T(8,128)(2,1)S(1)} %fusion), channel_id=1, source_target_pairs={{58,0},{60,2},{62,4},{0,6},{2,8},{4,10},{6,12},{8,14},{10,16},{12,... | collective-permute-start | bytes 3145736 | tf_op jit(solution)/shard_map/ppermute | solution.py:11
  200.9 56.9 %collective-permute-start.18 = (f32[16,512]{1,0:T(8,128)S(1)}, f32[16,512]{1,0:T(8,128)S(1)}, u32[]{:S(2)}, u32[]{:S(2)}) collective-permute-start(f32[16,512]{1,0:T(8,128)S(1)} %fusion.66), channel_id=1, source_target_pairs={{0,64},{64,128},{128,192},{192,256},{256,320},{320,384},{384,448},... | collective-permute-start | bytes 98312 | tf_op jit(solution)/shard_map/ppermute | solution.py:17
  257.4 0.8 copy-start.2
  257.4 0.8 copy-start.5
  257.4 0.8 copy-start.6
  257.4 0.8 copy-start.9
  257.4 0.8 copy-start.10
  257.4 0.8 copy-start.11

commit v4 on v3

--- a/solution.py
+++ b/solution.py
@@ -71,7 +71,7 @@
     return moved, backed
 
 
-def localize(members, search, loc_cols, loc_vals):
+def localize(members, search, loc_cols, loc_vals, partials):
     count_members = members.shape[0]
     block = members.shape[-1]
     products = (members.astype(jnp.float32) * search[None]).astype(jnp.bfloat16)
@@ -93,11 +93,12 @@
         picked = tiles[jnp.argmax(match)]
         return jnp.where(jnp.any(match), picked, jnp.zeros_like(picked))
 
+    partials, _ = lax.optimization_barrier((partials, [sources[offset] for offset in offsets[1:]]))
     total = jnp.dot(flat, weight_for(0), preferred_element_type=jnp.float32)
     for offset in offsets[1:]:
         total = total + jnp.dot(sources[offset], weight_for(offset), preferred_element_type=jnp.float32)
     spread = total.reshape(products.shape)
-    return jnp.sum(members.astype(jnp.float32) * spread, axis=0) / (count_members - 1)
+    return jnp.sum(members.astype(jnp.float32) * spread, axis=0) / (count_members - 1), partials
 
 
 def local(
@@ -127,8 +128,6 @@
         + jnp.sum(search_obs * search_obs)
         + jnp.sum(search_incr * search_incr)
     )
-    sums = butterfly_sum(jnp.stack([resid_local, search_local]), ("lon", "lat", "win"))
-    alpha = sums[0] / (sums[1] + 1e-06)
 
     packed = jnp.concatenate(
         [search_incr[0, :, 0][None], search_dual[0, :, 0][None], tangent_coefs[0, :, :, 0]], axis=0
@@ -140,7 +139,13 @@
     earlier = shifted(moved, "win", 1)[None, :, None]
     following = shifted(backed, "win", -1)[None, :, None]
 
-    covar = localize(ensemble[0, :, :, 0], search_dual[0, :, 0], loc_cols, loc_vals)[None, :, None]
+    covar, partials = localize(
+        ensemble[0, :, :, 0], search_dual[0, :, 0], loc_cols, loc_vals, jnp.stack([resid_local, search_local])
+    )
+    covar = covar[None, :, None]
+    partials, _ = lax.optimization_barrier((partials, other))
+    sums = butterfly_sum(partials, ("lon", "lat", "win"))
+    alpha = sums[0] / (sums[1] + 1e-06)
     image_dual = covar + search_incr - earlier
     image_obs = obs_var * search_obs + obs_weight * search_incr
     image_incr = search_dual - following + obs_weight * search_obs

time: 262 us -> 252 us (0.962)
  the two profiles are of different devices: /device:TPU:24 before, /device:TPU:20 now
where the time goes in v4:
time: 252 us; the launch traced here: 251 us
  starting transfers between devices  103 us (41%)
  waiting for transfers between devices  91.6 us (36%)
  between operations  19.7 us (8%)
  other arithmetic  16.3 us (6%)
  matrix products  14.7 us (6%)
  local copies, waits for them, and re-layouts  6.04 us (2%)
    ppermute x9, starting transfers between devices, butterfly_sum(): lax.ppermute(value, axis, [(i, i ^ step) for i in range(count)])  55.4 us
    ppermute x8, waiting for transfers between devices, from_offset(): lax.ppermute(value, axis, [((i + distance) % count, i) for i in range(cou...  40.7 us
    ppermute x8, starting transfers between devices, from_offset(): lax.ppermute(value, axis, [((i + distance) % count, i) for i in range(cou...  30.2 us
    ppermute x1, waiting for transfers between devices, lat_partner(): return lax.ppermute(value, 'lat', [(0, 1), (1, 0)])  25.6 us
    ppermute x9, waiting for transfers between devices, butterfly_sum(): lax.ppermute(value, axis, [(i, i ^ step) for i in range(count)])  25.3 us
    dot_general x6, matrix products, localize(): jnp.dot(sources[offset], weight_for(offset), preferred_element_type=jnp.f...  11.9 us
    ppermute x1, starting transfers between devices, lat_partner(): return lax.ppermute(value, 'lat', [(0, 1), (1, 0)])  11 us
    ppermute x2, starting transfers between devices, shifted(): lax.ppermute(value, axis, [(source, source + steps) for source in range(l...  5.84 us
  transfers between devices with their start and end apart: 20, of which 11 were waited for; matrix products, arithmetic and copies ran while one was open for 13% of the time, Pallas kernels for 0%

profile of v4, /device:TPU:20, one launch (start us, length us, event | category | flops | bytes accessed | tf_op | source)
XLA Modules:
  0.0 250.8 jit_solution(17658518785734657403)
XLA Ops:
  0.7 0.9 copy_bitcast_fusion.3
  1.6 2.4 fusion.2
  4.1 3.8 %collective-permute-start.5 = (bf16[1024,512]{1,0:T(8,128)(2,1)}, bf16[1024,512]{1,0:T(8,128)(2,1)}, u32[]{:S(2)}, u32[]{:S(2)}) collective-permute-start(bf16[1024,512]{1,0:T(8,128)(2,1)} %fusion.2), channel_id=1, source_target_pairs={{58,0},{60,2},{62,4},{0,6},{2,8},{4,10},{6,12},{8,14},{10,16},{12,... | collective-permute-start | bytes 3145736 | tf_op jit(solution)/shard_map/ppermute | solution.py:11
  7.9 3.7 %collective-permute-start.4 = (bf16[1024,512]{1,0:T(8,128)(2,1)}, bf16[1024,512]{1,0:T(8,128)(2,1)}, u32[]{:S(2)}, u32[]{:S(2)}) collective-permute-start(bf16[1024,512]{1,0:T(8,128)(2,1)} %fusion.2), channel_id=1, source_target_pairs={{6,0},{8,2},{10,4},{12,6},{14,8},{16,10},{18,12},{20,14},{22,16},{... | collective-permute-start | bytes 3145736 | tf_op jit(solution)/shard_map/ppermute | solution.py:11
  11.6 4.3 %collective-permute-start.3 = (bf16[1024,512]{1,0:T(8,128)(2,1)}, bf16[1024,512]{1,0:T(8,128)(2,1)}, u32[]{:S(2)}, u32[]{:S(2)}) collective-permute-start(bf16[1024,512]{1,0:T(8,128)(2,1)} %fusion.2), channel_id=1, source_target_pairs={{60,0},{62,2},{0,4},{2,6},{4,8},{6,10},{8,12},{10,14},{12,16},{14,... | collective-permute-start | bytes 3145736 | tf_op jit(solution)/shard_map/ppermute | solution.py:11
  15.9 0.7 pad_maximum_fusion.3
  16.7 2.3 collective-permute-start.6
  19.0 5.9 %collective-permute-start.7 = (f32[7,16,2]{2,1,0:T(8,128)}, f32[7,16,2]{2,1,0:T(8,128)}, u32[]{:S(2)}, u32[]{:S(2)}) collective-permute-start(f32[7,16,2]{2,1,0:T(8,128)} %get-tuple-element.55), channel_id=1, source_target_pairs={{2,0},{4,2},{6,4},{8,6},{10,8},{12,10},{14,12},{16,14},{18,16},{20... | collective-permute-start | bytes 2696 | tf_op jit(solution)/shard_map/ppermute | solution.py:11
  25.0 0.7 multiply_reduce_fusion.2
  25.7 0.7 multiply_reduce_fusion
  26.3 0.7 bitcast_reduce_fusion
  27.0 0.7 bitcast_reduce_fusion.6
  27.7 0.7 bitcast_reduce_fusion.5
  28.4 0.6 bitcast_reduce_fusion.4
  29.1 0.7 bitcast_reduce_fusion.3
  29.8 0.7 bitcast_reduce_fusion.2
  30.4 0.8 compare_reduce_fusion
  31.3 0.7 bitcast_reduce_fusion.1
  31.9 1.2 fusion
  33.2 0.7 multiply_reduce_fusion.1
  33.8 0.7 multiply_reduce_fusion.3
  37.6 0.7 multiply_reduce_fusion.4
  40.8 2.7 %fusion.17 = f32[1024,512]{1,0:T(8,128)S(1)} fusion(bf16[1024,512]{1,0:T(8,128)(2,1)} %bitcast.137, bf16[1,5,512,512]{3,2,1,0:T(8,128)(2,1)} %param.29, s32[]{:T(128)S(6)} %select_n.157, pred[]{:T(512)} %get-tuple-element.35), kind=kOutput, calls=%fused_computation.19 | convolution fusion | flops 537133056 | bytes 3670532 | tf_op jit(solution)/shard_map/dot_general | solution.py:97
  46.8 0.6 fusion.90
  55.8 25.1 %collective-permute-done.6 = f32[7,16,2]{2,1,0:T(8,128)} collective-permute-done((f32[7,16,2]{2,1,0:T(8,128)}, f32[7,16,2]{2,1,0:T(8,128)}, u32[]{:S(2)}, u32[]{:S(2)}) %collective-permute-start.6) | collective-permute-done | bytes 928 | tf_op jit(solution)/shard_map/ppermute | solution.py:11
  80.9 1.9 collective-permute-start.2
  82.8 1.0 pad_maximum_fusion
  83.9 11.0 %collective-permute-start.8 = (f32[7,16,516]{2,1,0:T(8,128)S(1)}, f32[7,16,516]{2,1,0:T(8,128)S(1)}, u32[]{:S(2)}, u32[]{:S(2)}) collective-permute-start(f32[7,16,516]{2,1,0:T(8,128)S(1)} %pad_maximum_fusion), channel_id=1, source_target_pairs={{0,1},{1,0},{2,3},{3,2},{4,5},{5,4},{6,7},{7,6},{8,9},{9,8},{10,11... | collective-permute-start | bytes 693512 | tf_op jit(solution)/shard_map/ppermute | solution.py:37
  95.2 25.6 %collective-permute-done.8 = f32[7,16,516]{2,1,0:T(8,128)S(1)} collective-permute-done((f32[7,16,516]{2,1,0:T(8,128)S(1)}, f32[7,16,516]{2,1,0:T(8,128)S(1)}, u32[]{:S(2)}, u32[]{:S(2)}) %collective-permute-start.8) | collective-permute-done | bytes 231200 | tf_op jit(solution)/shard_map/ppermute | solution.py:37
  120.8 1.9 collective-permute-start.1
  122.8 6.3 %collective-permute-start = (bf16[1024,512]{1,0:T(8,128)(2,1)}, bf16[1024,512]{1,0:T(8,128)(2,1)S(1)}, u32[]{:S(2)}, u32[]{:S(2)}) collective-permute-start(bf16[1024,512]{1,0:T(8,128)(2,1)} %fusion.2), channel_id=1, source_target_pairs={{2,0},{4,2},{6,4},{8,6},{10,8},{12,10},{14,12},{16,14},{18,16},{20... | collective-permute-start | bytes 3145736 | tf_op jit(solution)/shard_map/ppermute | solution.py:11
  130.2 3.5 %collective-permute-start.18 = (f32[16,512]{1,0:T(8,128)S(1)}, f32[16,512]{1,0:T(8,128)S(1)}, u32[]{:S(2)}, u32[]{:S(2)}) collective-permute-start(f32[16,512]{1,0:T(8,128)S(1)} %fusion.66), channel_id=1, source_target_pairs={{0,64},{64,128},{128,192},{192,256},{256,320},{320,384},{384,448},... | collective-permute-start | bytes 98312 | tf_op jit(solution)/shard_map/ppermute | solution.py:17
  133.7 2.4 collective-permute-start.19
  136.0 15.5 %collective-permute-done.1 = bf16[1024,512]{1,0:T(8,128)(2,1)S(1)} collective-permute-done((bf16[1024,512]{1,0:T(8,128)(2,1)}, bf16[1024,512]{1,0:T(8,128)(2,1)S(1)}, u32[]{:S(2)}, u32[]{:S(2)}) %collective-permute-start.1) | collective-permute-done | bytes 1048608 | tf_op jit(solution)/shard_map/ppermute | solution.py:11
  151.6 22.9 %collective-permute-start.9 = (f32[2]{0:T(128)S(1)}, f32[2]{0:T(128)S(1)}, u32[]{:S(2)}, u32[]{:S(2)}) collective-permute-start(f32[2]{0:T(128)S(1)} %pad_maximum_fusion.4), channel_id=1, source_target_pairs={{0,2},{2,0},{4,6},{6,4},{8,10},{10,8},{12,14},{14,12},{16,18},{18,... | collective-permute-start | bytes 32 | tf_op jit(solution)/shard_map/ppermute | solution.py:25
  174.5 1.3 fusion.15
  175.8 1.4 fusion.13
  177.2 1.3 fusion.11
  178.6 2.6 %fusion.9 = f32[1024,512]{1,0:T(8,128)S(1)} fusion(bf16[1024,512]{1,0:T(8,128)(2,1)} %collective-permute-done.3, bf16[1,5,512,512]{3,2,1,0:T(8,128)(2,1)S(1)} %copy-done.1, s32[]{:T(128)S(6)} %select_n.177, pred[]{:T(512)} %get-tuple-element.31), kind=kOutput, calls=%fused_computation.11 | convolution fusion | flops 537133056 | bytes 3670021 | tf_op jit(solution)/shard_map/dot_general | solution.py:99
  181.1 2.6 %fusion.7 = f32[1024,512]{1,0:T(8,128)S(1)} fusion(bf16[1024,512]{1,0:T(8,128)(2,1)} %collective-permute-done.4, bf16[1,5,512,512]{3,2,1,0:T(8,128)(2,1)S(1)} %copy-done.1, s32[]{:T(128)S(6)} %select_n.182, pred[]{:T(512)} %get-tuple-element.36), kind=kOutput, calls=%fused_computation.9 | convolution fusion | flops 537133056 | bytes 3670021 | tf_op jit(solution)/shard_map/dot_general | solution.py:99
  183.7 2.8 %add_add_fusion = f32[1024,512]{1,0:T(8,128)S(1)} fusion(f32[1024,512]{1,0:T(8,128)S(1)} %fusion.7, f32[1024,512]{1,0:T(8,128)S(1)} %fusion.9, f32[1024,512]{1,0:T(8,128)S(1)} %fusion.11, f32[1024,512]{1,0:T(8,128)S(1)} %fusion.13, f32[1024,512]{1,0:T(8,128)S(1)} %fusion.17, f32[1024,512]{1,0:T(8,128)S(1)} %fusion.15, ...), kind=kOutput, calls=%fused_computation.6 | convolution fusion | flops 540278784 | bytes 16252933 | tf_op jit(solution)/shard_map/dot_general | solution.py:99
  187.0 7.2 %collective-permute-start.10 = (f32[2]{0:T(128)S(1)}, f32[2]{0:T(128)S(1)}, u32[]{:S(2)}, u32[]{:S(2)}) collective-permute-start(f32[2]{0:T(128)S(1)} %add.240), channel_id=1, source_target_pairs={{0,4},{2,6},{4,0},{6,2},{8,12},{10,14},{12,8},{14,10},{16,20},{18,... | collective-permute-start | bytes 32 | tf_op jit(solution)/shard_map/ppermute | solution.py:25
  194.2 1.5 collective-permute-done.10
  195.7 3.2 %collective-permute-start.11 = (f32[2]{0:T(128)S(1)}, f32[2]{0:T(128)S(1)}, u32[]{:S(2)}, u32[]{:S(2)}) collective-permute-start(f32[2]{0:T(128)S(1)} %add.241), channel_id=1, source_target_pairs={{0,8},{2,10},{4,12},{6,14},{8,0},{10,2},{12,4},{14,6},{16,24},{18,... | collective-permute-start | bytes 32 | tf_op jit(solution)/shard_map/ppermute | solution.py:25
  198.9 3.1 %collective-permute-done.11 = f32[2]{0:T(128)S(1)} collective-permute-done((f32[2]{0:T(128)S(1)}, f32[2]{0:T(128)S(1)}, u32[]{:S(2)}, u32[]{:S(2)}) %collective-permute-start.11) | collective-permute-done | bytes 40 | tf_op jit(solution)/shard_map/ppermute | solution.py:25
  202.0 3.1 %collective-permute-start.12 = (f32[2]{0:T(128)S(1)}, f32[2]{0:T(128)S(1)}, u32[]{:S(2)}, u32[]{:S(2)}) collective-permute-start(f32[2]{0:T(128)S(1)} %add.242), channel_id=1, source_target_pairs={{0,16},{2,18},{4,20},{6,22},{8,24},{10,26},{12,28},{14,30},{16,0},... | collective-permute-start | bytes 32 | tf_op jit(solution)/shard_map/ppermute | solution.py:25
  205.1 2.3 collective-permute-done.12
  207.5 2.4 collective-permute-start.13
  209.9 4.5 %collective-permute-done.13 = f32[2]{0:T(128)S(1)} collective-permute-done((f32[2]{0:T(128)S(1)}, f32[2]{0:T(128)S(1)}, u32[]{:S(2)}, u32[]{:S(2)}) %collective-permute-start.13) | collective-permute-done | bytes 40 | tf_op jit(solution)/shard_map/ppermute | solution.py:25
  214.4 5.0 %collective-permute-start.14 = (f32[2]{0:T(128)S(1)}, f32[2]{0:T(128)S(1)}, u32[]{:S(2)}, u32[]{:S(2)}) collective-permute-start(f32[2]{0:T(128)S(1)} %add.244), channel_id=1, source_target_pairs={{0,1},{1,0},{2,3},{3,2},{4,5},{5,4},{6,7},{7,6},{8,9},{9,8},{10,11... | collective-permute-start | bytes 32 | tf_op jit(solution)/shard_map/ppermute | solution.py:25
  219.4 4.4 %collective-permute-done.14 = f32[2]{0:T(128)S(1)} collective-permute-done((f32[2]{0:T(128)S(1)}, f32[2]{0:T(128)S(1)}, u32[]{:S(2)}, u32[]{:S(2)}) %collective-permute-start.14) | collective-permute-done | bytes 40 | tf_op jit(solution)/shard_map/ppermute | solution.py:25
  223.7 3.5 %collective-permute-start.15 = (f32[2]{0:T(128)S(1)}, f32[2]{0:T(128)S(1)}, u32[]{:S(2)}, u32[]{:S(2)}) collective-permute-start(f32[2]{0:T(128)S(1)} %add.245), channel_id=1, source_target_pairs={{0,64},{64,0},{128,192},{192,128},{256,320},{320,256},{384,448},{4... | collective-permute-start | bytes 32 | tf_op jit(solution)/shard_map/ppermute | solution.py:25
  227.2 1.9 collective-permute-done.15
  229.2 2.2 collective-permute-start.16
  231.4 4.1 %collective-permute-done.16 = f32[2]{0:T(128)S(1)} collective-permute-done((f32[2]{0:T(128)S(1)}, f32[2]{0:T(128)S(1)}, u32[]{:S(2)}, u32[]{:S(2)}) %collective-permute-start.16) | collective-permute-done | bytes 40 | tf_op jit(solution)/shard_map/ppermute | solution.py:25
  235.5 5.9 %collective-permute-start.17 = (f32[2]{0:T(128)S(1)}, f32[2]{0:T(128)S(1)}, u32[]{:S(2)}, u32[]{:S(2)}) collective-permute-start(f32[2]{0:T(128)S(1)} %add.247), channel_id=1, source_target_pairs={{0,256},{64,320},{128,384},{192,448},{256,0},{320,64},{384,128},{4... | collective-permute-start | bytes 32 | tf_op jit(solution)/shard_map/ppermute | solution.py:25
  241.4 3.4 %collective-permute-done.17 = f32[2]{0:T(128)S(1)} collective-permute-done((f32[2]{0:T(128)S(1)}, f32[2]{0:T(128)S(1)}, u32[]{:S(2)}, u32[]{:S(2)}) %collective-permute-start.17) | collective-permute-done | bytes 40 | tf_op jit(solution)/shard_map/ppermute | solution.py:25
  244.8 0.6 fusion.92
  246.9 0.6 copy.38
  247.5 0.6 copy.42
  248.2 0.6 copy.40
  248.8 0.6 copy.41
  249.5 0.6 copy.39
  250.1 0.7 multiply_subtract_fusion
  (84 shorter events, 2.0 us)
Async XLA Ops:
  0.6 24.3 %copy-start.2 = (f32[1,16,1,512]{3,2,1,0:T(1,128)S(1)}, f32[1,16,1,512]{3,2,1,0:T(1,128)}, u32[]{:S(2)}) copy-start(f32[1,16,1,512]{3,2,1,0:T(1,128)} %param.21) | copy-start | bytes 98308
  0.6 25.0 %copy-start.4 = (f32[1,16,1,512]{3,2,1,0:T(1,128)S(1)}, f32[1,16,1,512]{3,2,1,0:T(1,128)}, u32[]{:S(2)}) copy-start(f32[1,16,1,512]{3,2,1,0:T(1,128)} %param.23) | copy-start | bytes 98308
  0.7 31.3 %copy-start = (bf16[1,64,16,1,512]{4,2,3,1,0:T(8,128)(2,1)S(1)}, bf16[1,64,16,1,512]{4,2,3,1,0:T(8,128)(2,1)}, u32[]{:S(2)}) copy-start(bf16[1,64,16,1,512]{4,2,3,1,0:T(8,128)(2,1)} %param.24) | copy-start | bytes 3145732
  0.7 15.2 %copy-start.3 = (f32[1,5,16,1,512]{4,3,2,1,0:T(1,128)S(1)}, f32[1,5,16,1,512]{4,3,2,1,0:T(1,128)}, u32[]{:S(2)}) copy-start(f32[1,5,16,1,512]{4,3,2,1,0:T(1,128)} %param.25) | copy-start | bytes 491524
  0.7 25.6 %copy-start.23 = (s32[1,5]{1,0:T(1,128)S(1)}, s32[1,5]{1,0:T(1,128)}, u32[]{:S(2)}) copy-start(s32[1,5]{1,0:T(1,128)} %param.28) | copy-start | bytes 64
  1.6 14.4 %copy-start.8 = (f32[1,16,512]{2,1,0:T(8,128)}, f32[1,16,512]{2,1,0:T(8,128)S(1)}, u32[]{:S(2)}) copy-start(f32[1,16,512]{2,1,0:T(8,128)S(1)} %get-tuple-element.69) | copy-start | bytes 98308
  1.6 15.1 %copy-start.9 = (f32[1,16,512]{2,1,0:T(8,128)}, f32[1,16,512]{2,1,0:T(8,128)S(1)}, u32[]{:S(2)}) copy-start(f32[1,16,512]{2,1,0:T(8,128)S(1)} %get-tuple-element.75) | copy-start | bytes 98308
  1.6 31.6 %copy-start.6 = (f32[1,16,1,512]{3,2,1,0:T(1,128)S(1)}, f32[1,16,1,512]{3,2,1,0:T(1,128)}, u32[]{:S(2)}) copy-start(f32[1,16,1,512]{3,2,1,0:T(1,128)} %param.22) | copy-start | bytes 98308
  1.6 32.2 %copy-start.17 = (f32[1,16,1,512]{3,2,1,0:T(1,128)S(1)}, f32[1,16,1,512]{3,2,1,0:T(1,128)}, u32[]{:S(2)}) copy-start(f32[1,16,1,512]{3,2,1,0:T(1,128)} %param.20) | copy-start | bytes 98308
  4.1 33.6 %copy-start.10 = (f32[1,16,1,512]{3,2,1,0:T(1,128)S(1)}, f32[1,16,1,512]{3,2,1,0:T(1,128)}, u32[]{:S(2)}) copy-start(f32[1,16,1,512]{3,2,1,0:T(1,128)} %param.19) | copy-start | bytes 98308
  4.1 33.6 %copy-start.12 = (f32[1,16,1,512]{3,2,1,0:T(1,128)S(1)}, f32[1,16,1,512]{3,2,1,0:T(1,128)}, u32[]{:S(2)}) copy-start(f32[1,16,1,512]{3,2,1,0:T(1,128)} %param.18) | copy-start | bytes 98308
  4.1 118.7 %collective-permute-start.5 = (bf16[1024,512]{1,0:T(8,128)(2,1)}, bf16[1024,512]{1,0:T(8,128)(2,1)}, u32[]{:S(2)}, u32[]{:S(2)}) collective-permute-start(bf16[1024,512]{1,0:T(8,128)(2,1)} %fusion.2), channel_id=1, source_target_pairs={{58,0},{60,2},{62,4},{0,6},{2,8},{4,10},{6,12},{8,14},{10,16},{12,... | collective-permute-start | bytes 3145736 | tf_op jit(solution)/shard_map/ppermute | solution.py:11
  7.9 122.2 %collective-permute-start.4 = (bf16[1024,512]{1,0:T(8,128)(2,1)}, bf16[1024,512]{1,0:T(8,128)(2,1)}, u32[]{:S(2)}, u32[]{:S(2)}) collective-permute-start(bf16[1024,512]{1,0:T(8,128)(2,1)} %fusion.2), channel_id=1, source_target_pairs={{6,0},{8,2},{10,4},{12,6},{14,8},{16,10},{18,12},{20,14},{22,16},{... | collective-permute-start | bytes 3145736 | tf_op jit(solution)/shard_map/ppermute | solution.py:11
  11.6 122.0 %collective-permute-start.3 = (bf16[1024,512]{1,0:T(8,128)(2,1)}, bf16[1024,512]{1,0:T(8,128)(2,1)}, u32[]{:S(2)}, u32[]{:S(2)}) collective-permute-start(bf16[1024,512]{1,0:T(8,128)(2,1)} %fusion.2), channel_id=1, source_target_pairs={{60,0},{62,2},{0,4},{2,6},{4,8},{6,10},{8,12},{10,14},{12,16},{14,... | collective-permute-start | bytes 3145736 | tf_op jit(solution)/shard_map/ppermute | solution.py:11
  16.7 64.2 %collective-permute-start.6 = (f32[7,16,2]{2,1,0:T(8,128)}, f32[7,16,2]{2,1,0:T(8,128)}, u32[]{:S(2)}, u32[]{:S(2)}) collective-permute-start(f32[7,16,2]{2,1,0:T(8,128)} %get-tuple-element.54), channel_id=1, source_target_pairs={{62,0},{0,2},{2,4},{4,6},{6,8},{8,10},{10,12},{12,14},{14,16},{16,... | collective-permute-start | bytes 2696 | tf_op jit(solution)/shard_map/ppermute | solution.py:11
  19.0 63.8 %collective-permute-start.7 = (f32[7,16,2]{2,1,0:T(8,128)}, f32[7,16,2]{2,1,0:T(8,128)}, u32[]{:S(2)}, u32[]{:S(2)}) collective-permute-start(f32[7,16,2]{2,1,0:T(8,128)} %get-tuple-element.55), channel_id=1, source_target_pairs={{2,0},{4,2},{6,4},{8,6},{10,8},{12,10},{14,12},{16,14},{18,16},{20... | collective-permute-start | bytes 2696 | tf_op jit(solution)/shard_map/ppermute | solution.py:11
  47.5 82.3 %copy-start.5 = (f32[1,1,16,1,512]{4,3,2,1,0:T(1,128)S(1)}, f32[1,1,16,1,512]{4,3,2,1,0:T(1,128)}, u32[]{:S(2)}) copy-start(f32[1,1,16,1,512]{4,3,2,1,0:T(1,128)} %get-tuple-element.56) | copy-start | bytes 98308
  55.7 74.0 %copy-start.15 = (f32[1,1,16,1,512]{4,3,2,1,0:T(1,128)S(1)}, f32[1,1,16,1,512]{4,3,2,1,0:T(1,128)}, u32[]{:S(2)}) copy-start(f32[1,1,16,1,512]{4,3,2,1,0:T(1,128)} %get-tuple-element.57) | copy-start | bytes 98308
  55.7 74.0 %copy-start.16 = (f32[1,1,16,1,512]{4,3,2,1,0:T(1,128)S(1)}, f32[1,1,16,1,512]{4,3,2,1,0:T(1,128)}, u32[]{:S(2)}) copy-start(f32[1,1,16,1,512]{4,3,2,1,0:T(1,128)} %get-tuple-element.58) | copy-start | bytes 98308
  80.9 55.1 %collective-permute-start.2 = (bf16[1024,512]{1,0:T(8,128)(2,1)}, bf16[1024,512]{1,0:T(8,128)(2,1)S(1)}, u32[]{:S(2)}, u32[]{:S(2)}) collective-permute-start(bf16[1024,512]{1,0:T(8,128)(2,1)} %fusion.2), channel_id=1, source_target_pairs={{4,0},{6,2},{8,4},{10,6},{12,8},{14,10},{16,12},{18,14},{20,16},{2... | collective-permute-start | bytes 3145736 | tf_op jit(solution)/shard_map/ppermute | solution.py:11
  83.9 90.7 %copy-start.1 = (bf16[1,5,512,512]{3,2,1,0:T(8,128)(2,1)S(1)}, bf16[1,5,512,512]{3,2,1,0:T(8,128)(2,1)}, u32[]{:S(2)}) copy-start(bf16[1,5,512,512]{3,2,1,0:T(8,128)(2,1)} %param.29) | copy-start | bytes 7864324
  83.9 36.9 %collective-permute-start.8 = (f32[7,16,516]{2,1,0:T(8,128)S(1)}, f32[7,16,516]{2,1,0:T(8,128)S(1)}, u32[]{:S(2)}, u32[]{:S(2)}) collective-permute-start(f32[7,16,516]{2,1,0:T(8,128)S(1)} %pad_maximum_fusion), channel_id=1, source_target_pairs={{0,1},{1,0},{2,3},{3,2},{4,5},{5,4},{6,7},{7,6},{8,9},{9,8},{10,11... | collective-permute-start | bytes 693512 | tf_op jit(solution)/shard_map/ppermute | solution.py:37
  120.8 30.8 %collective-permute-start.1 = (bf16[1024,512]{1,0:T(8,128)(2,1)}, bf16[1024,512]{1,0:T(8,128)(2,1)S(1)}, u32[]{:S(2)}, u32[]{:S(2)}) collective-permute-start(bf16[1024,512]{1,0:T(8,128)(2,1)} %fusion.2), channel_id=1, source_target_pairs={{62,0},{0,2},{2,4},{4,6},{6,8},{8,10},{10,12},{12,14},{14,16},{16,... | collective-permute-start | bytes 3145736 | tf_op jit(solution)/shard_map/ppermute | solution.py:11
  122.8 28.8 %collective-permute-start = (bf16[1024,512]{1,0:T(8,128)(2,1)}, bf16[1024,512]{1,0:T(8,128)(2,1)S(1)}, u32[]{:S(2)}, u32[]{:S(2)}) collective-permute-start(bf16[1024,512]{1,0:T(8,128)(2,1)} %fusion.2), channel_id=1, source_target_pairs={{2,0},{4,2},{6,4},{8,6},{10,8},{12,10},{14,12},{16,14},{18,16},{20... | collective-permute-start | bytes 3145736 | tf_op jit(solution)/shard_map/ppermute | solution.py:11
  130.2 116.6 %collective-permute-start.18 = (f32[16,512]{1,0:T(8,128)S(1)}, f32[16,512]{1,0:T(8,128)S(1)}, u32[]{:S(2)}, u32[]{:S(2)}) collective-permute-start(f32[16,512]{1,0:T(8,128)S(1)} %fusion.66), channel_id=1, source_target_pairs={{0,64},{64,128},{128,192},{192,256},{256,320},{320,384},{384,448},... | collective-permute-start | bytes 98312 | tf_op jit(solution)/shard_map/ppermute | solution.py:17
  133.7 116.4 %collective-permute-start.19 = (f32[16,512]{1,0:T(8,128)S(1)}, f32[16,512]{1,0:T(8,128)S(1)}, u32[]{:S(2)}, u32[]{:S(2)}) collective-permute-start(f32[16,512]{1,0:T(8,128)S(1)} %fusion.59), channel_id=1, source_target_pairs={{64,0},{128,64},{192,128},{256,192},{320,256},{384,320},{448,384},... | collective-permute-start | bytes 98312 | tf_op jit(solution)/shard_map/ppermute | solution.py:17
  151.6 35.4 %collective-permute-start.9 = (f32[2]{0:T(128)S(1)}, f32[2]{0:T(128)S(1)}, u32[]{:S(2)}, u32[]{:S(2)}) collective-permute-start(f32[2]{0:T(128)S(1)} %pad_maximum_fusion.4), channel_id=1, source_target_pairs={{0,2},{2,0},{4,6},{6,4},{8,10},{10,8},{12,14},{14,12},{16,18},{18,... | collective-permute-start | bytes 32 | tf_op jit(solution)/shard_map/ppermute | solution.py:25
  186.5 60.2 %copy-start.7 = (f32[1,16,1,512]{3,2,1,0:T(1,128)S(1)}, f32[1,16,1,512]{3,2,1,0:T(1,128)}, u32[]{:S(2)}) copy-start(f32[1,16,1,512]{3,2,1,0:T(1,128)} %param.22) | copy-start | bytes 98308
  186.5 60.2 %copy-start.11 = (f32[1,16,1,512]{3,2,1,0:T(1,128)S(1)}, f32[1,16,1,512]{3,2,1,0:T(1,128)}, u32[]{:S(2)}) copy-start(f32[1,16,1,512]{3,2,1,0:T(1,128)} %param.19) | copy-start | bytes 98308
  186.5 60.2 %copy-start.13 = (f32[1,16,1,512]{3,2,1,0:T(1,128)S(1)}, f32[1,16,1,512]{3,2,1,0:T(1,128)}, u32[]{:S(2)}) copy-start(f32[1,16,1,512]{3,2,1,0:T(1,128)} %param.18) | copy-start | bytes 98308
  186.5 60.2 %copy-start.14 = (f32[1,16,1,512]{3,2,1,0:T(1,128)S(1)}, f32[1,16,1,512]{3,2,1,0:T(1,128)}, u32[]{:S(2)}) copy-start(f32[1,16,1,512]{3,2,1,0:T(1,128)} %param.26) | copy-start | bytes 98308
  186.5 60.2 %copy-start.19 = (f32[1,16,1,512]{3,2,1,0:T(1,128)S(1)}, f32[1,16,1,512]{3,2,1,0:T(1,128)}, u32[]{:S(2)}) copy-start(f32[1,16,1,512]{3,2,1,0:T(1,128)} %param.27) | copy-start | bytes 98308
  186.6 60.2 %copy-start.20 = (f32[1,16,1,512]{3,2,1,0:T(1,128)S(1)}, f32[1,16,1,512]{3,2,1,0:T(1,128)}, u32[]{:S(2)}) copy-start(f32[1,16,1,512]{3,2,1,0:T(1,128)} %param.17) | copy-start | bytes 98308
  186.6 60.2 %copy-start.21 = (f32[1,16,1,512]{3,2,1,0:T(1,128)S(1)}, f32[1,16,1,512]{3,2,1,0:T(1,128)}, u32[]{:S(2)}) copy-start(f32[1,16,1,512]{3,2,1,0:T(1,128)} %param.16) | copy-start | bytes 98308
  186.6 60.3 %copy-start.22 = (f32[1,16,1,512]{3,2,1,0:T(1,128)S(1)}, f32[1,16,1,512]{3,2,1,0:T(1,128)}, u32[]{:S(2)}) copy-start(f32[1,16,1,512]{3,2,1,0:T(1,128)} %param.15) | copy-start | bytes 98308
  186.6 63.5 %copy-start.18 = (f32[1,16,1,512]{3,2,1,0:T(1,128)S(1)}, f32[1,16,1,512]{3,2,1,0:T(1,128)}, u32[]{:S(2)}) copy-start(f32[1,16,1,512]{3,2,1,0:T(1,128)} %param.20) | copy-start | bytes 98308
  187.0 8.7 %collective-permute-start.10 = (f32[2]{0:T(128)S(1)}, f32[2]{0:T(128)S(1)}, u32[]{:S(2)}, u32[]{:S(2)}) collective-permute-start(f32[2]{0:T(128)S(1)} %add.240), channel_id=1, source_target_pairs={{0,4},{2,6},{4,0},{6,2},{8,12},{10,14},{12,8},{14,10},{16,20},{18,... | collective-permute-start | bytes 32 | tf_op jit(solution)/shard_map/ppermute | solution.py:25
  195.7 6.3 %collective-permute-start.11 = (f32[2]{0:T(128)S(1)}, f32[2]{0:T(128)S(1)}, u32[]{:S(2)}, u32[]{:S(2)}) collective-permute-start(f32[2]{0:T(128)S(1)} %add.241), channel_id=1, source_target_pairs={{0,8},{2,10},{4,12},{6,14},{8,0},{10,2},{12,4},{14,6},{16,24},{18,... | collective-permute-start | bytes 32 | tf_op jit(solution)/shard_map/ppermute | solution.py:25
  202.0 5.4 %collective-permute-start.12 = (f32[2]{0:T(128)S(1)}, f32[2]{0:T(128)S(1)}, u32[]{:S(2)}, u32[]{:S(2)}) collective-permute-start(f32[2]{0:T(128)S(1)} %add.242), channel_id=1, source_target_pairs={{0,16},{2,18},{4,20},{6,22},{8,24},{10,26},{12,28},{14,30},{16,0},... | collective-permute-start | bytes 32 | tf_op jit(solution)/shard_map/ppermute | solution.py:25
  207.5 6.9 %collective-permute-start.13 = (f32[2]{0:T(128)S(1)}, f32[2]{0:T(128)S(1)}, u32[]{:S(2)}, u32[]{:S(2)}) collective-permute-start(f32[2]{0:T(128)S(1)} %add.243), channel_id=1, source_target_pairs={{0,32},{2,34},{4,36},{6,38},{8,40},{10,42},{12,44},{14,46},{16,48}... | collective-permute-start | bytes 32 | tf_op jit(solution)/shard_map/ppermute | solution.py:25
  214.4 9.3 %collective-permute-start.14 = (f32[2]{0:T(128)S(1)}, f32[2]{0:T(128)S(1)}, u32[]{:S(2)}, u32[]{:S(2)}) collective-permute-start(f32[2]{0:T(128)S(1)} %add.244), channel_id=1, source_target_pairs={{0,1},{1,0},{2,3},{3,2},{4,5},{5,4},{6,7},{7,6},{8,9},{9,8},{10,11... | collective-permute-start | bytes 32 | tf_op jit(solution)/shard_map/ppermute | solution.py:25
  223.7 5.4 %collective-permute-start.15 = (f32[2]{0:T(128)S(1)}, f32[2]{0:T(128)S(1)}, u32[]{:S(2)}, u32[]{:S(2)}) collective-permute-start(f32[2]{0:T(128)S(1)} %add.245), channel_id=1, source_target_pairs={{0,64},{64,0},{128,192},{192,128},{256,320},{320,256},{384,448},{4... | collective-permute-start | bytes 32 | tf_op jit(solution)/shard_map/ppermute | solution.py:25
  229.2 6.3 %collective-permute-start.16 = (f32[2]{0:T(128)S(1)}, f32[2]{0:T(128)S(1)}, u32[]{:S(2)}, u32[]{:S(2)}) collective-permute-start(f32[2]{0:T(128)S(1)} %add.246), channel_id=1, source_target_pairs={{0,128},{64,192},{128,0},{192,64},{256,384},{320,448},{384,256},{4... | collective-permute-start | bytes 32 | tf_op jit(solution)/shard_map/ppermute | solution.py:25
  235.5 9.3 %collective-permute-start.17 = (f32[2]{0:T(128)S(1)}, f32[2]{0:T(128)S(1)}, u32[]{:S(2)}, u32[]{:S(2)}) collective-permute-start(f32[2]{0:T(128)S(1)} %add.247), channel_id=1, source_target_pairs={{0,256},{64,320},{128,384},{192,448},{256,0},{320,64},{384,128},{4... | collective-permute-start | bytes 32 | tf_op jit(solution)/shard_map/ppermute | solution.py:25

commit v5 on v4

--- a/solution.py
+++ b/solution.py
@@ -76,16 +76,26 @@
     block = members.shape[-1]
     products = (members.astype(jnp.float32) * search[None]).astype(jnp.bfloat16)
     flat = products.reshape(-1, block)
+    rows = flat.shape[0]
     bands = lax.axis_size("lon")
     here = lax.axis_index("lon")
+    even = here % 2 == 0
     columns = loc_cols[0]
     tiles = loc_vals[0]
-    offsets = [0]
-    for distance in range(1, REACH + 1):
-        offsets += [distance, -distance]
-    sources = {0: flat}
-    for offset in offsets[1:]:
-        sources[offset] = from_offset(flat, "lon", offset)
+    partner = [(i, i ^ 1) for i in range(bands)]
+    beside = lax.ppermute(flat, "lon", partner)
+    ahead = from_offset(flat, "lon", 2)
+    behind = from_offset(flat, "lon", -2)
+    far = lax.ppermute(flat, "lon", [(s, (s + 3) % bands if s % 2 else (s - 3) % bands) for s in range(bands)])
+    relayed = lax.ppermute(jnp.concatenate([ahead, behind], axis=0), "lon", partner)
+    received = [
+        (beside, jnp.where(even, 1, -1)),
+        (ahead, 2),
+        (behind, -2),
+        (far, jnp.where(even, -3, 3)),
+        (relayed[:rows], jnp.where(even, 3, 1)),
+        (relayed[rows:], jnp.where(even, -1, -3)),
+    ]
 
     def weight_for(offset):
         target = (here + offset + bands) % bands
@@ -93,10 +103,10 @@
         picked = tiles[jnp.argmax(match)]
         return jnp.where(jnp.any(match), picked, jnp.zeros_like(picked))
 
-    partials, _ = lax.optimization_barrier((partials, [sources[offset] for offset in offsets[1:]]))
+    partials, _ = lax.optimization_barrier((partials, [value for value, _ in received]))
     total = jnp.dot(flat, weight_for(0), preferred_element_type=jnp.float32)
-    for offset in offsets[1:]:
-        total = total + jnp.dot(sources[offset], weight_for(offset), preferred_element_type=jnp.float32)
+    for value, offset in received:
+        total = total + jnp.dot(value, weight_for(offset), preferred_element_type=jnp.float32)
     spread = total.reshape(products.shape)
     return jnp.sum(members.astype(jnp.float32) * spread, axis=0) / (count_members - 1), partials
 
@@ -140,11 +150,15 @@
     following = shifted(backed, "win", -1)[None, :, None]
 
     covar, partials = localize(
-        ensemble[0, :, :, 0], search_dual[0, :, 0], loc_cols, loc_vals, jnp.stack([resid_local, search_local])
+        ensemble[0, :, :, 0],
+        search_dual[0, :, 0],
+        loc_cols,
+        loc_vals,
+        butterfly_sum(jnp.stack([resid_local, search_local]), ("win",)),
     )
     covar = covar[None, :, None]
     partials, _ = lax.optimization_barrier((partials, other))
-    sums = butterfly_sum(partials, ("lon", "lat", "win"))
+    sums = butterfly_sum(partials, ("lon", "lat"))
     alpha = sums[0] / (sums[1] + 1e-06)
     image_dual = covar + search_incr - earlier
     image_obs = obs_var * search_obs + obs_weight * search_incr

time: 252 us -> 192 us (0.76)
  the two profiles are of different devices: /device:TPU:20 before, /device:TPU:38 now
where the time goes in v5:
time: 192 us; the launch traced here: 190 us
  starting transfers between devices  93.2 us (49%)
  waiting for transfers between devices  43.3 us (23%)
  between operations  20.1 us (10%)
  other arithmetic  15.6 us (8%)
  matrix products  11.9 us (6%)
  local copies, waits for them, and re-layouts  6.38 us (3%)
    ppermute x9, starting transfers between devices, butterfly_sum(): lax.ppermute(value, axis, [(i, i ^ step) for i in range(count)])  53.2 us
    ppermute x1, waiting for transfers between devices, lat_partner(): return lax.ppermute(value, 'lat', [(0, 1), (1, 0)])  22.1 us
    ppermute x9, waiting for transfers between devices, butterfly_sum(): lax.ppermute(value, axis, [(i, i ^ step) for i in range(count)])  21.2 us
    ppermute x4, starting transfers between devices, from_offset(): lax.ppermute(value, axis, [((i + distance) % count, i) for i in range(cou...  14.4 us
    dot_general x6, matrix products, localize(): jnp.dot(value, weight_for(offset), preferred_element_type=jnp.float32)  9.54 us
    ppermute x1, starting transfers between devices, lat_partner(): return lax.ppermute(value, 'lat', [(0, 1), (1, 0)])  8.76 us
    ppermute x2, starting transfers between devices, shifted(): lax.ppermute(value, axis, [(source, source + steps) for source in range(l...  7.05 us
    ppermute x1, starting transfers between devices, localize(): lax.ppermute(flat, 'lon', [(s, (s + 3) % bands if s % 2 else (s - 3) % ba...  5.78 us
  transfers between devices with their start and end apart: 19, of which 8 were waited for; matrix products, arithmetic and copies ran while one was open for 14% of the time, Pallas kernels for 0%

profile of v5, /device:TPU:38, one launch (start us, length us, event | category | flops | bytes accessed | tf_op | source)
XLA Modules:
  0.0 190.4 jit_solution(15377314118691735732)
XLA Ops:
  0.7 0.9 copy_bitcast_fusion.3
  1.6 2.5 %fusion.2 = bf16[1024,512]{1,0:T(8,128)(2,1)} fusion(bf16[1,64,16,1,512]{4,2,3,1,0:T(8,128)(2,1)} %param.24, f32[16,512]{1,0:T(8,128)S(1)} %get-tuple-element.70), kind=kLoop, calls=%fused_computation.6 | loop fusion | flops 1572864 | bytes 2129920 | tf_op jit(solution)/shard_map/convert_element_type | solution.py:77
  4.1 5.8 %collective-permute-start.6 = (bf16[1024,512]{1,0:T(8,128)(2,1)}, bf16[1024,512]{1,0:T(8,128)(2,1)}, u32[]{:S(2)}, u32[]{:S(2)}) collective-permute-start(bf16[1024,512]{1,0:T(8,128)(2,1)} %fusion.2), channel_id=1, source_target_pairs={{0,58},{2,8},{4,62},{6,12},{8,2},{10,16},{12,6},{14,20},{16,10},{1... | collective-permute-start | bytes 3145736 | tf_op jit(solution)/shard_map/ppermute | solution.py:89
  9.9 4.3 %collective-permute-start.5 = (bf16[1024,512]{1,0:T(8,128)(2,1)}, bf16[1024,512]{1,0:T(8,128)(2,1)S(1)}, u32[]{:S(2)}, u32[]{:S(2)}) collective-permute-start(bf16[1024,512]{1,0:T(8,128)(2,1)} %fusion.2), channel_id=1, source_target_pairs={{60,0},{62,2},{0,4},{2,6},{4,8},{6,10},{8,12},{10,14},{12,16},{14,... | collective-permute-start | bytes 3145736 | tf_op jit(solution)/shard_map/ppermute | solution.py:11
  14.2 0.7 multiply_reduce_fusion.2
  14.8 0.7 multiply_reduce_fusion
  15.5 0.7 multiply_reduce_fusion.1
  16.2 0.7 multiply_reduce_fusion.3
  18.8 0.7 multiply_reduce_fusion.4
  21.5 2.6 %collective-permute-start = (f32[2]{0:T(128)S(1)}, f32[2]{0:T(128)S(1)}, u32[]{:S(2)}, u32[]{:S(2)}) collective-permute-start(f32[2]{0:T(128)S(1)} %pad_maximum_fusion.5), channel_id=1, source_target_pairs={{0,64},{64,0},{128,192},{192,128},{256,320},{320,256},{384,448},{4... | collective-permute-start | bytes 32 | tf_op jit(solution)/shard_map/ppermute | solution.py:25
  24.1 0.7 pad_maximum_fusion.4
  24.8 1.9 %collective-permute-start.8 = (f32[7,16,2]{2,1,0:T(8,128)}, f32[7,16,2]{2,1,0:T(8,128)}, u32[]{:S(2)}, u32[]{:S(2)}) collective-permute-start(f32[7,16,2]{2,1,0:T(8,128)} %get-tuple-element.54), channel_id=1, source_target_pairs={{62,0},{0,2},{2,4},{4,6},{6,8},{8,10},{10,12},{12,14},{14,16},{16,... | collective-permute-start | bytes 2696 | tf_op jit(solution)/shard_map/ppermute | solution.py:11
  26.7 6.3 %collective-permute-start.9 = (f32[7,16,2]{2,1,0:T(8,128)}, f32[7,16,2]{2,1,0:T(8,128)}, u32[]{:S(2)}, u32[]{:S(2)}) collective-permute-start(f32[7,16,2]{2,1,0:T(8,128)} %get-tuple-element.55), channel_id=1, source_target_pairs={{2,0},{4,2},{6,4},{8,6},{10,8},{12,10},{14,12},{16,14},{18,16},{20... | collective-permute-start | bytes 2696 | tf_op jit(solution)/shard_map/ppermute | solution.py:11
  33.2 0.7 bitcast_reduce_fusion
  35.1 0.7 bitcast_reduce_fusion.6
  37.3 0.7 bitcast_reduce_fusion.5
  39.2 0.7 bitcast_reduce_fusion.4
  41.2 0.7 bitcast_reduce_fusion.3
  43.1 0.7 bitcast_reduce_fusion.2
  45.1 0.8 compare_reduce_fusion
  45.9 0.7 bitcast_reduce_fusion.1
  47.9 0.6 fusion.92
  48.5 0.3 fusion
  53.3 2.3 %fusion.17 = f32[1024,512]{1,0:T(8,128)S(1)} fusion(bf16[1024,512]{1,0:T(8,128)(2,1)S(1)} %bitcast.135, bf16[1,5,512,512]{3,2,1,0:T(8,128)(2,1)} %param.29, s32[]{:T(128)S(6)} %select_n.174, pred[]{:T(512)} %get-tuple-element.35), kind=kOutput, calls=%fused_computation.20 | convolution fusion | flops 537133056 | bytes 3670532 | tf_op jit(solution)/shard_map/dot_general | solution.py:107
  55.7 2.7 %collective-permute-start.1 = (f32[2]{0:T(128)S(1)}, f32[2]{0:T(128)S(1)}, u32[]{:S(2)}, u32[]{:S(2)}) collective-permute-start(f32[2]{0:T(128)S(1)} %fusion.100), channel_id=1, source_target_pairs={{0,128},{64,192},{128,0},{192,64},{256,384},{320,448},{384,256},{4... | collective-permute-start | bytes 32 | tf_op jit(solution)/shard_map/ppermute | solution.py:25
  58.4 3.6 %collective-permute-done.1 = f32[2]{0:T(128)S(1)} collective-permute-done((f32[2]{0:T(128)S(1)}, f32[2]{0:T(128)S(1)}, u32[]{:S(2)}, u32[]{:S(2)}) %collective-permute-start.1) | collective-permute-done | bytes 40 | tf_op jit(solution)/shard_map/ppermute | solution.py:25
  62.1 2.9 %collective-permute-start.2 = (f32[2]{0:T(128)S(1)}, f32[2]{0:T(128)S(1)}, u32[]{:S(2)}, u32[]{:S(2)}) collective-permute-start(f32[2]{0:T(128)S(1)} %fusion.101), channel_id=1, source_target_pairs={{0,256},{64,320},{128,384},{192,448},{256,0},{320,64},{384,128},{4... | collective-permute-start | bytes 32 | tf_op jit(solution)/shard_map/ppermute | solution.py:25
  65.0 6.4 %collective-permute-done.2 = f32[2]{0:T(128)S(1)} collective-permute-done((f32[2]{0:T(128)S(1)}, f32[2]{0:T(128)S(1)}, u32[]{:S(2)}, u32[]{:S(2)}) %collective-permute-start.2) | collective-permute-done | bytes 40 | tf_op jit(solution)/shard_map/ppermute | solution.py:25
  71.4 1.9 %collective-permute-start.4 = (bf16[1024,512]{1,0:T(8,128)(2,1)}, bf16[1024,512]{1,0:T(8,128)(2,1)S(1)}, u32[]{:S(2)}, u32[]{:S(2)}) collective-permute-start(bf16[1024,512]{1,0:T(8,128)(2,1)} %fusion.2), channel_id=1, source_target_pairs={{4,0},{6,2},{8,4},{10,6},{12,8},{14,10},{16,12},{18,14},{20,16},{2... | collective-permute-start | bytes 3145736 | tf_op jit(solution)/shard_map/ppermute | solution.py:11
  73.4 1.9 %collective-permute-start.3 = (bf16[1024,512]{1,0:T(8,128)(2,1)}, bf16[1024,512]{1,0:T(8,128)(2,1)S(1)}, u32[]{:S(2)}, u32[]{:S(2)}) collective-permute-start(bf16[1024,512]{1,0:T(8,128)(2,1)} %fusion.2), channel_id=1, source_target_pairs={{0,2},{2,0},{4,6},{6,4},{8,10},{10,8},{12,14},{14,12},{16,18},{18,... | collective-permute-start | bytes 3145736 | tf_op jit(solution)/shard_map/ppermute | solution.py:86
  75.3 1.0 pad_maximum_fusion.1
  76.3 8.8 %collective-permute-start.10 = (f32[7,16,516]{2,1,0:T(8,128)S(1)}, f32[7,16,516]{2,1,0:T(8,128)S(1)}, u32[]{:S(2)}, u32[]{:S(2)}) collective-permute-start(f32[7,16,516]{2,1,0:T(8,128)S(1)} %pad_maximum_fusion.1), channel_id=1, source_target_pairs={{0,1},{1,0},{2,3},{3,2},{4,5},{5,4},{6,7},{7,6},{8,9},{9,8},{10,11... | collective-permute-start | bytes 693512 | tf_op jit(solution)/shard_map/ppermute | solution.py:37
  85.3 22.1 %collective-permute-done.10 = f32[7,16,516]{2,1,0:T(8,128)S(1)} collective-permute-done((f32[7,16,516]{2,1,0:T(8,128)S(1)}, f32[7,16,516]{2,1,0:T(8,128)S(1)}, u32[]{:S(2)}, u32[]{:S(2)}) %collective-permute-start.10) | collective-permute-done | bytes 231200 | tf_op jit(solution)/shard_map/ppermute | solution.py:37
  107.5 0.2 fusion.48
  108.3 2.1 %collective-permute-start.7 = (bf16[2048,512]{1,0:T(8,128)(2,1)S(1)}, bf16[2048,512]{1,0:T(8,128)(2,1)S(1)}, u32[]{:S(2)}, u32[]{:S(2)}) collective-permute-start(bf16[2048,512]{1,0:T(8,128)(2,1)S(1)} %pad_maximum_fusion), channel_id=1, source_target_pairs={{0,2},{2,0},{4,6},{6,4},{8,10},{10,8},{12,14},{14,12},{16,18},{18,... | collective-permute-start | bytes 6291464 | tf_op jit(solution)/shard_map/ppermute | solution.py:90
  110.5 3.0 %collective-permute-start.17 = (f32[16,512]{1,0:T(8,128)S(1)}, f32[16,512]{1,0:T(8,128)S(1)}, u32[]{:S(2)}, u32[]{:S(2)}) collective-permute-start(f32[16,512]{1,0:T(8,128)S(1)} %fusion.66), channel_id=1, source_target_pairs={{0,64},{64,128},{128,192},{192,256},{256,320},{320,384},{384,448},... | collective-permute-start | bytes 98312 | tf_op jit(solution)/shard_map/ppermute | solution.py:17
  113.6 0.2 fusion.59
  113.7 4.0 %collective-permute-start.18 = (f32[16,512]{1,0:T(8,128)S(1)}, f32[16,512]{1,0:T(8,128)S(1)}, u32[]{:S(2)}, u32[]{:S(2)}) collective-permute-start(f32[16,512]{1,0:T(8,128)S(1)} %fusion.59), channel_id=1, source_target_pairs={{64,0},{128,64},{192,128},{256,192},{320,256},{384,320},{448,384},... | collective-permute-start | bytes 98312 | tf_op jit(solution)/shard_map/ppermute | solution.py:17
  117.8 1.9 %collective-permute-start.11 = (f32[2]{0:T(128)S(1)}, f32[2]{0:T(128)S(1)}, u32[]{:S(2)}, u32[]{:S(2)}) collective-permute-start(f32[2]{0:T(128)S(1)} %add.245), channel_id=1, source_target_pairs={{0,2},{2,0},{4,6},{6,4},{8,10},{10,8},{12,14},{14,12},{16,18},{18,... | collective-permute-start | bytes 32 | tf_op jit(solution)/shard_map/ppermute | solution.py:25
  119.7 1.4 fusion.15
  121.1 1.3 fusion.13
  122.4 2.6 %fusion.9 = f32[1024,512]{1,0:T(8,128)S(1)} fusion(bf16[1024,512]{1,0:T(8,128)(2,1)} %collective-permute-done.6, bf16[1,5,512,512]{3,2,1,0:T(8,128)(2,1)S(1)} %copy-done.1, s32[]{:T(128)S(6)} %select_n.197, pred[]{:T(512)} %get-tuple-element.31), kind=kOutput, calls=%fused_computation.12 | convolution fusion | flops 537133056 | bytes 3670021 | tf_op jit(solution)/shard_map/dot_general | solution.py:109
  125.0 1.3 fusion.11
  126.4 23.3 %collective-permute-start.12 = (f32[2]{0:T(128)S(1)}, f32[2]{0:T(128)S(1)}, u32[]{:S(2)}, u32[]{:S(2)}) collective-permute-start(f32[2]{0:T(128)S(1)} %add.246), channel_id=1, source_target_pairs={{0,4},{2,6},{4,0},{6,2},{8,12},{10,14},{12,8},{14,10},{16,20},{18,... | collective-permute-start | bytes 32 | tf_op jit(solution)/shard_map/ppermute | solution.py:25
  149.8 1.5 collective-permute-done.12
  151.3 6.2 %collective-permute-start.13 = (f32[2]{0:T(128)S(1)}, f32[2]{0:T(128)S(1)}, u32[]{:S(2)}, u32[]{:S(2)}) collective-permute-start(f32[2]{0:T(128)S(1)} %add.247), channel_id=1, source_target_pairs={{0,8},{2,10},{4,12},{6,14},{8,0},{10,2},{12,4},{14,6},{16,24},{18,... | collective-permute-start | bytes 32 | tf_op jit(solution)/shard_map/ppermute | solution.py:25
  157.5 1.5 collective-permute-done.13
  159.0 2.7 %collective-permute-start.14 = (f32[2]{0:T(128)S(1)}, f32[2]{0:T(128)S(1)}, u32[]{:S(2)}, u32[]{:S(2)}) collective-permute-start(f32[2]{0:T(128)S(1)} %add.248), channel_id=1, source_target_pairs={{0,16},{2,18},{4,20},{6,22},{8,24},{10,26},{12,28},{14,30},{16,0},... | collective-permute-start | bytes 32 | tf_op jit(solution)/shard_map/ppermute | solution.py:25
  161.7 2.7 %collective-permute-done.14 = f32[2]{0:T(128)S(1)} collective-permute-done((f32[2]{0:T(128)S(1)}, f32[2]{0:T(128)S(1)}, u32[]{:S(2)}, u32[]{:S(2)}) %collective-permute-start.14) | collective-permute-done | bytes 40 | tf_op jit(solution)/shard_map/ppermute | solution.py:25
  164.4 3.3 %collective-permute-start.15 = (f32[2]{0:T(128)S(1)}, f32[2]{0:T(128)S(1)}, u32[]{:S(2)}, u32[]{:S(2)}) collective-permute-start(f32[2]{0:T(128)S(1)} %add.249), channel_id=1, source_target_pairs={{0,32},{2,34},{4,36},{6,38},{8,40},{10,42},{12,44},{14,46},{16,48}... | collective-permute-start | bytes 32 | tf_op jit(solution)/shard_map/ppermute | solution.py:25
  167.7 3.6 %collective-permute-done.15 = f32[2]{0:T(128)S(1)} collective-permute-done((f32[2]{0:T(128)S(1)}, f32[2]{0:T(128)S(1)}, u32[]{:S(2)}, u32[]{:S(2)}) %collective-permute-start.15) | collective-permute-done | bytes 40 | tf_op jit(solution)/shard_map/ppermute | solution.py:25
  171.4 7.5 %collective-permute-start.16 = (f32[2]{0:T(128)S(1)}, f32[2]{0:T(128)S(1)}, u32[]{:S(2)}, u32[]{:S(2)}) collective-permute-start(f32[2]{0:T(128)S(1)} %add.250), channel_id=1, source_target_pairs={{0,1},{1,0},{2,3},{3,2},{4,5},{5,4},{6,7},{7,6},{8,9},{9,8},{10,11... | collective-permute-start | bytes 32 | tf_op jit(solution)/shard_map/ppermute | solution.py:25
  178.9 1.8 collective-permute-done.16
  180.7 0.6 fusion.94
  182.6 0.6 copy.38
  183.3 0.7 multiply_subtract_fusion
  184.0 1.4 fusion.7
  185.4 1.5 add_add_fusion
  187.0 0.4 fusion.1
  187.4 0.3 copy-done.7
  187.8 0.6 copy.42
  188.4 0.6 copy.40
  189.1 0.6 copy.41
  189.7 0.6 copy.39
  (75 shorter events, 1.5 us)
Async XLA Ops:
  0.6 13.5 %copy-start.2 = (f32[1,16,1,512]{3,2,1,0:T(1,128)S(1)}, f32[1,16,1,512]{3,2,1,0:T(1,128)}, u32[]{:S(2)}) copy-start(f32[1,16,1,512]{3,2,1,0:T(1,128)} %param.21) | copy-start | bytes 98308
  0.6 14.2 %copy-start.4 = (f32[1,16,1,512]{3,2,1,0:T(1,128)S(1)}, f32[1,16,1,512]{3,2,1,0:T(1,128)}, u32[]{:S(2)}) copy-start(f32[1,16,1,512]{3,2,1,0:T(1,128)} %param.23) | copy-start | bytes 98308
  0.7 47.9 %copy-start = (bf16[1,64,16,1,512]{4,2,3,1,0:T(8,128)(2,1)S(1)}, bf16[1,64,16,1,512]{4,2,3,1,0:T(8,128)(2,1)}, u32[]{:S(2)}) copy-start(bf16[1,64,16,1,512]{4,2,3,1,0:T(8,128)(2,1)} %param.24) | copy-start | bytes 3145732
  0.7 14.8 %copy-start.5 = (f32[1,16,1,512]{3,2,1,0:T(1,128)S(1)}, f32[1,16,1,512]{3,2,1,0:T(1,128)}, u32[]{:S(2)}) copy-start(f32[1,16,1,512]{3,2,1,0:T(1,128)} %param.22) | copy-start | bytes 98308
  0.7 15.5 %copy-start.13 = (f32[1,16,1,512]{3,2,1,0:T(1,128)S(1)}, f32[1,16,1,512]{3,2,1,0:T(1,128)}, u32[]{:S(2)}) copy-start(f32[1,16,1,512]{3,2,1,0:T(1,128)} %param.20) | copy-start | bytes 98308
  0.7 18.1 %copy-start.6 = (f32[1,16,1,512]{3,2,1,0:T(1,128)S(1)}, f32[1,16,1,512]{3,2,1,0:T(1,128)}, u32[]{:S(2)}) copy-start(f32[1,16,1,512]{3,2,1,0:T(1,128)} %param.19) | copy-start | bytes 98308
  0.7 18.1 %copy-start.8 = (f32[1,16,1,512]{3,2,1,0:T(1,128)S(1)}, f32[1,16,1,512]{3,2,1,0:T(1,128)}, u32[]{:S(2)}) copy-start(f32[1,16,1,512]{3,2,1,0:T(1,128)} %param.18) | copy-start | bytes 98308
  0.7 23.4 %copy-start.3 = (f32[1,5,16,1,512]{4,3,2,1,0:T(1,128)S(1)}, f32[1,5,16,1,512]{4,3,2,1,0:T(1,128)}, u32[]{:S(2)}) copy-start(f32[1,5,16,1,512]{4,3,2,1,0:T(1,128)} %param.25) | copy-start | bytes 491524
  0.7 32.4 %copy-start.19 = (s32[1,5]{1,0:T(1,128)S(1)}, s32[1,5]{1,0:T(1,128)}, u32[]{:S(2)}) copy-start(s32[1,5]{1,0:T(1,128)} %param.28) | copy-start | bytes 64
  4.1 113.7 %collective-permute-start.6 = (bf16[1024,512]{1,0:T(8,128)(2,1)}, bf16[1024,512]{1,0:T(8,128)(2,1)}, u32[]{:S(2)}, u32[]{:S(2)}) collective-permute-start(bf16[1024,512]{1,0:T(8,128)(2,1)} %fusion.2), channel_id=1, source_target_pairs={{0,58},{2,8},{4,62},{6,12},{8,2},{10,16},{12,6},{14,20},{16,10},{1... | collective-permute-start | bytes 3145736 | tf_op jit(solution)/shard_map/ppermute | solution.py:89
  9.9 98.3 %collective-permute-start.5 = (bf16[1024,512]{1,0:T(8,128)(2,1)}, bf16[1024,512]{1,0:T(8,128)(2,1)S(1)}, u32[]{:S(2)}, u32[]{:S(2)}) collective-permute-start(bf16[1024,512]{1,0:T(8,128)(2,1)} %fusion.2), channel_id=1, source_target_pairs={{60,0},{62,2},{0,4},{2,6},{4,8},{6,10},{8,12},{10,14},{12,16},{14,... | collective-permute-start | bytes 3145736 | tf_op jit(solution)/shard_map/ppermute | solution.py:11
  21.5 34.1 %collective-permute-start = (f32[2]{0:T(128)S(1)}, f32[2]{0:T(128)S(1)}, u32[]{:S(2)}, u32[]{:S(2)}) collective-permute-start(f32[2]{0:T(128)S(1)} %pad_maximum_fusion.5), channel_id=1, source_target_pairs={{0,64},{64,0},{128,192},{192,128},{256,320},{320,256},{384,448},{4... | collective-permute-start | bytes 32 | tf_op jit(solution)/shard_map/ppermute | solution.py:25
  24.8 48.5 %collective-permute-start.8 = (f32[7,16,2]{2,1,0:T(8,128)}, f32[7,16,2]{2,1,0:T(8,128)}, u32[]{:S(2)}, u32[]{:S(2)}) collective-permute-start(f32[7,16,2]{2,1,0:T(8,128)} %get-tuple-element.54), channel_id=1, source_target_pairs={{62,0},{0,2},{2,4},{4,6},{6,8},{8,10},{10,12},{12,14},{14,16},{16,... | collective-permute-start | bytes 2696 | tf_op jit(solution)/shard_map/ppermute | solution.py:11
  26.7 48.6 %collective-permute-start.9 = (f32[7,16,2]{2,1,0:T(8,128)}, f32[7,16,2]{2,1,0:T(8,128)}, u32[]{:S(2)}, u32[]{:S(2)}) collective-permute-start(f32[7,16,2]{2,1,0:T(8,128)} %get-tuple-element.55), channel_id=1, source_target_pairs={{2,0},{4,2},{6,4},{8,6},{10,8},{12,10},{14,12},{16,14},{18,16},{20... | collective-permute-start | bytes 2696 | tf_op jit(solution)/shard_map/ppermute | solution.py:11
  55.6 52.4 %copy-start.11 = (f32[1,1,16,1,512]{4,3,2,1,0:T(1,128)S(1)}, f32[1,1,16,1,512]{4,3,2,1,0:T(1,128)}, u32[]{:S(2)}) copy-start(f32[1,1,16,1,512]{4,3,2,1,0:T(1,128)} %get-tuple-element.57) | copy-start | bytes 98308
  55.6 52.4 %copy-start.12 = (f32[1,1,16,1,512]{4,3,2,1,0:T(1,128)S(1)}, f32[1,1,16,1,512]{4,3,2,1,0:T(1,128)}, u32[]{:S(2)}) copy-start(f32[1,1,16,1,512]{4,3,2,1,0:T(1,128)} %get-tuple-element.58) | copy-start | bytes 98308
  55.7 6.3 %collective-permute-start.1 = (f32[2]{0:T(128)S(1)}, f32[2]{0:T(128)S(1)}, u32[]{:S(2)}, u32[]{:S(2)}) collective-permute-start(f32[2]{0:T(128)S(1)} %fusion.100), channel_id=1, source_target_pairs={{0,128},{64,192},{128,0},{192,64},{256,384},{320,448},{384,256},{4... | collective-permute-start | bytes 32 | tf_op jit(solution)/shard_map/ppermute | solution.py:25
  62.1 9.3 %collective-permute-start.2 = (f32[2]{0:T(128)S(1)}, f32[2]{0:T(128)S(1)}, u32[]{:S(2)}, u32[]{:S(2)}) collective-permute-start(f32[2]{0:T(128)S(1)} %fusion.101), channel_id=1, source_target_pairs={{0,256},{64,320},{128,384},{192,448},{256,0},{320,64},{384,128},{4... | collective-permute-start | bytes 32 | tf_op jit(solution)/shard_map/ppermute | solution.py:25
  71.4 36.7 %collective-permute-start.4 = (bf16[1024,512]{1,0:T(8,128)(2,1)}, bf16[1024,512]{1,0:T(8,128)(2,1)S(1)}, u32[]{:S(2)}, u32[]{:S(2)}) collective-permute-start(bf16[1024,512]{1,0:T(8,128)(2,1)} %fusion.2), channel_id=1, source_target_pairs={{4,0},{6,2},{8,4},{10,6},{12,8},{14,10},{16,12},{18,14},{20,16},{2... | collective-permute-start | bytes 3145736 | tf_op jit(solution)/shard_map/ppermute | solution.py:11
  73.4 44.4 %collective-permute-start.3 = (bf16[1024,512]{1,0:T(8,128)(2,1)}, bf16[1024,512]{1,0:T(8,128)(2,1)S(1)}, u32[]{:S(2)}, u32[]{:S(2)}) collective-permute-start(bf16[1024,512]{1,0:T(8,128)(2,1)} %fusion.2), channel_id=1, source_target_pairs={{0,2},{2,0},{4,6},{6,4},{8,10},{10,8},{12,14},{14,12},{16,18},{18,... | collective-permute-start | bytes 3145736 | tf_op jit(solution)/shard_map/ppermute | solution.py:86
  76.3 31.1 %collective-permute-start.10 = (f32[7,16,516]{2,1,0:T(8,128)S(1)}, f32[7,16,516]{2,1,0:T(8,128)S(1)}, u32[]{:S(2)}, u32[]{:S(2)}) collective-permute-start(f32[7,16,516]{2,1,0:T(8,128)S(1)} %pad_maximum_fusion.1), channel_id=1, source_target_pairs={{0,1},{1,0},{2,3},{3,2},{4,5},{5,4},{6,7},{7,6},{8,9},{9,8},{10,11... | collective-permute-start | bytes 693512 | tf_op jit(solution)/shard_map/ppermute | solution.py:37
  108.1 11.6 %copy-start.1 = (bf16[1,5,512,512]{3,2,1,0:T(8,128)(2,1)S(1)}, bf16[1,5,512,512]{3,2,1,0:T(8,128)(2,1)}, u32[]{:S(2)}) copy-start(bf16[1,5,512,512]{3,2,1,0:T(8,128)(2,1)} %param.29) | copy-start | bytes 7864324
  108.3 75.7 %collective-permute-start.7 = (bf16[2048,512]{1,0:T(8,128)(2,1)S(1)}, bf16[2048,512]{1,0:T(8,128)(2,1)S(1)}, u32[]{:S(2)}, u32[]{:S(2)}) collective-permute-start(bf16[2048,512]{1,0:T(8,128)(2,1)S(1)} %pad_maximum_fusion), channel_id=1, source_target_pairs={{0,2},{2,0},{4,6},{6,4},{8,10},{10,8},{12,14},{14,12},{16,18},{18,... | collective-permute-start | bytes 6291464 | tf_op jit(solution)/shard_map/ppermute | solution.py:90
  110.5 76.9 %collective-permute-start.17 = (f32[16,512]{1,0:T(8,128)S(1)}, f32[16,512]{1,0:T(8,128)S(1)}, u32[]{:S(2)}, u32[]{:S(2)}) collective-permute-start(f32[16,512]{1,0:T(8,128)S(1)} %fusion.66), channel_id=1, source_target_pairs={{0,64},{64,128},{128,192},{192,256},{256,320},{320,384},{384,448},... | collective-permute-start | bytes 98312 | tf_op jit(solution)/shard_map/ppermute | solution.py:17
  113.7 69.5 %collective-permute-start.18 = (f32[16,512]{1,0:T(8,128)S(1)}, f32[16,512]{1,0:T(8,128)S(1)}, u32[]{:S(2)}, u32[]{:S(2)}) collective-permute-start(f32[16,512]{1,0:T(8,128)S(1)} %fusion.59), channel_id=1, source_target_pairs={{64,0},{128,64},{192,128},{256,192},{320,256},{384,320},{448,384},... | collective-permute-start | bytes 98312 | tf_op jit(solution)/shard_map/ppermute | solution.py:17
  117.8 8.6 %collective-permute-start.11 = (f32[2]{0:T(128)S(1)}, f32[2]{0:T(128)S(1)}, u32[]{:S(2)}, u32[]{:S(2)}) collective-permute-start(f32[2]{0:T(128)S(1)} %add.245), channel_id=1, source_target_pairs={{0,2},{2,0},{4,6},{6,4},{8,10},{10,8},{12,14},{14,12},{16,18},{18,... | collective-permute-start | bytes 32 | tf_op jit(solution)/shard_map/ppermute | solution.py:25
  125.0 57.6 %copy-start.15 = (f32[1,16,1,512]{3,2,1,0:T(1,128)S(1)}, f32[1,16,1,512]{3,2,1,0:T(1,128)}, u32[]{:S(2)}) copy-start(f32[1,16,1,512]{3,2,1,0:T(1,128)} %param.15) | copy-start | bytes 98308
  125.0 58.3 %copy-start.10 = (f32[1,16,1,512]{3,2,1,0:T(1,128)S(1)}, f32[1,16,1,512]{3,2,1,0:T(1,128)}, u32[]{:S(2)}) copy-start(f32[1,16,1,512]{3,2,1,0:T(1,128)} %param.26) | copy-start | bytes 98308
  125.0 58.2 %copy-start.14 = (f32[1,16,1,512]{3,2,1,0:T(1,128)S(1)}, f32[1,16,1,512]{3,2,1,0:T(1,128)}, u32[]{:S(2)}) copy-start(f32[1,16,1,512]{3,2,1,0:T(1,128)} %param.20) | copy-start | bytes 98308
  126.4 24.8 %collective-permute-start.12 = (f32[2]{0:T(128)S(1)}, f32[2]{0:T(128)S(1)}, u32[]{:S(2)}, u32[]{:S(2)}) collective-permute-start(f32[2]{0:T(128)S(1)} %add.246), channel_id=1, source_target_pairs={{0,4},{2,6},{4,0},{6,2},{8,12},{10,14},{12,8},{14,10},{16,20},{18,... | collective-permute-start | bytes 32 | tf_op jit(solution)/shard_map/ppermute | solution.py:25
  151.3 7.7 %collective-permute-start.13 = (f32[2]{0:T(128)S(1)}, f32[2]{0:T(128)S(1)}, u32[]{:S(2)}, u32[]{:S(2)}) collective-permute-start(f32[2]{0:T(128)S(1)} %add.247), channel_id=1, source_target_pairs={{0,8},{2,10},{4,12},{6,14},{8,0},{10,2},{12,4},{14,6},{16,24},{18,... | collective-permute-start | bytes 32 | tf_op jit(solution)/shard_map/ppermute | solution.py:25
  159.0 5.4 %collective-permute-start.14 = (f32[2]{0:T(128)S(1)}, f32[2]{0:T(128)S(1)}, u32[]{:S(2)}, u32[]{:S(2)}) collective-permute-start(f32[2]{0:T(128)S(1)} %add.248), channel_id=1, source_target_pairs={{0,16},{2,18},{4,20},{6,22},{8,24},{10,26},{12,28},{14,30},{16,0},... | collective-permute-start | bytes 32 | tf_op jit(solution)/shard_map/ppermute | solution.py:25
  164.4 6.9 %collective-permute-start.15 = (f32[2]{0:T(128)S(1)}, f32[2]{0:T(128)S(1)}, u32[]{:S(2)}, u32[]{:S(2)}) collective-permute-start(f32[2]{0:T(128)S(1)} %add.249), channel_id=1, source_target_pairs={{0,32},{2,34},{4,36},{6,38},{8,40},{10,42},{12,44},{14,46},{16,48}... | collective-permute-start | bytes 32 | tf_op jit(solution)/shard_map/ppermute | solution.py:25
  171.4 9.3 %collective-permute-start.16 = (f32[2]{0:T(128)S(1)}, f32[2]{0:T(128)S(1)}, u32[]{:S(2)}, u32[]{:S(2)}) collective-permute-start(f32[2]{0:T(128)S(1)} %add.250), channel_id=1, source_target_pairs={{0,1},{1,0},{2,3},{3,2},{4,5},{5,4},{6,7},{7,6},{8,9},{9,8},{10,11... | collective-permute-start | bytes 32 | tf_op jit(solution)/shard_map/ppermute | solution.py:25
  186.9 0.8 copy-start.7
  186.9 0.8 copy-start.9
  187.0 0.8 copy-start.16
  187.0 0.8 copy-start.17
  187.0 0.8 copy-start.18

commit v6 on v5

--- a/solution.py
+++ b/solution.py
@@ -17,20 +17,20 @@
     return lax.ppermute(value, axis, [(source, source + steps) for source in range(leading, last)])
 
 
-def butterfly_sum(value, axes):
+def butterfly_sum(value, axes, first=1):
     for axis in axes:
         count = lax.axis_size(axis)
-        step = 1
+        step = first
         while step < count:
             value = value + lax.ppermute(value, axis, [(i, i ^ step) for i in range(count)])
             step *= 2
     return value
 
 
-def lon_extended(packed, width):
-    left = from_offset(packed[..., -width:], "lon", -1)
-    right = from_offset(packed[..., :width], "lon", 1)
-    return jnp.concatenate([left, packed, right], axis=-1)
+def lon_extended(packed, width, extra):
+    left = from_offset(jnp.concatenate([packed[..., -width:], extra]), "lon", -1)
+    right = from_offset(jnp.concatenate([packed[..., :width], extra]), "lon", 1)
+    return jnp.concatenate([left[:-1], packed, right[:-1]], axis=-1), left[-1], right[-1]
 
 
 def lat_partner(value):
@@ -142,8 +142,16 @@
     packed = jnp.concatenate(
         [search_incr[0, :, 0][None], search_dual[0, :, 0][None], tangent_coefs[0, :, :, 0]], axis=0
     )
-    own = lon_extended(packed, 2)
-    other = lat_partner(own)
+    partial = jnp.stack([resid_local, search_local])
+    rider = jnp.broadcast_to(partial[None, None, :], (1,) + packed.shape[1:2] + (2,))
+    own, from_left, from_right = lon_extended(packed, 2, rider)
+    even = lax.axis_index("lon") % 2 == 0
+    partial = partial + jnp.where(even, from_right[0], from_left[0])
+    partial = butterfly_sum(partial, ("win",))
+    rider = jnp.broadcast_to(jnp.pad(partial, (0, own.shape[-1] - 2))[None, None, :], (1,) + own.shape[1:])
+    other = lat_partner(jnp.concatenate([own, rider]))
+    partial = partial + other[-1, 0, :2]
+    other = other[:-1]
     first_row = lax.axis_index("lat") == 0
     moved, backed = propagate_both(own, other, first_row)
     earlier = shifted(moved, "win", 1)[None, :, None]
@@ -154,11 +162,10 @@
         search_dual[0, :, 0],
         loc_cols,
         loc_vals,
-        butterfly_sum(jnp.stack([resid_local, search_local]), ("win",)),
+        partial,
     )
     covar = covar[None, :, None]
-    partials, _ = lax.optimization_barrier((partials, other))
-    sums = butterfly_sum(partials, ("lon", "lat"))
+    sums = butterfly_sum(partials, ("lon",), first=2)
     alpha = sums[0] / (sums[1] + 1e-06)
     image_dual = covar + search_incr - earlier
     image_obs = obs_var * search_obs + obs_weight * search_incr

time: 192 us -> 194 us (1.010)
  the two profiles are of different devices: /device:TPU:38 before, /device:TPU:36 now
where the time goes in v6:
time: 194 us; the launch traced here: 193 us
  starting transfers between devices  78.5 us (40%)
  waiting for transfers between devices  54.1 us (28%)
  between operations  19.7 us (10%)
  other arithmetic  17.4 us (9%)
  matrix products  14.7 us (8%)
  local copies, waits for them, and re-layouts  8.65 us (4%)
    ppermute x7, starting transfers between devices, butterfly_sum(): lax.ppermute(value, axis, [(i, i ^ step) for i in range(count)])  34.2 us
    ppermute x4, waiting for transfers between devices, from_offset(): lax.ppermute(value, axis, [((i + distance) % count, i) for i in range(cou...  25.9 us
    ppermute x7, waiting for transfers between devices, butterfly_sum(): lax.ppermute(value, axis, [(i, i ^ step) for i in range(count)])  23.5 us
    ppermute x4, starting transfers between devices, from_offset(): lax.ppermute(value, axis, [((i + distance) % count, i) for i in range(cou...  12.9 us
    dot_general x6, matrix products, localize(): jnp.dot(value, weight_for(offset), preferred_element_type=jnp.float32)  12 us
    ppermute x1, starting transfers between devices, lat_partner(): return lax.ppermute(value, 'lat', [(0, 1), (1, 0)])  9.12 us
    ppermute x1, starting transfers between devices, localize(): beside = lax.ppermute(flat, 'lon', partner)  7.89 us
    ppermute x2, starting transfers between devices, shifted(): lax.ppermute(value, axis, [(source, source + steps) for source in range(l...  7.05 us
  transfers between devices with their start and end apart: 17, of which 8 were waited for; matrix products, arithmetic and copies ran while one was open for 17% of the time, Pallas kernels for 0%

profile of v6, /device:TPU:36, one launch (start us, length us, event | category | flops | bytes accessed | tf_op | source)
XLA Modules:
  0.0 193.1 jit_solution(18391688956223214298)
XLA Ops:
  0.7 0.8 copy.188
  1.6 2.4 %fusion.2 = bf16[1024,512]{1,0:T(8,128)(2,1)} fusion(bf16[1,64,16,1,512]{4,2,3,1,0:T(8,128)(2,1)} %param.24, f32[16,512]{1,0:T(8,128)S(1)} %bitcast.157), kind=kLoop, calls=%fused_computation.6 | loop fusion | flops 1572864 | bytes 2129920 | tf_op jit(solution)/shard_map/convert_element_type | solution.py:77
  4.0 5.5 %collective-permute-start.9 = (bf16[1024,512]{1,0:T(8,128)(2,1)}, bf16[1024,512]{1,0:T(8,128)(2,1)}, u32[]{:S(2)}, u32[]{:S(2)}) collective-permute-start(bf16[1024,512]{1,0:T(8,128)(2,1)} %fusion.2), channel_id=1, source_target_pairs={{0,58},{2,8},{4,62},{6,12},{8,2},{10,16},{12,6},{14,20},{16,10},{1... | collective-permute-start | bytes 3145736 | tf_op jit(solution)/shard_map/ppermute | solution.py:89
  9.5 4.3 %collective-permute-start.8 = (bf16[1024,512]{1,0:T(8,128)(2,1)}, bf16[1024,512]{1,0:T(8,128)(2,1)}, u32[]{:S(2)}, u32[]{:S(2)}) collective-permute-start(bf16[1024,512]{1,0:T(8,128)(2,1)} %fusion.2), channel_id=1, source_target_pairs={{60,0},{62,2},{0,4},{2,6},{4,8},{6,10},{8,12},{10,14},{12,16},{14,... | collective-permute-start | bytes 3145736 | tf_op jit(solution)/shard_map/ppermute | solution.py:11
  13.8 4.3 %collective-permute-start.7 = (bf16[1024,512]{1,0:T(8,128)(2,1)}, bf16[1024,512]{1,0:T(8,128)(2,1)}, u32[]{:S(2)}, u32[]{:S(2)}) collective-permute-start(bf16[1024,512]{1,0:T(8,128)(2,1)} %fusion.2), channel_id=1, source_target_pairs={{4,0},{6,2},{8,4},{10,6},{12,8},{14,10},{16,12},{18,14},{20,16},{2... | collective-permute-start | bytes 3145736 | tf_op jit(solution)/shard_map/ppermute | solution.py:11
  18.1 0.7 multiply_reduce_fusion.2
  18.7 0.7 multiply_reduce_fusion
  19.4 0.7 multiply_reduce_fusion.1
  20.1 0.7 multiply_reduce_fusion.3
  22.7 0.7 multiply_reduce_fusion.4
  25.4 0.7 pad_maximum_fusion.4
  26.1 1.9 %collective-permute-start = (f32[8,16,2]{2,1,0:T(8,128)}, f32[8,16,2]{2,1,0:T(8,128)}, u32[]{:S(2)}, u32[]{:S(2)}) collective-permute-start(f32[8,16,2]{2,1,0:T(8,128)} %get-tuple-element.70), channel_id=1, source_target_pairs={{2,0},{4,2},{6,4},{8,6},{10,8},{12,10},{14,12},{16,14},{18,16},{20... | collective-permute-start | bytes 3080 | tf_op jit(solution)/shard_map/ppermute | solution.py:11
  28.1 2.4 %collective-permute-start.1 = (f32[8,16,2]{2,1,0:T(8,128)}, f32[8,16,2]{2,1,0:T(8,128)}, u32[]{:S(2)}, u32[]{:S(2)}) collective-permute-start(f32[8,16,2]{2,1,0:T(8,128)} %get-tuple-element.71), channel_id=1, source_target_pairs={{62,0},{0,2},{2,4},{4,6},{6,8},{8,10},{10,12},{12,14},{14,16},{16,... | collective-permute-start | bytes 3080 | tf_op jit(solution)/shard_map/ppermute | solution.py:11
  30.5 0.7 bitcast_reduce_fusion
  32.3 0.7 bitcast_reduce_fusion.6
  34.5 0.6 bitcast_reduce_fusion.5
  36.3 0.7 bitcast_reduce_fusion.4
  37.0 0.7 bitcast_reduce_fusion.3
  37.6 0.7 bitcast_reduce_fusion.2
  38.4 0.8 compare_reduce_fusion
  39.2 0.7 bitcast_reduce_fusion.1
  39.8 0.6 fusion.98
  40.4 1.2 fusion
  42.4 2.6 %fusion.17 = f32[1024,512]{1,0:T(8,128)S(1)} fusion(bf16[1024,512]{1,0:T(8,128)(2,1)} %bitcast.153, bf16[1,5,512,512]{3,2,1,0:T(8,128)(2,1)} %param.29, s32[]{:T(128)S(6)} %select_n.191, pred[]{:T(512)} %get-tuple-element.51), kind=kOutput, calls=%fused_computation.20 | convolution fusion | flops 537133056 | bytes 3670532 | tf_op jit(solution)/shard_map/dot_general | solution.py:107
  53.9 25.9 %collective-permute-done = f32[8,16,2]{2,1,0:T(8,128)} collective-permute-done((f32[8,16,2]{2,1,0:T(8,128)}, f32[8,16,2]{2,1,0:T(8,128)}, u32[]{:S(2)}, u32[]{:S(2)}) %collective-permute-start) | collective-permute-done | bytes 1056 | tf_op jit(solution)/shard_map/ppermute | solution.py:11
  79.8 7.9 %collective-permute-start.6 = (bf16[1024,512]{1,0:T(8,128)(2,1)}, bf16[1024,512]{1,0:T(8,128)(2,1)S(1)}, u32[]{:S(2)}, u32[]{:S(2)}) collective-permute-start(bf16[1024,512]{1,0:T(8,128)(2,1)} %fusion.2), channel_id=1, source_target_pairs={{0,2},{2,0},{4,6},{6,4},{8,10},{10,8},{12,14},{14,12},{16,18},{18,... | collective-permute-start | bytes 3145736 | tf_op jit(solution)/shard_map/ppermute | solution.py:86
  87.7 0.8 fusion.87
  88.4 2.6 %collective-permute-start.2 = (f32[2]{0:T(128)S(1)}, f32[2]{0:T(128)S(1)}, u32[]{:S(2)}, u32[]{:S(2)}) collective-permute-start(f32[2]{0:T(128)S(1)} %fusion.87), channel_id=1, source_target_pairs={{0,64},{64,0},{128,192},{192,128},{256,320},{320,256},{384,448},{4... | collective-permute-start | bytes 32 | tf_op jit(solution)/shard_map/ppermute | solution.py:25
  91.0 0.8 slice.289
  91.8 0.8 slice.288
  92.8 1.0 collective-permute-done.2
  93.8 2.7 %collective-permute-start.3 = (f32[2]{0:T(128)S(1)}, f32[2]{0:T(128)S(1)}, u32[]{:S(2)}, u32[]{:S(2)}) collective-permute-start(f32[2]{0:T(128)S(1)} %add.248), channel_id=1, source_target_pairs={{0,128},{64,192},{128,0},{192,64},{256,384},{320,448},{384,256},{4... | collective-permute-start | bytes 32 | tf_op jit(solution)/shard_map/ppermute | solution.py:25
  96.5 3.6 %collective-permute-done.3 = f32[2]{0:T(128)S(1)} collective-permute-done((f32[2]{0:T(128)S(1)}, f32[2]{0:T(128)S(1)}, u32[]{:S(2)}, u32[]{:S(2)}) %collective-permute-start.3) | collective-permute-done | bytes 40 | tf_op jit(solution)/shard_map/ppermute | solution.py:25
  100.2 2.0 %collective-permute-start.4 = (f32[2]{0:T(128)S(1)}, f32[2]{0:T(128)S(1)}, u32[]{:S(2)}, u32[]{:S(2)}) collective-permute-start(f32[2]{0:T(128)S(1)} %add.249), channel_id=1, source_target_pairs={{0,256},{64,320},{128,384},{192,448},{256,0},{320,64},{384,128},{4... | collective-permute-start | bytes 32 | tf_op jit(solution)/shard_map/ppermute | solution.py:25
  102.2 7.3 %collective-permute-done.4 = f32[2]{0:T(128)S(1)} collective-permute-done((f32[2]{0:T(128)S(1)}, f32[2]{0:T(128)S(1)}, u32[]{:S(2)}, u32[]{:S(2)}) %collective-permute-start.4) | collective-permute-done | bytes 40 | tf_op jit(solution)/shard_map/ppermute | solution.py:25
  109.7 9.1 %collective-permute-start.5 = (f32[8,16,516]{2,1,0:T(8,128)S(1)}, f32[8,16,516]{2,1,0:T(8,128)S(1)}, u32[]{:S(2)}, u32[]{:S(2)}) collective-permute-start(f32[8,16,516]{2,1,0:T(8,128)S(1)} %pad_maximum_fusion.1), channel_id=1, source_target_pairs={{0,1},{1,0},{2,3},{3,2},{4,5},{5,4},{6,7},{7,6},{8,9},{9,8},{10,11... | collective-permute-start | bytes 792584 | tf_op jit(solution)/shard_map/ppermute | solution.py:37
  119.1 4.8 %collective-permute-done.5 = f32[8,16,516]{2,1,0:T(8,128)S(1)} collective-permute-done((f32[8,16,516]{2,1,0:T(8,128)S(1)}, f32[8,16,516]{2,1,0:T(8,128)S(1)}, u32[]{:S(2)}, u32[]{:S(2)}) %collective-permute-start.5) | collective-permute-done | bytes 264224 | tf_op jit(solution)/shard_map/ppermute | solution.py:37
  124.1 0.2 fusion.48
  124.4 1.8 pad_maximum_fusion
  126.2 1.9 collective-permute-start.10
  128.4 2.6 %collective-permute-start.15 = (f32[16,512]{1,0:T(8,128)S(1)}, f32[16,512]{1,0:T(8,128)S(1)}, u32[]{:S(2)}, u32[]{:S(2)}) collective-permute-start(f32[16,512]{1,0:T(8,128)S(1)} %fusion.66), channel_id=1, source_target_pairs={{0,64},{64,128},{128,192},{192,256},{256,320},{320,384},{384,448},... | collective-permute-start | bytes 98312 | tf_op jit(solution)/shard_map/ppermute | solution.py:17
  131.3 4.5 %collective-permute-start.16 = (f32[16,512]{1,0:T(8,128)S(1)}, f32[16,512]{1,0:T(8,128)S(1)}, u32[]{:S(2)}, u32[]{:S(2)}) collective-permute-start(f32[16,512]{1,0:T(8,128)S(1)} %fusion.59), channel_id=1, source_target_pairs={{64,0},{128,64},{192,128},{256,192},{320,256},{384,320},{448,384},... | collective-permute-start | bytes 98312 | tf_op jit(solution)/shard_map/ppermute | solution.py:17
  135.8 19.8 %collective-permute-start.11 = (f32[2]{0:T(128)S(1)}, f32[2]{0:T(128)S(1)}, u32[]{:S(2)}, u32[]{:S(2)}) collective-permute-start(f32[2]{0:T(128)S(1)} %fusion.88), channel_id=1, source_target_pairs={{0,4},{2,6},{4,0},{6,2},{8,12},{10,14},{12,8},{14,10},{16,20},{18,... | collective-permute-start | bytes 32 | tf_op jit(solution)/shard_map/ppermute | solution.py:25
  155.6 1.4 fusion.15
  157.0 2.6 %fusion.13 = f32[1024,512]{1,0:T(8,128)S(1)} fusion(bf16[1024,512]{1,0:T(8,128)(2,1)} %collective-permute-done.7, bf16[1,5,512,512]{3,2,1,0:T(8,128)(2,1)S(1)} %copy-done.1, s32[]{:T(128)S(6)} %select_n.202, pred[]{:T(512)} %get-tuple-element.49), kind=kOutput, calls=%fused_computation.16 | convolution fusion | flops 537133056 | bytes 3670021 | tf_op jit(solution)/shard_map/dot_general | solution.py:109
  159.6 2.6 %fusion.9 = f32[1024,512]{1,0:T(8,128)S(1)} fusion(bf16[1024,512]{1,0:T(8,128)(2,1)} %collective-permute-done.9, bf16[1,5,512,512]{3,2,1,0:T(8,128)(2,1)S(1)} %copy-done.1, s32[]{:T(128)S(6)} %select_n.213, pred[]{:T(512)} %get-tuple-element.47), kind=kOutput, calls=%fused_computation.12 | convolution fusion | flops 537133056 | bytes 3670021 | tf_op jit(solution)/shard_map/dot_general | solution.py:109
  162.2 2.5 %fusion.11 = f32[1024,512]{1,0:T(8,128)S(1)} fusion(bf16[1024,512]{1,0:T(8,128)(2,1)} %collective-permute-done.8, bf16[1,5,512,512]{3,2,1,0:T(8,128)(2,1)S(1)} %copy-done.1, s32[]{:T(128)S(6)} %select_n.207, pred[]{:T(512)} %get-tuple-element.48), kind=kOutput, calls=%fused_computation.14 | convolution fusion | flops 537133056 | bytes 3670021 | tf_op jit(solution)/shard_map/dot_general | solution.py:109
  164.7 1.9 %collective-permute-start.12 = (f32[2]{0:T(128)S(1)}, f32[2]{0:T(128)S(1)}, u32[]{:S(2)}, u32[]{:S(2)}) collective-permute-start(f32[2]{0:T(128)S(1)} %add.252), channel_id=1, source_target_pairs={{0,8},{2,10},{4,12},{6,14},{8,0},{10,2},{12,4},{14,6},{16,24},{18,... | collective-permute-start | bytes 32 | tf_op jit(solution)/shard_map/ppermute | solution.py:25
  166.6 4.4 %collective-permute-done.12 = f32[2]{0:T(128)S(1)} collective-permute-done((f32[2]{0:T(128)S(1)}, f32[2]{0:T(128)S(1)}, u32[]{:S(2)}, u32[]{:S(2)}) %collective-permute-start.12) | collective-permute-done | bytes 40 | tf_op jit(solution)/shard_map/ppermute | solution.py:25
  171.0 3.0 %collective-permute-start.13 = (f32[2]{0:T(128)S(1)}, f32[2]{0:T(128)S(1)}, u32[]{:S(2)}, u32[]{:S(2)}) collective-permute-start(f32[2]{0:T(128)S(1)} %add.253), channel_id=1, source_target_pairs={{0,16},{2,18},{4,20},{6,22},{8,24},{10,26},{12,28},{14,30},{16,0},... | collective-permute-start | bytes 32 | tf_op jit(solution)/shard_map/ppermute | solution.py:25
  174.0 2.4 %collective-permute-done.13 = f32[2]{0:T(128)S(1)} collective-permute-done((f32[2]{0:T(128)S(1)}, f32[2]{0:T(128)S(1)}, u32[]{:S(2)}, u32[]{:S(2)}) %collective-permute-start.13) | collective-permute-done | bytes 40 | tf_op jit(solution)/shard_map/ppermute | solution.py:25
  176.4 2.2 %collective-permute-start.14 = (f32[2]{0:T(128)S(1)}, f32[2]{0:T(128)S(1)}, u32[]{:S(2)}, u32[]{:S(2)}) collective-permute-start(f32[2]{0:T(128)S(1)} %add.254), channel_id=1, source_target_pairs={{0,32},{2,34},{4,36},{6,38},{8,40},{10,42},{12,44},{14,46},{16,48}... | collective-permute-start | bytes 32 | tf_op jit(solution)/shard_map/ppermute | solution.py:25
  178.7 4.7 %collective-permute-done.14 = f32[2]{0:T(128)S(1)} collective-permute-done((f32[2]{0:T(128)S(1)}, f32[2]{0:T(128)S(1)}, u32[]{:S(2)}, u32[]{:S(2)}) %collective-permute-start.14) | collective-permute-done | bytes 40 | tf_op jit(solution)/shard_map/ppermute | solution.py:25
  183.4 0.6 fusion.100
  185.3 1.4 fusion.7
  186.7 1.6 add_add_fusion
  188.4 0.4 fusion.1
  188.8 0.3 copy-done.8
  189.2 0.6 copy.139
  189.9 0.6 copy.138
  190.5 0.6 copy.136
  191.2 0.6 copy.137
  191.8 0.6 copy.134
  192.5 0.6 copy.135
  (75 shorter events, 1.7 us)
Async XLA Ops:
  0.6 17.4 %copy-start.3 = (f32[1,16,1,512]{3,2,1,0:T(1,128)S(1)}, f32[1,16,1,512]{3,2,1,0:T(1,128)}, u32[]{:S(2)}) copy-start(f32[1,16,1,512]{3,2,1,0:T(1,128)} %param.21) | copy-start | bytes 98308
  0.6 39.8 %copy-start = (bf16[1,64,16,1,512]{4,2,3,1,0:T(8,128)(2,1)S(1)}, bf16[1,64,16,1,512]{4,2,3,1,0:T(8,128)(2,1)}, u32[]{:S(2)}) copy-start(bf16[1,64,16,1,512]{4,2,3,1,0:T(8,128)(2,1)} %param.24) | copy-start | bytes 3145732
  0.7 18.1 %copy-start.4 = (f32[1,16,1,512]{3,2,1,0:T(1,128)S(1)}, f32[1,16,1,512]{3,2,1,0:T(1,128)}, u32[]{:S(2)}) copy-start(f32[1,16,1,512]{3,2,1,0:T(1,128)} %param.23) | copy-start | bytes 98308
  0.7 18.7 %copy-start.5 = (f32[1,16,1,512]{3,2,1,0:T(1,128)S(1)}, f32[1,16,1,512]{3,2,1,0:T(1,128)}, u32[]{:S(2)}) copy-start(f32[1,16,1,512]{3,2,1,0:T(1,128)} %param.22) | copy-start | bytes 98308
  0.7 19.4 %copy-start.9 = (f32[1,16,1,512]{3,2,1,0:T(1,128)S(1)}, f32[1,16,1,512]{3,2,1,0:T(1,128)}, u32[]{:S(2)}) copy-start(f32[1,16,1,512]{3,2,1,0:T(1,128)} %param.20) | copy-start | bytes 98308
  0.7 20.1 %copy-start.2 = (f32[1,5,16,1,512]{4,3,2,1,0:T(1,128)S(1)}, f32[1,5,16,1,512]{4,3,2,1,0:T(1,128)}, u32[]{:S(2)}) copy-start(f32[1,5,16,1,512]{4,3,2,1,0:T(1,128)} %param.25) | copy-start | bytes 491524
  0.7 22.0 %copy-start.6 = (f32[1,16,1,512]{3,2,1,0:T(1,128)S(1)}, f32[1,16,1,512]{3,2,1,0:T(1,128)}, u32[]{:S(2)}) copy-start(f32[1,16,1,512]{3,2,1,0:T(1,128)} %param.19) | copy-start | bytes 98308
  0.7 22.0 %copy-start.7 = (f32[1,16,1,512]{3,2,1,0:T(1,128)S(1)}, f32[1,16,1,512]{3,2,1,0:T(1,128)}, u32[]{:S(2)}) copy-start(f32[1,16,1,512]{3,2,1,0:T(1,128)} %param.18) | copy-start | bytes 98308
  0.7 29.8 %copy-start.18 = (s32[1,5]{1,0:T(1,128)S(1)}, s32[1,5]{1,0:T(1,128)}, u32[]{:S(2)}) copy-start(s32[1,5]{1,0:T(1,128)} %param.28) | copy-start | bytes 64
  4.0 131.8 %collective-permute-start.9 = (bf16[1024,512]{1,0:T(8,128)(2,1)}, bf16[1024,512]{1,0:T(8,128)(2,1)}, u32[]{:S(2)}, u32[]{:S(2)}) collective-permute-start(bf16[1024,512]{1,0:T(8,128)(2,1)} %fusion.2), channel_id=1, source_target_pairs={{0,58},{2,8},{4,62},{6,12},{8,2},{10,16},{12,6},{14,20},{16,10},{1... | collective-permute-start | bytes 3145736 | tf_op jit(solution)/shard_map/ppermute | solution.py:89
  9.5 114.9 %collective-permute-start.8 = (bf16[1024,512]{1,0:T(8,128)(2,1)}, bf16[1024,512]{1,0:T(8,128)(2,1)}, u32[]{:S(2)}, u32[]{:S(2)}) collective-permute-start(bf16[1024,512]{1,0:T(8,128)(2,1)} %fusion.2), channel_id=1, source_target_pairs={{60,0},{62,2},{0,4},{2,6},{4,8},{6,10},{8,12},{10,14},{12,16},{14,... | collective-permute-start | bytes 3145736 | tf_op jit(solution)/shard_map/ppermute | solution.py:11
  13.8 110.6 %collective-permute-start.7 = (bf16[1024,512]{1,0:T(8,128)(2,1)}, bf16[1024,512]{1,0:T(8,128)(2,1)}, u32[]{:S(2)}, u32[]{:S(2)}) collective-permute-start(bf16[1024,512]{1,0:T(8,128)(2,1)} %fusion.2), channel_id=1, source_target_pairs={{4,0},{6,2},{8,4},{10,6},{12,8},{14,10},{16,12},{18,14},{20,16},{2... | collective-permute-start | bytes 3145736 | tf_op jit(solution)/shard_map/ppermute | solution.py:11
  26.1 53.6 %collective-permute-start = (f32[8,16,2]{2,1,0:T(8,128)}, f32[8,16,2]{2,1,0:T(8,128)}, u32[]{:S(2)}, u32[]{:S(2)}) collective-permute-start(f32[8,16,2]{2,1,0:T(8,128)} %get-tuple-element.70), channel_id=1, source_target_pairs={{2,0},{4,2},{6,4},{8,6},{10,8},{12,10},{14,12},{16,14},{18,16},{20... | collective-permute-start | bytes 3080 | tf_op jit(solution)/shard_map/ppermute | solution.py:11
  28.1 59.6 %collective-permute-start.1 = (f32[8,16,2]{2,1,0:T(8,128)}, f32[8,16,2]{2,1,0:T(8,128)}, u32[]{:S(2)}, u32[]{:S(2)}) collective-permute-start(f32[8,16,2]{2,1,0:T(8,128)} %get-tuple-element.71), channel_id=1, source_target_pairs={{62,0},{0,2},{2,4},{4,6},{6,8},{8,10},{10,12},{12,14},{14,16},{16,... | collective-permute-start | bytes 3080 | tf_op jit(solution)/shard_map/ppermute | solution.py:11
  79.8 56.1 %collective-permute-start.6 = (bf16[1024,512]{1,0:T(8,128)(2,1)}, bf16[1024,512]{1,0:T(8,128)(2,1)S(1)}, u32[]{:S(2)}, u32[]{:S(2)}) collective-permute-start(bf16[1024,512]{1,0:T(8,128)(2,1)} %fusion.2), channel_id=1, source_target_pairs={{0,2},{2,0},{4,6},{6,4},{8,10},{10,8},{12,14},{14,12},{16,18},{18,... | collective-permute-start | bytes 3145736 | tf_op jit(solution)/shard_map/ppermute | solution.py:86
  88.4 5.4 %collective-permute-start.2 = (f32[2]{0:T(128)S(1)}, f32[2]{0:T(128)S(1)}, u32[]{:S(2)}, u32[]{:S(2)}) collective-permute-start(f32[2]{0:T(128)S(1)} %fusion.87), channel_id=1, source_target_pairs={{0,64},{64,0},{128,192},{192,128},{256,320},{320,256},{384,448},{4... | collective-permute-start | bytes 32 | tf_op jit(solution)/shard_map/ppermute | solution.py:25
  93.8 6.3 %collective-permute-start.3 = (f32[2]{0:T(128)S(1)}, f32[2]{0:T(128)S(1)}, u32[]{:S(2)}, u32[]{:S(2)}) collective-permute-start(f32[2]{0:T(128)S(1)} %add.248), channel_id=1, source_target_pairs={{0,128},{64,192},{128,0},{192,64},{256,384},{320,448},{384,256},{4... | collective-permute-start | bytes 32 | tf_op jit(solution)/shard_map/ppermute | solution.py:25
  100.2 9.3 %collective-permute-start.4 = (f32[2]{0:T(128)S(1)}, f32[2]{0:T(128)S(1)}, u32[]{:S(2)}, u32[]{:S(2)}) collective-permute-start(f32[2]{0:T(128)S(1)} %add.249), channel_id=1, source_target_pairs={{0,256},{64,320},{128,384},{192,448},{256,0},{320,64},{384,128},{4... | collective-permute-start | bytes 32 | tf_op jit(solution)/shard_map/ppermute | solution.py:25
  109.7 14.2 %collective-permute-start.5 = (f32[8,16,516]{2,1,0:T(8,128)S(1)}, f32[8,16,516]{2,1,0:T(8,128)S(1)}, u32[]{:S(2)}, u32[]{:S(2)}) collective-permute-start(f32[8,16,516]{2,1,0:T(8,128)S(1)} %pad_maximum_fusion.1), channel_id=1, source_target_pairs={{0,1},{1,0},{2,3},{3,2},{4,5},{5,4},{6,7},{7,6},{8,9},{9,8},{10,11... | collective-permute-start | bytes 792584 | tf_op jit(solution)/shard_map/ppermute | solution.py:37
  124.4 3.8 %copy-start.11 = (f32[1,1,16,1,512]{4,3,2,1,0:T(1,128)S(1)}, f32[1,1,16,1,512]{4,3,2,1,0:T(1,128)}, u32[]{:S(2)}) copy-start(f32[1,1,16,1,512]{4,3,2,1,0:T(1,128)} %get-tuple-element.73) | copy-start | bytes 98308
  124.4 3.8 %copy-start.12 = (f32[1,1,16,1,512]{4,3,2,1,0:T(1,128)S(1)}, f32[1,1,16,1,512]{4,3,2,1,0:T(1,128)}, u32[]{:S(2)}) copy-start(f32[1,1,16,1,512]{4,3,2,1,0:T(1,128)} %get-tuple-element.74) | copy-start | bytes 98308
  124.4 31.2 %copy-start.1 = (bf16[1,5,512,512]{3,2,1,0:T(8,128)(2,1)S(1)}, bf16[1,5,512,512]{3,2,1,0:T(8,128)(2,1)}, u32[]{:S(2)}) copy-start(bf16[1,5,512,512]{3,2,1,0:T(8,128)(2,1)} %param.29) | copy-start | bytes 7864324
  126.2 59.0 %collective-permute-start.10 = (bf16[2048,512]{1,0:T(8,128)(2,1)S(1)}, bf16[2048,512]{1,0:T(8,128)(2,1)S(1)}, u32[]{:S(2)}, u32[]{:S(2)}) collective-permute-start(bf16[2048,512]{1,0:T(8,128)(2,1)S(1)} %pad_maximum_fusion), channel_id=1, source_target_pairs={{0,2},{2,0},{4,6},{6,4},{8,10},{10,8},{12,14},{14,12},{16,18},{18,... | collective-permute-start | bytes 6291464 | tf_op jit(solution)/shard_map/ppermute | solution.py:90
  128.4 60.3 %collective-permute-start.15 = (f32[16,512]{1,0:T(8,128)S(1)}, f32[16,512]{1,0:T(8,128)S(1)}, u32[]{:S(2)}, u32[]{:S(2)}) collective-permute-start(f32[16,512]{1,0:T(8,128)S(1)} %fusion.66), channel_id=1, source_target_pairs={{0,64},{64,128},{128,192},{192,256},{256,320},{320,384},{384,448},... | collective-permute-start | bytes 98312 | tf_op jit(solution)/shard_map/ppermute | solution.py:17
  131.3 57.5 %collective-permute-start.16 = (f32[16,512]{1,0:T(8,128)S(1)}, f32[16,512]{1,0:T(8,128)S(1)}, u32[]{:S(2)}, u32[]{:S(2)}) collective-permute-start(f32[16,512]{1,0:T(8,128)S(1)} %fusion.59), channel_id=1, source_target_pairs={{64,0},{128,64},{192,128},{256,192},{320,256},{384,320},{448,384},... | collective-permute-start | bytes 98312 | tf_op jit(solution)/shard_map/ppermute | solution.py:17
  135.8 28.8 %collective-permute-start.11 = (f32[2]{0:T(128)S(1)}, f32[2]{0:T(128)S(1)}, u32[]{:S(2)}, u32[]{:S(2)}) collective-permute-start(f32[2]{0:T(128)S(1)} %fusion.88), channel_id=1, source_target_pairs={{0,4},{2,6},{4,0},{6,2},{8,12},{10,14},{12,8},{14,10},{16,20},{18,... | collective-permute-start | bytes 32 | tf_op jit(solution)/shard_map/ppermute | solution.py:25
  164.7 6.3 %collective-permute-start.12 = (f32[2]{0:T(128)S(1)}, f32[2]{0:T(128)S(1)}, u32[]{:S(2)}, u32[]{:S(2)}) collective-permute-start(f32[2]{0:T(128)S(1)} %add.252), channel_id=1, source_target_pairs={{0,8},{2,10},{4,12},{6,14},{8,0},{10,2},{12,4},{14,6},{16,24},{18,... | collective-permute-start | bytes 32 | tf_op jit(solution)/shard_map/ppermute | solution.py:25
  171.0 5.4 %collective-permute-start.13 = (f32[2]{0:T(128)S(1)}, f32[2]{0:T(128)S(1)}, u32[]{:S(2)}, u32[]{:S(2)}) collective-permute-start(f32[2]{0:T(128)S(1)} %add.253), channel_id=1, source_target_pairs={{0,16},{2,18},{4,20},{6,22},{8,24},{10,26},{12,28},{14,30},{16,0},... | collective-permute-start | bytes 32 | tf_op jit(solution)/shard_map/ppermute | solution.py:25
  176.4 6.9 %collective-permute-start.14 = (f32[2]{0:T(128)S(1)}, f32[2]{0:T(128)S(1)}, u32[]{:S(2)}, u32[]{:S(2)}) collective-permute-start(f32[2]{0:T(128)S(1)} %add.254), channel_id=1, source_target_pairs={{0,32},{2,34},{4,36},{6,38},{8,40},{10,42},{12,44},{14,46},{16,48}... | collective-permute-start | bytes 32 | tf_op jit(solution)/shard_map/ppermute | solution.py:25
  188.3 0.8 copy-start.8
  188.3 0.8 copy-start.10
  188.3 0.8 copy-start.13
  188.3 0.8 copy-start.14
  188.3 0.8 copy-start.15
  188.4 0.8 copy-start.16
  188.4 0.8 copy-start.17

commit v7 on v6

--- a/solution.py
+++ b/solution.py
@@ -83,18 +83,17 @@
     columns = loc_cols[0]
     tiles = loc_vals[0]
     partner = [(i, i ^ 1) for i in range(bands)]
-    beside = lax.ppermute(flat, "lon", partner)
     ahead = from_offset(flat, "lon", 2)
     behind = from_offset(flat, "lon", -2)
     far = lax.ppermute(flat, "lon", [(s, (s + 3) % bands if s % 2 else (s - 3) % bands) for s in range(bands)])
-    relayed = lax.ppermute(jnp.concatenate([ahead, behind], axis=0), "lon", partner)
+    relayed = lax.ppermute(jnp.concatenate([flat, ahead, behind], axis=0), "lon", partner)
     received = [
-        (beside, jnp.where(even, 1, -1)),
         (ahead, 2),
         (behind, -2),
         (far, jnp.where(even, -3, 3)),
-        (relayed[:rows], jnp.where(even, 3, 1)),
-        (relayed[rows:], jnp.where(even, -1, -3)),
+        (relayed[:rows], jnp.where(even, 1, -1)),
+        (relayed[rows : 2 * rows], jnp.where(even, 3, 1)),
+        (relayed[2 * rows :], jnp.where(even, -1, -3)),
     ]
 
     def weight_for(offset):

time: 194 us -> 195 us (level)
  the two profiles are of different devices: /device:TPU:36 before, /device:TPU:38 now
where the time goes in v7:
time: 195 us; the launch traced here: 194 us
  starting transfers between devices  78.6 us (40%)
  waiting for transfers between devices  55.9 us (29%)
  between operations  19.8 us (10%)
  other arithmetic  16.6 us (9%)
  matrix products  14.4 us (7%)
  local copies, waits for them, and re-layouts  8.65 us (4%)
    ppermute x7, starting transfers between devices, butterfly_sum(): lax.ppermute(value, axis, [(i, i ^ step) for i in range(count)])  40.5 us
    ppermute x4, waiting for transfers between devices, from_offset(): lax.ppermute(value, axis, [((i + distance) % count, i) for i in range(cou...  28.1 us
    ppermute x7, waiting for transfers between devices, butterfly_sum(): lax.ppermute(value, axis, [(i, i ^ step) for i in range(count)])  19.8 us
    ppermute x4, starting transfers between devices, from_offset(): lax.ppermute(value, axis, [((i + distance) % count, i) for i in range(cou...  12.9 us
    dot_general x6, matrix products, localize(): jnp.dot(value, weight_for(offset), preferred_element_type=jnp.float32)  12 us
    ppermute x1, starting transfers between devices, lat_partner(): return lax.ppermute(value, 'lat', [(0, 1), (1, 0)])  9.4 us
    ppermute x1, waiting for transfers between devices, lat_partner(): return lax.ppermute(value, 'lat', [(0, 1), (1, 0)])  7.93 us
    ppermute x2, starting transfers between devices, shifted(): lax.ppermute(value, axis, [(source, source + steps) for source in range(l...  7.05 us
  transfers between devices with their start and end apart: 16, of which 9 were waited for; matrix products, arithmetic and copies ran while one was open for 16% of the time, Pallas kernels for 0%

profile of v7, /device:TPU:38, one launch (start us, length us, event | category | flops | bytes accessed | tf_op | source)
XLA Modules:
  0.0 194.0 jit_solution(14370669632079594662)
XLA Ops:
  0.7 0.8 copy.188
  1.6 2.4 %fusion.2 = bf16[1024,512]{1,0:T(8,128)(2,1)} fusion(bf16[1,64,16,1,512]{4,2,3,1,0:T(8,128)(2,1)} %param.24, f32[16,512]{1,0:T(8,128)S(1)} %bitcast.156), kind=kLoop, calls=%fused_computation.6 | loop fusion | flops 1572864 | bytes 2129920 | tf_op jit(solution)/shard_map/convert_element_type | solution.py:77
  4.0 5.8 %collective-permute-start.8 = (bf16[1024,512]{1,0:T(8,128)(2,1)}, bf16[1024,512]{1,0:T(8,128)(2,1)}, u32[]{:S(2)}, u32[]{:S(2)}) collective-permute-start(bf16[1024,512]{1,0:T(8,128)(2,1)} %fusion.2), channel_id=1, source_target_pairs={{0,58},{2,8},{4,62},{6,12},{8,2},{10,16},{12,6},{14,20},{16,10},{1... | collective-permute-start | bytes 3145736 | tf_op jit(solution)/shard_map/ppermute | solution.py:88
  9.8 4.3 %collective-permute-start.7 = (bf16[1024,512]{1,0:T(8,128)(2,1)}, bf16[1024,512]{1,0:T(8,128)(2,1)}, u32[]{:S(2)}, u32[]{:S(2)}) collective-permute-start(bf16[1024,512]{1,0:T(8,128)(2,1)} %fusion.2), channel_id=1, source_target_pairs={{60,0},{62,2},{0,4},{2,6},{4,8},{6,10},{8,12},{10,14},{12,16},{14,... | collective-permute-start | bytes 3145736 | tf_op jit(solution)/shard_map/ppermute | solution.py:11
  14.1 4.3 %collective-permute-start.6 = (bf16[1024,512]{1,0:T(8,128)(2,1)}, bf16[1024,512]{1,0:T(8,128)(2,1)}, u32[]{:S(2)}, u32[]{:S(2)}) collective-permute-start(bf16[1024,512]{1,0:T(8,128)(2,1)} %fusion.2), channel_id=1, source_target_pairs={{4,0},{6,2},{8,4},{10,6},{12,8},{14,10},{16,12},{18,14},{20,16},{2... | collective-permute-start | bytes 3145736 | tf_op jit(solution)/shard_map/ppermute | solution.py:11
  18.4 0.7 multiply_reduce_fusion.2
  19.0 0.7 multiply_reduce_fusion
  19.7 0.7 multiply_reduce_fusion.1
  20.4 0.7 multiply_reduce_fusion.3
  23.0 0.7 multiply_reduce_fusion.4
  25.7 0.7 pad_maximum_fusion.4
  26.4 1.9 collective-permute-start
  28.3 2.4 %collective-permute-start.1 = (f32[8,16,2]{2,1,0:T(8,128)}, f32[8,16,2]{2,1,0:T(8,128)}, u32[]{:S(2)}, u32[]{:S(2)}) collective-permute-start(f32[8,16,2]{2,1,0:T(8,128)} %get-tuple-element.71), channel_id=1, source_target_pairs={{62,0},{0,2},{2,4},{4,6},{6,8},{8,10},{10,12},{12,14},{14,16},{16,... | collective-permute-start | bytes 3080 | tf_op jit(solution)/shard_map/ppermute | solution.py:11
  30.8 0.6 fusion.99
  31.5 0.7 bitcast_reduce_fusion
  32.2 0.7 bitcast_reduce_fusion.6
  32.8 0.7 bitcast_reduce_fusion.5
  33.6 0.6 bitcast_reduce_fusion.4
  34.2 0.7 bitcast_reduce_fusion.3
  34.9 0.7 bitcast_reduce_fusion.2
  35.7 0.7 bitcast_reduce_fusion.1
  40.6 0.8 compare_reduce_fusion
  41.4 0.2 fusion
  41.7 2.4 %fusion.17 = f32[1024,512]{1,0:T(8,128)S(1)} fusion(bf16[1024,512]{1,0:T(8,128)(2,1)S(1)} %bitcast.152, bf16[1,5,512,512]{3,2,1,0:T(8,128)(2,1)} %param.29, s32[]{:T(128)S(6)} %select_n.191, pred[]{:T(512)} %get-tuple-element.51), kind=kOutput, calls=%fused_computation.20 | convolution fusion | flops 537133056 | bytes 3670532 | tf_op jit(solution)/shard_map/dot_general | solution.py:106
  53.1 26.7 %collective-permute-done = f32[8,16,2]{2,1,0:T(8,128)} collective-permute-done((f32[8,16,2]{2,1,0:T(8,128)}, f32[8,16,2]{2,1,0:T(8,128)}, u32[]{:S(2)}, u32[]{:S(2)}) %collective-permute-start) | collective-permute-done | bytes 1056 | tf_op jit(solution)/shard_map/ppermute | solution.py:11
  79.8 1.4 collective-permute-done.1
  81.2 0.8 fusion.87
  82.0 2.6 %collective-permute-start.2 = (f32[2]{0:T(128)S(1)}, f32[2]{0:T(128)S(1)}, u32[]{:S(2)}, u32[]{:S(2)}) collective-permute-start(f32[2]{0:T(128)S(1)} %fusion.87), channel_id=1, source_target_pairs={{0,64},{64,0},{128,192},{192,128},{256,320},{320,256},{384,448},{4... | collective-permute-start | bytes 32 | tf_op jit(solution)/shard_map/ppermute | solution.py:25
  84.5 0.8 slice.293
  85.4 0.8 slice.292
  86.4 1.0 collective-permute-done.2
  87.4 2.7 %collective-permute-start.3 = (f32[2]{0:T(128)S(1)}, f32[2]{0:T(128)S(1)}, u32[]{:S(2)}, u32[]{:S(2)}) collective-permute-start(f32[2]{0:T(128)S(1)} %add.248), channel_id=1, source_target_pairs={{0,128},{64,192},{128,0},{192,64},{256,384},{320,448},{384,256},{4... | collective-permute-start | bytes 32 | tf_op jit(solution)/shard_map/ppermute | solution.py:25
  90.1 3.6 %collective-permute-done.3 = f32[2]{0:T(128)S(1)} collective-permute-done((f32[2]{0:T(128)S(1)}, f32[2]{0:T(128)S(1)}, u32[]{:S(2)}, u32[]{:S(2)}) %collective-permute-start.3) | collective-permute-done | bytes 40 | tf_op jit(solution)/shard_map/ppermute | solution.py:25
  93.7 2.0 %collective-permute-start.4 = (f32[2]{0:T(128)S(1)}, f32[2]{0:T(128)S(1)}, u32[]{:S(2)}, u32[]{:S(2)}) collective-permute-start(f32[2]{0:T(128)S(1)} %add.249), channel_id=1, source_target_pairs={{0,256},{64,320},{128,384},{192,448},{256,0},{320,64},{384,128},{4... | collective-permute-start | bytes 32 | tf_op jit(solution)/shard_map/ppermute | solution.py:25
  95.7 7.3 %collective-permute-done.4 = f32[2]{0:T(128)S(1)} collective-permute-done((f32[2]{0:T(128)S(1)}, f32[2]{0:T(128)S(1)}, u32[]{:S(2)}, u32[]{:S(2)}) %collective-permute-start.4) | collective-permute-done | bytes 40 | tf_op jit(solution)/shard_map/ppermute | solution.py:25
  103.1 2.0 %pad_maximum_fusion = bf16[3072,512]{1,0:T(8,128)(2,1)S(1)} fusion(bf16[1024,512]{1,0:T(8,128)(2,1)} %collective-permute-done.7, bf16[1024,512]{1,0:T(8,128)(2,1)} %collective-permute-done.6, bf16[1024,512]{1,0:T(8,128)(2,1)} %fusion.2), kind=kLoop, calls=%fused_computation | loop fusion | flops 9437184 | bytes 6291456 | tf_op jit(solution)/shard_map/concatenate | solution.py:89
  105.1 3.0 %collective-permute-start.9 = (bf16[3072,512]{1,0:T(8,128)(2,1)S(1)}, bf16[3072,512]{1,0:T(8,128)(2,1)S(1)}, u32[]{:S(2)}, u32[]{:S(2)}) collective-permute-start(bf16[3072,512]{1,0:T(8,128)(2,1)S(1)} %pad_maximum_fusion), channel_id=1, source_target_pairs={{0,2},{2,0},{4,6},{6,4},{8,10},{10,8},{12,14},{14,12},{16,18},{18,... | collective-permute-start | bytes 9437192 | tf_op jit(solution)/shard_map/ppermute | solution.py:89
  108.3 9.4 %collective-permute-start.5 = (f32[8,16,516]{2,1,0:T(8,128)S(1)}, f32[8,16,516]{2,1,0:T(8,128)S(1)}, u32[]{:S(2)}, u32[]{:S(2)}) collective-permute-start(f32[8,16,516]{2,1,0:T(8,128)S(1)} %pad_maximum_fusion.1), channel_id=1, source_target_pairs={{0,1},{1,0},{2,3},{3,2},{4,5},{5,4},{6,7},{7,6},{8,9},{9,8},{10,11... | collective-permute-start | bytes 792584 | tf_op jit(solution)/shard_map/ppermute | solution.py:37
  118.0 7.9 %collective-permute-done.5 = f32[8,16,516]{2,1,0:T(8,128)S(1)} collective-permute-done((f32[8,16,516]{2,1,0:T(8,128)S(1)}, f32[8,16,516]{2,1,0:T(8,128)S(1)}, u32[]{:S(2)}, u32[]{:S(2)}) %collective-permute-start.5) | collective-permute-done | bytes 264224 | tf_op jit(solution)/shard_map/ppermute | solution.py:37
  126.2 0.2 fusion.48
  126.7 2.8 %collective-permute-start.14 = (f32[16,512]{1,0:T(8,128)S(1)}, f32[16,512]{1,0:T(8,128)S(1)}, u32[]{:S(2)}, u32[]{:S(2)}) collective-permute-start(f32[16,512]{1,0:T(8,128)S(1)} %fusion.66), channel_id=1, source_target_pairs={{0,64},{64,128},{128,192},{192,256},{256,320},{320,384},{384,448},... | collective-permute-start | bytes 98312 | tf_op jit(solution)/shard_map/ppermute | solution.py:17
  129.7 4.3 %collective-permute-start.15 = (f32[16,512]{1,0:T(8,128)S(1)}, f32[16,512]{1,0:T(8,128)S(1)}, u32[]{:S(2)}, u32[]{:S(2)}) collective-permute-start(f32[16,512]{1,0:T(8,128)S(1)} %fusion.59), channel_id=1, source_target_pairs={{64,0},{128,64},{192,128},{256,192},{320,256},{384,320},{448,384},... | collective-permute-start | bytes 98312 | tf_op jit(solution)/shard_map/ppermute | solution.py:17
  134.0 19.6 %collective-permute-start.10 = (f32[2]{0:T(128)S(1)}, f32[2]{0:T(128)S(1)}, u32[]{:S(2)}, u32[]{:S(2)}) collective-permute-start(f32[2]{0:T(128)S(1)} %fusion.88), channel_id=1, source_target_pairs={{0,4},{2,6},{4,0},{6,2},{8,12},{10,14},{12,8},{14,10},{16,20},{18,... | collective-permute-start | bytes 32 | tf_op jit(solution)/shard_map/ppermute | solution.py:25
  153.7 2.6 %fusion.15 = f32[1024,512]{1,0:T(8,128)S(1)} fusion(bf16[1024,512]{1,0:T(8,128)(2,1)} %collective-permute-done.6, bf16[1,5,512,512]{3,2,1,0:T(8,128)(2,1)S(1)} %copy-done.1, s32[]{:T(128)S(6)} %select_n.196, pred[]{:T(512)} %get-tuple-element.50), kind=kOutput, calls=%fused_computation.18 | convolution fusion | flops 537133056 | bytes 3670021 | tf_op jit(solution)/shard_map/dot_general | solution.py:108
  156.2 2.6 %fusion.11 = f32[1024,512]{1,0:T(8,128)S(1)} fusion(bf16[1024,512]{1,0:T(8,128)(2,1)} %collective-permute-done.8, bf16[1,5,512,512]{3,2,1,0:T(8,128)(2,1)S(1)} %copy-done.1, s32[]{:T(128)S(6)} %select_n.207, pred[]{:T(512)} %get-tuple-element.48), kind=kOutput, calls=%fused_computation.14 | convolution fusion | flops 537133056 | bytes 3670021 | tf_op jit(solution)/shard_map/dot_general | solution.py:108
  158.8 2.6 %fusion.13 = f32[1024,512]{1,0:T(8,128)S(1)} fusion(bf16[1024,512]{1,0:T(8,128)(2,1)} %collective-permute-done.7, bf16[1,5,512,512]{3,2,1,0:T(8,128)(2,1)S(1)} %copy-done.1, s32[]{:T(128)S(6)} %select_n.201, pred[]{:T(512)} %get-tuple-element.49), kind=kOutput, calls=%fused_computation.16 | convolution fusion | flops 537133056 | bytes 3670021 | tf_op jit(solution)/shard_map/dot_general | solution.py:108
  161.4 7.7 %collective-permute-start.11 = (f32[2]{0:T(128)S(1)}, f32[2]{0:T(128)S(1)}, u32[]{:S(2)}, u32[]{:S(2)}) collective-permute-start(f32[2]{0:T(128)S(1)} %add.252), channel_id=1, source_target_pairs={{0,8},{2,10},{4,12},{6,14},{8,0},{10,2},{12,4},{14,6},{16,24},{18,... | collective-permute-start | bytes 32 | tf_op jit(solution)/shard_map/ppermute | solution.py:25
  169.1 1.5 collective-permute-done.11
  170.6 2.7 %collective-permute-start.12 = (f32[2]{0:T(128)S(1)}, f32[2]{0:T(128)S(1)}, u32[]{:S(2)}, u32[]{:S(2)}) collective-permute-start(f32[2]{0:T(128)S(1)} %add.253), channel_id=1, source_target_pairs={{0,16},{2,18},{4,20},{6,22},{8,24},{10,26},{12,28},{14,30},{16,0},... | collective-permute-start | bytes 32 | tf_op jit(solution)/shard_map/ppermute | solution.py:25
  173.3 2.7 %collective-permute-done.12 = f32[2]{0:T(128)S(1)} collective-permute-done((f32[2]{0:T(128)S(1)}, f32[2]{0:T(128)S(1)}, u32[]{:S(2)}, u32[]{:S(2)}) %collective-permute-start.12) | collective-permute-done | bytes 40 | tf_op jit(solution)/shard_map/ppermute | solution.py:25
  176.1 3.3 %collective-permute-start.13 = (f32[2]{0:T(128)S(1)}, f32[2]{0:T(128)S(1)}, u32[]{:S(2)}, u32[]{:S(2)}) collective-permute-start(f32[2]{0:T(128)S(1)} %add.254), channel_id=1, source_target_pairs={{0,32},{2,34},{4,36},{6,38},{8,40},{10,42},{12,44},{14,46},{16,48}... | collective-permute-start | bytes 32 | tf_op jit(solution)/shard_map/ppermute | solution.py:25
  179.3 3.6 %collective-permute-done.13 = f32[2]{0:T(128)S(1)} collective-permute-done((f32[2]{0:T(128)S(1)}, f32[2]{0:T(128)S(1)}, u32[]{:S(2)}, u32[]{:S(2)}) %collective-permute-start.13) | collective-permute-done | bytes 40 | tf_op jit(solution)/shard_map/ppermute | solution.py:25
  183.0 0.6 fusion.101
  184.9 1.3 fusion.7
  186.2 1.3 fusion.9
  187.5 1.6 add_add_fusion
  189.3 0.4 fusion.1
  189.7 0.3 copy-done.8
  190.1 0.6 copy.139
  190.7 0.6 copy.138
  191.4 0.6 copy.136
  192.0 0.6 copy.137
  192.7 0.6 copy.134
  193.3 0.6 copy.135
  (73 shorter events, 1.7 us)
Async XLA Ops:
  0.6 17.7 %copy-start.3 = (f32[1,16,1,512]{3,2,1,0:T(1,128)S(1)}, f32[1,16,1,512]{3,2,1,0:T(1,128)}, u32[]{:S(2)}) copy-start(f32[1,16,1,512]{3,2,1,0:T(1,128)} %param.21) | copy-start | bytes 98308
  0.6 40.8 %copy-start = (bf16[1,64,16,1,512]{4,2,3,1,0:T(8,128)(2,1)S(1)}, bf16[1,64,16,1,512]{4,2,3,1,0:T(8,128)(2,1)}, u32[]{:S(2)}) copy-start(bf16[1,64,16,1,512]{4,2,3,1,0:T(8,128)(2,1)} %param.24) | copy-start | bytes 3145732
  0.7 18.4 %copy-start.4 = (f32[1,16,1,512]{3,2,1,0:T(1,128)S(1)}, f32[1,16,1,512]{3,2,1,0:T(1,128)}, u32[]{:S(2)}) copy-start(f32[1,16,1,512]{3,2,1,0:T(1,128)} %param.23) | copy-start | bytes 98308
  0.7 19.0 %copy-start.5 = (f32[1,16,1,512]{3,2,1,0:T(1,128)S(1)}, f32[1,16,1,512]{3,2,1,0:T(1,128)}, u32[]{:S(2)}) copy-start(f32[1,16,1,512]{3,2,1,0:T(1,128)} %param.22) | copy-start | bytes 98308
  0.7 19.7 %copy-start.9 = (f32[1,16,1,512]{3,2,1,0:T(1,128)S(1)}, f32[1,16,1,512]{3,2,1,0:T(1,128)}, u32[]{:S(2)}) copy-start(f32[1,16,1,512]{3,2,1,0:T(1,128)} %param.20) | copy-start | bytes 98308
  0.7 20.3 %copy-start.2 = (f32[1,5,16,1,512]{4,3,2,1,0:T(1,128)S(1)}, f32[1,5,16,1,512]{4,3,2,1,0:T(1,128)}, u32[]{:S(2)}) copy-start(f32[1,5,16,1,512]{4,3,2,1,0:T(1,128)} %param.25) | copy-start | bytes 491524
  0.7 22.3 %copy-start.6 = (f32[1,16,1,512]{3,2,1,0:T(1,128)S(1)}, f32[1,16,1,512]{3,2,1,0:T(1,128)}, u32[]{:S(2)}) copy-start(f32[1,16,1,512]{3,2,1,0:T(1,128)} %param.19) | copy-start | bytes 98308
  0.7 22.3 %copy-start.7 = (f32[1,16,1,512]{3,2,1,0:T(1,128)S(1)}, f32[1,16,1,512]{3,2,1,0:T(1,128)}, u32[]{:S(2)}) copy-start(f32[1,16,1,512]{3,2,1,0:T(1,128)} %param.18) | copy-start | bytes 98308
  0.7 30.7 %copy-start.18 = (s32[1,5]{1,0:T(1,128)S(1)}, s32[1,5]{1,0:T(1,128)}, u32[]{:S(2)}) copy-start(s32[1,5]{1,0:T(1,128)} %param.28) | copy-start | bytes 64
  4.0 130.0 %collective-permute-start.8 = (bf16[1024,512]{1,0:T(8,128)(2,1)}, bf16[1024,512]{1,0:T(8,128)(2,1)}, u32[]{:S(2)}, u32[]{:S(2)}) collective-permute-start(bf16[1024,512]{1,0:T(8,128)(2,1)} %fusion.2), channel_id=1, source_target_pairs={{0,58},{2,8},{4,62},{6,12},{8,2},{10,16},{12,6},{14,20},{16,10},{1... | collective-permute-start | bytes 3145736 | tf_op jit(solution)/shard_map/ppermute | solution.py:88
  9.8 93.3 %collective-permute-start.7 = (bf16[1024,512]{1,0:T(8,128)(2,1)}, bf16[1024,512]{1,0:T(8,128)(2,1)}, u32[]{:S(2)}, u32[]{:S(2)}) collective-permute-start(bf16[1024,512]{1,0:T(8,128)(2,1)} %fusion.2), channel_id=1, source_target_pairs={{60,0},{62,2},{0,4},{2,6},{4,8},{6,10},{8,12},{10,14},{12,16},{14,... | collective-permute-start | bytes 3145736 | tf_op jit(solution)/shard_map/ppermute | solution.py:11
  14.1 89.0 %collective-permute-start.6 = (bf16[1024,512]{1,0:T(8,128)(2,1)}, bf16[1024,512]{1,0:T(8,128)(2,1)}, u32[]{:S(2)}, u32[]{:S(2)}) collective-permute-start(bf16[1024,512]{1,0:T(8,128)(2,1)} %fusion.2), channel_id=1, source_target_pairs={{4,0},{6,2},{8,4},{10,6},{12,8},{14,10},{16,12},{18,14},{20,16},{2... | collective-permute-start | bytes 3145736 | tf_op jit(solution)/shard_map/ppermute | solution.py:11
  26.4 53.4 %collective-permute-start = (f32[8,16,2]{2,1,0:T(8,128)}, f32[8,16,2]{2,1,0:T(8,128)}, u32[]{:S(2)}, u32[]{:S(2)}) collective-permute-start(f32[8,16,2]{2,1,0:T(8,128)} %get-tuple-element.70), channel_id=1, source_target_pairs={{2,0},{4,2},{6,4},{8,6},{10,8},{12,10},{14,12},{16,14},{18,16},{20... | collective-permute-start | bytes 3080 | tf_op jit(solution)/shard_map/ppermute | solution.py:11
  28.3 52.9 %collective-permute-start.1 = (f32[8,16,2]{2,1,0:T(8,128)}, f32[8,16,2]{2,1,0:T(8,128)}, u32[]{:S(2)}, u32[]{:S(2)}) collective-permute-start(f32[8,16,2]{2,1,0:T(8,128)} %get-tuple-element.71), channel_id=1, source_target_pairs={{62,0},{0,2},{2,4},{4,6},{6,8},{8,10},{10,12},{12,14},{14,16},{16,... | collective-permute-start | bytes 3080 | tf_op jit(solution)/shard_map/ppermute | solution.py:11
  82.0 5.4 %collective-permute-start.2 = (f32[2]{0:T(128)S(1)}, f32[2]{0:T(128)S(1)}, u32[]{:S(2)}, u32[]{:S(2)}) collective-permute-start(f32[2]{0:T(128)S(1)} %fusion.87), channel_id=1, source_target_pairs={{0,64},{64,0},{128,192},{192,128},{256,320},{320,256},{384,448},{4... | collective-permute-start | bytes 32 | tf_op jit(solution)/shard_map/ppermute | solution.py:25
  87.4 6.3 %collective-permute-start.3 = (f32[2]{0:T(128)S(1)}, f32[2]{0:T(128)S(1)}, u32[]{:S(2)}, u32[]{:S(2)}) collective-permute-start(f32[2]{0:T(128)S(1)} %add.248), channel_id=1, source_target_pairs={{0,128},{64,192},{128,0},{192,64},{256,384},{320,448},{384,256},{4... | collective-permute-start | bytes 32 | tf_op jit(solution)/shard_map/ppermute | solution.py:25
  93.7 9.3 %collective-permute-start.4 = (f32[2]{0:T(128)S(1)}, f32[2]{0:T(128)S(1)}, u32[]{:S(2)}, u32[]{:S(2)}) collective-permute-start(f32[2]{0:T(128)S(1)} %add.249), channel_id=1, source_target_pairs={{0,256},{64,320},{128,384},{192,448},{256,0},{320,64},{384,128},{4... | collective-permute-start | bytes 32 | tf_op jit(solution)/shard_map/ppermute | solution.py:25
  105.1 21.4 %copy-start.11 = (f32[1,1,16,1,512]{4,3,2,1,0:T(1,128)S(1)}, f32[1,1,16,1,512]{4,3,2,1,0:T(1,128)}, u32[]{:S(2)}) copy-start(f32[1,1,16,1,512]{4,3,2,1,0:T(1,128)} %get-tuple-element.73) | copy-start | bytes 98308
  105.1 21.4 %copy-start.12 = (f32[1,1,16,1,512]{4,3,2,1,0:T(1,128)S(1)}, f32[1,1,16,1,512]{4,3,2,1,0:T(1,128)}, u32[]{:S(2)}) copy-start(f32[1,1,16,1,512]{4,3,2,1,0:T(1,128)} %get-tuple-element.74) | copy-start | bytes 98308
  105.1 79.8 %collective-permute-start.9 = (bf16[3072,512]{1,0:T(8,128)(2,1)S(1)}, bf16[3072,512]{1,0:T(8,128)(2,1)S(1)}, u32[]{:S(2)}, u32[]{:S(2)}) collective-permute-start(bf16[3072,512]{1,0:T(8,128)(2,1)S(1)} %pad_maximum_fusion), channel_id=1, source_target_pairs={{0,2},{2,0},{4,6},{6,4},{8,10},{10,8},{12,14},{14,12},{16,18},{18,... | collective-permute-start | bytes 9437192 | tf_op jit(solution)/shard_map/ppermute | solution.py:89
  108.3 45.4 %copy-start.1 = (bf16[1,5,512,512]{3,2,1,0:T(8,128)(2,1)S(1)}, bf16[1,5,512,512]{3,2,1,0:T(8,128)(2,1)}, u32[]{:S(2)}) copy-start(bf16[1,5,512,512]{3,2,1,0:T(8,128)(2,1)} %param.29) | copy-start | bytes 7864324
  108.3 17.6 %collective-permute-start.5 = (f32[8,16,516]{2,1,0:T(8,128)S(1)}, f32[8,16,516]{2,1,0:T(8,128)S(1)}, u32[]{:S(2)}, u32[]{:S(2)}) collective-permute-start(f32[8,16,516]{2,1,0:T(8,128)S(1)} %pad_maximum_fusion.1), channel_id=1, source_target_pairs={{0,1},{1,0},{2,3},{3,2},{4,5},{5,4},{6,7},{7,6},{8,9},{9,8},{10,11... | collective-permute-start | bytes 792584 | tf_op jit(solution)/shard_map/ppermute | solution.py:37
  126.7 63.0 %collective-permute-start.14 = (f32[16,512]{1,0:T(8,128)S(1)}, f32[16,512]{1,0:T(8,128)S(1)}, u32[]{:S(2)}, u32[]{:S(2)}) collective-permute-start(f32[16,512]{1,0:T(8,128)S(1)} %fusion.66), channel_id=1, source_target_pairs={{0,64},{64,128},{128,192},{192,256},{256,320},{320,384},{384,448},... | collective-permute-start | bytes 98312 | tf_op jit(solution)/shard_map/ppermute | solution.py:17
  129.7 59.9 %collective-permute-start.15 = (f32[16,512]{1,0:T(8,128)S(1)}, f32[16,512]{1,0:T(8,128)S(1)}, u32[]{:S(2)}, u32[]{:S(2)}) collective-permute-start(f32[16,512]{1,0:T(8,128)S(1)} %fusion.59), channel_id=1, source_target_pairs={{64,0},{128,64},{192,128},{256,192},{320,256},{384,320},{448,384},... | collective-permute-start | bytes 98312 | tf_op jit(solution)/shard_map/ppermute | solution.py:17
  134.0 27.4 %collective-permute-start.10 = (f32[2]{0:T(128)S(1)}, f32[2]{0:T(128)S(1)}, u32[]{:S(2)}, u32[]{:S(2)}) collective-permute-start(f32[2]{0:T(128)S(1)} %fusion.88), channel_id=1, source_target_pairs={{0,4},{2,6},{4,0},{6,2},{8,12},{10,14},{12,8},{14,10},{16,20},{18,... | collective-permute-start | bytes 32 | tf_op jit(solution)/shard_map/ppermute | solution.py:25
  161.4 9.2 %collective-permute-start.11 = (f32[2]{0:T(128)S(1)}, f32[2]{0:T(128)S(1)}, u32[]{:S(2)}, u32[]{:S(2)}) collective-permute-start(f32[2]{0:T(128)S(1)} %add.252), channel_id=1, source_target_pairs={{0,8},{2,10},{4,12},{6,14},{8,0},{10,2},{12,4},{14,6},{16,24},{18,... | collective-permute-start | bytes 32 | tf_op jit(solution)/shard_map/ppermute | solution.py:25
  170.6 5.4 %collective-permute-start.12 = (f32[2]{0:T(128)S(1)}, f32[2]{0:T(128)S(1)}, u32[]{:S(2)}, u32[]{:S(2)}) collective-permute-start(f32[2]{0:T(128)S(1)} %add.253), channel_id=1, source_target_pairs={{0,16},{2,18},{4,20},{6,22},{8,24},{10,26},{12,28},{14,30},{16,0},... | collective-permute-start | bytes 32 | tf_op jit(solution)/shard_map/ppermute | solution.py:25
  176.1 6.9 %collective-permute-start.13 = (f32[2]{0:T(128)S(1)}, f32[2]{0:T(128)S(1)}, u32[]{:S(2)}, u32[]{:S(2)}) collective-permute-start(f32[2]{0:T(128)S(1)} %add.254), channel_id=1, source_target_pairs={{0,32},{2,34},{4,36},{6,38},{8,40},{10,42},{12,44},{14,46},{16,48}... | collective-permute-start | bytes 32 | tf_op jit(solution)/shard_map/ppermute | solution.py:25
  189.2 0.8 copy-start.8
  189.2 0.8 copy-start.10
  189.2 0.8 copy-start.13
  189.2 0.8 copy-start.14
  189.2 0.8 copy-start.15
  189.2 0.8 copy-start.16
  189.2 0.8 copy-start.17

commit v8 on v5

--- a/solution.py
+++ b/solution.py
@@ -37,37 +37,37 @@
     return lax.ppermute(value, "lat", [(0, 1), (1, 0)])
 
 
-def forward_pair(f_a, f_b, c_a, cn_a):
-    return (
-        (0.5 + c_a[0, :, 1:-1]) * f_a[:, 1:-1]
-        + c_a[1, :, 1:-1] * f_a[:, 2:]
-        + c_a[2, :, 1:-1] * f_a[:, :-2]
-        + cn_a[:, 1:-1] * f_b[:, 1:-1]
+def propagate_both(own, first_row):
+    u_a, w_a, c_a = own[0], own[1], own[2:]
+    k_a = jnp.where(first_row, c_a[3], c_a[4])
+    sent = lat_partner(jnp.stack([u_a[:, 1:-1], (k_a * w_a)[:, 1:-1]]))
+    u_b, g_b = sent[0], sent[1]
+    s_a = (
+        (0.5 + c_a[0, :, 1:-1]) * u_a[:, 1:-1]
+        + c_a[1, :, 1:-1] * u_a[:, 2:]
+        + c_a[2, :, 1:-1] * u_a[:, :-2]
+        + k_a[:, 1:-1] * u_b
     )
-
-
-def adjoint_pair(f_a, f_b, c_a, ca_a):
-    return (
-        (0.5 + c_a[0, :, 1:-1]) * f_a[:, 1:-1]
-        + (c_a[1] * f_a)[:, :-2]
-        + (c_a[2] * f_a)[:, 2:]
-        + ca_a[:, 1:-1] * f_b[:, 1:-1]
+    t_a = (
+        (0.5 + c_a[0, :, 1:-1]) * w_a[:, 1:-1]
+        + (c_a[1] * w_a)[:, :-2]
+        + (c_a[2] * w_a)[:, 2:]
+        + g_b
     )
-
-
-def propagate_both(own, other, first_row):
-    u_a, w_a, c_a = own[0], own[1], own[2:]
-    u_b, w_b, c_b = other[0], other[1], other[2:]
-    cn_a = jnp.where(first_row, c_a[3], c_a[4])
-    cn_b = jnp.where(first_row, c_b[4], c_b[3])
-    ca_a = jnp.where(first_row, c_b[4], c_b[3])
-    ca_b = jnp.where(first_row, c_a[3], c_a[4])
-    s_a = forward_pair(u_a, u_b, c_a, cn_a)
-    s_b = forward_pair(u_b, u_a, c_b, cn_b)
-    moved = forward_pair(s_a, s_b, c_a[:, :, 1:-1], cn_a[:, 1:-1])
-    t_a = adjoint_pair(w_a, w_b, c_a, ca_a)
-    t_b = adjoint_pair(w_b, w_a, c_b, ca_b)
-    backed = adjoint_pair(t_a, t_b, c_a[:, :, 1:-1], ca_a[:, 1:-1])
+    sent = lat_partner(jnp.stack([s_a[:, 1:-1], (k_a[:, 1:-1] * t_a)[:, 1:-1]]))
+    s_b, h_b = sent[0], sent[1]
+    moved = (
+        (0.5 + c_a[0, :, 2:-2]) * s_a[:, 1:-1]
+        + c_a[1, :, 2:-2] * s_a[:, 2:]
+        + c_a[2, :, 2:-2] * s_a[:, :-2]
+        + k_a[:, 2:-2] * s_b
+    )
+    backed = (
+        (0.5 + c_a[0, :, 2:-2]) * t_a[:, 1:-1]
+        + (c_a[1, :, 1:-1] * t_a)[:, :-2]
+        + (c_a[2, :, 1:-1] * t_a)[:, 2:]
+        + h_b
+    )
     return moved, backed
 
 
@@ -143,9 +143,8 @@
         [search_incr[0, :, 0][None], search_dual[0, :, 0][None], tangent_coefs[0, :, :, 0]], axis=0
     )
     own = lon_extended(packed, 2)
-    other = lat_partner(own)
     first_row = lax.axis_index("lat") == 0
-    moved, backed = propagate_both(own, other, first_row)
+    moved, backed = propagate_both(own, first_row)
     earlier = shifted(moved, "win", 1)[None, :, None]
     following = shifted(backed, "win", -1)[None, :, None]
 
@@ -157,7 +156,7 @@
         butterfly_sum(jnp.stack([resid_local, search_local]), ("win",)),
     )
     covar = covar[None, :, None]
-    partials, _ = lax.optimization_barrier((partials, other))
+    partials, _, _ = lax.optimization_barrier((partials, moved, backed))
     sums = butterfly_sum(partials, ("lon", "lat"))
     alpha = sums[0] / (sums[1] + 1e-06)
     image_dual = covar + search_incr - earlier

time: 192 us -> 203 us (1.057)
  the two profiles are of different devices: /device:TPU:38 before, /device:TPU:8 now
where the time goes in v8:
time: 203 us; the launch traced here: 201 us
  starting transfers between devices  104 us (51%)
  waiting for transfers between devices  41.3 us (20%)
  between operations  19.7 us (10%)
  other arithmetic  16.6 us (8%)
  matrix products  13.2 us (7%)
  local copies, waits for them, and re-layouts  6.06 us (3%)
    ppermute x9, starting transfers between devices, butterfly_sum(): lax.ppermute(value, axis, [(i, i ^ step) for i in range(count)])  55.5 us
    ppermute x4, waiting for transfers between devices, from_offset(): lax.ppermute(value, axis, [((i + distance) % count, i) for i in range(cou...  19.2 us
    ppermute x4, starting transfers between devices, from_offset(): lax.ppermute(value, axis, [((i + distance) % count, i) for i in range(cou...  19.2 us
    ppermute x9, waiting for transfers between devices, butterfly_sum(): lax.ppermute(value, axis, [(i, i ^ step) for i in range(count)])  17.6 us
    ppermute x2, starting transfers between devices, lat_partner(): return lax.ppermute(value, 'lat', [(0, 1), (1, 0)])  11.8 us
    dot_general x6, matrix products, localize(): jnp.dot(value, weight_for(offset), preferred_element_type=jnp.float32)  10.8 us
    ppermute x1, starting transfers between devices, localize(): lax.ppermute(flat, 'lon', [(s, (s + 3) % bands if s % 2 else (s - 3) % ba...  7.71 us
    ppermute x2, starting transfers between devices, shifted(): lax.ppermute(value, axis, [(source, source + steps) for source in range(l...  5.84 us
  transfers between devices with their start and end apart: 20, of which 8 were waited for; matrix products, arithmetic and copies ran while one was open for 15% of the time, Pallas kernels for 0%

profile of v8, /device:TPU:8, one launch (start us, length us, event | category | flops | bytes accessed | tf_op | source)
XLA Modules:
  0.0 201.3 jit_solution(1386682402602529714)
XLA Ops:
  0.7 0.9 copy_bitcast_fusion.3
  1.6 2.5 %fusion.2 = bf16[1024,512]{1,0:T(8,128)(2,1)} fusion(bf16[1,64,16,1,512]{4,2,3,1,0:T(8,128)(2,1)} %param.24, f32[16,512]{1,0:T(8,128)S(1)} %get-tuple-element.59), kind=kLoop, calls=%fused_computation.6 | loop fusion | flops 1572864 | bytes 2129920 | tf_op jit(solution)/shard_map/convert_element_type | solution.py:77
  4.1 7.7 %collective-permute-start.6 = (bf16[1024,512]{1,0:T(8,128)(2,1)}, bf16[1024,512]{1,0:T(8,128)(2,1)}, u32[]{:S(2)}, u32[]{:S(2)}) collective-permute-start(bf16[1024,512]{1,0:T(8,128)(2,1)} %fusion.2), channel_id=1, source_target_pairs={{0,58},{2,8},{4,62},{6,12},{8,2},{10,16},{12,6},{14,20},{16,10},{1... | collective-permute-start | bytes 3145736 | tf_op jit(solution)/shard_map/ppermute | solution.py:89
  11.8 4.3 %collective-permute-start.5 = (bf16[1024,512]{1,0:T(8,128)(2,1)}, bf16[1024,512]{1,0:T(8,128)(2,1)S(1)}, u32[]{:S(2)}, u32[]{:S(2)}) collective-permute-start(bf16[1024,512]{1,0:T(8,128)(2,1)} %fusion.2), channel_id=1, source_target_pairs={{60,0},{62,2},{0,4},{2,6},{4,8},{6,10},{8,12},{10,14},{12,16},{14,... | collective-permute-start | bytes 3145736 | tf_op jit(solution)/shard_map/ppermute | solution.py:11
  16.1 5.5 %collective-permute-start.4 = (bf16[1024,512]{1,0:T(8,128)(2,1)}, bf16[1024,512]{1,0:T(8,128)(2,1)}, u32[]{:S(2)}, u32[]{:S(2)}) collective-permute-start(bf16[1024,512]{1,0:T(8,128)(2,1)} %fusion.2), channel_id=1, source_target_pairs={{4,0},{6,2},{8,4},{10,6},{12,8},{14,10},{16,12},{18,14},{20,16},{2... | collective-permute-start | bytes 3145736 | tf_op jit(solution)/shard_map/ppermute | solution.py:11
  21.6 0.7 multiply_reduce_fusion.2
  22.2 0.7 multiply_reduce_fusion
  22.9 0.7 multiply_reduce_fusion.1
  23.6 0.7 multiply_reduce_fusion.3
  26.2 0.7 multiply_reduce_fusion.4
  28.9 2.3 %collective-permute-start = (f32[2]{0:T(128)S(1)}, f32[2]{0:T(128)S(1)}, u32[]{:S(2)}, u32[]{:S(2)}) collective-permute-start(f32[2]{0:T(128)S(1)} %pad_maximum_fusion.7), channel_id=1, source_target_pairs={{0,64},{64,0},{128,192},{192,128},{256,320},{320,256},{384,448},{4... | collective-permute-start | bytes 32 | tf_op jit(solution)/shard_map/ppermute | solution.py:25
  31.3 0.7 pad_maximum_fusion.6
  32.0 1.9 collective-permute-start.8
  34.0 0.6 bitcast_reduce_fusion
  35.8 0.7 bitcast_reduce_fusion.6
  37.8 0.7 bitcast_reduce_fusion.5
  39.7 0.7 bitcast_reduce_fusion.4
  41.9 0.7 bitcast_reduce_fusion.3
  43.6 0.7 bitcast_reduce_fusion.2
  45.6 0.8 compare_reduce_fusion
  46.4 0.7 bitcast_reduce_fusion.1
  48.4 0.6 fusion.85
  49.0 0.3 fusion
  53.7 2.5 %fusion.17 = f32[1024,512]{1,0:T(8,128)S(1)} fusion(bf16[1024,512]{1,0:T(8,128)(2,1)S(1)} %bitcast.146, bf16[1,5,512,512]{3,2,1,0:T(8,128)(2,1)} %param.29, s32[]{:T(128)S(6)} %select_n.166, pred[]{:T(512)} %get-tuple-element.35), kind=kOutput, calls=%fused_computation.20 | convolution fusion | flops 537133056 | bytes 3670532 | tf_op jit(solution)/shard_map/dot_general | solution.py:107
  56.2 7.6 %collective-permute-start.9 = (f32[7,16,2]{2,1,0:T(8,128)S(1)}, f32[7,16,2]{2,1,0:T(8,128)S(1)}, u32[]{:S(2)}, u32[]{:S(2)}) collective-permute-start(f32[7,16,2]{2,1,0:T(8,128)S(1)} %copy-done.15), channel_id=1, source_target_pairs={{2,0},{4,2},{6,4},{8,6},{10,8},{12,10},{14,12},{16,14},{18,16},{20... | collective-permute-start | bytes 2696 | tf_op jit(solution)/shard_map/ppermute | solution.py:11
  63.8 19.2 %collective-permute-done.8 = f32[7,16,2]{2,1,0:T(8,128)} collective-permute-done((f32[7,16,2]{2,1,0:T(8,128)}, f32[7,16,2]{2,1,0:T(8,128)}, u32[]{:S(2)}, u32[]{:S(2)}) %collective-permute-start.8) | collective-permute-done | bytes 928 | tf_op jit(solution)/shard_map/ppermute | solution.py:11
  83.0 4.5 %collective-permute-start.1 = (f32[2]{0:T(128)S(1)}, f32[2]{0:T(128)S(1)}, u32[]{:S(2)}, u32[]{:S(2)}) collective-permute-start(f32[2]{0:T(128)S(1)} %fusion.92), channel_id=1, source_target_pairs={{0,128},{64,192},{128,0},{192,64},{256,384},{320,448},{384,256},{4... | collective-permute-start | bytes 32 | tf_op jit(solution)/shard_map/ppermute | solution.py:25
  87.5 1.0 pad_maximum_fusion.1
  88.7 9.6 %collective-permute-start.10 = (f32[2,16,514]{2,1,0:T(8,128)S(1)}, f32[2,16,514]{2,1,0:T(8,128)S(1)}, u32[]{:S(2)}, u32[]{:S(2)}) collective-permute-start(f32[2,16,514]{2,1,0:T(8,128)S(1)} %pad_maximum_fusion.2), channel_id=1, source_target_pairs={{0,1},{1,0},{2,3},{3,2},{4,5},{5,4},{6,7},{7,6},{8,9},{9,8},{10,11... | collective-permute-start | bytes 197384 | tf_op jit(solution)/shard_map/ppermute | solution.py:37
  98.5 5.0 %collective-permute-start.2 = (f32[2]{0:T(128)S(1)}, f32[2]{0:T(128)S(1)}, u32[]{:S(2)}, u32[]{:S(2)}) collective-permute-start(f32[2]{0:T(128)S(1)} %fusion.93), channel_id=1, source_target_pairs={{0,256},{64,320},{128,384},{192,448},{256,0},{320,64},{384,128},{4... | collective-permute-start | bytes 32 | tf_op jit(solution)/shard_map/ppermute | solution.py:25
  103.5 4.3 %collective-permute-done.2 = f32[2]{0:T(128)S(1)} collective-permute-done((f32[2]{0:T(128)S(1)}, f32[2]{0:T(128)S(1)}, u32[]{:S(2)}, u32[]{:S(2)}) %collective-permute-start.2) | collective-permute-done | bytes 40 | tf_op jit(solution)/shard_map/ppermute | solution.py:25
  107.8 1.9 collective-permute-start.3
  110.2 2.2 %collective-permute-start.11 = (f32[2,16,512]{2,1,0:T(8,128)S(1)}, f32[2,16,512]{2,1,0:T(8,128)S(1)}, u32[]{:S(2)}, u32[]{:S(2)}) collective-permute-start(f32[2,16,512]{2,1,0:T(8,128)S(1)} %pad_maximum_fusion.3), channel_id=1, source_target_pairs={{0,1},{1,0},{2,3},{3,2},{4,5},{5,4},{6,7},{7,6},{8,9},{9,8},{10,11... | collective-permute-start | bytes 196616 | tf_op jit(solution)/shard_map/ppermute | solution.py:37
  112.4 1.4 pad_maximum_fusion
  113.7 2.4 %collective-permute-start.7 = (bf16[2048,512]{1,0:T(8,128)(2,1)S(1)}, bf16[2048,512]{1,0:T(8,128)(2,1)S(1)}, u32[]{:S(2)}, u32[]{:S(2)}) collective-permute-start(bf16[2048,512]{1,0:T(8,128)(2,1)S(1)} %pad_maximum_fusion), channel_id=1, source_target_pairs={{0,2},{2,0},{4,6},{6,4},{8,10},{10,8},{12,14},{14,12},{16,18},{18,... | collective-permute-start | bytes 6291464 | tf_op jit(solution)/shard_map/ppermute | solution.py:90
  116.2 4.5 %collective-permute-done.11 = f32[2,16,512]{2,1,0:T(8,128)S(1)} collective-permute-done((f32[2,16,512]{2,1,0:T(8,128)S(1)}, f32[2,16,512]{2,1,0:T(8,128)S(1)}, u32[]{:S(2)}, u32[]{:S(2)}) %collective-permute-start.11) | collective-permute-done | bytes 65568 | tf_op jit(solution)/shard_map/ppermute | solution.py:37
  120.9 2.4 %collective-permute-start.19 = (f32[16,512]{1,0:T(8,128)S(1)}, f32[16,512]{1,0:T(8,128)S(1)}, u32[]{:S(2)}, u32[]{:S(2)}) collective-permute-start(f32[16,512]{1,0:T(8,128)S(1)} %get-tuple-element.51), channel_id=1, source_target_pairs={{64,0},{128,64},{192,128},{256,192},{320,256},{384,320},{448,384},... | collective-permute-start | bytes 98312 | tf_op jit(solution)/shard_map/ppermute | solution.py:17
  123.2 3.5 %collective-permute-start.18 = (f32[16,512]{1,0:T(8,128)S(1)}, f32[16,512]{1,0:T(8,128)S(1)}, u32[]{:S(2)}, u32[]{:S(2)}) collective-permute-start(f32[16,512]{1,0:T(8,128)S(1)} %get-tuple-element.52), channel_id=1, source_target_pairs={{0,64},{64,128},{128,192},{192,256},{256,320},{320,384},{384,448},... | collective-permute-start | bytes 98312 | tf_op jit(solution)/shard_map/ppermute | solution.py:17
  126.7 1.9 collective-permute-start.12
  128.7 1.4 fusion.15
  130.1 2.5 %fusion.13 = f32[1024,512]{1,0:T(8,128)S(1)} fusion(bf16[1024,512]{1,0:T(8,128)(2,1)} %collective-permute-done.4, bf16[1,5,512,512]{3,2,1,0:T(8,128)(2,1)S(1)} %copy-done.1, s32[]{:T(128)S(6)} %select_n.178, pred[]{:T(512)} %get-tuple-element.33), kind=kOutput, calls=%fused_computation.16 | convolution fusion | flops 537133056 | bytes 3670021 | tf_op jit(solution)/shard_map/dot_general | solution.py:109
  132.6 2.6 %fusion.9 = f32[1024,512]{1,0:T(8,128)S(1)} fusion(bf16[1024,512]{1,0:T(8,128)(2,1)} %collective-permute-done.6, bf16[1,5,512,512]{3,2,1,0:T(8,128)(2,1)S(1)} %copy-done.1, s32[]{:T(128)S(6)} %select_n.189, pred[]{:T(512)} %get-tuple-element.31), kind=kOutput, calls=%fused_computation.12 | convolution fusion | flops 537133056 | bytes 3670021 | tf_op jit(solution)/shard_map/dot_general | solution.py:109
  135.2 1.3 fusion.11
  136.6 22.7 %collective-permute-start.13 = (f32[2]{0:T(128)S(1)}, f32[2]{0:T(128)S(1)}, u32[]{:S(2)}, u32[]{:S(2)}) collective-permute-start(f32[2]{0:T(128)S(1)} %add.237), channel_id=1, source_target_pairs={{0,4},{2,6},{4,0},{6,2},{8,12},{10,14},{12,8},{14,10},{16,20},{18,... | collective-permute-start | bytes 32 | tf_op jit(solution)/shard_map/ppermute | solution.py:25
  159.3 1.5 collective-permute-done.13
  160.8 7.7 %collective-permute-start.14 = (f32[2]{0:T(128)S(1)}, f32[2]{0:T(128)S(1)}, u32[]{:S(2)}, u32[]{:S(2)}) collective-permute-start(f32[2]{0:T(128)S(1)} %add.238), channel_id=1, source_target_pairs={{0,8},{2,10},{4,12},{6,14},{8,0},{10,2},{12,4},{14,6},{16,24},{18,... | collective-permute-start | bytes 32 | tf_op jit(solution)/shard_map/ppermute | solution.py:25
  168.5 1.5 collective-permute-done.14
  170.0 3.4 %collective-permute-start.15 = (f32[2]{0:T(128)S(1)}, f32[2]{0:T(128)S(1)}, u32[]{:S(2)}, u32[]{:S(2)}) collective-permute-start(f32[2]{0:T(128)S(1)} %add.239), channel_id=1, source_target_pairs={{0,16},{2,18},{4,20},{6,22},{8,24},{10,26},{12,28},{14,30},{16,0},... | collective-permute-start | bytes 32 | tf_op jit(solution)/shard_map/ppermute | solution.py:25
  173.4 2.0 %collective-permute-done.15 = f32[2]{0:T(128)S(1)} collective-permute-done((f32[2]{0:T(128)S(1)}, f32[2]{0:T(128)S(1)}, u32[]{:S(2)}, u32[]{:S(2)}) %collective-permute-start.15) | collective-permute-done | bytes 40 | tf_op jit(solution)/shard_map/ppermute | solution.py:25
  175.4 4.9 %collective-permute-start.16 = (f32[2]{0:T(128)S(1)}, f32[2]{0:T(128)S(1)}, u32[]{:S(2)}, u32[]{:S(2)}) collective-permute-start(f32[2]{0:T(128)S(1)} %add.240), channel_id=1, source_target_pairs={{0,32},{2,34},{4,36},{6,38},{8,40},{10,42},{12,44},{14,46},{16,48}... | collective-permute-start | bytes 32 | tf_op jit(solution)/shard_map/ppermute | solution.py:25
  180.3 2.0 collective-permute-done.16
  182.3 3.1 %collective-permute-start.17 = (f32[2]{0:T(128)S(1)}, f32[2]{0:T(128)S(1)}, u32[]{:S(2)}, u32[]{:S(2)}) collective-permute-start(f32[2]{0:T(128)S(1)} %add.241), channel_id=1, source_target_pairs={{0,1},{1,0},{2,3},{3,2},{4,5},{5,4},{6,7},{7,6},{8,9},{9,8},{10,11... | collective-permute-start | bytes 32 | tf_op jit(solution)/shard_map/ppermute | solution.py:25
  185.4 6.2 %collective-permute-done.17 = f32[2]{0:T(128)S(1)} collective-permute-done((f32[2]{0:T(128)S(1)}, f32[2]{0:T(128)S(1)}, u32[]{:S(2)}, u32[]{:S(2)}) %collective-permute-start.17) | collective-permute-done | bytes 40 | tf_op jit(solution)/shard_map/ppermute | solution.py:25
  191.7 0.6 fusion.86
  193.6 0.6 copy.38
  194.2 0.7 multiply_subtract_fusion
  194.9 1.3 fusion.7
  196.3 1.6 add_add_fusion
  198.0 0.4 fusion.1
  198.3 0.3 copy-done.8
  198.8 0.6 copy.42
  199.4 0.6 copy.40
  200.0 0.6 copy.41
  200.7 0.6 copy.39
  (76 shorter events, 1.2 us)
Async XLA Ops:
  0.6 20.9 %copy-start.2 = (f32[1,16,1,512]{3,2,1,0:T(1,128)S(1)}, f32[1,16,1,512]{3,2,1,0:T(1,128)}, u32[]{:S(2)}) copy-start(f32[1,16,1,512]{3,2,1,0:T(1,128)} %param.21) | copy-start | bytes 98308
  0.6 21.6 %copy-start.4 = (f32[1,16,1,512]{3,2,1,0:T(1,128)S(1)}, f32[1,16,1,512]{3,2,1,0:T(1,128)}, u32[]{:S(2)}) copy-start(f32[1,16,1,512]{3,2,1,0:T(1,128)} %param.23) | copy-start | bytes 98308
  0.7 48.4 %copy-start = (bf16[1,64,16,1,512]{4,2,3,1,0:T(8,128)(2,1)S(1)}, bf16[1,64,16,1,512]{4,2,3,1,0:T(8,128)(2,1)}, u32[]{:S(2)}) copy-start(bf16[1,64,16,1,512]{4,2,3,1,0:T(8,128)(2,1)} %param.24) | copy-start | bytes 3145732
  0.7 22.2 %copy-start.5 = (f32[1,16,1,512]{3,2,1,0:T(1,128)S(1)}, f32[1,16,1,512]{3,2,1,0:T(1,128)}, u32[]{:S(2)}) copy-start(f32[1,16,1,512]{3,2,1,0:T(1,128)} %param.22) | copy-start | bytes 98308
  0.7 22.9 %copy-start.13 = (f32[1,16,1,512]{3,2,1,0:T(1,128)S(1)}, f32[1,16,1,512]{3,2,1,0:T(1,128)}, u32[]{:S(2)}) copy-start(f32[1,16,1,512]{3,2,1,0:T(1,128)} %param.20) | copy-start | bytes 98308
  0.7 25.5 %copy-start.6 = (f32[1,16,1,512]{3,2,1,0:T(1,128)S(1)}, f32[1,16,1,512]{3,2,1,0:T(1,128)}, u32[]{:S(2)}) copy-start(f32[1,16,1,512]{3,2,1,0:T(1,128)} %param.19) | copy-start | bytes 98308
  0.7 25.5 %copy-start.7 = (f32[1,16,1,512]{3,2,1,0:T(1,128)S(1)}, f32[1,16,1,512]{3,2,1,0:T(1,128)}, u32[]{:S(2)}) copy-start(f32[1,16,1,512]{3,2,1,0:T(1,128)} %param.18) | copy-start | bytes 98308
  0.7 30.6 %copy-start.3 = (f32[1,5,16,1,512]{4,3,2,1,0:T(1,128)S(1)}, f32[1,5,16,1,512]{4,3,2,1,0:T(1,128)}, u32[]{:S(2)}) copy-start(f32[1,5,16,1,512]{4,3,2,1,0:T(1,128)} %param.25) | copy-start | bytes 491524
  0.7 33.3 %copy-start.20 = (s32[1,5]{1,0:T(1,128)S(1)}, s32[1,5]{1,0:T(1,128)}, u32[]{:S(2)}) copy-start(s32[1,5]{1,0:T(1,128)} %param.28) | copy-start | bytes 64
  4.1 122.7 %collective-permute-start.6 = (bf16[1024,512]{1,0:T(8,128)(2,1)}, bf16[1024,512]{1,0:T(8,128)(2,1)}, u32[]{:S(2)}, u32[]{:S(2)}) collective-permute-start(bf16[1024,512]{1,0:T(8,128)(2,1)} %fusion.2), channel_id=1, source_target_pairs={{0,58},{2,8},{4,62},{6,12},{8,2},{10,16},{12,6},{14,20},{16,10},{1... | collective-permute-start | bytes 3145736 | tf_op jit(solution)/shard_map/ppermute | solution.py:89
  11.8 100.6 %collective-permute-start.5 = (bf16[1024,512]{1,0:T(8,128)(2,1)}, bf16[1024,512]{1,0:T(8,128)(2,1)S(1)}, u32[]{:S(2)}, u32[]{:S(2)}) collective-permute-start(bf16[1024,512]{1,0:T(8,128)(2,1)} %fusion.2), channel_id=1, source_target_pairs={{60,0},{62,2},{0,4},{2,6},{4,8},{6,10},{8,12},{10,14},{12,16},{14,... | collective-permute-start | bytes 3145736 | tf_op jit(solution)/shard_map/ppermute | solution.py:11
  16.1 96.3 %collective-permute-start.4 = (bf16[1024,512]{1,0:T(8,128)(2,1)}, bf16[1024,512]{1,0:T(8,128)(2,1)}, u32[]{:S(2)}, u32[]{:S(2)}) collective-permute-start(bf16[1024,512]{1,0:T(8,128)(2,1)} %fusion.2), channel_id=1, source_target_pairs={{4,0},{6,2},{8,4},{10,6},{12,8},{14,10},{16,12},{18,14},{20,16},{2... | collective-permute-start | bytes 3145736 | tf_op jit(solution)/shard_map/ppermute | solution.py:11
  28.9 27.2 %collective-permute-start = (f32[2]{0:T(128)S(1)}, f32[2]{0:T(128)S(1)}, u32[]{:S(2)}, u32[]{:S(2)}) collective-permute-start(f32[2]{0:T(128)S(1)} %pad_maximum_fusion.7), channel_id=1, source_target_pairs={{0,64},{64,0},{128,192},{192,128},{256,320},{320,256},{384,448},{4... | collective-permute-start | bytes 32 | tf_op jit(solution)/shard_map/ppermute | solution.py:25
  32.0 51.0 %collective-permute-start.8 = (f32[7,16,2]{2,1,0:T(8,128)}, f32[7,16,2]{2,1,0:T(8,128)}, u32[]{:S(2)}, u32[]{:S(2)}) collective-permute-start(f32[7,16,2]{2,1,0:T(8,128)} %get-tuple-element.46), channel_id=1, source_target_pairs={{62,0},{0,2},{2,4},{4,6},{6,8},{8,10},{10,12},{12,14},{14,16},{16,... | collective-permute-start | bytes 2696 | tf_op jit(solution)/shard_map/ppermute | solution.py:11
  53.7 2.5 %copy-start.15 = (f32[7,16,2]{2,1,0:T(8,128)S(1)}, f32[7,16,2]{2,1,0:T(8,128)}, u32[]{:S(2)}) copy-start(f32[7,16,2]{2,1,0:T(8,128)} %get-tuple-element.47) | copy-start | bytes 2692
  56.2 31.4 %collective-permute-start.9 = (f32[7,16,2]{2,1,0:T(8,128)S(1)}, f32[7,16,2]{2,1,0:T(8,128)S(1)}, u32[]{:S(2)}, u32[]{:S(2)}) collective-permute-start(f32[7,16,2]{2,1,0:T(8,128)S(1)} %copy-done.15), channel_id=1, source_target_pairs={{2,0},{4,2},{6,4},{8,6},{10,8},{12,10},{14,12},{16,14},{18,16},{20... | collective-permute-start | bytes 2696 | tf_op jit(solution)/shard_map/ppermute | solution.py:11
  83.0 15.4 %collective-permute-start.1 = (f32[2]{0:T(128)S(1)}, f32[2]{0:T(128)S(1)}, u32[]{:S(2)}, u32[]{:S(2)}) collective-permute-start(f32[2]{0:T(128)S(1)} %fusion.92), channel_id=1, source_target_pairs={{0,128},{64,192},{128,0},{192,64},{256,384},{320,448},{384,256},{4... | collective-permute-start | bytes 32 | tf_op jit(solution)/shard_map/ppermute | solution.py:25
  88.7 21.0 %collective-permute-start.10 = (f32[2,16,514]{2,1,0:T(8,128)S(1)}, f32[2,16,514]{2,1,0:T(8,128)S(1)}, u32[]{:S(2)}, u32[]{:S(2)}) collective-permute-start(f32[2,16,514]{2,1,0:T(8,128)S(1)} %pad_maximum_fusion.2), channel_id=1, source_target_pairs={{0,1},{1,0},{2,3},{3,2},{4,5},{5,4},{6,7},{7,6},{8,9},{9,8},{10,11... | collective-permute-start | bytes 197384 | tf_op jit(solution)/shard_map/ppermute | solution.py:37
  98.5 9.3 %collective-permute-start.2 = (f32[2]{0:T(128)S(1)}, f32[2]{0:T(128)S(1)}, u32[]{:S(2)}, u32[]{:S(2)}) collective-permute-start(f32[2]{0:T(128)S(1)} %fusion.93), channel_id=1, source_target_pairs={{0,256},{64,320},{128,384},{192,448},{256,0},{320,64},{384,128},{4... | collective-permute-start | bytes 32 | tf_op jit(solution)/shard_map/ppermute | solution.py:25
  107.8 18.9 %collective-permute-start.3 = (bf16[1024,512]{1,0:T(8,128)(2,1)}, bf16[1024,512]{1,0:T(8,128)(2,1)S(1)}, u32[]{:S(2)}, u32[]{:S(2)}) collective-permute-start(bf16[1024,512]{1,0:T(8,128)(2,1)} %fusion.2), channel_id=1, source_target_pairs={{0,2},{2,0},{4,6},{6,4},{8,10},{10,8},{12,14},{14,12},{16,18},{18,... | collective-permute-start | bytes 3145736 | tf_op jit(solution)/shard_map/ppermute | solution.py:86
  110.1 10.6 %copy-start.10 = (f32[1,1,16,1,512]{4,3,2,1,0:T(1,128)S(1)}, f32[1,1,16,1,512]{4,3,2,1,0:T(1,128)}, u32[]{:S(2)}) copy-start(f32[1,1,16,1,512]{4,3,2,1,0:T(1,128)} %get-tuple-element.48) | copy-start | bytes 98308
  110.1 10.6 %copy-start.11 = (f32[1,1,16,1,512]{4,3,2,1,0:T(1,128)S(1)}, f32[1,1,16,1,512]{4,3,2,1,0:T(1,128)}, u32[]{:S(2)}) copy-start(f32[1,1,16,1,512]{4,3,2,1,0:T(1,128)} %get-tuple-element.49) | copy-start | bytes 98308
  110.1 10.6 %copy-start.12 = (f32[1,1,16,1,512]{4,3,2,1,0:T(1,128)S(1)}, f32[1,1,16,1,512]{4,3,2,1,0:T(1,128)}, u32[]{:S(2)}) copy-start(f32[1,1,16,1,512]{4,3,2,1,0:T(1,128)} %get-tuple-element.50) | copy-start | bytes 98308
  110.1 18.5 %copy-start.1 = (bf16[1,5,512,512]{3,2,1,0:T(8,128)(2,1)S(1)}, bf16[1,5,512,512]{3,2,1,0:T(8,128)(2,1)}, u32[]{:S(2)}) copy-start(bf16[1,5,512,512]{3,2,1,0:T(8,128)(2,1)} %param.29) | copy-start | bytes 7864324
  110.2 10.6 %collective-permute-start.11 = (f32[2,16,512]{2,1,0:T(8,128)S(1)}, f32[2,16,512]{2,1,0:T(8,128)S(1)}, u32[]{:S(2)}, u32[]{:S(2)}) collective-permute-start(f32[2,16,512]{2,1,0:T(8,128)S(1)} %pad_maximum_fusion.3), channel_id=1, source_target_pairs={{0,1},{1,0},{2,3},{3,2},{4,5},{5,4},{6,7},{7,6},{8,9},{9,8},{10,11... | collective-permute-start | bytes 196616 | tf_op jit(solution)/shard_map/ppermute | solution.py:37
  113.7 81.2 %collective-permute-start.7 = (bf16[2048,512]{1,0:T(8,128)(2,1)S(1)}, bf16[2048,512]{1,0:T(8,128)(2,1)S(1)}, u32[]{:S(2)}, u32[]{:S(2)}) collective-permute-start(bf16[2048,512]{1,0:T(8,128)(2,1)S(1)} %pad_maximum_fusion), channel_id=1, source_target_pairs={{0,2},{2,0},{4,6},{6,4},{8,10},{10,8},{12,14},{14,12},{16,18},{18,... | collective-permute-start | bytes 6291464 | tf_op jit(solution)/shard_map/ppermute | solution.py:90
  120.9 73.4 %collective-permute-start.19 = (f32[16,512]{1,0:T(8,128)S(1)}, f32[16,512]{1,0:T(8,128)S(1)}, u32[]{:S(2)}, u32[]{:S(2)}) collective-permute-start(f32[16,512]{1,0:T(8,128)S(1)} %get-tuple-element.51), channel_id=1, source_target_pairs={{64,0},{128,64},{192,128},{256,192},{320,256},{384,320},{448,384},... | collective-permute-start | bytes 98312 | tf_op jit(solution)/shard_map/ppermute | solution.py:17
  123.2 75.1 %collective-permute-start.18 = (f32[16,512]{1,0:T(8,128)S(1)}, f32[16,512]{1,0:T(8,128)S(1)}, u32[]{:S(2)}, u32[]{:S(2)}) collective-permute-start(f32[16,512]{1,0:T(8,128)S(1)} %get-tuple-element.52), channel_id=1, source_target_pairs={{0,64},{64,128},{128,192},{192,256},{256,320},{320,384},{384,448},... | collective-permute-start | bytes 98312 | tf_op jit(solution)/shard_map/ppermute | solution.py:17
  126.7 9.8 %collective-permute-start.12 = (f32[2]{0:T(128)S(1)}, f32[2]{0:T(128)S(1)}, u32[]{:S(2)}, u32[]{:S(2)}) collective-permute-start(f32[2]{0:T(128)S(1)} %add.220), channel_id=1, source_target_pairs={{0,2},{2,0},{4,6},{6,4},{8,10},{10,8},{12,14},{14,12},{16,18},{18,... | collective-permute-start | bytes 32 | tf_op jit(solution)/shard_map/ppermute | solution.py:25
  135.2 58.4 %copy-start.16 = (f32[1,16,1,512]{3,2,1,0:T(1,128)S(1)}, f32[1,16,1,512]{3,2,1,0:T(1,128)}, u32[]{:S(2)}) copy-start(f32[1,16,1,512]{3,2,1,0:T(1,128)} %param.15) | copy-start | bytes 98308
  135.2 59.1 %copy-start.9 = (f32[1,16,1,512]{3,2,1,0:T(1,128)S(1)}, f32[1,16,1,512]{3,2,1,0:T(1,128)}, u32[]{:S(2)}) copy-start(f32[1,16,1,512]{3,2,1,0:T(1,128)} %param.26) | copy-start | bytes 98308
  135.2 59.1 %copy-start.14 = (f32[1,16,1,512]{3,2,1,0:T(1,128)S(1)}, f32[1,16,1,512]{3,2,1,0:T(1,128)}, u32[]{:S(2)}) copy-start(f32[1,16,1,512]{3,2,1,0:T(1,128)} %param.20) | copy-start | bytes 98308
  136.6 24.2 %collective-permute-start.13 = (f32[2]{0:T(128)S(1)}, f32[2]{0:T(128)S(1)}, u32[]{:S(2)}, u32[]{:S(2)}) collective-permute-start(f32[2]{0:T(128)S(1)} %add.237), channel_id=1, source_target_pairs={{0,4},{2,6},{4,0},{6,2},{8,12},{10,14},{12,8},{14,10},{16,20},{18,... | collective-permute-start | bytes 32 | tf_op jit(solution)/shard_map/ppermute | solution.py:25
  160.8 9.2 %collective-permute-start.14 = (f32[2]{0:T(128)S(1)}, f32[2]{0:T(128)S(1)}, u32[]{:S(2)}, u32[]{:S(2)}) collective-permute-start(f32[2]{0:T(128)S(1)} %add.238), channel_id=1, source_target_pairs={{0,8},{2,10},{4,12},{6,14},{8,0},{10,2},{12,4},{14,6},{16,24},{18,... | collective-permute-start | bytes 32 | tf_op jit(solution)/shard_map/ppermute | solution.py:25
  170.0 5.4 %collective-permute-start.15 = (f32[2]{0:T(128)S(1)}, f32[2]{0:T(128)S(1)}, u32[]{:S(2)}, u32[]{:S(2)}) collective-permute-start(f32[2]{0:T(128)S(1)} %add.239), channel_id=1, source_target_pairs={{0,16},{2,18},{4,20},{6,22},{8,24},{10,26},{12,28},{14,30},{16,0},... | collective-permute-start | bytes 32 | tf_op jit(solution)/shard_map/ppermute | solution.py:25
  175.4 6.9 %collective-permute-start.16 = (f32[2]{0:T(128)S(1)}, f32[2]{0:T(128)S(1)}, u32[]{:S(2)}, u32[]{:S(2)}) collective-permute-start(f32[2]{0:T(128)S(1)} %add.240), channel_id=1, source_target_pairs={{0,32},{2,34},{4,36},{6,38},{8,40},{10,42},{12,44},{14,46},{16,48}... | collective-permute-start | bytes 32 | tf_op jit(solution)/shard_map/ppermute | solution.py:25
  182.3 9.3 %collective-permute-start.17 = (f32[2]{0:T(128)S(1)}, f32[2]{0:T(128)S(1)}, u32[]{:S(2)}, u32[]{:S(2)}) collective-permute-start(f32[2]{0:T(128)S(1)} %add.241), channel_id=1, source_target_pairs={{0,1},{1,0},{2,3},{3,2},{4,5},{5,4},{6,7},{7,6},{8,9},{9,8},{10,11... | collective-permute-start | bytes 32 | tf_op jit(solution)/shard_map/ppermute | solution.py:25
  197.9 0.8 copy-start.8
  197.9 0.8 copy-start.17
  197.9 0.8 copy-start.18
  197.9 0.8 copy-start.19

commit v9 on v5

--- a/solution.py
+++ b/solution.py
@@ -87,14 +87,15 @@
     ahead = from_offset(flat, "lon", 2)
     behind = from_offset(flat, "lon", -2)
     far = lax.ppermute(flat, "lon", [(s, (s + 3) % bands if s % 2 else (s - 3) % bands) for s in range(bands)])
-    relayed = lax.ppermute(jnp.concatenate([ahead, behind], axis=0), "lon", partner)
+    relayed_ahead = lax.ppermute(ahead, "lon", partner)
+    relayed_behind = lax.ppermute(behind, "lon", partner)
     received = [
         (beside, jnp.where(even, 1, -1)),
         (ahead, 2),
         (behind, -2),
         (far, jnp.where(even, -3, 3)),
-        (relayed[:rows], jnp.where(even, 3, 1)),
-        (relayed[rows:], jnp.where(even, -1, -3)),
+        (relayed_ahead, jnp.where(even, 3, 1)),
+        (relayed_behind, jnp.where(even, -1, -3)),
     ]
 
     def weight_for(offset):
@@ -103,7 +104,7 @@
         picked = tiles[jnp.argmax(match)]
         return jnp.where(jnp.any(match), picked, jnp.zeros_like(picked))
 
-    partials, _ = lax.optimization_barrier((partials, [value for value, _ in received]))
+    partials, _ = lax.optimization_barrier((partials, [value for value, _ in received[:4]]))
     total = jnp.dot(flat, weight_for(0), preferred_element_type=jnp.float32)
     for value, offset in received:
         total = total + jnp.dot(value, weight_for(offset), preferred_element_type=jnp.float32)

time: 192 us -> 194 us (1.010)
  starting transfers between devices: 93.2 us -> 96 us
    ppermute x1 -> x2, starting transfers between devices: 2.05 us -> 4.33 us  [the longest x1 2.41 us: localize(): relayed_behind = lax.ppermute(behind, 'lon', partner)]
  transfers between devices with their start and end apart: 19 -> 20, of which waited for: 8 -> 8; matrix products, arithmetic and copies ran while one was open for 14% -> 14% of each run, Pallas kernels for 0% -> 0%
where the time goes in v9:
time: 194 us; the launch traced here: 193 us
  starting transfers between devices  96 us (49%)
  waiting for transfers between devices  43.1 us (22%)
  between operations  20.1 us (10%)
  other arithmetic  15.4 us (8%)
  matrix products  11.8 us (6%)
  local copies, waits for them, and re-layouts  6.38 us (3%)
    ppermute x9, starting transfers between devices, butterfly_sum(): lax.ppermute(value, axis, [(i, i ^ step) for i in range(count)])  53.5 us
    ppermute x1, waiting for transfers between devices, lat_partner(): return lax.ppermute(value, 'lat', [(0, 1), (1, 0)])  21.9 us
    ppermute x9, waiting for transfers between devices, butterfly_sum(): lax.ppermute(value, axis, [(i, i ^ step) for i in range(count)])  21.2 us
    ppermute x4, starting transfers between devices, from_offset(): lax.ppermute(value, axis, [((i + distance) % count, i) for i in range(cou...  14.4 us
    dot_general x6, matrix products, localize(): jnp.dot(value, weight_for(offset), preferred_element_type=jnp.float32)  9.53 us
    ppermute x1, starting transfers between devices, lat_partner(): return lax.ppermute(value, 'lat', [(0, 1), (1, 0)])  9.02 us
    ppermute x2, starting transfers between devices, shifted(): lax.ppermute(value, axis, [(source, source + steps) for source in range(l...  7.05 us
    ppermute x1, starting transfers between devices, localize(): lax.ppermute(flat, 'lon', [(s, (s + 3) % bands if s % 2 else (s - 3) % ba...  5.78 us
  transfers between devices with their start and end apart: 20, of which 8 were waited for; matrix products, arithmetic and copies ran while one was open for 14% of the time, Pallas kernels for 0%

profile of v9, /device:TPU:38, one launch (start us, length us, event | category | flops | bytes accessed | tf_op | source)
XLA Modules:
  0.0 192.8 jit_solution(10241049345186158215)
XLA Ops:
  0.7 0.9 copy_bitcast_fusion.3
  1.6 2.5 %fusion.2 = bf16[1024,512]{1,0:T(8,128)(2,1)} fusion(bf16[1,64,16,1,512]{4,2,3,1,0:T(8,128)(2,1)} %param.24, f32[16,512]{1,0:T(8,128)S(1)} %get-tuple-element.70), kind=kLoop, calls=%fused_computation.5 | loop fusion | flops 1572864 | bytes 2129920 | tf_op jit(solution)/shard_map/convert_element_type | solution.py:77
  4.1 5.8 %collective-permute-start.6 = (bf16[1024,512]{1,0:T(8,128)(2,1)}, bf16[1024,512]{1,0:T(8,128)(2,1)}, u32[]{:S(2)}, u32[]{:S(2)}) collective-permute-start(bf16[1024,512]{1,0:T(8,128)(2,1)} %fusion.2), channel_id=1, source_target_pairs={{0,58},{2,8},{4,62},{6,12},{8,2},{10,16},{12,6},{14,20},{16,10},{1... | collective-permute-start | bytes 3145736 | tf_op jit(solution)/shard_map/ppermute | solution.py:89
  9.9 4.3 %collective-permute-start.5 = (bf16[1024,512]{1,0:T(8,128)(2,1)}, bf16[1024,512]{1,0:T(8,128)(2,1)S(1)}, u32[]{:S(2)}, u32[]{:S(2)}) collective-permute-start(bf16[1024,512]{1,0:T(8,128)(2,1)} %fusion.2), channel_id=1, source_target_pairs={{60,0},{62,2},{0,4},{2,6},{4,8},{6,10},{8,12},{10,14},{12,16},{14,... | collective-permute-start | bytes 3145736 | tf_op jit(solution)/shard_map/ppermute | solution.py:11
  14.2 0.7 multiply_reduce_fusion.2
  14.8 0.7 multiply_reduce_fusion
  15.5 0.7 multiply_reduce_fusion.1
  16.2 0.7 multiply_reduce_fusion.3
  18.8 0.7 multiply_reduce_fusion.4
  21.5 2.6 %collective-permute-start = (f32[2]{0:T(128)S(1)}, f32[2]{0:T(128)S(1)}, u32[]{:S(2)}, u32[]{:S(2)}) collective-permute-start(f32[2]{0:T(128)S(1)} %pad_maximum_fusion.4), channel_id=1, source_target_pairs={{0,64},{64,0},{128,192},{192,128},{256,320},{320,256},{384,448},{4... | collective-permute-start | bytes 32 | tf_op jit(solution)/shard_map/ppermute | solution.py:25
  24.1 0.7 pad_maximum_fusion.3
  24.8 1.9 collective-permute-start.7
  26.7 6.3 %collective-permute-start.8 = (f32[7,16,2]{2,1,0:T(8,128)}, f32[7,16,2]{2,1,0:T(8,128)}, u32[]{:S(2)}, u32[]{:S(2)}) collective-permute-start(f32[7,16,2]{2,1,0:T(8,128)} %get-tuple-element.55), channel_id=1, source_target_pairs={{2,0},{4,2},{6,4},{8,6},{10,8},{12,10},{14,12},{16,14},{18,16},{20... | collective-permute-start | bytes 2696 | tf_op jit(solution)/shard_map/ppermute | solution.py:11
  33.2 0.7 bitcast_reduce_fusion
  35.1 0.7 bitcast_reduce_fusion.6
  37.3 0.7 bitcast_reduce_fusion.5
  39.2 0.7 bitcast_reduce_fusion.4
  41.2 0.7 bitcast_reduce_fusion.3
  43.1 0.7 bitcast_reduce_fusion.2
  45.1 0.8 compare_reduce_fusion
  45.9 0.7 bitcast_reduce_fusion.1
  47.8 0.6 fusion.90
  48.5 0.3 fusion
  53.2 2.3 %fusion.17 = f32[1024,512]{1,0:T(8,128)S(1)} fusion(bf16[1024,512]{1,0:T(8,128)(2,1)S(1)} %bitcast.137, bf16[1,5,512,512]{3,2,1,0:T(8,128)(2,1)} %param.29, s32[]{:T(128)S(6)} %select_n.174, pred[]{:T(512)} %get-tuple-element.35), kind=kOutput, calls=%fused_computation.19 | convolution fusion | flops 537133056 | bytes 3670532 | tf_op jit(solution)/shard_map/dot_general | solution.py:108
  55.7 2.7 %collective-permute-start.1 = (f32[2]{0:T(128)S(1)}, f32[2]{0:T(128)S(1)}, u32[]{:S(2)}, u32[]{:S(2)}) collective-permute-start(f32[2]{0:T(128)S(1)} %fusion.100), channel_id=1, source_target_pairs={{0,128},{64,192},{128,0},{192,64},{256,384},{320,448},{384,256},{4... | collective-permute-start | bytes 32 | tf_op jit(solution)/shard_map/ppermute | solution.py:25
  58.4 3.6 %collective-permute-done.1 = f32[2]{0:T(128)S(1)} collective-permute-done((f32[2]{0:T(128)S(1)}, f32[2]{0:T(128)S(1)}, u32[]{:S(2)}, u32[]{:S(2)}) %collective-permute-start.1) | collective-permute-done | bytes 40 | tf_op jit(solution)/shard_map/ppermute | solution.py:25
  62.1 2.9 %collective-permute-start.2 = (f32[2]{0:T(128)S(1)}, f32[2]{0:T(128)S(1)}, u32[]{:S(2)}, u32[]{:S(2)}) collective-permute-start(f32[2]{0:T(128)S(1)} %fusion.101), channel_id=1, source_target_pairs={{0,256},{64,320},{128,384},{192,448},{256,0},{320,64},{384,128},{4... | collective-permute-start | bytes 32 | tf_op jit(solution)/shard_map/ppermute | solution.py:25
  65.0 6.4 %collective-permute-done.2 = f32[2]{0:T(128)S(1)} collective-permute-done((f32[2]{0:T(128)S(1)}, f32[2]{0:T(128)S(1)}, u32[]{:S(2)}, u32[]{:S(2)}) %collective-permute-start.2) | collective-permute-done | bytes 40 | tf_op jit(solution)/shard_map/ppermute | solution.py:25
  71.4 1.9 collective-permute-start.4
  73.3 1.9 collective-permute-start.3
  75.3 1.0 pad_maximum_fusion
  76.3 9.0 %collective-permute-start.9 = (f32[7,16,516]{2,1,0:T(8,128)S(1)}, f32[7,16,516]{2,1,0:T(8,128)S(1)}, u32[]{:S(2)}, u32[]{:S(2)}) collective-permute-start(f32[7,16,516]{2,1,0:T(8,128)S(1)} %pad_maximum_fusion), channel_id=1, source_target_pairs={{0,1},{1,0},{2,3},{3,2},{4,5},{5,4},{6,7},{7,6},{8,9},{9,8},{10,11... | collective-permute-start | bytes 693512 | tf_op jit(solution)/shard_map/ppermute | solution.py:37
  85.6 21.9 %collective-permute-done.9 = f32[7,16,516]{2,1,0:T(8,128)S(1)} collective-permute-done((f32[7,16,516]{2,1,0:T(8,128)S(1)}, f32[7,16,516]{2,1,0:T(8,128)S(1)}, u32[]{:S(2)}, u32[]{:S(2)}) %collective-permute-start.9) | collective-permute-done | bytes 231200 | tf_op jit(solution)/shard_map/ppermute | solution.py:37
  107.8 0.2 fusion.48
  108.2 3.0 %collective-permute-start.18 = (f32[16,512]{1,0:T(8,128)S(1)}, f32[16,512]{1,0:T(8,128)S(1)}, u32[]{:S(2)}, u32[]{:S(2)}) collective-permute-start(f32[16,512]{1,0:T(8,128)S(1)} %fusion.66), channel_id=1, source_target_pairs={{0,64},{64,128},{128,192},{192,256},{256,320},{320,384},{384,448},... | collective-permute-start | bytes 98312 | tf_op jit(solution)/shard_map/ppermute | solution.py:17
  111.5 4.1 %collective-permute-start.19 = (f32[16,512]{1,0:T(8,128)S(1)}, f32[16,512]{1,0:T(8,128)S(1)}, u32[]{:S(2)}, u32[]{:S(2)}) collective-permute-start(f32[16,512]{1,0:T(8,128)S(1)} %fusion.59), channel_id=1, source_target_pairs={{64,0},{128,64},{192,128},{256,192},{320,256},{384,320},{448,384},... | collective-permute-start | bytes 98312 | tf_op jit(solution)/shard_map/ppermute | solution.py:17
  115.6 1.9 collective-permute-start.10
  117.5 2.4 %collective-permute-start.17 = (bf16[1024,512]{1,0:T(8,128)(2,1)S(1)}, bf16[1024,512]{1,0:T(8,128)(2,1)S(1)}, u32[]{:S(2)}, u32[]{:S(2)}) collective-permute-start(bf16[1024,512]{1,0:T(8,128)(2,1)S(1)} %collective-permute-done.5), channel_id=1, source_target_pairs={{0,2},{2,0},{4,6},{6,4},{8,10},{10,8},{12,14},{14,12},{16,18},{18,... | collective-permute-start | bytes 3145736 | tf_op jit(solution)/shard_map/ppermute | solution.py:91
  120.0 1.9 collective-permute-start.16
  121.9 1.4 fusion.15
  123.3 1.3 fusion.13
  124.6 1.4 fusion.11
  126.0 2.6 %fusion.9 = f32[1024,512]{1,0:T(8,128)S(1)} fusion(bf16[1024,512]{1,0:T(8,128)(2,1)} %collective-permute-done.6, bf16[1,5,512,512]{3,2,1,0:T(8,128)(2,1)S(1)} %copy-done.1, s32[]{:T(128)S(6)} %select_n.197, pred[]{:T(512)} %get-tuple-element.31), kind=kOutput, calls=%fused_computation.11 | convolution fusion | flops 537133056 | bytes 3670021 | tf_op jit(solution)/shard_map/dot_general | solution.py:110
  128.6 23.6 %collective-permute-start.11 = (f32[2]{0:T(128)S(1)}, f32[2]{0:T(128)S(1)}, u32[]{:S(2)}, u32[]{:S(2)}) collective-permute-start(f32[2]{0:T(128)S(1)} %add.246), channel_id=1, source_target_pairs={{0,4},{2,6},{4,0},{6,2},{8,12},{10,14},{12,8},{14,10},{16,20},{18,... | collective-permute-start | bytes 32 | tf_op jit(solution)/shard_map/ppermute | solution.py:25
  152.2 1.5 collective-permute-done.11
  153.7 6.2 %collective-permute-start.12 = (f32[2]{0:T(128)S(1)}, f32[2]{0:T(128)S(1)}, u32[]{:S(2)}, u32[]{:S(2)}) collective-permute-start(f32[2]{0:T(128)S(1)} %add.247), channel_id=1, source_target_pairs={{0,8},{2,10},{4,12},{6,14},{8,0},{10,2},{12,4},{14,6},{16,24},{18,... | collective-permute-start | bytes 32 | tf_op jit(solution)/shard_map/ppermute | solution.py:25
  160.0 1.5 collective-permute-done.12
  161.5 2.7 %collective-permute-start.13 = (f32[2]{0:T(128)S(1)}, f32[2]{0:T(128)S(1)}, u32[]{:S(2)}, u32[]{:S(2)}) collective-permute-start(f32[2]{0:T(128)S(1)} %add.248), channel_id=1, source_target_pairs={{0,16},{2,18},{4,20},{6,22},{8,24},{10,26},{12,28},{14,30},{16,0},... | collective-permute-start | bytes 32 | tf_op jit(solution)/shard_map/ppermute | solution.py:25
  164.2 2.7 %collective-permute-done.13 = f32[2]{0:T(128)S(1)} collective-permute-done((f32[2]{0:T(128)S(1)}, f32[2]{0:T(128)S(1)}, u32[]{:S(2)}, u32[]{:S(2)}) %collective-permute-start.13) | collective-permute-done | bytes 40 | tf_op jit(solution)/shard_map/ppermute | solution.py:25
  166.9 3.3 %collective-permute-start.14 = (f32[2]{0:T(128)S(1)}, f32[2]{0:T(128)S(1)}, u32[]{:S(2)}, u32[]{:S(2)}) collective-permute-start(f32[2]{0:T(128)S(1)} %add.249), channel_id=1, source_target_pairs={{0,32},{2,34},{4,36},{6,38},{8,40},{10,42},{12,44},{14,46},{16,48}... | collective-permute-start | bytes 32 | tf_op jit(solution)/shard_map/ppermute | solution.py:25
  170.2 3.6 %collective-permute-done.14 = f32[2]{0:T(128)S(1)} collective-permute-done((f32[2]{0:T(128)S(1)}, f32[2]{0:T(128)S(1)}, u32[]{:S(2)}, u32[]{:S(2)}) %collective-permute-start.14) | collective-permute-done | bytes 40 | tf_op jit(solution)/shard_map/ppermute | solution.py:25
  173.8 7.5 %collective-permute-start.15 = (f32[2]{0:T(128)S(1)}, f32[2]{0:T(128)S(1)}, u32[]{:S(2)}, u32[]{:S(2)}) collective-permute-start(f32[2]{0:T(128)S(1)} %add.250), channel_id=1, source_target_pairs={{0,1},{1,0},{2,3},{3,2},{4,5},{5,4},{6,7},{7,6},{8,9},{9,8},{10,11... | collective-permute-start | bytes 32 | tf_op jit(solution)/shard_map/ppermute | solution.py:25
  181.4 1.8 collective-permute-done.15
  183.2 0.6 fusion.92
  185.1 0.6 copy.38
  185.7 0.7 multiply_subtract_fusion
  186.4 1.3 fusion.7
  187.8 1.5 add_add_fusion
  189.4 0.4 fusion.1
  189.8 0.3 copy-done.7
  190.2 0.6 copy.42
  190.9 0.6 copy.40
  191.5 0.6 copy.41
  192.2 0.6 copy.39
  (76 shorter events, 1.5 us)
Async XLA Ops:
  0.6 13.5 %copy-start.2 = (f32[1,16,1,512]{3,2,1,0:T(1,128)S(1)}, f32[1,16,1,512]{3,2,1,0:T(1,128)}, u32[]{:S(2)}) copy-start(f32[1,16,1,512]{3,2,1,0:T(1,128)} %param.21) | copy-start | bytes 98308
  0.6 14.2 %copy-start.4 = (f32[1,16,1,512]{3,2,1,0:T(1,128)S(1)}, f32[1,16,1,512]{3,2,1,0:T(1,128)}, u32[]{:S(2)}) copy-start(f32[1,16,1,512]{3,2,1,0:T(1,128)} %param.23) | copy-start | bytes 98308
  0.7 47.8 %copy-start = (bf16[1,64,16,1,512]{4,2,3,1,0:T(8,128)(2,1)S(1)}, bf16[1,64,16,1,512]{4,2,3,1,0:T(8,128)(2,1)}, u32[]{:S(2)}) copy-start(bf16[1,64,16,1,512]{4,2,3,1,0:T(8,128)(2,1)} %param.24) | copy-start | bytes 3145732
  0.7 14.8 %copy-start.5 = (f32[1,16,1,512]{3,2,1,0:T(1,128)S(1)}, f32[1,16,1,512]{3,2,1,0:T(1,128)}, u32[]{:S(2)}) copy-start(f32[1,16,1,512]{3,2,1,0:T(1,128)} %param.22) | copy-start | bytes 98308
  0.7 15.5 %copy-start.13 = (f32[1,16,1,512]{3,2,1,0:T(1,128)S(1)}, f32[1,16,1,512]{3,2,1,0:T(1,128)}, u32[]{:S(2)}) copy-start(f32[1,16,1,512]{3,2,1,0:T(1,128)} %param.20) | copy-start | bytes 98308
  0.7 18.1 %copy-start.6 = (f32[1,16,1,512]{3,2,1,0:T(1,128)S(1)}, f32[1,16,1,512]{3,2,1,0:T(1,128)}, u32[]{:S(2)}) copy-start(f32[1,16,1,512]{3,2,1,0:T(1,128)} %param.19) | copy-start | bytes 98308
  0.7 18.1 %copy-start.8 = (f32[1,16,1,512]{3,2,1,0:T(1,128)S(1)}, f32[1,16,1,512]{3,2,1,0:T(1,128)}, u32[]{:S(2)}) copy-start(f32[1,16,1,512]{3,2,1,0:T(1,128)} %param.18) | copy-start | bytes 98308
  0.7 23.4 %copy-start.3 = (f32[1,5,16,1,512]{4,3,2,1,0:T(1,128)S(1)}, f32[1,5,16,1,512]{4,3,2,1,0:T(1,128)}, u32[]{:S(2)}) copy-start(f32[1,5,16,1,512]{4,3,2,1,0:T(1,128)} %param.25) | copy-start | bytes 491524
  0.7 32.4 %copy-start.19 = (s32[1,5]{1,0:T(1,128)S(1)}, s32[1,5]{1,0:T(1,128)}, u32[]{:S(2)}) copy-start(s32[1,5]{1,0:T(1,128)} %param.28) | copy-start | bytes 64
  4.1 107.4 %collective-permute-start.6 = (bf16[1024,512]{1,0:T(8,128)(2,1)}, bf16[1024,512]{1,0:T(8,128)(2,1)}, u32[]{:S(2)}, u32[]{:S(2)}) collective-permute-start(bf16[1024,512]{1,0:T(8,128)(2,1)} %fusion.2), channel_id=1, source_target_pairs={{0,58},{2,8},{4,62},{6,12},{8,2},{10,16},{12,6},{14,20},{16,10},{1... | collective-permute-start | bytes 3145736 | tf_op jit(solution)/shard_map/ppermute | solution.py:89
  9.9 105.7 %collective-permute-start.5 = (bf16[1024,512]{1,0:T(8,128)(2,1)}, bf16[1024,512]{1,0:T(8,128)(2,1)S(1)}, u32[]{:S(2)}, u32[]{:S(2)}) collective-permute-start(bf16[1024,512]{1,0:T(8,128)(2,1)} %fusion.2), channel_id=1, source_target_pairs={{60,0},{62,2},{0,4},{2,6},{4,8},{6,10},{8,12},{10,14},{12,16},{14,... | collective-permute-start | bytes 3145736 | tf_op jit(solution)/shard_map/ppermute | solution.py:11
  21.5 34.1 %collective-permute-start = (f32[2]{0:T(128)S(1)}, f32[2]{0:T(128)S(1)}, u32[]{:S(2)}, u32[]{:S(2)}) collective-permute-start(f32[2]{0:T(128)S(1)} %pad_maximum_fusion.4), channel_id=1, source_target_pairs={{0,64},{64,0},{128,192},{192,128},{256,320},{320,256},{384,448},{4... | collective-permute-start | bytes 32 | tf_op jit(solution)/shard_map/ppermute | solution.py:25
  24.8 48.5 %collective-permute-start.7 = (f32[7,16,2]{2,1,0:T(8,128)}, f32[7,16,2]{2,1,0:T(8,128)}, u32[]{:S(2)}, u32[]{:S(2)}) collective-permute-start(f32[7,16,2]{2,1,0:T(8,128)} %get-tuple-element.54), channel_id=1, source_target_pairs={{62,0},{0,2},{2,4},{4,6},{6,8},{8,10},{10,12},{12,14},{14,16},{16,... | collective-permute-start | bytes 2696 | tf_op jit(solution)/shard_map/ppermute | solution.py:11
  26.7 48.5 %collective-permute-start.8 = (f32[7,16,2]{2,1,0:T(8,128)}, f32[7,16,2]{2,1,0:T(8,128)}, u32[]{:S(2)}, u32[]{:S(2)}) collective-permute-start(f32[7,16,2]{2,1,0:T(8,128)} %get-tuple-element.55), channel_id=1, source_target_pairs={{2,0},{4,2},{6,4},{8,6},{10,8},{12,10},{14,12},{16,14},{18,16},{20... | collective-permute-start | bytes 2696 | tf_op jit(solution)/shard_map/ppermute | solution.py:11
  55.5 52.5 %copy-start.11 = (f32[1,1,16,1,512]{4,3,2,1,0:T(1,128)S(1)}, f32[1,1,16,1,512]{4,3,2,1,0:T(1,128)}, u32[]{:S(2)}) copy-start(f32[1,1,16,1,512]{4,3,2,1,0:T(1,128)} %get-tuple-element.57) | copy-start | bytes 98308
  55.5 52.5 %copy-start.12 = (f32[1,1,16,1,512]{4,3,2,1,0:T(1,128)S(1)}, f32[1,1,16,1,512]{4,3,2,1,0:T(1,128)}, u32[]{:S(2)}) copy-start(f32[1,1,16,1,512]{4,3,2,1,0:T(1,128)} %get-tuple-element.58) | copy-start | bytes 98308
  55.7 6.3 %collective-permute-start.1 = (f32[2]{0:T(128)S(1)}, f32[2]{0:T(128)S(1)}, u32[]{:S(2)}, u32[]{:S(2)}) collective-permute-start(f32[2]{0:T(128)S(1)} %fusion.100), channel_id=1, source_target_pairs={{0,128},{64,192},{128,0},{192,64},{256,384},{320,448},{384,256},{4... | collective-permute-start | bytes 32 | tf_op jit(solution)/shard_map/ppermute | solution.py:25
  62.1 9.3 %collective-permute-start.2 = (f32[2]{0:T(128)S(1)}, f32[2]{0:T(128)S(1)}, u32[]{:S(2)}, u32[]{:S(2)}) collective-permute-start(f32[2]{0:T(128)S(1)} %fusion.101), channel_id=1, source_target_pairs={{0,256},{64,320},{128,384},{192,448},{256,0},{320,64},{384,128},{4... | collective-permute-start | bytes 32 | tf_op jit(solution)/shard_map/ppermute | solution.py:25
  71.4 44.2 %collective-permute-start.4 = (bf16[1024,512]{1,0:T(8,128)(2,1)}, bf16[1024,512]{1,0:T(8,128)(2,1)S(1)}, u32[]{:S(2)}, u32[]{:S(2)}) collective-permute-start(bf16[1024,512]{1,0:T(8,128)(2,1)} %fusion.2), channel_id=1, source_target_pairs={{4,0},{6,2},{8,4},{10,6},{12,8},{14,10},{16,12},{18,14},{20,16},{2... | collective-permute-start | bytes 3145736 | tf_op jit(solution)/shard_map/ppermute | solution.py:11
  73.3 42.3 %collective-permute-start.3 = (bf16[1024,512]{1,0:T(8,128)(2,1)}, bf16[1024,512]{1,0:T(8,128)(2,1)S(1)}, u32[]{:S(2)}, u32[]{:S(2)}) collective-permute-start(bf16[1024,512]{1,0:T(8,128)(2,1)} %fusion.2), channel_id=1, source_target_pairs={{0,2},{2,0},{4,6},{6,4},{8,10},{10,8},{12,14},{14,12},{16,18},{18,... | collective-permute-start | bytes 3145736 | tf_op jit(solution)/shard_map/ppermute | solution.py:86
  76.3 45.6 %copy-start.1 = (bf16[1,5,512,512]{3,2,1,0:T(8,128)(2,1)S(1)}, bf16[1,5,512,512]{3,2,1,0:T(8,128)(2,1)}, u32[]{:S(2)}) copy-start(bf16[1,5,512,512]{3,2,1,0:T(8,128)(2,1)} %param.29) | copy-start | bytes 7864324
  76.3 31.2 %collective-permute-start.9 = (f32[7,16,516]{2,1,0:T(8,128)S(1)}, f32[7,16,516]{2,1,0:T(8,128)S(1)}, u32[]{:S(2)}, u32[]{:S(2)}) collective-permute-start(f32[7,16,516]{2,1,0:T(8,128)S(1)} %pad_maximum_fusion), channel_id=1, source_target_pairs={{0,1},{1,0},{2,3},{3,2},{4,5},{5,4},{6,7},{7,6},{8,9},{9,8},{10,11... | collective-permute-start | bytes 693512 | tf_op jit(solution)/shard_map/ppermute | solution.py:37
  108.2 81.6 %collective-permute-start.18 = (f32[16,512]{1,0:T(8,128)S(1)}, f32[16,512]{1,0:T(8,128)S(1)}, u32[]{:S(2)}, u32[]{:S(2)}) collective-permute-start(f32[16,512]{1,0:T(8,128)S(1)} %fusion.66), channel_id=1, source_target_pairs={{0,64},{64,128},{128,192},{192,256},{256,320},{320,384},{384,448},... | collective-permute-start | bytes 98312 | tf_op jit(solution)/shard_map/ppermute | solution.py:17
  111.5 74.2 %collective-permute-start.19 = (f32[16,512]{1,0:T(8,128)S(1)}, f32[16,512]{1,0:T(8,128)S(1)}, u32[]{:S(2)}, u32[]{:S(2)}) collective-permute-start(f32[16,512]{1,0:T(8,128)S(1)} %fusion.59), channel_id=1, source_target_pairs={{64,0},{128,64},{192,128},{256,192},{320,256},{384,320},{448,384},... | collective-permute-start | bytes 98312 | tf_op jit(solution)/shard_map/ppermute | solution.py:17
  115.6 13.0 %collective-permute-start.10 = (f32[2]{0:T(128)S(1)}, f32[2]{0:T(128)S(1)}, u32[]{:S(2)}, u32[]{:S(2)}) collective-permute-start(f32[2]{0:T(128)S(1)} %add.245), channel_id=1, source_target_pairs={{0,2},{2,0},{4,6},{6,4},{8,10},{10,8},{12,14},{14,12},{16,18},{18,... | collective-permute-start | bytes 32 | tf_op jit(solution)/shard_map/ppermute | solution.py:25
  117.5 70.2 %collective-permute-start.17 = (bf16[1024,512]{1,0:T(8,128)(2,1)S(1)}, bf16[1024,512]{1,0:T(8,128)(2,1)S(1)}, u32[]{:S(2)}, u32[]{:S(2)}) collective-permute-start(bf16[1024,512]{1,0:T(8,128)(2,1)S(1)} %collective-permute-done.5), channel_id=1, source_target_pairs={{0,2},{2,0},{4,6},{6,4},{8,10},{10,8},{12,14},{14,12},{16,18},{18,... | collective-permute-start | bytes 3145736 | tf_op jit(solution)/shard_map/ppermute | solution.py:91
  120.0 66.5 %collective-permute-start.16 = (bf16[1024,512]{1,0:T(8,128)(2,1)S(1)}, bf16[1024,512]{1,0:T(8,128)(2,1)S(1)}, u32[]{:S(2)}, u32[]{:S(2)}) collective-permute-start(bf16[1024,512]{1,0:T(8,128)(2,1)S(1)} %collective-permute-done.4), channel_id=1, source_target_pairs={{0,2},{2,0},{4,6},{6,4},{8,10},{10,8},{12,14},{14,12},{16,18},{18,... | collective-permute-start | bytes 3145736 | tf_op jit(solution)/shard_map/ppermute | solution.py:90
  126.0 59.1 %copy-start.15 = (f32[1,16,1,512]{3,2,1,0:T(1,128)S(1)}, f32[1,16,1,512]{3,2,1,0:T(1,128)}, u32[]{:S(2)}) copy-start(f32[1,16,1,512]{3,2,1,0:T(1,128)} %param.15) | copy-start | bytes 98308
  126.0 59.8 %copy-start.10 = (f32[1,16,1,512]{3,2,1,0:T(1,128)S(1)}, f32[1,16,1,512]{3,2,1,0:T(1,128)}, u32[]{:S(2)}) copy-start(f32[1,16,1,512]{3,2,1,0:T(1,128)} %param.26) | copy-start | bytes 98308
  126.0 59.8 %copy-start.14 = (f32[1,16,1,512]{3,2,1,0:T(1,128)S(1)}, f32[1,16,1,512]{3,2,1,0:T(1,128)}, u32[]{:S(2)}) copy-start(f32[1,16,1,512]{3,2,1,0:T(1,128)} %param.20) | copy-start | bytes 98308
  128.6 25.1 %collective-permute-start.11 = (f32[2]{0:T(128)S(1)}, f32[2]{0:T(128)S(1)}, u32[]{:S(2)}, u32[]{:S(2)}) collective-permute-start(f32[2]{0:T(128)S(1)} %add.246), channel_id=1, source_target_pairs={{0,4},{2,6},{4,0},{6,2},{8,12},{10,14},{12,8},{14,10},{16,20},{18,... | collective-permute-start | bytes 32 | tf_op jit(solution)/shard_map/ppermute | solution.py:25
  153.7 7.7 %collective-permute-start.12 = (f32[2]{0:T(128)S(1)}, f32[2]{0:T(128)S(1)}, u32[]{:S(2)}, u32[]{:S(2)}) collective-permute-start(f32[2]{0:T(128)S(1)} %add.247), channel_id=1, source_target_pairs={{0,8},{2,10},{4,12},{6,14},{8,0},{10,2},{12,4},{14,6},{16,24},{18,... | collective-permute-start | bytes 32 | tf_op jit(solution)/shard_map/ppermute | solution.py:25
  161.5 5.4 %collective-permute-start.13 = (f32[2]{0:T(128)S(1)}, f32[2]{0:T(128)S(1)}, u32[]{:S(2)}, u32[]{:S(2)}) collective-permute-start(f32[2]{0:T(128)S(1)} %add.248), channel_id=1, source_target_pairs={{0,16},{2,18},{4,20},{6,22},{8,24},{10,26},{12,28},{14,30},{16,0},... | collective-permute-start | bytes 32 | tf_op jit(solution)/shard_map/ppermute | solution.py:25
  166.9 6.9 %collective-permute-start.14 = (f32[2]{0:T(128)S(1)}, f32[2]{0:T(128)S(1)}, u32[]{:S(2)}, u32[]{:S(2)}) collective-permute-start(f32[2]{0:T(128)S(1)} %add.249), channel_id=1, source_target_pairs={{0,32},{2,34},{4,36},{6,38},{8,40},{10,42},{12,44},{14,46},{16,48}... | collective-permute-start | bytes 32 | tf_op jit(solution)/shard_map/ppermute | solution.py:25
  173.8 9.3 %collective-permute-start.15 = (f32[2]{0:T(128)S(1)}, f32[2]{0:T(128)S(1)}, u32[]{:S(2)}, u32[]{:S(2)}) collective-permute-start(f32[2]{0:T(128)S(1)} %add.250), channel_id=1, source_target_pairs={{0,1},{1,0},{2,3},{3,2},{4,5},{5,4},{6,7},{7,6},{8,9},{9,8},{10,11... | collective-permute-start | bytes 32 | tf_op jit(solution)/shard_map/ppermute | solution.py:25
  189.3 0.8 copy-start.7
  189.4 0.8 copy-start.9
  189.4 0.8 copy-start.16
  189.4 0.8 copy-start.17
  189.4 0.8 copy-start.18

commit v10 on v5

--- a/solution.py
+++ b/solution.py
@@ -57,11 +57,11 @@
 
 def propagate_both(own, other, first_row):
     u_a, w_a, c_a = own[0], own[1], own[2:]
-    u_b, w_b, c_b = other[0], other[1], other[2:]
-    cn_a = jnp.where(first_row, c_a[3], c_a[4])
-    cn_b = jnp.where(first_row, c_b[4], c_b[3])
-    ca_a = jnp.where(first_row, c_b[4], c_b[3])
-    ca_b = jnp.where(first_row, c_a[3], c_a[4])
+    u_b, w_b, c_b, k_b = other[0], other[1], other[2:5], other[5]
+    cn_a = coupling(own[2:], first_row)
+    cn_b = k_b
+    ca_a = k_b
+    ca_b = cn_a
     s_a = forward_pair(u_a, u_b, c_a, cn_a)
     s_b = forward_pair(u_b, u_a, c_b, cn_b)
     moved = forward_pair(s_a, s_b, c_a[:, :, 1:-1], cn_a[:, 1:-1])
@@ -69,6 +69,10 @@
     t_b = adjoint_pair(w_b, w_a, c_b, ca_b)
     backed = adjoint_pair(t_a, t_b, c_a[:, :, 1:-1], ca_a[:, 1:-1])
     return moved, backed
+
+
+def coupling(coefs, first_row):
+    return jnp.where(first_row, coefs[3], coefs[4])
 
 
 def localize(members, search, loc_cols, loc_vals, partials):
@@ -143,11 +147,11 @@
         [search_incr[0, :, 0][None], search_dual[0, :, 0][None], tangent_coefs[0, :, :, 0]], axis=0
     )
     own = lon_extended(packed, 2)
-    other = lat_partner(own)
     first_row = lax.axis_index("lat") == 0
+    other = lat_partner(jnp.concatenate([own[:5], coupling(own[2:], first_row)[None]]))
     moved, backed = propagate_both(own, other, first_row)
-    earlier = shifted(moved, "win", 1)[None, :, None]
-    following = shifted(backed, "win", -1)[None, :, None]
+    earlier = shifted(moved.astype(jnp.bfloat16), "win", 1).astype(jnp.float32)[None, :, None]
+    following = shifted(backed.astype(jnp.bfloat16), "win", -1).astype(jnp.float32)[None, :, None]
 
     covar, partials = localize(
         ensemble[0, :, :, 0],

time: 192 us -> 190 us (0.990)
  the two profiles are of different devices: /device:TPU:38 before, /device:TPU:30 now
where the time goes in v10:
time: 190 us; the launch traced here: 189 us
  starting transfers between devices  95 us (50%)
  waiting for transfers between devices  40 us (21%)
  between operations  20.1 us (11%)
  other arithmetic  15.6 us (8%)
  matrix products  11.9 us (6%)
  local copies, waits for them, and re-layouts  6.39 us (3%)
    ppermute x9, starting transfers between devices, butterfly_sum(): lax.ppermute(value, axis, [(i, i ^ step) for i in range(count)])  55 us
    ppermute x1, waiting for transfers between devices, lat_partner(): return lax.ppermute(value, 'lat', [(0, 1), (1, 0)])  21.4 us
    ppermute x9, waiting for transfers between devices, butterfly_sum(): lax.ppermute(value, axis, [(i, i ^ step) for i in range(count)])  18.6 us
    ppermute x4, starting transfers between devices, from_offset(): lax.ppermute(value, axis, [((i + distance) % count, i) for i in range(cou...  14.4 us
    dot_general x6, matrix products, localize(): jnp.dot(value, weight_for(offset), preferred_element_type=jnp.float32)  9.54 us
    ppermute x1, starting transfers between devices, lat_partner(): return lax.ppermute(value, 'lat', [(0, 1), (1, 0)])  8.76 us
    ppermute x2, starting transfers between devices, shifted(): lax.ppermute(value, axis, [(source, source + steps) for source in range(l...  7.05 us
    ppermute x1, starting transfers between devices, localize(): lax.ppermute(flat, 'lon', [(s, (s + 3) % bands if s % 2 else (s - 3) % ba...  5.78 us
  transfers between devices with their start and end apart: 19, of which 8 were waited for; matrix products, arithmetic and copies ran while one was open for 15% of the time, Pallas kernels for 0%

profile of v10, /device:TPU:30, one launch (start us, length us, event | category | flops | bytes accessed | tf_op | source)
XLA Modules:
  0.0 188.9 jit_solution(7846615853397885505)
XLA Ops:
  0.7 0.9 copy_bitcast_fusion.3
  1.6 2.5 %fusion.2 = bf16[1024,512]{1,0:T(8,128)(2,1)} fusion(bf16[1,64,16,1,512]{4,2,3,1,0:T(8,128)(2,1)} %param.24, f32[16,512]{1,0:T(8,128)S(1)} %get-tuple-element.70), kind=kLoop, calls=%fused_computation.6 | loop fusion | flops 1572864 | bytes 2129920 | tf_op jit(solution)/shard_map/convert_element_type | solution.py:81
  4.1 5.8 %collective-permute-start.6 = (bf16[1024,512]{1,0:T(8,128)(2,1)}, bf16[1024,512]{1,0:T(8,128)(2,1)}, u32[]{:S(2)}, u32[]{:S(2)}) collective-permute-start(bf16[1024,512]{1,0:T(8,128)(2,1)} %fusion.2), channel_id=1, source_target_pairs={{0,58},{2,8},{4,62},{6,12},{8,2},{10,16},{12,6},{14,20},{16,10},{1... | collective-permute-start | bytes 3145736 | tf_op jit(solution)/shard_map/ppermute | solution.py:93
  9.9 4.3 %collective-permute-start.5 = (bf16[1024,512]{1,0:T(8,128)(2,1)}, bf16[1024,512]{1,0:T(8,128)(2,1)S(1)}, u32[]{:S(2)}, u32[]{:S(2)}) collective-permute-start(bf16[1024,512]{1,0:T(8,128)(2,1)} %fusion.2), channel_id=1, source_target_pairs={{60,0},{62,2},{0,4},{2,6},{4,8},{6,10},{8,12},{10,14},{12,16},{14,... | collective-permute-start | bytes 3145736 | tf_op jit(solution)/shard_map/ppermute | solution.py:11
  14.2 0.7 multiply_reduce_fusion.2
  14.8 0.7 multiply_reduce_fusion
  15.5 0.7 multiply_reduce_fusion.1
  16.2 0.7 multiply_reduce_fusion.3
  18.8 0.7 multiply_reduce_fusion.4
  21.5 2.3 %collective-permute-start = (f32[2]{0:T(128)S(1)}, f32[2]{0:T(128)S(1)}, u32[]{:S(2)}, u32[]{:S(2)}) collective-permute-start(f32[2]{0:T(128)S(1)} %pad_maximum_fusion.6), channel_id=1, source_target_pairs={{0,64},{64,0},{128,192},{192,128},{256,320},{320,256},{384,448},{4... | collective-permute-start | bytes 32 | tf_op jit(solution)/shard_map/ppermute | solution.py:25
  23.9 0.7 pad_maximum_fusion.5
  24.6 1.9 %collective-permute-start.8 = (f32[7,16,2]{2,1,0:T(8,128)}, f32[7,16,2]{2,1,0:T(8,128)}, u32[]{:S(2)}, u32[]{:S(2)}) collective-permute-start(f32[7,16,2]{2,1,0:T(8,128)} %get-tuple-element.54), channel_id=1, source_target_pairs={{62,0},{0,2},{2,4},{4,6},{6,8},{8,10},{10,12},{12,14},{14,16},{16,... | collective-permute-start | bytes 2696 | tf_op jit(solution)/shard_map/ppermute | solution.py:11
  26.5 6.3 %collective-permute-start.9 = (f32[7,16,2]{2,1,0:T(8,128)}, f32[7,16,2]{2,1,0:T(8,128)}, u32[]{:S(2)}, u32[]{:S(2)}) collective-permute-start(f32[7,16,2]{2,1,0:T(8,128)} %get-tuple-element.55), channel_id=1, source_target_pairs={{2,0},{4,2},{6,4},{8,6},{10,8},{12,10},{14,12},{16,14},{18,16},{20... | collective-permute-start | bytes 2696 | tf_op jit(solution)/shard_map/ppermute | solution.py:11
  32.9 0.7 bitcast_reduce_fusion
  34.9 0.7 bitcast_reduce_fusion.6
  37.0 0.7 bitcast_reduce_fusion.5
  39.0 0.7 bitcast_reduce_fusion.4
  41.0 0.7 bitcast_reduce_fusion.3
  42.9 0.7 bitcast_reduce_fusion.2
  44.9 0.8 compare_reduce_fusion
  45.7 0.7 bitcast_reduce_fusion.1
  47.6 0.6 fusion.95
  48.3 0.3 fusion
  53.0 2.3 %fusion.17 = f32[1024,512]{1,0:T(8,128)S(1)} fusion(bf16[1024,512]{1,0:T(8,128)(2,1)S(1)} %bitcast.131, bf16[1,5,512,512]{3,2,1,0:T(8,128)(2,1)} %param.29, s32[]{:T(128)S(6)} %select_n.168, pred[]{:T(512)} %get-tuple-element.35), kind=kOutput, calls=%fused_computation.20 | convolution fusion | flops 537133056 | bytes 3670532 | tf_op jit(solution)/shard_map/dot_general | solution.py:111
  55.4 2.2 %collective-permute-start.1 = (f32[2]{0:T(128)S(1)}, f32[2]{0:T(128)S(1)}, u32[]{:S(2)}, u32[]{:S(2)}) collective-permute-start(f32[2]{0:T(128)S(1)} %fusion.103), channel_id=1, source_target_pairs={{0,128},{64,192},{128,0},{192,64},{256,384},{320,448},{384,256},{4... | collective-permute-start | bytes 32 | tf_op jit(solution)/shard_map/ppermute | solution.py:25
  57.7 4.1 %collective-permute-done.1 = f32[2]{0:T(128)S(1)} collective-permute-done((f32[2]{0:T(128)S(1)}, f32[2]{0:T(128)S(1)}, u32[]{:S(2)}, u32[]{:S(2)}) %collective-permute-start.1) | collective-permute-done | bytes 40 | tf_op jit(solution)/shard_map/ppermute | solution.py:25
  61.8 5.9 %collective-permute-start.2 = (f32[2]{0:T(128)S(1)}, f32[2]{0:T(128)S(1)}, u32[]{:S(2)}, u32[]{:S(2)}) collective-permute-start(f32[2]{0:T(128)S(1)} %fusion.104), channel_id=1, source_target_pairs={{0,256},{64,320},{128,384},{192,448},{256,0},{320,64},{384,128},{4... | collective-permute-start | bytes 32 | tf_op jit(solution)/shard_map/ppermute | solution.py:25
  67.8 3.4 %collective-permute-done.2 = f32[2]{0:T(128)S(1)} collective-permute-done((f32[2]{0:T(128)S(1)}, f32[2]{0:T(128)S(1)}, u32[]{:S(2)}, u32[]{:S(2)}) %collective-permute-start.2) | collective-permute-done | bytes 40 | tf_op jit(solution)/shard_map/ppermute | solution.py:25
  71.2 1.9 %collective-permute-start.4 = (bf16[1024,512]{1,0:T(8,128)(2,1)}, bf16[1024,512]{1,0:T(8,128)(2,1)S(1)}, u32[]{:S(2)}, u32[]{:S(2)}) collective-permute-start(bf16[1024,512]{1,0:T(8,128)(2,1)} %fusion.2), channel_id=1, source_target_pairs={{4,0},{6,2},{8,4},{10,6},{12,8},{14,10},{16,12},{18,14},{20,16},{2... | collective-permute-start | bytes 3145736 | tf_op jit(solution)/shard_map/ppermute | solution.py:11
  73.1 1.9 %collective-permute-start.3 = (bf16[1024,512]{1,0:T(8,128)(2,1)}, bf16[1024,512]{1,0:T(8,128)(2,1)S(1)}, u32[]{:S(2)}, u32[]{:S(2)}) collective-permute-start(bf16[1024,512]{1,0:T(8,128)(2,1)} %fusion.2), channel_id=1, source_target_pairs={{0,2},{2,0},{4,6},{6,4},{8,10},{10,8},{12,14},{14,12},{16,18},{18,... | collective-permute-start | bytes 3145736 | tf_op jit(solution)/shard_map/ppermute | solution.py:90
  75.0 1.0 pad_maximum_fusion.1
  76.3 8.8 %collective-permute-start.10 = (f32[6,16,516]{2,1,0:T(8,128)S(1)}, f32[6,16,516]{2,1,0:T(8,128)S(1)}, u32[]{:S(2)}, u32[]{:S(2)}) collective-permute-start(f32[6,16,516]{2,1,0:T(8,128)S(1)} %pad_maximum_fusion.2), channel_id=1, source_target_pairs={{0,1},{1,0},{2,3},{3,2},{4,5},{5,4},{6,7},{7,6},{8,9},{9,8},{10,11... | collective-permute-start | bytes 594440 | tf_op jit(solution)/shard_map/ppermute | solution.py:37
  85.1 21.4 %collective-permute-done.10 = f32[6,16,516]{2,1,0:T(8,128)S(1)} collective-permute-done((f32[6,16,516]{2,1,0:T(8,128)S(1)}, f32[6,16,516]{2,1,0:T(8,128)S(1)}, u32[]{:S(2)}, u32[]{:S(2)}) %collective-permute-start.10) | collective-permute-done | bytes 198176 | tf_op jit(solution)/shard_map/ppermute | solution.py:37
  106.8 0.2 fusion.48
  107.2 2.1 %collective-permute-start.7 = (bf16[2048,512]{1,0:T(8,128)(2,1)S(1)}, bf16[2048,512]{1,0:T(8,128)(2,1)S(1)}, u32[]{:S(2)}, u32[]{:S(2)}) collective-permute-start(bf16[2048,512]{1,0:T(8,128)(2,1)S(1)} %pad_maximum_fusion), channel_id=1, source_target_pairs={{0,2},{2,0},{4,6},{6,4},{8,10},{10,8},{12,14},{14,12},{16,18},{18,... | collective-permute-start | bytes 6291464 | tf_op jit(solution)/shard_map/ppermute | solution.py:94
  109.3 0.2 fusion.58
  109.6 3.1 %collective-permute-start.18 = (bf16[16,512]{1,0:T(8,128)(2,1)S(1)}, bf16[16,512]{1,0:T(8,128)(2,1)S(1)}, u32[]{:S(2)}, u32[]{:S(2)}) collective-permute-start(bf16[16,512]{1,0:T(8,128)(2,1)S(1)} %fusion.58), channel_id=1, source_target_pairs={{64,0},{128,64},{192,128},{256,192},{320,256},{384,320},{448,384},... | collective-permute-start | bytes 49160 | tf_op jit(solution)/shard_map/ppermute | solution.py:17
  112.9 4.0 %collective-permute-start.17 = (bf16[16,512]{1,0:T(8,128)(2,1)S(1)}, bf16[16,512]{1,0:T(8,128)(2,1)S(1)}, u32[]{:S(2)}, u32[]{:S(2)}) collective-permute-start(bf16[16,512]{1,0:T(8,128)(2,1)S(1)} %fusion.66), channel_id=1, source_target_pairs={{0,64},{64,128},{128,192},{192,256},{256,320},{320,384},{384,448},... | collective-permute-start | bytes 49160 | tf_op jit(solution)/shard_map/ppermute | solution.py:17
  116.9 1.9 %collective-permute-start.11 = (f32[2]{0:T(128)S(1)}, f32[2]{0:T(128)S(1)}, u32[]{:S(2)}, u32[]{:S(2)}) collective-permute-start(f32[2]{0:T(128)S(1)} %add.245), channel_id=1, source_target_pairs={{0,2},{2,0},{4,6},{6,4},{8,10},{10,8},{12,14},{14,12},{16,18},{18,... | collective-permute-start | bytes 32 | tf_op jit(solution)/shard_map/ppermute | solution.py:25
  118.9 1.4 fusion.15
  120.2 1.3 fusion.13
  121.5 2.6 %fusion.9 = f32[1024,512]{1,0:T(8,128)S(1)} fusion(bf16[1024,512]{1,0:T(8,128)(2,1)} %collective-permute-done.6, bf16[1,5,512,512]{3,2,1,0:T(8,128)(2,1)S(1)} %copy-done.1, s32[]{:T(128)S(6)} %select_n.191, pred[]{:T(512)} %get-tuple-element.31), kind=kOutput, calls=%fused_computation.12 | convolution fusion | flops 537133056 | bytes 3670021 | tf_op jit(solution)/shard_map/dot_general | solution.py:113
  124.2 1.3 fusion.11
  125.5 22.8 %collective-permute-start.12 = (f32[2]{0:T(128)S(1)}, f32[2]{0:T(128)S(1)}, u32[]{:S(2)}, u32[]{:S(2)}) collective-permute-start(f32[2]{0:T(128)S(1)} %add.246), channel_id=1, source_target_pairs={{0,4},{2,6},{4,0},{6,2},{8,12},{10,14},{12,8},{14,10},{16,20},{18,... | collective-permute-start | bytes 32 | tf_op jit(solution)/shard_map/ppermute | solution.py:25
  148.3 1.5 collective-permute-done.12
  149.8 6.2 %collective-permute-start.13 = (f32[2]{0:T(128)S(1)}, f32[2]{0:T(128)S(1)}, u32[]{:S(2)}, u32[]{:S(2)}) collective-permute-start(f32[2]{0:T(128)S(1)} %add.247), channel_id=1, source_target_pairs={{0,8},{2,10},{4,12},{6,14},{8,0},{10,2},{12,4},{14,6},{16,24},{18,... | collective-permute-start | bytes 32 | tf_op jit(solution)/shard_map/ppermute | solution.py:25
  156.0 1.5 collective-permute-done.13
  157.5 2.7 %collective-permute-start.14 = (f32[2]{0:T(128)S(1)}, f32[2]{0:T(128)S(1)}, u32[]{:S(2)}, u32[]{:S(2)}) collective-permute-start(f32[2]{0:T(128)S(1)} %add.248), channel_id=1, source_target_pairs={{0,16},{2,18},{4,20},{6,22},{8,24},{10,26},{12,28},{14,30},{16,0},... | collective-permute-start | bytes 32 | tf_op jit(solution)/shard_map/ppermute | solution.py:25
  160.3 2.7 %collective-permute-done.14 = f32[2]{0:T(128)S(1)} collective-permute-done((f32[2]{0:T(128)S(1)}, f32[2]{0:T(128)S(1)}, u32[]{:S(2)}, u32[]{:S(2)}) %collective-permute-start.14) | collective-permute-done | bytes 40 | tf_op jit(solution)/shard_map/ppermute | solution.py:25
  163.0 3.3 %collective-permute-start.15 = (f32[2]{0:T(128)S(1)}, f32[2]{0:T(128)S(1)}, u32[]{:S(2)}, u32[]{:S(2)}) collective-permute-start(f32[2]{0:T(128)S(1)} %add.249), channel_id=1, source_target_pairs={{0,32},{2,34},{4,36},{6,38},{8,40},{10,42},{12,44},{14,46},{16,48}... | collective-permute-start | bytes 32 | tf_op jit(solution)/shard_map/ppermute | solution.py:25
  166.3 3.6 %collective-permute-done.15 = f32[2]{0:T(128)S(1)} collective-permute-done((f32[2]{0:T(128)S(1)}, f32[2]{0:T(128)S(1)}, u32[]{:S(2)}, u32[]{:S(2)}) %collective-permute-start.15) | collective-permute-done | bytes 40 | tf_op jit(solution)/shard_map/ppermute | solution.py:25
  169.9 7.5 %collective-permute-start.16 = (f32[2]{0:T(128)S(1)}, f32[2]{0:T(128)S(1)}, u32[]{:S(2)}, u32[]{:S(2)}) collective-permute-start(f32[2]{0:T(128)S(1)} %add.250), channel_id=1, source_target_pairs={{0,1},{1,0},{2,3},{3,2},{4,5},{5,4},{6,7},{7,6},{8,9},{9,8},{10,11... | collective-permute-start | bytes 32 | tf_op jit(solution)/shard_map/ppermute | solution.py:25
  177.5 1.8 collective-permute-done.16
  179.2 0.6 fusion.97
  181.2 0.6 copy.38
  181.8 0.7 fusion.78
  182.5 1.4 fusion.7
  183.9 1.5 add_add_fusion
  185.5 0.4 fusion.1
  185.9 0.3 copy-done.11
  186.3 0.6 copy.42
  187.0 0.6 copy.40
  187.6 0.6 copy.41
  188.3 0.6 copy.39
  (78 shorter events, 1.5 us)
Async XLA Ops:
  0.6 13.5 %copy-start.2 = (f32[1,16,1,512]{3,2,1,0:T(1,128)S(1)}, f32[1,16,1,512]{3,2,1,0:T(1,128)}, u32[]{:S(2)}) copy-start(f32[1,16,1,512]{3,2,1,0:T(1,128)} %param.21) | copy-start | bytes 98308
  0.6 14.2 %copy-start.4 = (f32[1,16,1,512]{3,2,1,0:T(1,128)S(1)}, f32[1,16,1,512]{3,2,1,0:T(1,128)}, u32[]{:S(2)}) copy-start(f32[1,16,1,512]{3,2,1,0:T(1,128)} %param.23) | copy-start | bytes 98308
  0.7 47.6 %copy-start = (bf16[1,64,16,1,512]{4,2,3,1,0:T(8,128)(2,1)S(1)}, bf16[1,64,16,1,512]{4,2,3,1,0:T(8,128)(2,1)}, u32[]{:S(2)}) copy-start(bf16[1,64,16,1,512]{4,2,3,1,0:T(8,128)(2,1)} %param.24) | copy-start | bytes 3145732
  0.7 14.8 %copy-start.5 = (f32[1,16,1,512]{3,2,1,0:T(1,128)S(1)}, f32[1,16,1,512]{3,2,1,0:T(1,128)}, u32[]{:S(2)}) copy-start(f32[1,16,1,512]{3,2,1,0:T(1,128)} %param.22) | copy-start | bytes 98308
  0.7 15.5 %copy-start.8 = (f32[1,16,1,512]{3,2,1,0:T(1,128)S(1)}, f32[1,16,1,512]{3,2,1,0:T(1,128)}, u32[]{:S(2)}) copy-start(f32[1,16,1,512]{3,2,1,0:T(1,128)} %param.20) | copy-start | bytes 98308
  0.7 18.1 %copy-start.10 = (f32[1,16,1,512]{3,2,1,0:T(1,128)S(1)}, f32[1,16,1,512]{3,2,1,0:T(1,128)}, u32[]{:S(2)}) copy-start(f32[1,16,1,512]{3,2,1,0:T(1,128)} %param.19) | copy-start | bytes 98308
  0.7 18.1 %copy-start.12 = (f32[1,16,1,512]{3,2,1,0:T(1,128)S(1)}, f32[1,16,1,512]{3,2,1,0:T(1,128)}, u32[]{:S(2)}) copy-start(f32[1,16,1,512]{3,2,1,0:T(1,128)} %param.18) | copy-start | bytes 98308
  0.7 23.1 %copy-start.3 = (f32[1,5,16,1,512]{4,3,2,1,0:T(1,128)S(1)}, f32[1,5,16,1,512]{4,3,2,1,0:T(1,128)}, u32[]{:S(2)}) copy-start(f32[1,5,16,1,512]{4,3,2,1,0:T(1,128)} %param.25) | copy-start | bytes 491524
  0.7 32.2 %copy-start.16 = (s32[1,5]{1,0:T(1,128)S(1)}, s32[1,5]{1,0:T(1,128)}, u32[]{:S(2)}) copy-start(s32[1,5]{1,0:T(1,128)} %param.28) | copy-start | bytes 64
  4.1 112.8 %collective-permute-start.6 = (bf16[1024,512]{1,0:T(8,128)(2,1)}, bf16[1024,512]{1,0:T(8,128)(2,1)}, u32[]{:S(2)}, u32[]{:S(2)}) collective-permute-start(bf16[1024,512]{1,0:T(8,128)(2,1)} %fusion.2), channel_id=1, source_target_pairs={{0,58},{2,8},{4,62},{6,12},{8,2},{10,16},{12,6},{14,20},{16,10},{1... | collective-permute-start | bytes 3145736 | tf_op jit(solution)/shard_map/ppermute | solution.py:93
  9.9 97.2 %collective-permute-start.5 = (bf16[1024,512]{1,0:T(8,128)(2,1)}, bf16[1024,512]{1,0:T(8,128)(2,1)S(1)}, u32[]{:S(2)}, u32[]{:S(2)}) collective-permute-start(bf16[1024,512]{1,0:T(8,128)(2,1)} %fusion.2), channel_id=1, source_target_pairs={{60,0},{62,2},{0,4},{2,6},{4,8},{6,10},{8,12},{10,14},{12,16},{14,... | collective-permute-start | bytes 3145736 | tf_op jit(solution)/shard_map/ppermute | solution.py:11
  21.5 33.8 %collective-permute-start = (f32[2]{0:T(128)S(1)}, f32[2]{0:T(128)S(1)}, u32[]{:S(2)}, u32[]{:S(2)}) collective-permute-start(f32[2]{0:T(128)S(1)} %pad_maximum_fusion.6), channel_id=1, source_target_pairs={{0,64},{64,0},{128,192},{192,128},{256,320},{320,256},{384,448},{4... | collective-permute-start | bytes 32 | tf_op jit(solution)/shard_map/ppermute | solution.py:25
  24.6 48.5 %collective-permute-start.8 = (f32[7,16,2]{2,1,0:T(8,128)}, f32[7,16,2]{2,1,0:T(8,128)}, u32[]{:S(2)}, u32[]{:S(2)}) collective-permute-start(f32[7,16,2]{2,1,0:T(8,128)} %get-tuple-element.54), channel_id=1, source_target_pairs={{62,0},{0,2},{2,4},{4,6},{6,8},{8,10},{10,12},{12,14},{14,16},{16,... | collective-permute-start | bytes 2696 | tf_op jit(solution)/shard_map/ppermute | solution.py:11
  26.5 48.5 %collective-permute-start.9 = (f32[7,16,2]{2,1,0:T(8,128)}, f32[7,16,2]{2,1,0:T(8,128)}, u32[]{:S(2)}, u32[]{:S(2)}) collective-permute-start(f32[7,16,2]{2,1,0:T(8,128)} %get-tuple-element.55), channel_id=1, source_target_pairs={{2,0},{4,2},{6,4},{8,6},{10,8},{12,10},{14,12},{16,14},{18,16},{20... | collective-permute-start | bytes 2696 | tf_op jit(solution)/shard_map/ppermute | solution.py:11
  55.4 6.3 %collective-permute-start.1 = (f32[2]{0:T(128)S(1)}, f32[2]{0:T(128)S(1)}, u32[]{:S(2)}, u32[]{:S(2)}) collective-permute-start(f32[2]{0:T(128)S(1)} %fusion.103), channel_id=1, source_target_pairs={{0,128},{64,192},{128,0},{192,64},{256,384},{320,448},{384,256},{4... | collective-permute-start | bytes 32 | tf_op jit(solution)/shard_map/ppermute | solution.py:25
  61.8 9.3 %collective-permute-start.2 = (f32[2]{0:T(128)S(1)}, f32[2]{0:T(128)S(1)}, u32[]{:S(2)}, u32[]{:S(2)}) collective-permute-start(f32[2]{0:T(128)S(1)} %fusion.104), channel_id=1, source_target_pairs={{0,256},{64,320},{128,384},{192,448},{256,0},{320,64},{384,128},{4... | collective-permute-start | bytes 32 | tf_op jit(solution)/shard_map/ppermute | solution.py:25
  71.2 35.9 %collective-permute-start.4 = (bf16[1024,512]{1,0:T(8,128)(2,1)}, bf16[1024,512]{1,0:T(8,128)(2,1)S(1)}, u32[]{:S(2)}, u32[]{:S(2)}) collective-permute-start(bf16[1024,512]{1,0:T(8,128)(2,1)} %fusion.2), channel_id=1, source_target_pairs={{4,0},{6,2},{8,4},{10,6},{12,8},{14,10},{16,12},{18,14},{20,16},{2... | collective-permute-start | bytes 3145736 | tf_op jit(solution)/shard_map/ppermute | solution.py:11
  73.1 43.8 %collective-permute-start.3 = (bf16[1024,512]{1,0:T(8,128)(2,1)}, bf16[1024,512]{1,0:T(8,128)(2,1)S(1)}, u32[]{:S(2)}, u32[]{:S(2)}) collective-permute-start(bf16[1024,512]{1,0:T(8,128)(2,1)} %fusion.2), channel_id=1, source_target_pairs={{0,2},{2,0},{4,6},{6,4},{8,10},{10,8},{12,14},{14,12},{16,18},{18,... | collective-permute-start | bytes 3145736 | tf_op jit(solution)/shard_map/ppermute | solution.py:90
  76.3 30.2 %collective-permute-start.10 = (f32[6,16,516]{2,1,0:T(8,128)S(1)}, f32[6,16,516]{2,1,0:T(8,128)S(1)}, u32[]{:S(2)}, u32[]{:S(2)}) collective-permute-start(f32[6,16,516]{2,1,0:T(8,128)S(1)} %pad_maximum_fusion.2), channel_id=1, source_target_pairs={{0,1},{1,0},{2,3},{3,2},{4,5},{5,4},{6,7},{7,6},{8,9},{9,8},{10,11... | collective-permute-start | bytes 594440 | tf_op jit(solution)/shard_map/ppermute | solution.py:37
  107.0 5.7 %copy-start.6 = (f32[1,1,16,1,512]{4,3,2,1,0:T(1,128)S(1)}, f32[1,1,16,1,512]{4,3,2,1,0:T(1,128)}, u32[]{:S(2)}) copy-start(f32[1,1,16,1,512]{4,3,2,1,0:T(1,128)} %get-tuple-element.57) | copy-start | bytes 98308
  107.0 5.7 %copy-start.7 = (f32[1,1,16,1,512]{4,3,2,1,0:T(1,128)S(1)}, f32[1,1,16,1,512]{4,3,2,1,0:T(1,128)}, u32[]{:S(2)}) copy-start(f32[1,1,16,1,512]{4,3,2,1,0:T(1,128)} %get-tuple-element.58) | copy-start | bytes 98308
  107.0 11.8 %copy-start.1 = (bf16[1,5,512,512]{3,2,1,0:T(8,128)(2,1)S(1)}, bf16[1,5,512,512]{3,2,1,0:T(8,128)(2,1)}, u32[]{:S(2)}) copy-start(bf16[1,5,512,512]{3,2,1,0:T(8,128)(2,1)} %param.29) | copy-start | bytes 7864324
  107.2 75.3 %collective-permute-start.7 = (bf16[2048,512]{1,0:T(8,128)(2,1)S(1)}, bf16[2048,512]{1,0:T(8,128)(2,1)S(1)}, u32[]{:S(2)}, u32[]{:S(2)}) collective-permute-start(bf16[2048,512]{1,0:T(8,128)(2,1)S(1)} %pad_maximum_fusion), channel_id=1, source_target_pairs={{0,2},{2,0},{4,6},{6,4},{8,10},{10,8},{12,14},{14,12},{16,18},{18,... | collective-permute-start | bytes 6291464 | tf_op jit(solution)/shard_map/ppermute | solution.py:94
  109.6 7.3 %collective-permute-start.18 = (bf16[16,512]{1,0:T(8,128)(2,1)S(1)}, bf16[16,512]{1,0:T(8,128)(2,1)S(1)}, u32[]{:S(2)}, u32[]{:S(2)}) collective-permute-start(bf16[16,512]{1,0:T(8,128)(2,1)S(1)} %fusion.58), channel_id=1, source_target_pairs={{64,0},{128,64},{192,128},{256,192},{320,256},{384,320},{448,384},... | collective-permute-start | bytes 49160 | tf_op jit(solution)/shard_map/ppermute | solution.py:17
  112.9 73.0 %collective-permute-start.17 = (bf16[16,512]{1,0:T(8,128)(2,1)S(1)}, bf16[16,512]{1,0:T(8,128)(2,1)S(1)}, u32[]{:S(2)}, u32[]{:S(2)}) collective-permute-start(bf16[16,512]{1,0:T(8,128)(2,1)S(1)} %fusion.66), channel_id=1, source_target_pairs={{0,64},{64,128},{128,192},{192,256},{256,320},{320,384},{384,448},... | collective-permute-start | bytes 49160 | tf_op jit(solution)/shard_map/ppermute | solution.py:17
  116.9 8.6 %collective-permute-start.11 = (f32[2]{0:T(128)S(1)}, f32[2]{0:T(128)S(1)}, u32[]{:S(2)}, u32[]{:S(2)}) collective-permute-start(f32[2]{0:T(128)S(1)} %add.245), channel_id=1, source_target_pairs={{0,2},{2,0},{4,6},{6,4},{8,10},{10,8},{12,14},{14,12},{16,18},{18,... | collective-permute-start | bytes 32 | tf_op jit(solution)/shard_map/ppermute | solution.py:25
  124.1 57.0 %copy-start.15 = (f32[1,16,1,512]{3,2,1,0:T(1,128)S(1)}, f32[1,16,1,512]{3,2,1,0:T(1,128)}, u32[]{:S(2)}) copy-start(f32[1,16,1,512]{3,2,1,0:T(1,128)} %param.15) | copy-start | bytes 98308
  124.1 57.7 %copy-start.9 = (f32[1,16,1,512]{3,2,1,0:T(1,128)S(1)}, f32[1,16,1,512]{3,2,1,0:T(1,128)}, u32[]{:S(2)}) copy-start(f32[1,16,1,512]{3,2,1,0:T(1,128)} %param.20) | copy-start | bytes 98308
  124.1 57.7 %copy-start.14 = (f32[1,16,1,512]{3,2,1,0:T(1,128)S(1)}, f32[1,16,1,512]{3,2,1,0:T(1,128)}, u32[]{:S(2)}) copy-start(f32[1,16,1,512]{3,2,1,0:T(1,128)} %param.26) | copy-start | bytes 98308
  125.5 24.3 %collective-permute-start.12 = (f32[2]{0:T(128)S(1)}, f32[2]{0:T(128)S(1)}, u32[]{:S(2)}, u32[]{:S(2)}) collective-permute-start(f32[2]{0:T(128)S(1)} %add.246), channel_id=1, source_target_pairs={{0,4},{2,6},{4,0},{6,2},{8,12},{10,14},{12,8},{14,10},{16,20},{18,... | collective-permute-start | bytes 32 | tf_op jit(solution)/shard_map/ppermute | solution.py:25
  149.8 7.7 %collective-permute-start.13 = (f32[2]{0:T(128)S(1)}, f32[2]{0:T(128)S(1)}, u32[]{:S(2)}, u32[]{:S(2)}) collective-permute-start(f32[2]{0:T(128)S(1)} %add.247), channel_id=1, source_target_pairs={{0,8},{2,10},{4,12},{6,14},{8,0},{10,2},{12,4},{14,6},{16,24},{18,... | collective-permute-start | bytes 32 | tf_op jit(solution)/shard_map/ppermute | solution.py:25
  157.5 5.4 %collective-permute-start.14 = (f32[2]{0:T(128)S(1)}, f32[2]{0:T(128)S(1)}, u32[]{:S(2)}, u32[]{:S(2)}) collective-permute-start(f32[2]{0:T(128)S(1)} %add.248), channel_id=1, source_target_pairs={{0,16},{2,18},{4,20},{6,22},{8,24},{10,26},{12,28},{14,30},{16,0},... | collective-permute-start | bytes 32 | tf_op jit(solution)/shard_map/ppermute | solution.py:25
  163.0 6.9 %collective-permute-start.15 = (f32[2]{0:T(128)S(1)}, f32[2]{0:T(128)S(1)}, u32[]{:S(2)}, u32[]{:S(2)}) collective-permute-start(f32[2]{0:T(128)S(1)} %add.249), channel_id=1, source_target_pairs={{0,32},{2,34},{4,36},{6,38},{8,40},{10,42},{12,44},{14,46},{16,48}... | collective-permute-start | bytes 32 | tf_op jit(solution)/shard_map/ppermute | solution.py:25
  169.9 9.3 %collective-permute-start.16 = (f32[2]{0:T(128)S(1)}, f32[2]{0:T(128)S(1)}, u32[]{:S(2)}, u32[]{:S(2)}) collective-permute-start(f32[2]{0:T(128)S(1)} %add.250), channel_id=1, source_target_pairs={{0,1},{1,0},{2,3},{3,2},{4,5},{5,4},{6,7},{7,6},{8,9},{9,8},{10,11... | collective-permute-start | bytes 32 | tf_op jit(solution)/shard_map/ppermute | solution.py:25
  185.5 0.8 copy-start.11
  185.5 0.8 copy-start.13
  185.5 0.8 copy-start.17
  185.5 0.8 copy-start.18
  185.5 0.8 copy-start.19

commit v11 on v10

--- a/solution.py
+++ b/solution.py
@@ -148,7 +148,9 @@
     )
     own = lon_extended(packed, 2)
     first_row = lax.axis_index("lat") == 0
-    other = lat_partner(jnp.concatenate([own[:5], coupling(own[2:], first_row)[None]]))
+    other = lat_partner(
+        jnp.concatenate([own[:5], coupling(own[2:], first_row)[None]]).astype(jnp.bfloat16)
+    ).astype(jnp.float32)
     moved, backed = propagate_both(own, other, first_row)
     earlier = shifted(moved.astype(jnp.bfloat16), "win", 1).astype(jnp.float32)[None, :, None]
     following = shifted(backed.astype(jnp.bfloat16), "win", -1).astype(jnp.float32)[None, :, None]

time: 190 us -> 185 us (0.974)
  the two profiles are of different devices: /device:TPU:30 before, /device:TPU:38 now
where the time goes in v11:
time: 185 us; the launch traced here: 182 us
  starting transfers between devices  88.6 us (48%)
  waiting for transfers between devices  39.7 us (21%)
  between operations  20.1 us (11%)
  other arithmetic  15.7 us (8%)
  matrix products  11.9 us (6%)
  local copies, waits for them, and re-layouts  6.4 us (3%)
    ppermute x9, starting transfers between devices, butterfly_sum(): lax.ppermute(value, axis, [(i, i ^ step) for i in range(count)])  49.8 us
    ppermute x9, waiting for transfers between devices, butterfly_sum(): lax.ppermute(value, axis, [(i, i ^ step) for i in range(count)])  21.2 us
    ppermute x1, waiting for transfers between devices, lat_partner(): return lax.ppermute(value, 'lat', [(0, 1), (1, 0)])  18.6 us
    ppermute x4, starting transfers between devices, from_offset(): lax.ppermute(value, axis, [((i + distance) % count, i) for i in range(cou...  14.4 us
    dot_general x6, matrix products, localize(): jnp.dot(value, weight_for(offset), preferred_element_type=jnp.float32)  9.54 us
    ppermute x1, starting transfers between devices, lat_partner(): return lax.ppermute(value, 'lat', [(0, 1), (1, 0)])  8.76 us
    ppermute x2, starting transfers between devices, shifted(): lax.ppermute(value, axis, [(source, source + steps) for source in range(l...  5.84 us
    ppermute x1, starting transfers between devices, localize(): lax.ppermute(flat, 'lon', [(s, (s + 3) % bands if s % 2 else (s - 3) % ba...  5.78 us
  transfers between devices with their start and end apart: 19, of which 8 were waited for; matrix products, arithmetic and copies ran while one was open for 15% of the time, Pallas kernels for 0%

profile of v11, /device:TPU:38, one launch (start us, length us, event | category | flops | bytes accessed | tf_op | source)
XLA Modules:
  0.0 182.3 jit_solution(13680679852989756391)
XLA Ops:
  0.7 0.9 copy_bitcast_fusion.3
  1.6 2.5 %fusion.2 = bf16[1024,512]{1,0:T(8,128)(2,1)} fusion(bf16[1,64,16,1,512]{4,2,3,1,0:T(8,128)(2,1)} %param.24, f32[16,512]{1,0:T(8,128)S(1)} %get-tuple-element.70), kind=kLoop, calls=%fused_computation.6 | loop fusion | flops 1572864 | bytes 2129920 | tf_op jit(solution)/shard_map/convert_element_type | solution.py:81
  4.1 5.8 %collective-permute-start.6 = (bf16[1024,512]{1,0:T(8,128)(2,1)}, bf16[1024,512]{1,0:T(8,128)(2,1)}, u32[]{:S(2)}, u32[]{:S(2)}) collective-permute-start(bf16[1024,512]{1,0:T(8,128)(2,1)} %fusion.2), channel_id=1, source_target_pairs={{0,58},{2,8},{4,62},{6,12},{8,2},{10,16},{12,6},{14,20},{16,10},{1... | collective-permute-start | bytes 3145736 | tf_op jit(solution)/shard_map/ppermute | solution.py:93
  9.9 4.3 %collective-permute-start.5 = (bf16[1024,512]{1,0:T(8,128)(2,1)}, bf16[1024,512]{1,0:T(8,128)(2,1)S(1)}, u32[]{:S(2)}, u32[]{:S(2)}) collective-permute-start(bf16[1024,512]{1,0:T(8,128)(2,1)} %fusion.2), channel_id=1, source_target_pairs={{60,0},{62,2},{0,4},{2,6},{4,8},{6,10},{8,12},{10,14},{12,16},{14,... | collective-permute-start | bytes 3145736 | tf_op jit(solution)/shard_map/ppermute | solution.py:11
  14.2 0.7 multiply_reduce_fusion.2
  14.8 0.7 multiply_reduce_fusion
  15.5 0.7 multiply_reduce_fusion.1
  16.2 0.7 multiply_reduce_fusion.3
  18.8 0.7 multiply_reduce_fusion.4
  21.5 2.6 %collective-permute-start = (f32[2]{0:T(128)S(1)}, f32[2]{0:T(128)S(1)}, u32[]{:S(2)}, u32[]{:S(2)}) collective-permute-start(f32[2]{0:T(128)S(1)} %pad_maximum_fusion.6), channel_id=1, source_target_pairs={{0,64},{64,0},{128,192},{192,128},{256,320},{320,256},{384,448},{4... | collective-permute-start | bytes 32 | tf_op jit(solution)/shard_map/ppermute | solution.py:25
  24.1 0.7 pad_maximum_fusion.5
  24.8 1.9 %collective-permute-start.8 = (f32[7,16,2]{2,1,0:T(8,128)}, f32[7,16,2]{2,1,0:T(8,128)}, u32[]{:S(2)}, u32[]{:S(2)}) collective-permute-start(f32[7,16,2]{2,1,0:T(8,128)} %get-tuple-element.54), channel_id=1, source_target_pairs={{62,0},{0,2},{2,4},{4,6},{6,8},{8,10},{10,12},{12,14},{14,16},{16,... | collective-permute-start | bytes 2696 | tf_op jit(solution)/shard_map/ppermute | solution.py:11
  26.7 6.3 %collective-permute-start.9 = (f32[7,16,2]{2,1,0:T(8,128)}, f32[7,16,2]{2,1,0:T(8,128)}, u32[]{:S(2)}, u32[]{:S(2)}) collective-permute-start(f32[7,16,2]{2,1,0:T(8,128)} %get-tuple-element.55), channel_id=1, source_target_pairs={{2,0},{4,2},{6,4},{8,6},{10,8},{12,10},{14,12},{16,14},{18,16},{20... | collective-permute-start | bytes 2696 | tf_op jit(solution)/shard_map/ppermute | solution.py:11
  33.2 0.7 bitcast_reduce_fusion
  35.1 0.7 bitcast_reduce_fusion.6
  37.3 0.7 bitcast_reduce_fusion.5
  39.2 0.7 bitcast_reduce_fusion.4
  41.2 0.7 bitcast_reduce_fusion.3
  43.1 0.7 bitcast_reduce_fusion.2
  45.1 0.8 compare_reduce_fusion
  45.9 0.7 bitcast_reduce_fusion.1
  47.9 0.6 fusion.97
  48.5 0.3 fusion
  53.3 2.3 %fusion.17 = f32[1024,512]{1,0:T(8,128)S(1)} fusion(bf16[1024,512]{1,0:T(8,128)(2,1)S(1)} %bitcast.132, bf16[1,5,512,512]{3,2,1,0:T(8,128)(2,1)} %param.29, s32[]{:T(128)S(6)} %select_n.168, pred[]{:T(512)} %get-tuple-element.35), kind=kOutput, calls=%fused_computation.20 | convolution fusion | flops 537133056 | bytes 3670532 | tf_op jit(solution)/shard_map/dot_general | solution.py:111
  55.7 2.7 %collective-permute-start.1 = (f32[2]{0:T(128)S(1)}, f32[2]{0:T(128)S(1)}, u32[]{:S(2)}, u32[]{:S(2)}) collective-permute-start(f32[2]{0:T(128)S(1)} %fusion.105), channel_id=1, source_target_pairs={{0,128},{64,192},{128,0},{192,64},{256,384},{320,448},{384,256},{4... | collective-permute-start | bytes 32 | tf_op jit(solution)/shard_map/ppermute | solution.py:25
  58.4 3.6 %collective-permute-done.1 = f32[2]{0:T(128)S(1)} collective-permute-done((f32[2]{0:T(128)S(1)}, f32[2]{0:T(128)S(1)}, u32[]{:S(2)}, u32[]{:S(2)}) %collective-permute-start.1) | collective-permute-done | bytes 40 | tf_op jit(solution)/shard_map/ppermute | solution.py:25
  62.1 2.9 %collective-permute-start.2 = (f32[2]{0:T(128)S(1)}, f32[2]{0:T(128)S(1)}, u32[]{:S(2)}, u32[]{:S(2)}) collective-permute-start(f32[2]{0:T(128)S(1)} %fusion.106), channel_id=1, source_target_pairs={{0,256},{64,320},{128,384},{192,448},{256,0},{320,64},{384,128},{4... | collective-permute-start | bytes 32 | tf_op jit(solution)/shard_map/ppermute | solution.py:25
  65.0 6.4 %collective-permute-done.2 = f32[2]{0:T(128)S(1)} collective-permute-done((f32[2]{0:T(128)S(1)}, f32[2]{0:T(128)S(1)}, u32[]{:S(2)}, u32[]{:S(2)}) %collective-permute-start.2) | collective-permute-done | bytes 40 | tf_op jit(solution)/shard_map/ppermute | solution.py:25
  71.4 1.9 %collective-permute-start.4 = (bf16[1024,512]{1,0:T(8,128)(2,1)}, bf16[1024,512]{1,0:T(8,128)(2,1)S(1)}, u32[]{:S(2)}, u32[]{:S(2)}) collective-permute-start(bf16[1024,512]{1,0:T(8,128)(2,1)} %fusion.2), channel_id=1, source_target_pairs={{4,0},{6,2},{8,4},{10,6},{12,8},{14,10},{16,12},{18,14},{20,16},{2... | collective-permute-start | bytes 3145736 | tf_op jit(solution)/shard_map/ppermute | solution.py:11
  73.3 1.9 %collective-permute-start.3 = (bf16[1024,512]{1,0:T(8,128)(2,1)}, bf16[1024,512]{1,0:T(8,128)(2,1)S(1)}, u32[]{:S(2)}, u32[]{:S(2)}) collective-permute-start(bf16[1024,512]{1,0:T(8,128)(2,1)} %fusion.2), channel_id=1, source_target_pairs={{0,2},{2,0},{4,6},{6,4},{8,10},{10,8},{12,14},{14,12},{16,18},{18,... | collective-permute-start | bytes 3145736 | tf_op jit(solution)/shard_map/ppermute | solution.py:90
  75.3 1.0 pad_maximum_fusion.1
  76.4 8.8 %collective-permute-start.10 = (bf16[6,16,516]{2,1,0:T(8,128)(2,1)S(1)}, bf16[6,16,516]{2,1,0:T(8,128)(2,1)S(1)}, u32[]{:S(2)}, u32[]{:S(2)}) collective-permute-start(bf16[6,16,516]{2,1,0:T(8,128)(2,1)S(1)} %pad_maximum_fusion.2), channel_id=1, source_target_pairs={{0,1},{1,0},{2,3},{3,2},{4,5},{5,4},{6,7},{7,6},{8,9},{9,8},{10,11... | collective-permute-start | bytes 297224 | tf_op jit(solution)/shard_map/ppermute | solution.py:37
  85.4 18.6 %collective-permute-done.10 = bf16[6,16,516]{2,1,0:T(8,128)(2,1)S(1)} collective-permute-done((bf16[6,16,516]{2,1,0:T(8,128)(2,1)S(1)}, bf16[6,16,516]{2,1,0:T(8,128)(2,1)S(1)}, u32[]{:S(2)}, u32[]{:S(2)}) %collective-permute-start.10) | collective-permute-done | bytes 99104 | tf_op jit(solution)/shard_map/ppermute | solution.py:37
  104.2 0.2 fusion.48
  104.7 2.1 %collective-permute-start.7 = (bf16[2048,512]{1,0:T(8,128)(2,1)S(1)}, bf16[2048,512]{1,0:T(8,128)(2,1)S(1)}, u32[]{:S(2)}, u32[]{:S(2)}) collective-permute-start(bf16[2048,512]{1,0:T(8,128)(2,1)S(1)} %pad_maximum_fusion), channel_id=1, source_target_pairs={{0,2},{2,0},{4,6},{6,4},{8,10},{10,8},{12,14},{14,12},{16,18},{18,... | collective-permute-start | bytes 6291464 | tf_op jit(solution)/shard_map/ppermute | solution.py:94
  106.7 0.2 fusion.58
  107.1 2.3 %collective-permute-start.18 = (bf16[16,512]{1,0:T(8,128)(2,1)S(1)}, bf16[16,512]{1,0:T(8,128)(2,1)S(1)}, u32[]{:S(2)}, u32[]{:S(2)}) collective-permute-start(bf16[16,512]{1,0:T(8,128)(2,1)S(1)} %fusion.58), channel_id=1, source_target_pairs={{64,0},{128,64},{192,128},{256,192},{320,256},{384,320},{448,384},... | collective-permute-start | bytes 49160 | tf_op jit(solution)/shard_map/ppermute | solution.py:17
  109.5 3.6 %collective-permute-start.17 = (bf16[16,512]{1,0:T(8,128)(2,1)S(1)}, bf16[16,512]{1,0:T(8,128)(2,1)S(1)}, u32[]{:S(2)}, u32[]{:S(2)}) collective-permute-start(bf16[16,512]{1,0:T(8,128)(2,1)S(1)} %fusion.66), channel_id=1, source_target_pairs={{0,64},{64,128},{128,192},{192,256},{256,320},{320,384},{384,448},... | collective-permute-start | bytes 49160 | tf_op jit(solution)/shard_map/ppermute | solution.py:17
  113.2 1.9 %collective-permute-start.11 = (f32[2]{0:T(128)S(1)}, f32[2]{0:T(128)S(1)}, u32[]{:S(2)}, u32[]{:S(2)}) collective-permute-start(f32[2]{0:T(128)S(1)} %add.245), channel_id=1, source_target_pairs={{0,2},{2,0},{4,6},{6,4},{8,10},{10,8},{12,14},{14,12},{16,18},{18,... | collective-permute-start | bytes 32 | tf_op jit(solution)/shard_map/ppermute | solution.py:25
  115.1 1.4 fusion.15
  116.5 1.3 fusion.13
  117.8 2.6 %fusion.9 = f32[1024,512]{1,0:T(8,128)S(1)} fusion(bf16[1024,512]{1,0:T(8,128)(2,1)} %collective-permute-done.6, bf16[1,5,512,512]{3,2,1,0:T(8,128)(2,1)S(1)} %copy-done.1, s32[]{:T(128)S(6)} %select_n.191, pred[]{:T(512)} %get-tuple-element.31), kind=kOutput, calls=%fused_computation.12 | convolution fusion | flops 537133056 | bytes 3670021 | tf_op jit(solution)/shard_map/dot_general | solution.py:113
  120.4 1.3 fusion.11
  121.8 19.9 %collective-permute-start.12 = (f32[2]{0:T(128)S(1)}, f32[2]{0:T(128)S(1)}, u32[]{:S(2)}, u32[]{:S(2)}) collective-permute-start(f32[2]{0:T(128)S(1)} %add.246), channel_id=1, source_target_pairs={{0,4},{2,6},{4,0},{6,2},{8,12},{10,14},{12,8},{14,10},{16,20},{18,... | collective-permute-start | bytes 32 | tf_op jit(solution)/shard_map/ppermute | solution.py:25
  141.7 1.5 collective-permute-done.12
  143.2 6.2 %collective-permute-start.13 = (f32[2]{0:T(128)S(1)}, f32[2]{0:T(128)S(1)}, u32[]{:S(2)}, u32[]{:S(2)}) collective-permute-start(f32[2]{0:T(128)S(1)} %add.247), channel_id=1, source_target_pairs={{0,8},{2,10},{4,12},{6,14},{8,0},{10,2},{12,4},{14,6},{16,24},{18,... | collective-permute-start | bytes 32 | tf_op jit(solution)/shard_map/ppermute | solution.py:25
  149.4 1.5 collective-permute-done.13
  151.0 2.7 %collective-permute-start.14 = (f32[2]{0:T(128)S(1)}, f32[2]{0:T(128)S(1)}, u32[]{:S(2)}, u32[]{:S(2)}) collective-permute-start(f32[2]{0:T(128)S(1)} %add.248), channel_id=1, source_target_pairs={{0,16},{2,18},{4,20},{6,22},{8,24},{10,26},{12,28},{14,30},{16,0},... | collective-permute-start | bytes 32 | tf_op jit(solution)/shard_map/ppermute | solution.py:25
  153.7 2.7 %collective-permute-done.14 = f32[2]{0:T(128)S(1)} collective-permute-done((f32[2]{0:T(128)S(1)}, f32[2]{0:T(128)S(1)}, u32[]{:S(2)}, u32[]{:S(2)}) %collective-permute-start.14) | collective-permute-done | bytes 40 | tf_op jit(solution)/shard_map/ppermute | solution.py:25
  156.4 3.3 %collective-permute-start.15 = (f32[2]{0:T(128)S(1)}, f32[2]{0:T(128)S(1)}, u32[]{:S(2)}, u32[]{:S(2)}) collective-permute-start(f32[2]{0:T(128)S(1)} %add.249), channel_id=1, source_target_pairs={{0,32},{2,34},{4,36},{6,38},{8,40},{10,42},{12,44},{14,46},{16,48}... | collective-permute-start | bytes 32 | tf_op jit(solution)/shard_map/ppermute | solution.py:25
  159.7 3.6 %collective-permute-done.15 = f32[2]{0:T(128)S(1)} collective-permute-done((f32[2]{0:T(128)S(1)}, f32[2]{0:T(128)S(1)}, u32[]{:S(2)}, u32[]{:S(2)}) %collective-permute-start.15) | collective-permute-done | bytes 40 | tf_op jit(solution)/shard_map/ppermute | solution.py:25
  163.3 7.5 %collective-permute-start.16 = (f32[2]{0:T(128)S(1)}, f32[2]{0:T(128)S(1)}, u32[]{:S(2)}, u32[]{:S(2)}) collective-permute-start(f32[2]{0:T(128)S(1)} %add.250), channel_id=1, source_target_pairs={{0,1},{1,0},{2,3},{3,2},{4,5},{5,4},{6,7},{7,6},{8,9},{9,8},{10,11... | collective-permute-start | bytes 32 | tf_op jit(solution)/shard_map/ppermute | solution.py:25
  170.9 1.8 collective-permute-done.16
  172.6 0.6 fusion.99
  174.6 0.6 copy.38
  175.2 0.7 fusion.78
  175.9 1.4 fusion.7
  177.3 1.5 add_add_fusion
  178.9 0.4 fusion.1
  179.3 0.3 copy-done.11
  179.7 0.6 copy.42
  180.4 0.6 copy.40
  181.0 0.6 copy.41
  181.7 0.6 copy.39
  (80 shorter events, 1.6 us)
Async XLA Ops:
  0.6 13.5 %copy-start.2 = (f32[1,16,1,512]{3,2,1,0:T(1,128)S(1)}, f32[1,16,1,512]{3,2,1,0:T(1,128)}, u32[]{:S(2)}) copy-start(f32[1,16,1,512]{3,2,1,0:T(1,128)} %param.21) | copy-start | bytes 98308
  0.6 14.2 %copy-start.4 = (f32[1,16,1,512]{3,2,1,0:T(1,128)S(1)}, f32[1,16,1,512]{3,2,1,0:T(1,128)}, u32[]{:S(2)}) copy-start(f32[1,16,1,512]{3,2,1,0:T(1,128)} %param.23) | copy-start | bytes 98308
  0.7 47.9 %copy-start = (bf16[1,64,16,1,512]{4,2,3,1,0:T(8,128)(2,1)S(1)}, bf16[1,64,16,1,512]{4,2,3,1,0:T(8,128)(2,1)}, u32[]{:S(2)}) copy-start(bf16[1,64,16,1,512]{4,2,3,1,0:T(8,128)(2,1)} %param.24) | copy-start | bytes 3145732
  0.7 14.8 %copy-start.5 = (f32[1,16,1,512]{3,2,1,0:T(1,128)S(1)}, f32[1,16,1,512]{3,2,1,0:T(1,128)}, u32[]{:S(2)}) copy-start(f32[1,16,1,512]{3,2,1,0:T(1,128)} %param.22) | copy-start | bytes 98308
  0.7 15.5 %copy-start.8 = (f32[1,16,1,512]{3,2,1,0:T(1,128)S(1)}, f32[1,16,1,512]{3,2,1,0:T(1,128)}, u32[]{:S(2)}) copy-start(f32[1,16,1,512]{3,2,1,0:T(1,128)} %param.20) | copy-start | bytes 98308
  0.7 18.1 %copy-start.10 = (f32[1,16,1,512]{3,2,1,0:T(1,128)S(1)}, f32[1,16,1,512]{3,2,1,0:T(1,128)}, u32[]{:S(2)}) copy-start(f32[1,16,1,512]{3,2,1,0:T(1,128)} %param.19) | copy-start | bytes 98308
  0.7 18.1 %copy-start.12 = (f32[1,16,1,512]{3,2,1,0:T(1,128)S(1)}, f32[1,16,1,512]{3,2,1,0:T(1,128)}, u32[]{:S(2)}) copy-start(f32[1,16,1,512]{3,2,1,0:T(1,128)} %param.18) | copy-start | bytes 98308
  0.7 23.4 %copy-start.3 = (f32[1,5,16,1,512]{4,3,2,1,0:T(1,128)S(1)}, f32[1,5,16,1,512]{4,3,2,1,0:T(1,128)}, u32[]{:S(2)}) copy-start(f32[1,5,16,1,512]{4,3,2,1,0:T(1,128)} %param.25) | copy-start | bytes 491524
  0.7 32.4 %copy-start.16 = (s32[1,5]{1,0:T(1,128)S(1)}, s32[1,5]{1,0:T(1,128)}, u32[]{:S(2)}) copy-start(s32[1,5]{1,0:T(1,128)} %param.28) | copy-start | bytes 64
  4.1 109.1 %collective-permute-start.6 = (bf16[1024,512]{1,0:T(8,128)(2,1)}, bf16[1024,512]{1,0:T(8,128)(2,1)}, u32[]{:S(2)}, u32[]{:S(2)}) collective-permute-start(bf16[1024,512]{1,0:T(8,128)(2,1)} %fusion.2), channel_id=1, source_target_pairs={{0,58},{2,8},{4,62},{6,12},{8,2},{10,16},{12,6},{14,20},{16,10},{1... | collective-permute-start | bytes 3145736 | tf_op jit(solution)/shard_map/ppermute | solution.py:93
  9.9 94.6 %collective-permute-start.5 = (bf16[1024,512]{1,0:T(8,128)(2,1)}, bf16[1024,512]{1,0:T(8,128)(2,1)S(1)}, u32[]{:S(2)}, u32[]{:S(2)}) collective-permute-start(bf16[1024,512]{1,0:T(8,128)(2,1)} %fusion.2), channel_id=1, source_target_pairs={{60,0},{62,2},{0,4},{2,6},{4,8},{6,10},{8,12},{10,14},{12,16},{14,... | collective-permute-start | bytes 3145736 | tf_op jit(solution)/shard_map/ppermute | solution.py:11
  21.5 34.1 %collective-permute-start = (f32[2]{0:T(128)S(1)}, f32[2]{0:T(128)S(1)}, u32[]{:S(2)}, u32[]{:S(2)}) collective-permute-start(f32[2]{0:T(128)S(1)} %pad_maximum_fusion.6), channel_id=1, source_target_pairs={{0,64},{64,0},{128,192},{192,128},{256,320},{320,256},{384,448},{4... | collective-permute-start | bytes 32 | tf_op jit(solution)/shard_map/ppermute | solution.py:25
  24.8 48.5 %collective-permute-start.8 = (f32[7,16,2]{2,1,0:T(8,128)}, f32[7,16,2]{2,1,0:T(8,128)}, u32[]{:S(2)}, u32[]{:S(2)}) collective-permute-start(f32[7,16,2]{2,1,0:T(8,128)} %get-tuple-element.54), channel_id=1, source_target_pairs={{62,0},{0,2},{2,4},{4,6},{6,8},{8,10},{10,12},{12,14},{14,16},{16,... | collective-permute-start | bytes 2696 | tf_op jit(solution)/shard_map/ppermute | solution.py:11
  26.7 48.5 %collective-permute-start.9 = (f32[7,16,2]{2,1,0:T(8,128)}, f32[7,16,2]{2,1,0:T(8,128)}, u32[]{:S(2)}, u32[]{:S(2)}) collective-permute-start(f32[7,16,2]{2,1,0:T(8,128)} %get-tuple-element.55), channel_id=1, source_target_pairs={{2,0},{4,2},{6,4},{8,6},{10,8},{12,10},{14,12},{16,14},{18,16},{20... | collective-permute-start | bytes 2696 | tf_op jit(solution)/shard_map/ppermute | solution.py:11
  55.7 6.3 %collective-permute-start.1 = (f32[2]{0:T(128)S(1)}, f32[2]{0:T(128)S(1)}, u32[]{:S(2)}, u32[]{:S(2)}) collective-permute-start(f32[2]{0:T(128)S(1)} %fusion.105), channel_id=1, source_target_pairs={{0,128},{64,192},{128,0},{192,64},{256,384},{320,448},{384,256},{4... | collective-permute-start | bytes 32 | tf_op jit(solution)/shard_map/ppermute | solution.py:25
  62.1 9.3 %collective-permute-start.2 = (f32[2]{0:T(128)S(1)}, f32[2]{0:T(128)S(1)}, u32[]{:S(2)}, u32[]{:S(2)}) collective-permute-start(f32[2]{0:T(128)S(1)} %fusion.106), channel_id=1, source_target_pairs={{0,256},{64,320},{128,384},{192,448},{256,0},{320,64},{384,128},{4... | collective-permute-start | bytes 32 | tf_op jit(solution)/shard_map/ppermute | solution.py:25
  71.4 33.1 %collective-permute-start.4 = (bf16[1024,512]{1,0:T(8,128)(2,1)}, bf16[1024,512]{1,0:T(8,128)(2,1)S(1)}, u32[]{:S(2)}, u32[]{:S(2)}) collective-permute-start(bf16[1024,512]{1,0:T(8,128)(2,1)} %fusion.2), channel_id=1, source_target_pairs={{4,0},{6,2},{8,4},{10,6},{12,8},{14,10},{16,12},{18,14},{20,16},{2... | collective-permute-start | bytes 3145736 | tf_op jit(solution)/shard_map/ppermute | solution.py:11
  73.3 39.8 %collective-permute-start.3 = (bf16[1024,512]{1,0:T(8,128)(2,1)}, bf16[1024,512]{1,0:T(8,128)(2,1)S(1)}, u32[]{:S(2)}, u32[]{:S(2)}) collective-permute-start(bf16[1024,512]{1,0:T(8,128)(2,1)} %fusion.2), channel_id=1, source_target_pairs={{0,2},{2,0},{4,6},{6,4},{8,10},{10,8},{12,14},{14,12},{16,18},{18,... | collective-permute-start | bytes 3145736 | tf_op jit(solution)/shard_map/ppermute | solution.py:90
  76.4 27.6 %collective-permute-start.10 = (bf16[6,16,516]{2,1,0:T(8,128)(2,1)S(1)}, bf16[6,16,516]{2,1,0:T(8,128)(2,1)S(1)}, u32[]{:S(2)}, u32[]{:S(2)}) collective-permute-start(bf16[6,16,516]{2,1,0:T(8,128)(2,1)S(1)} %pad_maximum_fusion.2), channel_id=1, source_target_pairs={{0,1},{1,0},{2,3},{3,2},{4,5},{5,4},{6,7},{7,6},{8,9},{9,8},{10,11... | collective-permute-start | bytes 297224 | tf_op jit(solution)/shard_map/ppermute | solution.py:37
  104.5 4.9 %copy-start.6 = (f32[1,1,16,1,512]{4,3,2,1,0:T(1,128)S(1)}, f32[1,1,16,1,512]{4,3,2,1,0:T(1,128)}, u32[]{:S(2)}) copy-start(f32[1,1,16,1,512]{4,3,2,1,0:T(1,128)} %get-tuple-element.57) | copy-start | bytes 98308
  104.5 4.9 %copy-start.7 = (f32[1,1,16,1,512]{4,3,2,1,0:T(1,128)S(1)}, f32[1,1,16,1,512]{4,3,2,1,0:T(1,128)}, u32[]{:S(2)}) copy-start(f32[1,1,16,1,512]{4,3,2,1,0:T(1,128)} %get-tuple-element.58) | copy-start | bytes 98308
  104.5 10.6 %copy-start.1 = (bf16[1,5,512,512]{3,2,1,0:T(8,128)(2,1)S(1)}, bf16[1,5,512,512]{3,2,1,0:T(8,128)(2,1)}, u32[]{:S(2)}) copy-start(bf16[1,5,512,512]{3,2,1,0:T(8,128)(2,1)} %param.29) | copy-start | bytes 7864324
  104.7 71.2 %collective-permute-start.7 = (bf16[2048,512]{1,0:T(8,128)(2,1)S(1)}, bf16[2048,512]{1,0:T(8,128)(2,1)S(1)}, u32[]{:S(2)}, u32[]{:S(2)}) collective-permute-start(bf16[2048,512]{1,0:T(8,128)(2,1)S(1)} %pad_maximum_fusion), channel_id=1, source_target_pairs={{0,2},{2,0},{4,6},{6,4},{8,10},{10,8},{12,14},{14,12},{16,18},{18,... | collective-permute-start | bytes 6291464 | tf_op jit(solution)/shard_map/ppermute | solution.py:94
  107.1 6.1 %collective-permute-start.18 = (bf16[16,512]{1,0:T(8,128)(2,1)S(1)}, bf16[16,512]{1,0:T(8,128)(2,1)S(1)}, u32[]{:S(2)}, u32[]{:S(2)}) collective-permute-start(bf16[16,512]{1,0:T(8,128)(2,1)S(1)} %fusion.58), channel_id=1, source_target_pairs={{64,0},{128,64},{192,128},{256,192},{320,256},{384,320},{448,384},... | collective-permute-start | bytes 49160 | tf_op jit(solution)/shard_map/ppermute | solution.py:17
  109.5 69.8 %collective-permute-start.17 = (bf16[16,512]{1,0:T(8,128)(2,1)S(1)}, bf16[16,512]{1,0:T(8,128)(2,1)S(1)}, u32[]{:S(2)}, u32[]{:S(2)}) collective-permute-start(bf16[16,512]{1,0:T(8,128)(2,1)S(1)} %fusion.66), channel_id=1, source_target_pairs={{0,64},{64,128},{128,192},{192,256},{256,320},{320,384},{384,448},... | collective-permute-start | bytes 49160 | tf_op jit(solution)/shard_map/ppermute | solution.py:17
  113.2 8.6 %collective-permute-start.11 = (f32[2]{0:T(128)S(1)}, f32[2]{0:T(128)S(1)}, u32[]{:S(2)}, u32[]{:S(2)}) collective-permute-start(f32[2]{0:T(128)S(1)} %add.245), channel_id=1, source_target_pairs={{0,2},{2,0},{4,6},{6,4},{8,10},{10,8},{12,14},{14,12},{16,18},{18,... | collective-permute-start | bytes 32 | tf_op jit(solution)/shard_map/ppermute | solution.py:25
  120.4 54.2 %copy-start.15 = (f32[1,16,1,512]{3,2,1,0:T(1,128)S(1)}, f32[1,16,1,512]{3,2,1,0:T(1,128)}, u32[]{:S(2)}) copy-start(f32[1,16,1,512]{3,2,1,0:T(1,128)} %param.15) | copy-start | bytes 98308
  120.4 54.8 %copy-start.9 = (f32[1,16,1,512]{3,2,1,0:T(1,128)S(1)}, f32[1,16,1,512]{3,2,1,0:T(1,128)}, u32[]{:S(2)}) copy-start(f32[1,16,1,512]{3,2,1,0:T(1,128)} %param.20) | copy-start | bytes 98308
  120.4 54.8 %copy-start.14 = (f32[1,16,1,512]{3,2,1,0:T(1,128)S(1)}, f32[1,16,1,512]{3,2,1,0:T(1,128)}, u32[]{:S(2)}) copy-start(f32[1,16,1,512]{3,2,1,0:T(1,128)} %param.26) | copy-start | bytes 98308
  121.8 21.4 %collective-permute-start.12 = (f32[2]{0:T(128)S(1)}, f32[2]{0:T(128)S(1)}, u32[]{:S(2)}, u32[]{:S(2)}) collective-permute-start(f32[2]{0:T(128)S(1)} %add.246), channel_id=1, source_target_pairs={{0,4},{2,6},{4,0},{6,2},{8,12},{10,14},{12,8},{14,10},{16,20},{18,... | collective-permute-start | bytes 32 | tf_op jit(solution)/shard_map/ppermute | solution.py:25
  143.2 7.7 %collective-permute-start.13 = (f32[2]{0:T(128)S(1)}, f32[2]{0:T(128)S(1)}, u32[]{:S(2)}, u32[]{:S(2)}) collective-permute-start(f32[2]{0:T(128)S(1)} %add.247), channel_id=1, source_target_pairs={{0,8},{2,10},{4,12},{6,14},{8,0},{10,2},{12,4},{14,6},{16,24},{18,... | collective-permute-start | bytes 32 | tf_op jit(solution)/shard_map/ppermute | solution.py:25
  151.0 5.4 %collective-permute-start.14 = (f32[2]{0:T(128)S(1)}, f32[2]{0:T(128)S(1)}, u32[]{:S(2)}, u32[]{:S(2)}) collective-permute-start(f32[2]{0:T(128)S(1)} %add.248), channel_id=1, source_target_pairs={{0,16},{2,18},{4,20},{6,22},{8,24},{10,26},{12,28},{14,30},{16,0},... | collective-permute-start | bytes 32 | tf_op jit(solution)/shard_map/ppermute | solution.py:25
  156.4 6.9 %collective-permute-start.15 = (f32[2]{0:T(128)S(1)}, f32[2]{0:T(128)S(1)}, u32[]{:S(2)}, u32[]{:S(2)}) collective-permute-start(f32[2]{0:T(128)S(1)} %add.249), channel_id=1, source_target_pairs={{0,32},{2,34},{4,36},{6,38},{8,40},{10,42},{12,44},{14,46},{16,48}... | collective-permute-start | bytes 32 | tf_op jit(solution)/shard_map/ppermute | solution.py:25
  163.3 9.3 %collective-permute-start.16 = (f32[2]{0:T(128)S(1)}, f32[2]{0:T(128)S(1)}, u32[]{:S(2)}, u32[]{:S(2)}) collective-permute-start(f32[2]{0:T(128)S(1)} %add.250), channel_id=1, source_target_pairs={{0,1},{1,0},{2,3},{3,2},{4,5},{5,4},{6,7},{7,6},{8,9},{9,8},{10,11... | collective-permute-start | bytes 32 | tf_op jit(solution)/shard_map/ppermute | solution.py:25
  178.9 0.8 copy-start.11
  178.9 0.8 copy-start.13
  178.9 0.8 copy-start.17
  178.9 0.8 copy-start.18
  178.9 0.8 copy-start.19

commit v12 on v10

--- a/solution.py
+++ b/solution.py
@@ -148,7 +148,15 @@
     )
     own = lon_extended(packed, 2)
     first_row = lax.axis_index("lat") == 0
-    other = lat_partner(jnp.concatenate([own[:5], coupling(own[2:], first_row)[None]]))
+    six = jnp.concatenate([packed[:5], coupling(packed[2:], first_row)[None]]).astype(jnp.bfloat16)
+    bands = lax.axis_size("lon")
+    diagonal = [
+        [(i * 2 + a, ((i + step) % bands) * 2 + 1 - a) for i in range(bands) for a in range(2)]
+        for step in (1, -1)
+    ]
+    from_west = lax.ppermute(six[..., -2:], ("lon", "lat"), diagonal[0])
+    from_east = lax.ppermute(six[..., :2], ("lon", "lat"), diagonal[1])
+    other = jnp.concatenate([from_west, lat_partner(six), from_east], axis=-1).astype(jnp.float32)
     moved, backed = propagate_both(own, other, first_row)
     earlier = shifted(moved.astype(jnp.bfloat16), "win", 1).astype(jnp.float32)[None, :, None]
     following = shifted(backed.astype(jnp.bfloat16), "win", -1).astype(jnp.float32)[None, :, None]

time: 190 us -> 195 us (1.026)
  the two profiles are of different devices: /device:TPU:30 before, /device:TPU:16 now
where the time goes in v12:
time: 195 us; the launch traced here: 193 us
  starting transfers between devices  78.1 us (40%)
  waiting for transfers between devices  58.4 us (30%)
  between operations  19.8 us (10%)
  other arithmetic  18.5 us (9%)
  matrix products  12 us (6%)
  local copies, waits for them, and re-layouts  6.42 us (3%)
    ppermute x1, waiting for transfers between devices, localize(): lax.ppermute(flat, 'lon', [(s, (s + 3) % bands if s % 2 else (s - 3) % ba...  31 us
    ppermute x9, waiting for transfers between devices, butterfly_sum(): lax.ppermute(value, axis, [(i, i ^ step) for i in range(count)])  27.4 us
    ppermute x9, starting transfers between devices, butterfly_sum(): lax.ppermute(value, axis, [(i, i ^ step) for i in range(count)])  27.1 us
    ppermute x4, starting transfers between devices, from_offset(): lax.ppermute(value, axis, [((i + distance) % count, i) for i in range(cou...  21.5 us
    dot_general x6, matrix products, localize(): jnp.dot(value, weight_for(offset), preferred_element_type=jnp.float32)  9.62 us
    ppermute x1, starting transfers between devices, lat_partner(): return lax.ppermute(value, 'lat', [(0, 1), (1, 0)])  8.65 us
    ppermute x1, starting transfers between devices, local(): from_east = lax.ppermute(six[..., :2], ('lon', 'lat'), diagonal[1])  6.96 us
    ppermute x2, starting transfers between devices, shifted(): lax.ppermute(value, axis, [(source, source + steps) for source in range(l...  5.84 us
  transfers between devices with their start and end apart: 21, of which 8 were waited for; matrix products, arithmetic and copies ran while one was open for 16% of the time, Pallas kernels for 0%

profile of v12, /device:TPU:16, one launch (start us, length us, event | category | flops | bytes accessed | tf_op | source)
XLA Modules:
  0.0 193.3 jit_solution(8720029362234952201)
XLA Ops:
  0.7 0.8 copy_bitcast_fusion.3
  1.6 2.6 %fusion.2 = bf16[1024,512]{1,0:T(8,128)(2,1)} fusion(bf16[1,64,16,1,512]{4,2,3,1,0:T(8,128)(2,1)} %param.24, f32[16,512]{1,0:T(8,128)S(1)} %get-tuple-element.74), kind=kLoop, calls=%fused_computation.6 | loop fusion | flops 1572864 | bytes 2129920 | tf_op jit(solution)/shard_map/convert_element_type | solution.py:81
  4.1 4.3 %collective-permute-start.5 = (bf16[1024,512]{1,0:T(8,128)(2,1)}, bf16[1024,512]{1,0:T(8,128)(2,1)S(1)}, u32[]{:S(2)}, u32[]{:S(2)}) collective-permute-start(bf16[1024,512]{1,0:T(8,128)(2,1)} %fusion.2), channel_id=1, source_target_pairs={{60,0},{62,2},{0,4},{2,6},{4,8},{6,10},{8,12},{10,14},{12,16},{14,... | collective-permute-start | bytes 3145736 | tf_op jit(solution)/shard_map/ppermute | solution.py:11
  8.4 7.7 %collective-permute-start.4 = (bf16[1024,512]{1,0:T(8,128)(2,1)}, bf16[1024,512]{1,0:T(8,128)(2,1)}, u32[]{:S(2)}, u32[]{:S(2)}) collective-permute-start(bf16[1024,512]{1,0:T(8,128)(2,1)} %fusion.2), channel_id=1, source_target_pairs={{4,0},{6,2},{8,4},{10,6},{12,8},{14,10},{16,12},{18,14},{20,16},{2... | collective-permute-start | bytes 3145736 | tf_op jit(solution)/shard_map/ppermute | solution.py:11
  16.1 0.7 multiply_reduce_fusion.2
  16.8 0.7 multiply_reduce_fusion
  17.5 0.7 multiply_reduce_fusion.1
  18.2 0.7 multiply_reduce_fusion.3
  20.8 0.7 multiply_reduce_fusion.4
  23.5 3.5 %collective-permute-start = (f32[2]{0:T(128)S(1)}, f32[2]{0:T(128)S(1)}, u32[]{:S(2)}, u32[]{:S(2)}) collective-permute-start(f32[2]{0:T(128)S(1)} %pad_maximum_fusion.6), channel_id=1, source_target_pairs={{0,64},{64,0},{128,192},{192,128},{256,320},{320,256},{384,448},{4... | collective-permute-start | bytes 32 | tf_op jit(solution)/shard_map/ppermute | solution.py:25
  27.0 0.7 pad_maximum_fusion.5
  27.7 1.9 collective-permute-start.17
  29.6 7.6 %collective-permute-start.18 = (f32[7,16,2]{2,1,0:T(8,128)}, f32[7,16,2]{2,1,0:T(8,128)}, u32[]{:S(2)}, u32[]{:S(2)}) collective-permute-start(f32[7,16,2]{2,1,0:T(8,128)} %get-tuple-element.55), channel_id=1, source_target_pairs={{2,0},{4,2},{6,4},{8,6},{10,8},{12,10},{14,12},{16,14},{18,16},{20... | collective-permute-start | bytes 2696 | tf_op jit(solution)/shard_map/ppermute | solution.py:11
  37.3 0.6 bitcast_reduce_fusion
  39.1 0.7 bitcast_reduce_fusion.6
  41.0 0.7 bitcast_reduce_fusion.5
  43.0 0.7 bitcast_reduce_fusion.4
  45.1 0.6 bitcast_reduce_fusion.3
  46.9 0.7 bitcast_reduce_fusion.2
  48.8 0.8 compare_reduce_fusion
  49.6 0.7 bitcast_reduce_fusion.1
  51.7 0.6 fusion.100
  52.4 0.7 fusion.81
  53.1 0.6 pad_maximum_fusion.3
  58.4 2.4 %fusion.17 = f32[1024,512]{1,0:T(8,128)S(1)} fusion(bf16[1024,512]{1,0:T(8,128)(2,1)S(1)} %bitcast.134, bf16[1,5,512,512]{3,2,1,0:T(8,128)(2,1)} %param.29, s32[]{:T(128)S(6)} %select_n.184, pred[]{:T(512)} %get-tuple-element.35), kind=kOutput, calls=%fused_computation.20 | convolution fusion | flops 537133056 | bytes 3670532 | tf_op jit(solution)/shard_map/dot_general | solution.py:111
  60.9 3.8 %collective-permute-start.1 = (f32[2]{0:T(128)S(1)}, f32[2]{0:T(128)S(1)}, u32[]{:S(2)}, u32[]{:S(2)}) collective-permute-start(f32[2]{0:T(128)S(1)} %fusion.109), channel_id=1, source_target_pairs={{0,128},{64,192},{128,0},{192,64},{256,384},{320,448},{384,256},{4... | collective-permute-start | bytes 32 | tf_op jit(solution)/shard_map/ppermute | solution.py:25
  64.7 2.5 %collective-permute-done.1 = f32[2]{0:T(128)S(1)} collective-permute-done((f32[2]{0:T(128)S(1)}, f32[2]{0:T(128)S(1)}, u32[]{:S(2)}, u32[]{:S(2)}) %collective-permute-start.1) | collective-permute-done | bytes 40 | tf_op jit(solution)/shard_map/ppermute | solution.py:25
  67.3 5.0 %collective-permute-start.2 = (f32[2]{0:T(128)S(1)}, f32[2]{0:T(128)S(1)}, u32[]{:S(2)}, u32[]{:S(2)}) collective-permute-start(f32[2]{0:T(128)S(1)} %fusion.110), channel_id=1, source_target_pairs={{0,256},{64,320},{128,384},{192,448},{256,0},{320,64},{384,128},{4... | collective-permute-start | bytes 32 | tf_op jit(solution)/shard_map/ppermute | solution.py:25
  72.3 4.3 %collective-permute-done.2 = f32[2]{0:T(128)S(1)} collective-permute-done((f32[2]{0:T(128)S(1)}, f32[2]{0:T(128)S(1)}, u32[]{:S(2)}, u32[]{:S(2)}) %collective-permute-start.2) | collective-permute-done | bytes 40 | tf_op jit(solution)/shard_map/ppermute | solution.py:25
  76.6 1.9 collective-permute-start.8
  78.6 7.0 %collective-permute-start.10 = (bf16[6,16,2]{2,1,0:T(8,128)(2,1)S(1)}, bf16[6,16,2]{2,1,0:T(8,128)(2,1)S(1)}, u32[]{:S(2)}, u32[]{:S(2)}) collective-permute-start(bf16[6,16,2]{2,1,0:T(8,128)(2,1)S(1)} %copy-done.21), channel_id=1, source_target_pairs={{0,63},{1,62},{2,1},{3,0},{4,3},{5,2},{6,5},{7,4},{8,7},{9,6},{10,... | collective-permute-start | bytes 1160 | tf_op jit(solution)/shard_map/ppermute | solution.py:158
  85.6 8.7 %collective-permute-start.9 = (bf16[6,16,512]{2,1,0:T(8,128)(2,1)S(1)}, bf16[6,16,512]{2,1,0:T(8,128)(2,1)S(1)}, u32[]{:S(2)}, u32[]{:S(2)}) collective-permute-start(bf16[6,16,512]{2,1,0:T(8,128)(2,1)S(1)} %copy-done.15), channel_id=1, source_target_pairs={{0,1},{1,0},{2,3},{3,2},{4,5},{5,4},{6,7},{7,6},{8,9},{9,8},{10,11... | collective-permute-start | bytes 294920 | tf_op jit(solution)/shard_map/ppermute | solution.py:37
  94.2 1.0 pad_maximum_fusion.1
  95.5 1.9 collective-permute-start.6
  97.5 1.9 collective-permute-start.3
  100.1 1.5 pad_maximum_fusion
  101.6 2.4 %collective-permute-start.7 = (bf16[2048,512]{1,0:T(8,128)(2,1)S(1)}, bf16[2048,512]{1,0:T(8,128)(2,1)S(1)}, u32[]{:S(2)}, u32[]{:S(2)}) collective-permute-start(bf16[2048,512]{1,0:T(8,128)(2,1)S(1)} %pad_maximum_fusion), channel_id=1, source_target_pairs={{0,2},{2,0},{4,6},{6,4},{8,10},{10,8},{12,14},{14,12},{16,18},{18,... | collective-permute-start | bytes 6291464 | tf_op jit(solution)/shard_map/ppermute | solution.py:94
  104.3 1.9 collective-permute-start.20
  106.5 3.9 %collective-permute-start.19 = (bf16[16,512]{1,0:T(8,128)(2,1)S(1)}, bf16[16,512]{1,0:T(8,128)(2,1)S(1)}, u32[]{:S(2)}, u32[]{:S(2)}) collective-permute-start(bf16[16,512]{1,0:T(8,128)(2,1)S(1)} %fusion.67), channel_id=1, source_target_pairs={{0,64},{64,128},{128,192},{192,256},{256,320},{320,384},{384,448},... | collective-permute-start | bytes 49160 | tf_op jit(solution)/shard_map/ppermute | solution.py:17
  110.4 31.0 %collective-permute-done.6 = bf16[1024,512]{1,0:T(8,128)(2,1)S(1)} collective-permute-done((bf16[1024,512]{1,0:T(8,128)(2,1)}, bf16[1024,512]{1,0:T(8,128)(2,1)S(1)}, u32[]{:S(2)}, u32[]{:S(2)}) %collective-permute-start.6) | collective-permute-done | bytes 1048608 | tf_op jit(solution)/shard_map/ppermute | solution.py:93
  141.5 1.9 collective-permute-start.11
  143.4 1.4 fusion.15
  144.8 2.6 %fusion.13 = f32[1024,512]{1,0:T(8,128)S(1)} fusion(bf16[1024,512]{1,0:T(8,128)(2,1)} %collective-permute-done.4, bf16[1,5,512,512]{3,2,1,0:T(8,128)(2,1)S(1)} %copy-done.1, s32[]{:T(128)S(6)} %select_n.196, pred[]{:T(512)} %get-tuple-element.33), kind=kOutput, calls=%fused_computation.16 | convolution fusion | flops 537133056 | bytes 3670021 | tf_op jit(solution)/shard_map/dot_general | solution.py:113
  147.4 1.3 fusion.9
  148.8 1.4 fusion.11
  150.1 1.9 collective-permute-start.12
  152.1 3.5 %collective-permute-done.12 = f32[2]{0:T(128)S(1)} collective-permute-done((f32[2]{0:T(128)S(1)}, f32[2]{0:T(128)S(1)}, u32[]{:S(2)}, u32[]{:S(2)}) %collective-permute-start.12) | collective-permute-done | bytes 40 | tf_op jit(solution)/shard_map/ppermute | solution.py:25
  155.6 1.9 collective-permute-start.13
  157.5 4.4 %collective-permute-done.13 = f32[2]{0:T(128)S(1)} collective-permute-done((f32[2]{0:T(128)S(1)}, f32[2]{0:T(128)S(1)}, u32[]{:S(2)}, u32[]{:S(2)}) %collective-permute-start.13) | collective-permute-done | bytes 40 | tf_op jit(solution)/shard_map/ppermute | solution.py:25
  161.9 1.9 collective-permute-start.14
  163.8 3.5 %collective-permute-done.14 = f32[2]{0:T(128)S(1)} collective-permute-done((f32[2]{0:T(128)S(1)}, f32[2]{0:T(128)S(1)}, u32[]{:S(2)}, u32[]{:S(2)}) %collective-permute-start.14) | collective-permute-done | bytes 40 | tf_op jit(solution)/shard_map/ppermute | solution.py:25
  167.3 2.7 %collective-permute-start.15 = (f32[2]{0:T(128)S(1)}, f32[2]{0:T(128)S(1)}, u32[]{:S(2)}, u32[]{:S(2)}) collective-permute-start(f32[2]{0:T(128)S(1)} %add.249), channel_id=1, source_target_pairs={{0,32},{2,34},{4,36},{6,38},{8,40},{10,42},{12,44},{14,46},{16,48}... | collective-permute-start | bytes 32 | tf_op jit(solution)/shard_map/ppermute | solution.py:25
  170.1 4.2 %collective-permute-done.15 = f32[2]{0:T(128)S(1)} collective-permute-done((f32[2]{0:T(128)S(1)}, f32[2]{0:T(128)S(1)}, u32[]{:S(2)}, u32[]{:S(2)}) %collective-permute-start.15) | collective-permute-done | bytes 40 | tf_op jit(solution)/shard_map/ppermute | solution.py:25
  174.3 4.4 %collective-permute-start.16 = (f32[2]{0:T(128)S(1)}, f32[2]{0:T(128)S(1)}, u32[]{:S(2)}, u32[]{:S(2)}) collective-permute-start(f32[2]{0:T(128)S(1)} %add.250), channel_id=1, source_target_pairs={{0,1},{1,0},{2,3},{3,2},{4,5},{5,4},{6,7},{7,6},{8,9},{9,8},{10,11... | collective-permute-start | bytes 32 | tf_op jit(solution)/shard_map/ppermute | solution.py:25
  178.7 4.9 %collective-permute-done.16 = f32[2]{0:T(128)S(1)} collective-permute-done((f32[2]{0:T(128)S(1)}, f32[2]{0:T(128)S(1)}, u32[]{:S(2)}, u32[]{:S(2)}) %collective-permute-start.16) | collective-permute-done | bytes 40 | tf_op jit(solution)/shard_map/ppermute | solution.py:25
  183.6 0.6 fusion.103
  185.5 0.6 copy.40
  186.2 0.7 fusion.80
  186.9 1.3 fusion.7
  188.2 1.6 add_add_fusion
  190.7 0.6 copy.44
  191.3 0.6 copy.42
  192.0 0.6 copy.43
  192.6 0.6 copy.41
  (93 shorter events, 2.9 us)
Async XLA Ops:
  0.6 15.5 %copy-start.3 = (f32[1,16,1,512]{3,2,1,0:T(1,128)S(1)}, f32[1,16,1,512]{3,2,1,0:T(1,128)}, u32[]{:S(2)}) copy-start(f32[1,16,1,512]{3,2,1,0:T(1,128)} %param.21) | copy-start | bytes 98308
  0.6 16.2 %copy-start.4 = (f32[1,16,1,512]{3,2,1,0:T(1,128)S(1)}, f32[1,16,1,512]{3,2,1,0:T(1,128)}, u32[]{:S(2)}) copy-start(f32[1,16,1,512]{3,2,1,0:T(1,128)} %param.23) | copy-start | bytes 98308
  0.7 16.8 %copy-start.5 = (f32[1,16,1,512]{3,2,1,0:T(1,128)S(1)}, f32[1,16,1,512]{3,2,1,0:T(1,128)}, u32[]{:S(2)}) copy-start(f32[1,16,1,512]{3,2,1,0:T(1,128)} %param.22) | copy-start | bytes 98308
  0.7 17.5 %copy-start.8 = (f32[1,16,1,512]{3,2,1,0:T(1,128)S(1)}, f32[1,16,1,512]{3,2,1,0:T(1,128)}, u32[]{:S(2)}) copy-start(f32[1,16,1,512]{3,2,1,0:T(1,128)} %param.20) | copy-start | bytes 98308
  0.7 20.1 %copy-start.10 = (f32[1,16,1,512]{3,2,1,0:T(1,128)S(1)}, f32[1,16,1,512]{3,2,1,0:T(1,128)}, u32[]{:S(2)}) copy-start(f32[1,16,1,512]{3,2,1,0:T(1,128)} %param.19) | copy-start | bytes 98308
  0.7 20.1 %copy-start.12 = (f32[1,16,1,512]{3,2,1,0:T(1,128)S(1)}, f32[1,16,1,512]{3,2,1,0:T(1,128)}, u32[]{:S(2)}) copy-start(f32[1,16,1,512]{3,2,1,0:T(1,128)} %param.18) | copy-start | bytes 98308
  0.7 26.3 %copy-start.2 = (f32[1,5,16,1,512]{4,3,2,1,0:T(1,128)S(1)}, f32[1,5,16,1,512]{4,3,2,1,0:T(1,128)}, u32[]{:S(2)}) copy-start(f32[1,5,16,1,512]{4,3,2,1,0:T(1,128)} %param.25) | copy-start | bytes 491524
  0.7 36.6 %copy-start.17 = (s32[1,5]{1,0:T(1,128)S(1)}, s32[1,5]{1,0:T(1,128)}, u32[]{:S(2)}) copy-start(s32[1,5]{1,0:T(1,128)} %param.28) | copy-start | bytes 64
  1.6 52.2 %copy-start = (bf16[1,64,16,1,512]{4,2,3,1,0:T(8,128)(2,1)S(1)}, bf16[1,64,16,1,512]{4,2,3,1,0:T(8,128)(2,1)}, u32[]{:S(2)}) copy-start(bf16[1,64,16,1,512]{4,2,3,1,0:T(8,128)(2,1)} %param.24) | copy-start | bytes 3145732
  4.1 95.9 %collective-permute-start.5 = (bf16[1024,512]{1,0:T(8,128)(2,1)}, bf16[1024,512]{1,0:T(8,128)(2,1)S(1)}, u32[]{:S(2)}, u32[]{:S(2)}) collective-permute-start(bf16[1024,512]{1,0:T(8,128)(2,1)} %fusion.2), channel_id=1, source_target_pairs={{60,0},{62,2},{0,4},{2,6},{4,8},{6,10},{8,12},{10,14},{12,16},{14,... | collective-permute-start | bytes 3145736 | tf_op jit(solution)/shard_map/ppermute | solution.py:11
  8.4 91.7 %collective-permute-start.4 = (bf16[1024,512]{1,0:T(8,128)(2,1)}, bf16[1024,512]{1,0:T(8,128)(2,1)}, u32[]{:S(2)}, u32[]{:S(2)}) collective-permute-start(bf16[1024,512]{1,0:T(8,128)(2,1)} %fusion.2), channel_id=1, source_target_pairs={{4,0},{6,2},{8,4},{10,6},{12,8},{14,10},{16,12},{18,14},{20,16},{2... | collective-permute-start | bytes 3145736 | tf_op jit(solution)/shard_map/ppermute | solution.py:11
  23.5 37.3 %collective-permute-start = (f32[2]{0:T(128)S(1)}, f32[2]{0:T(128)S(1)}, u32[]{:S(2)}, u32[]{:S(2)}) collective-permute-start(f32[2]{0:T(128)S(1)} %pad_maximum_fusion.6), channel_id=1, source_target_pairs={{0,64},{64,0},{128,192},{192,128},{256,320},{320,256},{384,448},{4... | collective-permute-start | bytes 32 | tf_op jit(solution)/shard_map/ppermute | solution.py:25
  27.7 50.9 %collective-permute-start.17 = (f32[7,16,2]{2,1,0:T(8,128)}, f32[7,16,2]{2,1,0:T(8,128)}, u32[]{:S(2)}, u32[]{:S(2)}) collective-permute-start(f32[7,16,2]{2,1,0:T(8,128)} %get-tuple-element.54), channel_id=1, source_target_pairs={{62,0},{0,2},{2,4},{4,6},{6,8},{8,10},{10,12},{12,14},{14,16},{16,... | collective-permute-start | bytes 2696 | tf_op jit(solution)/shard_map/ppermute | solution.py:11
  29.6 55.9 %collective-permute-start.18 = (f32[7,16,2]{2,1,0:T(8,128)}, f32[7,16,2]{2,1,0:T(8,128)}, u32[]{:S(2)}, u32[]{:S(2)}) collective-permute-start(f32[7,16,2]{2,1,0:T(8,128)} %get-tuple-element.55), channel_id=1, source_target_pairs={{2,0},{4,2},{6,4},{8,6},{10,8},{12,10},{14,12},{16,14},{18,16},{20... | collective-permute-start | bytes 2696 | tf_op jit(solution)/shard_map/ppermute | solution.py:11
  58.4 18.3 %copy-start.22 = (bf16[6,16,2]{2,1,0:T(8,128)(2,1)S(1)}, bf16[6,16,2]{2,1,0:T(8,128)(2,1)}, u32[]{:S(2)}) copy-start(bf16[6,16,2]{2,1,0:T(8,128)(2,1)} %get-tuple-element.61) | copy-start | bytes 1156
  58.4 20.2 %copy-start.21 = (bf16[6,16,2]{2,1,0:T(8,128)(2,1)S(1)}, bf16[6,16,2]{2,1,0:T(8,128)(2,1)}, u32[]{:S(2)}) copy-start(bf16[6,16,2]{2,1,0:T(8,128)(2,1)} %get-tuple-element.62) | copy-start | bytes 1156
  58.4 27.2 %copy-start.15 = (bf16[6,16,512]{2,1,0:T(8,128)(2,1)S(1)}, bf16[6,16,512]{2,1,0:T(8,128)(2,1)}, u32[]{:S(2)}) copy-start(bf16[6,16,512]{2,1,0:T(8,128)(2,1)} %pad_maximum_fusion.3) | copy-start | bytes 294916
  60.9 6.3 %collective-permute-start.1 = (f32[2]{0:T(128)S(1)}, f32[2]{0:T(128)S(1)}, u32[]{:S(2)}, u32[]{:S(2)}) collective-permute-start(f32[2]{0:T(128)S(1)} %fusion.109), channel_id=1, source_target_pairs={{0,128},{64,192},{128,0},{192,64},{256,384},{320,448},{384,256},{4... | collective-permute-start | bytes 32 | tf_op jit(solution)/shard_map/ppermute | solution.py:25
  67.3 9.3 %collective-permute-start.2 = (f32[2]{0:T(128)S(1)}, f32[2]{0:T(128)S(1)}, u32[]{:S(2)}, u32[]{:S(2)}) collective-permute-start(f32[2]{0:T(128)S(1)} %fusion.110), channel_id=1, source_target_pairs={{0,256},{64,320},{128,384},{192,448},{256,0},{320,64},{384,128},{4... | collective-permute-start | bytes 32 | tf_op jit(solution)/shard_map/ppermute | solution.py:25
  76.6 18.9 %collective-permute-start.8 = (bf16[6,16,2]{2,1,0:T(8,128)(2,1)S(1)}, bf16[6,16,2]{2,1,0:T(8,128)(2,1)S(1)}, u32[]{:S(2)}, u32[]{:S(2)}) collective-permute-start(bf16[6,16,2]{2,1,0:T(8,128)(2,1)S(1)} %copy-done.22), channel_id=1, source_target_pairs={{0,3},{1,2},{2,5},{3,4},{4,7},{5,6},{6,9},{7,8},{8,11},{9,10},{10,... | collective-permute-start | bytes 1160 | tf_op jit(solution)/shard_map/ppermute | solution.py:157
  78.6 18.9 %collective-permute-start.10 = (bf16[6,16,2]{2,1,0:T(8,128)(2,1)S(1)}, bf16[6,16,2]{2,1,0:T(8,128)(2,1)S(1)}, u32[]{:S(2)}, u32[]{:S(2)}) collective-permute-start(bf16[6,16,2]{2,1,0:T(8,128)(2,1)S(1)} %copy-done.21), channel_id=1, source_target_pairs={{0,63},{1,62},{2,1},{3,0},{4,3},{5,2},{6,5},{7,4},{8,7},{9,6},{10,... | collective-permute-start | bytes 1160 | tf_op jit(solution)/shard_map/ppermute | solution.py:158
  85.6 13.8 %collective-permute-start.9 = (bf16[6,16,512]{2,1,0:T(8,128)(2,1)S(1)}, bf16[6,16,512]{2,1,0:T(8,128)(2,1)S(1)}, u32[]{:S(2)}, u32[]{:S(2)}) collective-permute-start(bf16[6,16,512]{2,1,0:T(8,128)(2,1)S(1)} %copy-done.15), channel_id=1, source_target_pairs={{0,1},{1,0},{2,3},{3,2},{4,5},{5,4},{6,7},{7,6},{8,9},{9,8},{10,11... | collective-permute-start | bytes 294920 | tf_op jit(solution)/shard_map/ppermute | solution.py:37
  95.5 46.0 %collective-permute-start.6 = (bf16[1024,512]{1,0:T(8,128)(2,1)}, bf16[1024,512]{1,0:T(8,128)(2,1)S(1)}, u32[]{:S(2)}, u32[]{:S(2)}) collective-permute-start(bf16[1024,512]{1,0:T(8,128)(2,1)} %fusion.2), channel_id=1, source_target_pairs={{0,58},{2,8},{4,62},{6,12},{8,2},{10,16},{12,6},{14,20},{16,10},{1... | collective-permute-start | bytes 3145736 | tf_op jit(solution)/shard_map/ppermute | solution.py:93
  97.5 44.0 %collective-permute-start.3 = (bf16[1024,512]{1,0:T(8,128)(2,1)}, bf16[1024,512]{1,0:T(8,128)(2,1)S(1)}, u32[]{:S(2)}, u32[]{:S(2)}) collective-permute-start(bf16[1024,512]{1,0:T(8,128)(2,1)} %fusion.2), channel_id=1, source_target_pairs={{0,2},{2,0},{4,6},{6,4},{8,10},{10,8},{12,14},{14,12},{16,18},{18,... | collective-permute-start | bytes 3145736 | tf_op jit(solution)/shard_map/ppermute | solution.py:90
  100.0 6.3 %copy-start.6 = (f32[1,1,16,1,512]{4,3,2,1,0:T(1,128)S(1)}, f32[1,1,16,1,512]{4,3,2,1,0:T(1,128)}, u32[]{:S(2)}) copy-start(f32[1,1,16,1,512]{4,3,2,1,0:T(1,128)} %get-tuple-element.57) | copy-start | bytes 98308
  100.0 6.3 %copy-start.7 = (f32[1,1,16,1,512]{4,3,2,1,0:T(1,128)S(1)}, f32[1,1,16,1,512]{4,3,2,1,0:T(1,128)}, u32[]{:S(2)}) copy-start(f32[1,1,16,1,512]{4,3,2,1,0:T(1,128)} %get-tuple-element.58) | copy-start | bytes 98308
  100.0 43.4 %copy-start.1 = (bf16[1,5,512,512]{3,2,1,0:T(8,128)(2,1)S(1)}, bf16[1,5,512,512]{3,2,1,0:T(8,128)(2,1)}, u32[]{:S(2)}) copy-start(bf16[1,5,512,512]{3,2,1,0:T(8,128)(2,1)} %param.29) | copy-start | bytes 7864324
  101.6 85.3 %collective-permute-start.7 = (bf16[2048,512]{1,0:T(8,128)(2,1)S(1)}, bf16[2048,512]{1,0:T(8,128)(2,1)S(1)}, u32[]{:S(2)}, u32[]{:S(2)}) collective-permute-start(bf16[2048,512]{1,0:T(8,128)(2,1)S(1)} %pad_maximum_fusion), channel_id=1, source_target_pairs={{0,2},{2,0},{4,6},{6,4},{8,10},{10,8},{12,14},{14,12},{16,18},{18,... | collective-permute-start | bytes 6291464 | tf_op jit(solution)/shard_map/ppermute | solution.py:94
  104.3 6.1 %collective-permute-start.20 = (bf16[16,512]{1,0:T(8,128)(2,1)S(1)}, bf16[16,512]{1,0:T(8,128)(2,1)S(1)}, u32[]{:S(2)}, u32[]{:S(2)}) collective-permute-start(bf16[16,512]{1,0:T(8,128)(2,1)S(1)} %fusion.59), channel_id=1, source_target_pairs={{64,0},{128,64},{192,128},{256,192},{320,256},{384,320},{448,384},... | collective-permute-start | bytes 49160 | tf_op jit(solution)/shard_map/ppermute | solution.py:17
  106.5 83.8 %collective-permute-start.19 = (bf16[16,512]{1,0:T(8,128)(2,1)S(1)}, bf16[16,512]{1,0:T(8,128)(2,1)S(1)}, u32[]{:S(2)}, u32[]{:S(2)}) collective-permute-start(bf16[16,512]{1,0:T(8,128)(2,1)S(1)} %fusion.67), channel_id=1, source_target_pairs={{0,64},{64,128},{128,192},{192,256},{256,320},{320,384},{384,448},... | collective-permute-start | bytes 49160 | tf_op jit(solution)/shard_map/ppermute | solution.py:17
  141.5 8.7 %collective-permute-start.11 = (f32[2]{0:T(128)S(1)}, f32[2]{0:T(128)S(1)}, u32[]{:S(2)}, u32[]{:S(2)}) collective-permute-start(f32[2]{0:T(128)S(1)} %add.245), channel_id=1, source_target_pairs={{0,2},{2,0},{4,6},{6,4},{8,10},{10,8},{12,14},{14,12},{16,18},{18,... | collective-permute-start | bytes 32 | tf_op jit(solution)/shard_map/ppermute | solution.py:25
  148.7 36.8 %copy-start.16 = (f32[1,16,1,512]{3,2,1,0:T(1,128)S(1)}, f32[1,16,1,512]{3,2,1,0:T(1,128)}, u32[]{:S(2)}) copy-start(f32[1,16,1,512]{3,2,1,0:T(1,128)} %param.15) | copy-start | bytes 98308
  148.7 37.4 %copy-start.9 = (f32[1,16,1,512]{3,2,1,0:T(1,128)S(1)}, f32[1,16,1,512]{3,2,1,0:T(1,128)}, u32[]{:S(2)}) copy-start(f32[1,16,1,512]{3,2,1,0:T(1,128)} %param.20) | copy-start | bytes 98308
  148.8 37.4 %copy-start.14 = (f32[1,16,1,512]{3,2,1,0:T(1,128)S(1)}, f32[1,16,1,512]{3,2,1,0:T(1,128)}, u32[]{:S(2)}) copy-start(f32[1,16,1,512]{3,2,1,0:T(1,128)} %param.26) | copy-start | bytes 98308
  150.1 5.4 %collective-permute-start.12 = (f32[2]{0:T(128)S(1)}, f32[2]{0:T(128)S(1)}, u32[]{:S(2)}, u32[]{:S(2)}) collective-permute-start(f32[2]{0:T(128)S(1)} %add.246), channel_id=1, source_target_pairs={{0,4},{2,6},{4,0},{6,2},{8,12},{10,14},{12,8},{14,10},{16,20},{18,... | collective-permute-start | bytes 32 | tf_op jit(solution)/shard_map/ppermute | solution.py:25
  155.6 6.3 %collective-permute-start.13 = (f32[2]{0:T(128)S(1)}, f32[2]{0:T(128)S(1)}, u32[]{:S(2)}, u32[]{:S(2)}) collective-permute-start(f32[2]{0:T(128)S(1)} %add.247), channel_id=1, source_target_pairs={{0,8},{2,10},{4,12},{6,14},{8,0},{10,2},{12,4},{14,6},{16,24},{18,... | collective-permute-start | bytes 32 | tf_op jit(solution)/shard_map/ppermute | solution.py:25
  161.9 5.4 %collective-permute-start.14 = (f32[2]{0:T(128)S(1)}, f32[2]{0:T(128)S(1)}, u32[]{:S(2)}, u32[]{:S(2)}) collective-permute-start(f32[2]{0:T(128)S(1)} %add.248), channel_id=1, source_target_pairs={{0,16},{2,18},{4,20},{6,22},{8,24},{10,26},{12,28},{14,30},{16,0},... | collective-permute-start | bytes 32 | tf_op jit(solution)/shard_map/ppermute | solution.py:25
  167.3 6.9 %collective-permute-start.15 = (f32[2]{0:T(128)S(1)}, f32[2]{0:T(128)S(1)}, u32[]{:S(2)}, u32[]{:S(2)}) collective-permute-start(f32[2]{0:T(128)S(1)} %add.249), channel_id=1, source_target_pairs={{0,32},{2,34},{4,36},{6,38},{8,40},{10,42},{12,44},{14,46},{16,48}... | collective-permute-start | bytes 32 | tf_op jit(solution)/shard_map/ppermute | solution.py:25
  174.3 9.3 %collective-permute-start.16 = (f32[2]{0:T(128)S(1)}, f32[2]{0:T(128)S(1)}, u32[]{:S(2)}, u32[]{:S(2)}) collective-permute-start(f32[2]{0:T(128)S(1)} %add.250), channel_id=1, source_target_pairs={{0,1},{1,0},{2,3},{3,2},{4,5},{5,4},{6,7},{7,6},{8,9},{9,8},{10,11... | collective-permute-start | bytes 32 | tf_op jit(solution)/shard_map/ppermute | solution.py:25
  189.8 0.8 copy-start.11
  189.8 0.8 copy-start.13
  189.9 0.8 copy-start.18
  189.9 0.8 copy-start.19
  189.9 0.8 copy-start.20

commit v13 on v10

--- a/solution.py
+++ b/solution.py
@@ -75,7 +75,7 @@
     return jnp.where(first_row, coefs[3], coefs[4])
 
 
-def localize(members, search, loc_cols, loc_vals, partials):
+def localize(members, search, loc_cols, loc_vals, partials, own):
     count_members = members.shape[0]
     block = members.shape[-1]
     products = (members.astype(jnp.float32) * search[None]).astype(jnp.bfloat16)
@@ -107,12 +107,12 @@
         picked = tiles[jnp.argmax(match)]
         return jnp.where(jnp.any(match), picked, jnp.zeros_like(picked))
 
-    partials, _ = lax.optimization_barrier((partials, [value for value, _ in received]))
+    partials, own, _ = lax.optimization_barrier((partials, own, [value for value, _ in received]))
     total = jnp.dot(flat, weight_for(0), preferred_element_type=jnp.float32)
     for value, offset in received:
         total = total + jnp.dot(value, weight_for(offset), preferred_element_type=jnp.float32)
     spread = total.reshape(products.shape)
-    return jnp.sum(members.astype(jnp.float32) * spread, axis=0) / (count_members - 1), partials
+    return jnp.sum(members.astype(jnp.float32) * spread, axis=0) / (count_members - 1), partials, own
 
 
 def local(
@@ -148,20 +148,21 @@
     )
     own = lon_extended(packed, 2)
     first_row = lax.axis_index("lat") == 0
-    other = lat_partner(jnp.concatenate([own[:5], coupling(own[2:], first_row)[None]]))
-    moved, backed = propagate_both(own, other, first_row)
-    earlier = shifted(moved.astype(jnp.bfloat16), "win", 1).astype(jnp.float32)[None, :, None]
-    following = shifted(backed.astype(jnp.bfloat16), "win", -1).astype(jnp.float32)[None, :, None]
-
-    covar, partials = localize(
+    covar, partials, own = localize(
         ensemble[0, :, :, 0],
         search_dual[0, :, 0],
         loc_cols,
         loc_vals,
         butterfly_sum(jnp.stack([resid_local, search_local]), ("win",)),
+        own,
     )
     covar = covar[None, :, None]
-    partials, _ = lax.optimization_barrier((partials, other))
+    other = lat_partner(
+        jnp.concatenate([own[:5], coupling(own[2:], first_row)[None]]).astype(jnp.bfloat16)
+    ).astype(jnp.float32)
+    moved, backed = propagate_both(own, other, first_row)
+    earlier = shifted(moved.astype(jnp.bfloat16), "win", 1).astype(jnp.float32)[None, :, None]
+    following = shifted(backed.astype(jnp.bfloat16), "win", -1).astype(jnp.float32)[None, :, None]
     sums = butterfly_sum(partials, ("lon", "lat"))
     alpha = sums[0] / (sums[1] + 1e-06)
     image_dual = covar + search_incr - earlier

time: 190 us -> 194 us (1.021)
  matrix products: 11.9 us -> 15.9 us
  starting transfers between devices: 95 us -> 91.8 us
  other arithmetic: 15.6 us -> 18.3 us
    ppermute x1, waiting for transfers between devices: 21.4 us -> 0.01 us  [lat_partner(): return lax.ppermute(value, 'lat', [(0, 1), (1, 0)])]
    ppermute x4, waiting for transfers between devices: 0.01 us -> 17.1 us  [from_offset(): lax.ppermute(value, axis, [((i + distance) % count, i) for i in range(cou...]
    ppermute x9, waiting for transfers between devices: 18.6 us -> 24.3 us  [butterfly_sum(): lax.ppermute(value, axis, [(i, i ^ step) for i in range(count)])]
    dot_general x6, matrix products: 9.54 us -> 13.2 us  [localize(): jnp.dot(value, weight_for(offset), preferred_element_type=jnp.float32)]
    ppermute x4, starting transfers between devices: 14.4 us -> 12.4 us  [from_offset(): lax.ppermute(value, axis, [((i + distance) % count, i) for i in range(cou...]
    unnamed x47 -> x40, local copies, waits for them, and re-layouts: 4.61 us -> 4.55 us
  transfers between devices with their start and end apart: 19 -> 19, of which waited for: 8 -> 8; matrix products, arithmetic and copies ran while one was open for 15% -> 17% of each run, Pallas kernels for 0% -> 0%
where the time goes in v13:
time: 194 us; the launch traced here: 193 us
  starting transfers between devices  91.8 us (47%)
  waiting for transfers between devices  41.4 us (21%)
  between operations  19.8 us (10%)
  other arithmetic  18.3 us (9%)
  matrix products  15.9 us (8%)
  local copies, waits for them, and re-layouts  5.7 us (3%)
    ppermute x9, starting transfers between devices, butterfly_sum(): lax.ppermute(value, axis, [(i, i ^ step) for i in range(count)])  53.3 us
    ppermute x9, waiting for transfers between devices, butterfly_sum(): lax.ppermute(value, axis, [(i, i ^ step) for i in range(count)])  24.3 us
    ppermute x4, waiting for transfers between devices, from_offset(): lax.ppermute(value, axis, [((i + distance) % count, i) for i in range(cou...  17.1 us
    dot_general x6, matrix products, localize(): jnp.dot(value, weight_for(offset), preferred_element_type=jnp.float32)  13.2 us
    ppermute x4, starting transfers between devices, from_offset(): lax.ppermute(value, axis, [((i + distance) % count, i) for i in range(cou...  12.4 us
    ppermute x1, starting transfers between devices, lat_partner(): return lax.ppermute(value, 'lat', [(0, 1), (1, 0)])  9.45 us
    ppermute x2, starting transfers between devices, shifted(): lax.ppermute(value, axis, [(source, source + steps) for source in range(l...  7.05 us
    ppermute x1, starting transfers between devices, localize(): lax.ppermute(flat, 'lon', [(s, (s + 3) % bands if s % 2 else (s - 3) % ba...  5.78 us
  transfers between devices with their start and end apart: 19, of which 8 were waited for; matrix products, arithmetic and copies ran while one was open for 17% of the time, Pallas kernels for 0%

profile of v13, /device:TPU:30, one launch (start us, length us, event | category | flops | bytes accessed | tf_op | source)
XLA Modules:
  0.0 192.9 jit_solution(5244851392656492848)
XLA Ops:
  0.7 0.8 copy.70
  1.6 2.5 %fusion.2 = bf16[1024,512]{1,0:T(8,128)(2,1)} fusion(bf16[1,64,16,1,512]{4,2,3,1,0:T(8,128)(2,1)} %param.24, f32[16,512]{1,0:T(8,128)S(1)} %bitcast.131), kind=kLoop, calls=%fused_computation.6 | loop fusion | flops 1572864 | bytes 2129920 | tf_op jit(solution)/shard_map/convert_element_type | solution.py:81
  4.0 5.8 %collective-permute-start.8 = (bf16[1024,512]{1,0:T(8,128)(2,1)}, bf16[1024,512]{1,0:T(8,128)(2,1)}, u32[]{:S(2)}, u32[]{:S(2)}) collective-permute-start(bf16[1024,512]{1,0:T(8,128)(2,1)} %fusion.2), channel_id=1, source_target_pairs={{0,58},{2,8},{4,62},{6,12},{8,2},{10,16},{12,6},{14,20},{16,10},{1... | collective-permute-start | bytes 3145736 | tf_op jit(solution)/shard_map/ppermute | solution.py:93
  9.8 4.3 %collective-permute-start.7 = (bf16[1024,512]{1,0:T(8,128)(2,1)}, bf16[1024,512]{1,0:T(8,128)(2,1)}, u32[]{:S(2)}, u32[]{:S(2)}) collective-permute-start(bf16[1024,512]{1,0:T(8,128)(2,1)} %fusion.2), channel_id=1, source_target_pairs={{60,0},{62,2},{0,4},{2,6},{4,8},{6,10},{8,12},{10,14},{12,16},{14,... | collective-permute-start | bytes 3145736 | tf_op jit(solution)/shard_map/ppermute | solution.py:11
  14.1 4.3 %collective-permute-start.6 = (bf16[1024,512]{1,0:T(8,128)(2,1)}, bf16[1024,512]{1,0:T(8,128)(2,1)}, u32[]{:S(2)}, u32[]{:S(2)}) collective-permute-start(bf16[1024,512]{1,0:T(8,128)(2,1)} %fusion.2), channel_id=1, source_target_pairs={{4,0},{6,2},{8,4},{10,6},{12,8},{14,10},{16,12},{18,14},{20,16},{2... | collective-permute-start | bytes 3145736 | tf_op jit(solution)/shard_map/ppermute | solution.py:11
  18.4 1.9 collective-permute-start.5
  20.3 0.7 multiply_reduce_fusion.2
  21.0 0.7 multiply_reduce_fusion
  21.6 0.7 multiply_reduce_fusion.1
  22.3 0.7 multiply_reduce_fusion.3
  24.9 0.7 multiply_reduce_fusion.4
  27.6 2.3 %collective-permute-start = (f32[2]{0:T(128)S(1)}, f32[2]{0:T(128)S(1)}, u32[]{:S(2)}, u32[]{:S(2)}) collective-permute-start(f32[2]{0:T(128)S(1)} %pad_maximum_fusion.6), channel_id=1, source_target_pairs={{0,64},{64,0},{128,192},{192,128},{256,320},{320,256},{384,448},{4... | collective-permute-start | bytes 32 | tf_op jit(solution)/shard_map/ppermute | solution.py:25
  30.1 1.3 fusion
  31.4 0.7 bitcast_reduce_fusion
  32.1 0.7 bitcast_reduce_fusion.6
  34.0 0.7 bitcast_reduce_fusion.5
  34.7 0.7 bitcast_reduce_fusion.4
  35.5 0.6 bitcast_reduce_fusion.3
  36.8 0.8 compare_reduce_fusion
  37.6 2.7 %fusion.17 = f32[1024,512]{1,0:T(8,128)S(1)} fusion(bf16[1024,512]{1,0:T(8,128)(2,1)} %bitcast.128, bf16[1,5,512,512]{3,2,1,0:T(8,128)(2,1)} %param.29, s32[]{:T(128)S(6)} %select_n.166, pred[]{:T(512)} %get-tuple-element.35), kind=kOutput, calls=%fused_computation.20 | convolution fusion | flops 537133056 | bytes 3670532 | tf_op jit(solution)/shard_map/dot_general | solution.py:111
  40.3 0.7 pad_maximum_fusion.5
  41.0 0.7 bitcast_reduce_fusion.2
  41.8 2.2 %collective-permute-start.1 = (f32[2]{0:T(128)S(1)}, f32[2]{0:T(128)S(1)}, u32[]{:S(2)}, u32[]{:S(2)}) collective-permute-start(f32[2]{0:T(128)S(1)} %fusion.102), channel_id=1, source_target_pairs={{0,128},{64,192},{128,0},{192,64},{256,384},{320,448},{384,256},{4... | collective-permute-start | bytes 32 | tf_op jit(solution)/shard_map/ppermute | solution.py:25
  44.0 4.1 %collective-permute-done.1 = f32[2]{0:T(128)S(1)} collective-permute-done((f32[2]{0:T(128)S(1)}, f32[2]{0:T(128)S(1)}, u32[]{:S(2)}, u32[]{:S(2)}) %collective-permute-start.1) | collective-permute-done | bytes 40 | tf_op jit(solution)/shard_map/ppermute | solution.py:25
  48.2 5.9 %collective-permute-start.2 = (f32[2]{0:T(128)S(1)}, f32[2]{0:T(128)S(1)}, u32[]{:S(2)}, u32[]{:S(2)}) collective-permute-start(f32[2]{0:T(128)S(1)} %fusion.103), channel_id=1, source_target_pairs={{0,256},{64,320},{128,384},{192,448},{256,0},{320,64},{384,128},{4... | collective-permute-start | bytes 32 | tf_op jit(solution)/shard_map/ppermute | solution.py:25
  54.1 3.4 %collective-permute-done.2 = f32[2]{0:T(128)S(1)} collective-permute-done((f32[2]{0:T(128)S(1)}, f32[2]{0:T(128)S(1)}, u32[]{:S(2)}, u32[]{:S(2)}) %collective-permute-start.2) | collective-permute-done | bytes 40 | tf_op jit(solution)/shard_map/ppermute | solution.py:25
  57.5 1.9 collective-permute-start.3
  59.4 0.7 bitcast_reduce_fusion.1
  64.0 17.1 %collective-permute-done.3 = f32[7,16,2]{2,1,0:T(8,128)} collective-permute-done((f32[7,16,2]{2,1,0:T(8,128)}, f32[7,16,2]{2,1,0:T(8,128)}, u32[]{:S(2)}, u32[]{:S(2)}) %collective-permute-start.3) | collective-permute-done | bytes 928 | tf_op jit(solution)/shard_map/ppermute | solution.py:11
  81.1 1.9 collective-permute-start.4
  90.5 1.0 pad_maximum_fusion.1
  91.6 2.4 %collective-permute-start.10 = (f32[2]{0:T(128)S(1)}, f32[2]{0:T(128)S(1)}, u32[]{:S(2)}, u32[]{:S(2)}) collective-permute-start(f32[2]{0:T(128)S(1)} %add.245), channel_id=1, source_target_pairs={{0,2},{2,0},{4,6},{6,4},{8,10},{10,8},{12,14},{14,12},{16,18},{18,... | collective-permute-start | bytes 32 | tf_op jit(solution)/shard_map/ppermute | solution.py:25
  94.0 9.4 %collective-permute-start.16 = (bf16[6,16,516]{2,1,0:T(8,128)(2,1)S(1)}, bf16[6,16,516]{2,1,0:T(8,128)(2,1)S(1)}, u32[]{:S(2)}, u32[]{:S(2)}) collective-permute-start(bf16[6,16,516]{2,1,0:T(8,128)(2,1)S(1)} %pad_maximum_fusion.2), channel_id=1, source_target_pairs={{0,1},{1,0},{2,3},{3,2},{4,5},{5,4},{6,7},{7,6},{8,9},{9,8},{10,11... | collective-permute-start | bytes 297224 | tf_op jit(solution)/shard_map/ppermute | solution.py:37
  103.6 1.8 pad_maximum_fusion
  105.5 1.9 collective-permute-start.9
  107.4 2.6 %fusion.15 = f32[1024,512]{1,0:T(8,128)S(1)} fusion(bf16[1024,512]{1,0:T(8,128)(2,1)} %collective-permute-done.5, bf16[1,5,512,512]{3,2,1,0:T(8,128)(2,1)S(1)} %copy-done.1, s32[]{:T(128)S(6)} %select_n.173, pred[]{:T(512)} %get-tuple-element.34), kind=kOutput, calls=%fused_computation.18 | convolution fusion | flops 537133056 | bytes 3670021 | tf_op jit(solution)/shard_map/dot_general | solution.py:113
  110.0 2.6 %fusion.13 = f32[1024,512]{1,0:T(8,128)S(1)} fusion(bf16[1024,512]{1,0:T(8,128)(2,1)} %collective-permute-done.6, bf16[1,5,512,512]{3,2,1,0:T(8,128)(2,1)S(1)} %copy-done.1, s32[]{:T(128)S(6)} %select_n.178, pred[]{:T(512)} %get-tuple-element.33), kind=kOutput, calls=%fused_computation.16 | convolution fusion | flops 537133056 | bytes 3670021 | tf_op jit(solution)/shard_map/dot_general | solution.py:113
  112.6 2.6 %fusion.9 = f32[1024,512]{1,0:T(8,128)S(1)} fusion(bf16[1024,512]{1,0:T(8,128)(2,1)} %collective-permute-done.8, bf16[1,5,512,512]{3,2,1,0:T(8,128)(2,1)S(1)} %copy-done.1, s32[]{:T(128)S(6)} %select_n.189, pred[]{:T(512)} %get-tuple-element.31), kind=kOutput, calls=%fused_computation.12 | convolution fusion | flops 537133056 | bytes 3670021 | tf_op jit(solution)/shard_map/dot_general | solution.py:113
  115.2 2.5 %fusion.11 = f32[1024,512]{1,0:T(8,128)S(1)} fusion(bf16[1024,512]{1,0:T(8,128)(2,1)} %collective-permute-done.7, bf16[1,5,512,512]{3,2,1,0:T(8,128)(2,1)S(1)} %copy-done.1, s32[]{:T(128)S(6)} %select_n.183, pred[]{:T(512)} %get-tuple-element.32), kind=kOutput, calls=%fused_computation.14 | convolution fusion | flops 537133056 | bytes 3670021 | tf_op jit(solution)/shard_map/dot_general | solution.py:113
  117.8 26.3 %collective-permute-start.11 = (f32[2]{0:T(128)S(1)}, f32[2]{0:T(128)S(1)}, u32[]{:S(2)}, u32[]{:S(2)}) collective-permute-start(f32[2]{0:T(128)S(1)} %add.246), channel_id=1, source_target_pairs={{0,4},{2,6},{4,0},{6,2},{8,12},{10,14},{12,8},{14,10},{16,20},{18,... | collective-permute-start | bytes 32 | tf_op jit(solution)/shard_map/ppermute | solution.py:25
  144.1 1.5 collective-permute-done.11
  145.6 6.2 %collective-permute-start.12 = (f32[2]{0:T(128)S(1)}, f32[2]{0:T(128)S(1)}, u32[]{:S(2)}, u32[]{:S(2)}) collective-permute-start(f32[2]{0:T(128)S(1)} %add.247), channel_id=1, source_target_pairs={{0,8},{2,10},{4,12},{6,14},{8,0},{10,2},{12,4},{14,6},{16,24},{18,... | collective-permute-start | bytes 32 | tf_op jit(solution)/shard_map/ppermute | solution.py:25
  151.8 1.5 collective-permute-done.12
  153.4 2.7 %collective-permute-start.13 = (f32[2]{0:T(128)S(1)}, f32[2]{0:T(128)S(1)}, u32[]{:S(2)}, u32[]{:S(2)}) collective-permute-start(f32[2]{0:T(128)S(1)} %add.248), channel_id=1, source_target_pairs={{0,16},{2,18},{4,20},{6,22},{8,24},{10,26},{12,28},{14,30},{16,0},... | collective-permute-start | bytes 32 | tf_op jit(solution)/shard_map/ppermute | solution.py:25
  156.1 2.7 %collective-permute-done.13 = f32[2]{0:T(128)S(1)} collective-permute-done((f32[2]{0:T(128)S(1)}, f32[2]{0:T(128)S(1)}, u32[]{:S(2)}, u32[]{:S(2)}) %collective-permute-start.13) | collective-permute-done | bytes 40 | tf_op jit(solution)/shard_map/ppermute | solution.py:25
  158.8 3.3 %collective-permute-start.14 = (f32[2]{0:T(128)S(1)}, f32[2]{0:T(128)S(1)}, u32[]{:S(2)}, u32[]{:S(2)}) collective-permute-start(f32[2]{0:T(128)S(1)} %add.249), channel_id=1, source_target_pairs={{0,32},{2,34},{4,36},{6,38},{8,40},{10,42},{12,44},{14,46},{16,48}... | collective-permute-start | bytes 32 | tf_op jit(solution)/shard_map/ppermute | solution.py:25
  162.1 3.6 %collective-permute-done.14 = f32[2]{0:T(128)S(1)} collective-permute-done((f32[2]{0:T(128)S(1)}, f32[2]{0:T(128)S(1)}, u32[]{:S(2)}, u32[]{:S(2)}) %collective-permute-start.14) | collective-permute-done | bytes 40 | tf_op jit(solution)/shard_map/ppermute | solution.py:25
  165.7 1.9 collective-permute-start.15
  167.6 7.4 %collective-permute-done.15 = f32[2]{0:T(128)S(1)} collective-permute-done((f32[2]{0:T(128)S(1)}, f32[2]{0:T(128)S(1)}, u32[]{:S(2)}, u32[]{:S(2)}) %collective-permute-start.15) | collective-permute-done | bytes 40 | tf_op jit(solution)/shard_map/ppermute | solution.py:25
  175.1 0.6 fusion.96
  177.0 0.6 copy.35
  178.1 0.2 fusion.48
  178.5 2.4 %collective-permute-start.18 = (bf16[16,512]{1,0:T(8,128)(2,1)S(1)}, bf16[16,512]{1,0:T(8,128)(2,1)S(1)}, u32[]{:S(2)}, u32[]{:S(2)}) collective-permute-start(bf16[16,512]{1,0:T(8,128)(2,1)S(1)} %fusion.57), channel_id=1, source_target_pairs={{64,0},{128,64},{192,128},{256,192},{320,256},{384,320},{448,384},... | collective-permute-start | bytes 49160 | tf_op jit(solution)/shard_map/ppermute | solution.py:17
  180.9 0.2 fusion.65
  181.1 4.7 %collective-permute-start.17 = (bf16[16,512]{1,0:T(8,128)(2,1)S(1)}, bf16[16,512]{1,0:T(8,128)(2,1)S(1)}, u32[]{:S(2)}, u32[]{:S(2)}) collective-permute-start(bf16[16,512]{1,0:T(8,128)(2,1)S(1)} %fusion.65), channel_id=1, source_target_pairs={{0,64},{64,128},{128,192},{192,256},{256,320},{320,384},{384,448},... | collective-permute-start | bytes 49160 | tf_op jit(solution)/shard_map/ppermute | solution.py:17
  185.8 0.7 fusion.76
  186.5 1.3 fusion.7
  187.9 1.6 add_add_fusion
  189.5 0.4 fusion.1
  189.9 0.3 copy-done.9
  190.3 0.6 copy.39
  191.0 0.6 copy.37
  191.6 0.6 copy.38
  192.3 0.6 copy.36
  (72 shorter events, 1.4 us)
Async XLA Ops:
  0.6 19.7 %copy-start.2 = (f32[1,16,1,512]{3,2,1,0:T(1,128)S(1)}, f32[1,16,1,512]{3,2,1,0:T(1,128)}, u32[]{:S(2)}) copy-start(f32[1,16,1,512]{3,2,1,0:T(1,128)} %param.21) | copy-start | bytes 98308
  0.6 29.4 %copy-start = (bf16[1,64,16,1,512]{4,2,3,1,0:T(8,128)(2,1)S(1)}, bf16[1,64,16,1,512]{4,2,3,1,0:T(8,128)(2,1)}, u32[]{:S(2)}) copy-start(bf16[1,64,16,1,512]{4,2,3,1,0:T(8,128)(2,1)} %param.24) | copy-start | bytes 3145732
  0.7 20.3 %copy-start.3 = (f32[1,16,1,512]{3,2,1,0:T(1,128)S(1)}, f32[1,16,1,512]{3,2,1,0:T(1,128)}, u32[]{:S(2)}) copy-start(f32[1,16,1,512]{3,2,1,0:T(1,128)} %param.23) | copy-start | bytes 98308
  0.7 21.0 %copy-start.4 = (f32[1,16,1,512]{3,2,1,0:T(1,128)S(1)}, f32[1,16,1,512]{3,2,1,0:T(1,128)}, u32[]{:S(2)}) copy-start(f32[1,16,1,512]{3,2,1,0:T(1,128)} %param.22) | copy-start | bytes 98308
  0.7 21.6 %copy-start.6 = (f32[1,16,1,512]{3,2,1,0:T(1,128)S(1)}, f32[1,16,1,512]{3,2,1,0:T(1,128)}, u32[]{:S(2)}) copy-start(f32[1,16,1,512]{3,2,1,0:T(1,128)} %param.20) | copy-start | bytes 98308
  0.7 24.2 %copy-start.7 = (f32[1,16,1,512]{3,2,1,0:T(1,128)S(1)}, f32[1,16,1,512]{3,2,1,0:T(1,128)}, u32[]{:S(2)}) copy-start(f32[1,16,1,512]{3,2,1,0:T(1,128)} %param.19) | copy-start | bytes 98308
  0.7 24.2 %copy-start.8 = (f32[1,16,1,512]{3,2,1,0:T(1,128)S(1)}, f32[1,16,1,512]{3,2,1,0:T(1,128)}, u32[]{:S(2)}) copy-start(f32[1,16,1,512]{3,2,1,0:T(1,128)} %param.18) | copy-start | bytes 98308
  1.5 29.8 %copy-start.12 = (s32[1,5]{1,0:T(1,128)S(1)}, s32[1,5]{1,0:T(1,128)}, u32[]{:S(2)}) copy-start(s32[1,5]{1,0:T(1,128)} %param.28) | copy-start | bytes 64
  1.5 34.6 %copy-start.5 = (f32[1,5,16,1,512]{4,3,2,1,0:T(1,128)S(1)}, f32[1,5,16,1,512]{4,3,2,1,0:T(1,128)}, u32[]{:S(2)}) copy-start(f32[1,5,16,1,512]{4,3,2,1,0:T(1,128)} %param.25) | copy-start | bytes 491524
  4.0 87.5 %collective-permute-start.8 = (bf16[1024,512]{1,0:T(8,128)(2,1)}, bf16[1024,512]{1,0:T(8,128)(2,1)}, u32[]{:S(2)}, u32[]{:S(2)}) collective-permute-start(bf16[1024,512]{1,0:T(8,128)(2,1)} %fusion.2), channel_id=1, source_target_pairs={{0,58},{2,8},{4,62},{6,12},{8,2},{10,16},{12,6},{14,20},{16,10},{1... | collective-permute-start | bytes 3145736 | tf_op jit(solution)/shard_map/ppermute | solution.py:93
  9.8 81.7 %collective-permute-start.7 = (bf16[1024,512]{1,0:T(8,128)(2,1)}, bf16[1024,512]{1,0:T(8,128)(2,1)}, u32[]{:S(2)}, u32[]{:S(2)}) collective-permute-start(bf16[1024,512]{1,0:T(8,128)(2,1)} %fusion.2), channel_id=1, source_target_pairs={{60,0},{62,2},{0,4},{2,6},{4,8},{6,10},{8,12},{10,14},{12,16},{14,... | collective-permute-start | bytes 3145736 | tf_op jit(solution)/shard_map/ppermute | solution.py:11
  14.1 77.4 %collective-permute-start.6 = (bf16[1024,512]{1,0:T(8,128)(2,1)}, bf16[1024,512]{1,0:T(8,128)(2,1)}, u32[]{:S(2)}, u32[]{:S(2)}) collective-permute-start(bf16[1024,512]{1,0:T(8,128)(2,1)} %fusion.2), channel_id=1, source_target_pairs={{4,0},{6,2},{8,4},{10,6},{12,8},{14,10},{16,12},{18,14},{20,16},{2... | collective-permute-start | bytes 3145736 | tf_op jit(solution)/shard_map/ppermute | solution.py:11
  18.4 73.2 %collective-permute-start.5 = (bf16[1024,512]{1,0:T(8,128)(2,1)}, bf16[1024,512]{1,0:T(8,128)(2,1)}, u32[]{:S(2)}, u32[]{:S(2)}) collective-permute-start(bf16[1024,512]{1,0:T(8,128)(2,1)} %fusion.2), channel_id=1, source_target_pairs={{0,2},{2,0},{4,6},{6,4},{8,10},{10,8},{12,14},{14,12},{16,18},{18,... | collective-permute-start | bytes 3145736 | tf_op jit(solution)/shard_map/ppermute | solution.py:90
  27.6 14.1 %collective-permute-start = (f32[2]{0:T(128)S(1)}, f32[2]{0:T(128)S(1)}, u32[]{:S(2)}, u32[]{:S(2)}) collective-permute-start(f32[2]{0:T(128)S(1)} %pad_maximum_fusion.6), channel_id=1, source_target_pairs={{0,64},{64,0},{128,192},{192,128},{256,320},{320,256},{384,448},{4... | collective-permute-start | bytes 32 | tf_op jit(solution)/shard_map/ppermute | solution.py:25
  41.8 6.3 %collective-permute-start.1 = (f32[2]{0:T(128)S(1)}, f32[2]{0:T(128)S(1)}, u32[]{:S(2)}, u32[]{:S(2)}) collective-permute-start(f32[2]{0:T(128)S(1)} %fusion.102), channel_id=1, source_target_pairs={{0,128},{64,192},{128,0},{192,64},{256,384},{320,448},{384,256},{4... | collective-permute-start | bytes 32 | tf_op jit(solution)/shard_map/ppermute | solution.py:25
  48.2 9.3 %collective-permute-start.2 = (f32[2]{0:T(128)S(1)}, f32[2]{0:T(128)S(1)}, u32[]{:S(2)}, u32[]{:S(2)}) collective-permute-start(f32[2]{0:T(128)S(1)} %fusion.103), channel_id=1, source_target_pairs={{0,256},{64,320},{128,384},{192,448},{256,0},{320,64},{384,128},{4... | collective-permute-start | bytes 32 | tf_op jit(solution)/shard_map/ppermute | solution.py:25
  57.5 23.6 %collective-permute-start.3 = (f32[7,16,2]{2,1,0:T(8,128)}, f32[7,16,2]{2,1,0:T(8,128)}, u32[]{:S(2)}, u32[]{:S(2)}) collective-permute-start(f32[7,16,2]{2,1,0:T(8,128)} %get-tuple-element.54), channel_id=1, source_target_pairs={{62,0},{0,2},{2,4},{4,6},{6,8},{8,10},{10,12},{12,14},{14,16},{16,... | collective-permute-start | bytes 2696 | tf_op jit(solution)/shard_map/ppermute | solution.py:11
  81.1 9.4 %collective-permute-start.4 = (f32[7,16,2]{2,1,0:T(8,128)}, f32[7,16,2]{2,1,0:T(8,128)}, u32[]{:S(2)}, u32[]{:S(2)}) collective-permute-start(f32[7,16,2]{2,1,0:T(8,128)} %get-tuple-element.55), channel_id=1, source_target_pairs={{2,0},{4,2},{6,4},{8,6},{10,8},{12,10},{14,12},{16,14},{18,16},{20... | collective-permute-start | bytes 2696 | tf_op jit(solution)/shard_map/ppermute | solution.py:11
  91.6 26.2 %collective-permute-start.10 = (f32[2]{0:T(128)S(1)}, f32[2]{0:T(128)S(1)}, u32[]{:S(2)}, u32[]{:S(2)}) collective-permute-start(f32[2]{0:T(128)S(1)} %add.245), channel_id=1, source_target_pairs={{0,2},{2,0},{4,6},{6,4},{8,10},{10,8},{12,14},{14,12},{16,18},{18,... | collective-permute-start | bytes 32 | tf_op jit(solution)/shard_map/ppermute | solution.py:25
  94.0 83.6 %collective-permute-start.16 = (bf16[6,16,516]{2,1,0:T(8,128)(2,1)S(1)}, bf16[6,16,516]{2,1,0:T(8,128)(2,1)S(1)}, u32[]{:S(2)}, u32[]{:S(2)}) collective-permute-start(bf16[6,16,516]{2,1,0:T(8,128)(2,1)S(1)} %pad_maximum_fusion.2), channel_id=1, source_target_pairs={{0,1},{1,0},{2,3},{3,2},{4,5},{5,4},{6,7},{7,6},{8,9},{9,8},{10,11... | collective-permute-start | bytes 297224 | tf_op jit(solution)/shard_map/ppermute | solution.py:37
  103.6 3.8 %copy-start.1 = (bf16[1,5,512,512]{3,2,1,0:T(8,128)(2,1)S(1)}, bf16[1,5,512,512]{3,2,1,0:T(8,128)(2,1)}, u32[]{:S(2)}) copy-start(bf16[1,5,512,512]{3,2,1,0:T(8,128)(2,1)} %param.29) | copy-start | bytes 7864324
  105.5 81.0 %collective-permute-start.9 = (bf16[2048,512]{1,0:T(8,128)(2,1)S(1)}, bf16[2048,512]{1,0:T(8,128)(2,1)S(1)}, u32[]{:S(2)}, u32[]{:S(2)}) collective-permute-start(bf16[2048,512]{1,0:T(8,128)(2,1)S(1)} %pad_maximum_fusion), channel_id=1, source_target_pairs={{0,2},{2,0},{4,6},{6,4},{8,10},{10,8},{12,14},{14,12},{16,18},{18,... | collective-permute-start | bytes 6291464 | tf_op jit(solution)/shard_map/ppermute | solution.py:94
  115.2 61.8 %copy-start.11 = (f32[1,16,1,512]{3,2,1,0:T(1,128)S(1)}, f32[1,16,1,512]{3,2,1,0:T(1,128)}, u32[]{:S(2)}) copy-start(f32[1,16,1,512]{3,2,1,0:T(1,128)} %param.15) | copy-start | bytes 98308
  117.7 68.1 %copy-start.10 = (f32[1,16,1,512]{3,2,1,0:T(1,128)S(1)}, f32[1,16,1,512]{3,2,1,0:T(1,128)}, u32[]{:S(2)}) copy-start(f32[1,16,1,512]{3,2,1,0:T(1,128)} %param.26) | copy-start | bytes 98308
  117.8 27.8 %collective-permute-start.11 = (f32[2]{0:T(128)S(1)}, f32[2]{0:T(128)S(1)}, u32[]{:S(2)}, u32[]{:S(2)}) collective-permute-start(f32[2]{0:T(128)S(1)} %add.246), channel_id=1, source_target_pairs={{0,4},{2,6},{4,0},{6,2},{8,12},{10,14},{12,8},{14,10},{16,20},{18,... | collective-permute-start | bytes 32 | tf_op jit(solution)/shard_map/ppermute | solution.py:25
  145.6 7.7 %collective-permute-start.12 = (f32[2]{0:T(128)S(1)}, f32[2]{0:T(128)S(1)}, u32[]{:S(2)}, u32[]{:S(2)}) collective-permute-start(f32[2]{0:T(128)S(1)} %add.247), channel_id=1, source_target_pairs={{0,8},{2,10},{4,12},{6,14},{8,0},{10,2},{12,4},{14,6},{16,24},{18,... | collective-permute-start | bytes 32 | tf_op jit(solution)/shard_map/ppermute | solution.py:25
  153.4 5.4 %collective-permute-start.13 = (f32[2]{0:T(128)S(1)}, f32[2]{0:T(128)S(1)}, u32[]{:S(2)}, u32[]{:S(2)}) collective-permute-start(f32[2]{0:T(128)S(1)} %add.248), channel_id=1, source_target_pairs={{0,16},{2,18},{4,20},{6,22},{8,24},{10,26},{12,28},{14,30},{16,0},... | collective-permute-start | bytes 32 | tf_op jit(solution)/shard_map/ppermute | solution.py:25
  158.8 6.9 %collective-permute-start.14 = (f32[2]{0:T(128)S(1)}, f32[2]{0:T(128)S(1)}, u32[]{:S(2)}, u32[]{:S(2)}) collective-permute-start(f32[2]{0:T(128)S(1)} %add.249), channel_id=1, source_target_pairs={{0,32},{2,34},{4,36},{6,38},{8,40},{10,42},{12,44},{14,46},{16,48}... | collective-permute-start | bytes 32 | tf_op jit(solution)/shard_map/ppermute | solution.py:25
  165.7 9.3 %collective-permute-start.15 = (f32[2]{0:T(128)S(1)}, f32[2]{0:T(128)S(1)}, u32[]{:S(2)}, u32[]{:S(2)}) collective-permute-start(f32[2]{0:T(128)S(1)} %add.250), channel_id=1, source_target_pairs={{0,1},{1,0},{2,3},{3,2},{4,5},{5,4},{6,7},{7,6},{8,9},{9,8},{10,11... | collective-permute-start | bytes 32 | tf_op jit(solution)/shard_map/ppermute | solution.py:25
  178.5 7.3 %collective-permute-start.18 = (bf16[16,512]{1,0:T(8,128)(2,1)S(1)}, bf16[16,512]{1,0:T(8,128)(2,1)S(1)}, u32[]{:S(2)}, u32[]{:S(2)}) collective-permute-start(bf16[16,512]{1,0:T(8,128)(2,1)S(1)} %fusion.57), channel_id=1, source_target_pairs={{64,0},{128,64},{192,128},{256,192},{320,256},{384,320},{448,384},... | collective-permute-start | bytes 49160 | tf_op jit(solution)/shard_map/ppermute | solution.py:17
  181.1 8.9 %collective-permute-start.17 = (bf16[16,512]{1,0:T(8,128)(2,1)S(1)}, bf16[16,512]{1,0:T(8,128)(2,1)S(1)}, u32[]{:S(2)}, u32[]{:S(2)}) collective-permute-start(bf16[16,512]{1,0:T(8,128)(2,1)S(1)} %fusion.65), channel_id=1, source_target_pairs={{0,64},{64,128},{128,192},{192,256},{256,320},{320,384},{384,448},... | collective-permute-start | bytes 49160 | tf_op jit(solution)/shard_map/ppermute | solution.py:17
  189.5 0.8 copy-start.9
  189.5 0.8 copy-start.13
  189.5 0.8 copy-start.14
  189.5 0.8 copy-start.15

commit v14 on v11

--- a/solution.py
+++ b/solution.py
@@ -87,10 +87,11 @@
     columns = loc_cols[0]
     tiles = loc_vals[0]
     partner = [(i, i ^ 1) for i in range(bands)]
-    beside = lax.ppermute(flat, "lon", partner)
     ahead = from_offset(flat, "lon", 2)
     behind = from_offset(flat, "lon", -2)
-    far = lax.ppermute(flat, "lon", [(s, (s + 3) % bands if s % 2 else (s - 3) % bands) for s in range(bands)])
+    late, _, _ = lax.optimization_barrier((flat, ahead, behind))
+    beside = lax.ppermute(late, "lon", partner)
+    far = lax.ppermute(late, "lon", [(s, (s + 3) % bands if s % 2 else (s - 3) % bands) for s in range(bands)])
     relayed = lax.ppermute(jnp.concatenate([ahead, behind], axis=0), "lon", partner)
     received = [
         (beside, jnp.where(even, 1, -1)),

time: 185 us -> 183 us (0.989)
  the two profiles are of different devices: /device:TPU:38 before, /device:TPU:16 now
where the time goes in v14:
time: 183 us; the launch traced here: 182 us
  starting transfers between devices  74.2 us (41%)
  waiting for transfers between devices  52.8 us (29%)
  between operations  20.1 us (11%)
  other arithmetic  16.8 us (9%)
  matrix products  11.9 us (7%)
  local copies, waits for them, and re-layouts  6.4 us (3%)
    ppermute x9, starting transfers between devices, butterfly_sum(): lax.ppermute(value, axis, [(i, i ^ step) for i in range(count)])  31.8 us
    ppermute x1, waiting for transfers between devices, localize(): lax.ppermute(late, 'lon', [(s, (s + 3) % bands if s % 2 else (s - 3) % ba...  27.6 us
    ppermute x9, waiting for transfers between devices, butterfly_sum(): lax.ppermute(value, axis, [(i, i ^ step) for i in range(count)])  22.6 us
    ppermute x4, starting transfers between devices, from_offset(): lax.ppermute(value, axis, [((i + distance) % count, i) for i in range(cou...  21.5 us
    dot_general x6, matrix products, localize(): jnp.dot(value, weight_for(offset), preferred_element_type=jnp.float32)  9.54 us
    ppermute x1, starting transfers between devices, lat_partner(): return lax.ppermute(value, 'lat', [(0, 1), (1, 0)])  8.65 us
    ppermute x2, starting transfers between devices, shifted(): lax.ppermute(value, axis, [(source, source + steps) for source in range(l...  5.84 us
    another operation x7, other arithmetic, weight_for(): picked = tiles[jnp.argmax(match)]  4.82 us
  transfers between devices with their start and end apart: 19, of which 9 were waited for; matrix products, arithmetic and copies ran while one was open for 16% of the time, Pallas kernels for 0%

profile of v14, /device:TPU:16, one launch (start us, length us, event | category | flops | bytes accessed | tf_op | source)
XLA Modules:
  0.0 182.1 jit_solution(15303366571001211839)
XLA Ops:
  0.7 0.9 copy_bitcast_fusion.3
  1.6 2.4 %fusion.2 = bf16[1024,512]{1,0:T(8,128)(2,1)} fusion(bf16[1,64,16,1,512]{4,2,3,1,0:T(8,128)(2,1)} %param.24, f32[16,512]{1,0:T(8,128)S(1)} %get-tuple-element.72), kind=kLoop, calls=%fused_computation.6 | loop fusion | flops 1572864 | bytes 2129920 | tf_op jit(solution)/shard_map/convert_element_type | solution.py:81
  4.0 4.3 %collective-permute-start.4 = (bf16[1024,512]{1,0:T(8,128)(2,1)}, bf16[1024,512]{1,0:T(8,128)(2,1)S(1)}, u32[]{:S(2)}, u32[]{:S(2)}) collective-permute-start(bf16[1024,512]{1,0:T(8,128)(2,1)} %fusion.2), channel_id=1, source_target_pairs={{60,0},{62,2},{0,4},{2,6},{4,8},{6,10},{8,12},{10,14},{12,16},{14,... | collective-permute-start | bytes 3145736 | tf_op jit(solution)/shard_map/ppermute | solution.py:11
  8.3 7.7 %collective-permute-start.3 = (bf16[1024,512]{1,0:T(8,128)(2,1)}, bf16[1024,512]{1,0:T(8,128)(2,1)}, u32[]{:S(2)}, u32[]{:S(2)}) collective-permute-start(bf16[1024,512]{1,0:T(8,128)(2,1)} %fusion.2), channel_id=1, source_target_pairs={{4,0},{6,2},{8,4},{10,6},{12,8},{14,10},{16,12},{18,14},{20,16},{2... | collective-permute-start | bytes 3145736 | tf_op jit(solution)/shard_map/ppermute | solution.py:11
  16.1 0.7 multiply_reduce_fusion.2
  16.7 0.7 multiply_reduce_fusion
  17.4 0.7 multiply_reduce_fusion.1
  18.1 0.7 multiply_reduce_fusion.3
  20.7 0.7 multiply_reduce_fusion.4
  23.4 3.5 %collective-permute-start = (f32[2]{0:T(128)S(1)}, f32[2]{0:T(128)S(1)}, u32[]{:S(2)}, u32[]{:S(2)}) collective-permute-start(f32[2]{0:T(128)S(1)} %pad_maximum_fusion.6), channel_id=1, source_target_pairs={{0,64},{64,0},{128,192},{192,128},{256,320},{320,256},{384,448},{4... | collective-permute-start | bytes 32 | tf_op jit(solution)/shard_map/ppermute | solution.py:25
  26.9 0.7 pad_maximum_fusion.5
  27.6 1.9 %collective-permute-start.8 = (f32[7,16,2]{2,1,0:T(8,128)}, f32[7,16,2]{2,1,0:T(8,128)}, u32[]{:S(2)}, u32[]{:S(2)}) collective-permute-start(f32[7,16,2]{2,1,0:T(8,128)} %get-tuple-element.56), channel_id=1, source_target_pairs={{62,0},{0,2},{2,4},{4,6},{6,8},{8,10},{10,12},{12,14},{14,16},{16,... | collective-permute-start | bytes 2696 | tf_op jit(solution)/shard_map/ppermute | solution.py:11
  29.5 7.6 %collective-permute-start.9 = (f32[7,16,2]{2,1,0:T(8,128)}, f32[7,16,2]{2,1,0:T(8,128)}, u32[]{:S(2)}, u32[]{:S(2)}) collective-permute-start(f32[7,16,2]{2,1,0:T(8,128)} %get-tuple-element.57), channel_id=1, source_target_pairs={{2,0},{4,2},{6,4},{8,6},{10,8},{12,10},{14,12},{16,14},{18,16},{20... | collective-permute-start | bytes 2696 | tf_op jit(solution)/shard_map/ppermute | solution.py:11
  37.2 0.7 bitcast_reduce_fusion
  39.1 0.7 bitcast_reduce_fusion.6
  41.3 0.7 bitcast_reduce_fusion.5
  43.2 0.7 bitcast_reduce_fusion.4
  45.2 0.7 bitcast_reduce_fusion.3
  47.1 0.7 bitcast_reduce_fusion.2
  49.1 0.8 compare_reduce_fusion
  49.9 0.7 bitcast_reduce_fusion.1
  51.9 0.6 fusion.97
  52.5 0.3 fusion
  57.3 2.3 %fusion.17 = f32[1024,512]{1,0:T(8,128)S(1)} fusion(bf16[1024,512]{1,0:T(8,128)(2,1)S(1)} %bitcast.132, bf16[1,5,512,512]{3,2,1,0:T(8,128)(2,1)} %param.29, s32[]{:T(128)S(6)} %select_n.168, pred[]{:T(512)} %get-tuple-element.37), kind=kOutput, calls=%fused_computation.20 | convolution fusion | flops 537133056 | bytes 3670532 | tf_op jit(solution)/shard_map/dot_general | solution.py:112
  59.7 3.8 %collective-permute-start.1 = (f32[2]{0:T(128)S(1)}, f32[2]{0:T(128)S(1)}, u32[]{:S(2)}, u32[]{:S(2)}) collective-permute-start(f32[2]{0:T(128)S(1)} %fusion.105), channel_id=1, source_target_pairs={{0,128},{64,192},{128,0},{192,64},{256,384},{320,448},{384,256},{4... | collective-permute-start | bytes 32 | tf_op jit(solution)/shard_map/ppermute | solution.py:25
  63.5 2.5 %collective-permute-done.1 = f32[2]{0:T(128)S(1)} collective-permute-done((f32[2]{0:T(128)S(1)}, f32[2]{0:T(128)S(1)}, u32[]{:S(2)}, u32[]{:S(2)}) %collective-permute-start.1) | collective-permute-done | bytes 40 | tf_op jit(solution)/shard_map/ppermute | solution.py:25
  66.1 5.0 %collective-permute-start.2 = (f32[2]{0:T(128)S(1)}, f32[2]{0:T(128)S(1)}, u32[]{:S(2)}, u32[]{:S(2)}) collective-permute-start(f32[2]{0:T(128)S(1)} %fusion.106), channel_id=1, source_target_pairs={{0,256},{64,320},{128,384},{192,448},{256,0},{320,64},{384,128},{4... | collective-permute-start | bytes 32 | tf_op jit(solution)/shard_map/ppermute | solution.py:25
  71.1 4.3 %collective-permute-done.2 = f32[2]{0:T(128)S(1)} collective-permute-done((f32[2]{0:T(128)S(1)}, f32[2]{0:T(128)S(1)}, u32[]{:S(2)}, u32[]{:S(2)}) %collective-permute-start.2) | collective-permute-done | bytes 40 | tf_op jit(solution)/shard_map/ppermute | solution.py:25
  75.4 1.0 pad_maximum_fusion.1
  76.5 8.7 %collective-permute-start.10 = (bf16[6,16,516]{2,1,0:T(8,128)(2,1)S(1)}, bf16[6,16,516]{2,1,0:T(8,128)(2,1)S(1)}, u32[]{:S(2)}, u32[]{:S(2)}) collective-permute-start(bf16[6,16,516]{2,1,0:T(8,128)(2,1)S(1)} %pad_maximum_fusion.2), channel_id=1, source_target_pairs={{0,1},{1,0},{2,3},{3,2},{4,5},{5,4},{6,7},{7,6},{8,9},{9,8},{10,11... | collective-permute-start | bytes 297224 | tf_op jit(solution)/shard_map/ppermute | solution.py:37
  85.4 2.6 %collective-permute-done.10 = bf16[6,16,516]{2,1,0:T(8,128)(2,1)S(1)} collective-permute-done((bf16[6,16,516]{2,1,0:T(8,128)(2,1)S(1)}, bf16[6,16,516]{2,1,0:T(8,128)(2,1)S(1)}, u32[]{:S(2)}, u32[]{:S(2)}) %collective-permute-start.10) | collective-permute-done | bytes 99104 | tf_op jit(solution)/shard_map/ppermute | solution.py:37
  88.6 2.1 %collective-permute-start.6 = (bf16[1024,512]{1,0:T(8,128)(2,1)}, bf16[1024,512]{1,0:T(8,128)(2,1)S(1)}, u32[]{:S(2)}, u32[]{:S(2)}) collective-permute-start(bf16[1024,512]{1,0:T(8,128)(2,1)} %fusion.2), channel_id=1, source_target_pairs={{0,58},{2,8},{4,62},{6,12},{8,2},{10,16},{12,6},{14,20},{16,10},{1... | collective-permute-start | bytes 3145736 | tf_op jit(solution)/shard_map/ppermute | solution.py:94
  90.7 1.9 %collective-permute-start.5 = (bf16[1024,512]{1,0:T(8,128)(2,1)}, bf16[1024,512]{1,0:T(8,128)(2,1)S(1)}, u32[]{:S(2)}, u32[]{:S(2)}) collective-permute-start(bf16[1024,512]{1,0:T(8,128)(2,1)} %fusion.2), channel_id=1, source_target_pairs={{0,2},{2,0},{4,6},{6,4},{8,10},{10,8},{12,14},{14,12},{16,18},{18,... | collective-permute-start | bytes 3145736 | tf_op jit(solution)/shard_map/ppermute | solution.py:93
  92.6 1.4 pad_maximum_fusion
  94.0 2.4 %collective-permute-start.7 = (bf16[2048,512]{1,0:T(8,128)(2,1)S(1)}, bf16[2048,512]{1,0:T(8,128)(2,1)S(1)}, u32[]{:S(2)}, u32[]{:S(2)}) collective-permute-start(bf16[2048,512]{1,0:T(8,128)(2,1)S(1)} %pad_maximum_fusion), channel_id=1, source_target_pairs={{0,2},{2,0},{4,6},{6,4},{8,10},{10,8},{12,14},{14,12},{16,18},{18,... | collective-permute-start | bytes 6291464 | tf_op jit(solution)/shard_map/ppermute | solution.py:95
  96.7 3.5 %collective-permute-start.18 = (bf16[16,512]{1,0:T(8,128)(2,1)S(1)}, bf16[16,512]{1,0:T(8,128)(2,1)S(1)}, u32[]{:S(2)}, u32[]{:S(2)}) collective-permute-start(bf16[16,512]{1,0:T(8,128)(2,1)S(1)} %fusion.58), channel_id=1, source_target_pairs={{64,0},{128,64},{192,128},{256,192},{320,256},{384,320},{448,384},... | collective-permute-start | bytes 49160 | tf_op jit(solution)/shard_map/ppermute | solution.py:17
  100.4 2.3 %collective-permute-start.17 = (bf16[16,512]{1,0:T(8,128)(2,1)S(1)}, bf16[16,512]{1,0:T(8,128)(2,1)S(1)}, u32[]{:S(2)}, u32[]{:S(2)}) collective-permute-start(bf16[16,512]{1,0:T(8,128)(2,1)S(1)} %fusion.66), channel_id=1, source_target_pairs={{0,64},{64,128},{128,192},{192,256},{256,320},{320,384},{384,448},... | collective-permute-start | bytes 49160 | tf_op jit(solution)/shard_map/ppermute | solution.py:17
  102.8 2.6 %fusion.13 = f32[1024,512]{1,0:T(8,128)S(1)} fusion(bf16[1024,512]{1,0:T(8,128)(2,1)} %collective-permute-done.3, bf16[1,5,512,512]{3,2,1,0:T(8,128)(2,1)S(1)} %copy-done.1, s32[]{:T(128)S(6)} %select_n.180, pred[]{:T(512)} %get-tuple-element.35), kind=kOutput, calls=%fused_computation.16 | convolution fusion | flops 537133056 | bytes 3670021 | tf_op jit(solution)/shard_map/dot_general | solution.py:114
  105.4 1.3 fusion.11
  106.7 27.6 %collective-permute-done.6 = bf16[1024,512]{1,0:T(8,128)(2,1)S(1)} collective-permute-done((bf16[1024,512]{1,0:T(8,128)(2,1)}, bf16[1024,512]{1,0:T(8,128)(2,1)S(1)}, u32[]{:S(2)}, u32[]{:S(2)}) %collective-permute-start.6) | collective-permute-done | bytes 1048608 | tf_op jit(solution)/shard_map/ppermute | solution.py:94
  134.3 1.9 %collective-permute-start.11 = (f32[2]{0:T(128)S(1)}, f32[2]{0:T(128)S(1)}, u32[]{:S(2)}, u32[]{:S(2)}) collective-permute-start(f32[2]{0:T(128)S(1)} %add.245), channel_id=1, source_target_pairs={{0,2},{2,0},{4,6},{6,4},{8,10},{10,8},{12,14},{14,12},{16,18},{18,... | collective-permute-start | bytes 32 | tf_op jit(solution)/shard_map/ppermute | solution.py:25
  136.2 1.3 fusion.15
  137.6 1.4 fusion.9
  139.0 1.9 %collective-permute-start.12 = (f32[2]{0:T(128)S(1)}, f32[2]{0:T(128)S(1)}, u32[]{:S(2)}, u32[]{:S(2)}) collective-permute-start(f32[2]{0:T(128)S(1)} %add.246), channel_id=1, source_target_pairs={{0,4},{2,6},{4,0},{6,2},{8,12},{10,14},{12,8},{14,10},{16,20},{18,... | collective-permute-start | bytes 32 | tf_op jit(solution)/shard_map/ppermute | solution.py:25
  140.9 3.5 %collective-permute-done.12 = f32[2]{0:T(128)S(1)} collective-permute-done((f32[2]{0:T(128)S(1)}, f32[2]{0:T(128)S(1)}, u32[]{:S(2)}, u32[]{:S(2)}) %collective-permute-start.12) | collective-permute-done | bytes 40 | tf_op jit(solution)/shard_map/ppermute | solution.py:25
  144.4 2.9 %collective-permute-start.13 = (f32[2]{0:T(128)S(1)}, f32[2]{0:T(128)S(1)}, u32[]{:S(2)}, u32[]{:S(2)}) collective-permute-start(f32[2]{0:T(128)S(1)} %add.247), channel_id=1, source_target_pairs={{0,8},{2,10},{4,12},{6,14},{8,0},{10,2},{12,4},{14,6},{16,24},{18,... | collective-permute-start | bytes 32 | tf_op jit(solution)/shard_map/ppermute | solution.py:25
  147.3 3.5 %collective-permute-done.13 = f32[2]{0:T(128)S(1)} collective-permute-done((f32[2]{0:T(128)S(1)}, f32[2]{0:T(128)S(1)}, u32[]{:S(2)}, u32[]{:S(2)}) %collective-permute-start.13) | collective-permute-done | bytes 40 | tf_op jit(solution)/shard_map/ppermute | solution.py:25
  150.7 2.4 %collective-permute-start.14 = (f32[2]{0:T(128)S(1)}, f32[2]{0:T(128)S(1)}, u32[]{:S(2)}, u32[]{:S(2)}) collective-permute-start(f32[2]{0:T(128)S(1)} %add.248), channel_id=1, source_target_pairs={{0,16},{2,18},{4,20},{6,22},{8,24},{10,26},{12,28},{14,30},{16,0},... | collective-permute-start | bytes 32 | tf_op jit(solution)/shard_map/ppermute | solution.py:25
  153.1 3.0 %collective-permute-done.14 = f32[2]{0:T(128)S(1)} collective-permute-done((f32[2]{0:T(128)S(1)}, f32[2]{0:T(128)S(1)}, u32[]{:S(2)}, u32[]{:S(2)}) %collective-permute-start.14) | collective-permute-done | bytes 40 | tf_op jit(solution)/shard_map/ppermute | solution.py:25
  156.2 2.7 %collective-permute-start.15 = (f32[2]{0:T(128)S(1)}, f32[2]{0:T(128)S(1)}, u32[]{:S(2)}, u32[]{:S(2)}) collective-permute-start(f32[2]{0:T(128)S(1)} %add.249), channel_id=1, source_target_pairs={{0,32},{2,34},{4,36},{6,38},{8,40},{10,42},{12,44},{14,46},{16,48}... | collective-permute-start | bytes 32 | tf_op jit(solution)/shard_map/ppermute | solution.py:25
  158.9 4.2 %collective-permute-done.15 = f32[2]{0:T(128)S(1)} collective-permute-done((f32[2]{0:T(128)S(1)}, f32[2]{0:T(128)S(1)}, u32[]{:S(2)}, u32[]{:S(2)}) %collective-permute-start.15) | collective-permute-done | bytes 40 | tf_op jit(solution)/shard_map/ppermute | solution.py:25
  163.1 7.8 %collective-permute-start.16 = (f32[2]{0:T(128)S(1)}, f32[2]{0:T(128)S(1)}, u32[]{:S(2)}, u32[]{:S(2)}) collective-permute-start(f32[2]{0:T(128)S(1)} %add.250), channel_id=1, source_target_pairs={{0,1},{1,0},{2,3},{3,2},{4,5},{5,4},{6,7},{7,6},{8,9},{9,8},{10,11... | collective-permute-start | bytes 32 | tf_op jit(solution)/shard_map/ppermute | solution.py:25
  170.9 1.5 collective-permute-done.16
  172.4 0.6 fusion.99
  174.4 0.6 copy.38
  175.0 0.7 fusion.78
  175.7 1.4 fusion.7
  177.1 1.5 add_add_fusion
  178.7 0.4 fusion.1
  179.1 0.3 copy-done.11
  179.5 0.6 copy.42
  180.2 0.6 copy.40
  180.8 0.6 copy.41
  181.5 0.6 copy.39
  (80 shorter events, 1.8 us)
Async XLA Ops:
  0.6 15.4 %copy-start.2 = (f32[1,16,1,512]{3,2,1,0:T(1,128)S(1)}, f32[1,16,1,512]{3,2,1,0:T(1,128)}, u32[]{:S(2)}) copy-start(f32[1,16,1,512]{3,2,1,0:T(1,128)} %param.21) | copy-start | bytes 98308
  0.6 16.1 %copy-start.4 = (f32[1,16,1,512]{3,2,1,0:T(1,128)S(1)}, f32[1,16,1,512]{3,2,1,0:T(1,128)}, u32[]{:S(2)}) copy-start(f32[1,16,1,512]{3,2,1,0:T(1,128)} %param.23) | copy-start | bytes 98308
  0.7 51.9 %copy-start = (bf16[1,64,16,1,512]{4,2,3,1,0:T(8,128)(2,1)S(1)}, bf16[1,64,16,1,512]{4,2,3,1,0:T(8,128)(2,1)}, u32[]{:S(2)}) copy-start(bf16[1,64,16,1,512]{4,2,3,1,0:T(8,128)(2,1)} %param.24) | copy-start | bytes 3145732
  0.7 16.7 %copy-start.5 = (f32[1,16,1,512]{3,2,1,0:T(1,128)S(1)}, f32[1,16,1,512]{3,2,1,0:T(1,128)}, u32[]{:S(2)}) copy-start(f32[1,16,1,512]{3,2,1,0:T(1,128)} %param.22) | copy-start | bytes 98308
  0.7 17.4 %copy-start.8 = (f32[1,16,1,512]{3,2,1,0:T(1,128)S(1)}, f32[1,16,1,512]{3,2,1,0:T(1,128)}, u32[]{:S(2)}) copy-start(f32[1,16,1,512]{3,2,1,0:T(1,128)} %param.20) | copy-start | bytes 98308
  0.7 20.0 %copy-start.10 = (f32[1,16,1,512]{3,2,1,0:T(1,128)S(1)}, f32[1,16,1,512]{3,2,1,0:T(1,128)}, u32[]{:S(2)}) copy-start(f32[1,16,1,512]{3,2,1,0:T(1,128)} %param.19) | copy-start | bytes 98308
  0.7 20.0 %copy-start.12 = (f32[1,16,1,512]{3,2,1,0:T(1,128)S(1)}, f32[1,16,1,512]{3,2,1,0:T(1,128)}, u32[]{:S(2)}) copy-start(f32[1,16,1,512]{3,2,1,0:T(1,128)} %param.18) | copy-start | bytes 98308
  0.7 26.2 %copy-start.3 = (f32[1,5,16,1,512]{4,3,2,1,0:T(1,128)S(1)}, f32[1,5,16,1,512]{4,3,2,1,0:T(1,128)}, u32[]{:S(2)}) copy-start(f32[1,5,16,1,512]{4,3,2,1,0:T(1,128)} %param.25) | copy-start | bytes 491524
  0.7 36.4 %copy-start.16 = (s32[1,5]{1,0:T(1,128)S(1)}, s32[1,5]{1,0:T(1,128)}, u32[]{:S(2)}) copy-start(s32[1,5]{1,0:T(1,128)} %param.28) | copy-start | bytes 64
  4.0 84.6 %collective-permute-start.4 = (bf16[1024,512]{1,0:T(8,128)(2,1)}, bf16[1024,512]{1,0:T(8,128)(2,1)S(1)}, u32[]{:S(2)}, u32[]{:S(2)}) collective-permute-start(bf16[1024,512]{1,0:T(8,128)(2,1)} %fusion.2), channel_id=1, source_target_pairs={{60,0},{62,2},{0,4},{2,6},{4,8},{6,10},{8,12},{10,14},{12,16},{14,... | collective-permute-start | bytes 3145736 | tf_op jit(solution)/shard_map/ppermute | solution.py:11
  8.3 80.3 %collective-permute-start.3 = (bf16[1024,512]{1,0:T(8,128)(2,1)}, bf16[1024,512]{1,0:T(8,128)(2,1)}, u32[]{:S(2)}, u32[]{:S(2)}) collective-permute-start(bf16[1024,512]{1,0:T(8,128)(2,1)} %fusion.2), channel_id=1, source_target_pairs={{4,0},{6,2},{8,4},{10,6},{12,8},{14,10},{16,12},{18,14},{20,16},{2... | collective-permute-start | bytes 3145736 | tf_op jit(solution)/shard_map/ppermute | solution.py:11
  23.4 36.2 %collective-permute-start = (f32[2]{0:T(128)S(1)}, f32[2]{0:T(128)S(1)}, u32[]{:S(2)}, u32[]{:S(2)}) collective-permute-start(f32[2]{0:T(128)S(1)} %pad_maximum_fusion.6), channel_id=1, source_target_pairs={{0,64},{64,0},{128,192},{192,128},{256,320},{320,256},{384,448},{4... | collective-permute-start | bytes 32 | tf_op jit(solution)/shard_map/ppermute | solution.py:25
  27.6 47.8 %collective-permute-start.8 = (f32[7,16,2]{2,1,0:T(8,128)}, f32[7,16,2]{2,1,0:T(8,128)}, u32[]{:S(2)}, u32[]{:S(2)}) collective-permute-start(f32[7,16,2]{2,1,0:T(8,128)} %get-tuple-element.56), channel_id=1, source_target_pairs={{62,0},{0,2},{2,4},{4,6},{6,8},{8,10},{10,12},{12,14},{14,16},{16,... | collective-permute-start | bytes 2696 | tf_op jit(solution)/shard_map/ppermute | solution.py:11
  29.5 45.9 %collective-permute-start.9 = (f32[7,16,2]{2,1,0:T(8,128)}, f32[7,16,2]{2,1,0:T(8,128)}, u32[]{:S(2)}, u32[]{:S(2)}) collective-permute-start(f32[7,16,2]{2,1,0:T(8,128)} %get-tuple-element.57), channel_id=1, source_target_pairs={{2,0},{4,2},{6,4},{8,6},{10,8},{12,10},{14,12},{16,14},{18,16},{20... | collective-permute-start | bytes 2696 | tf_op jit(solution)/shard_map/ppermute | solution.py:11
  59.7 6.3 %collective-permute-start.1 = (f32[2]{0:T(128)S(1)}, f32[2]{0:T(128)S(1)}, u32[]{:S(2)}, u32[]{:S(2)}) collective-permute-start(f32[2]{0:T(128)S(1)} %fusion.105), channel_id=1, source_target_pairs={{0,128},{64,192},{128,0},{192,64},{256,384},{320,448},{384,256},{4... | collective-permute-start | bytes 32 | tf_op jit(solution)/shard_map/ppermute | solution.py:25
  66.1 9.3 %collective-permute-start.2 = (f32[2]{0:T(128)S(1)}, f32[2]{0:T(128)S(1)}, u32[]{:S(2)}, u32[]{:S(2)}) collective-permute-start(f32[2]{0:T(128)S(1)} %fusion.106), channel_id=1, source_target_pairs={{0,256},{64,320},{128,384},{192,448},{256,0},{320,64},{384,128},{4... | collective-permute-start | bytes 32 | tf_op jit(solution)/shard_map/ppermute | solution.py:25
  76.5 11.5 %collective-permute-start.10 = (bf16[6,16,516]{2,1,0:T(8,128)(2,1)S(1)}, bf16[6,16,516]{2,1,0:T(8,128)(2,1)S(1)}, u32[]{:S(2)}, u32[]{:S(2)}) collective-permute-start(bf16[6,16,516]{2,1,0:T(8,128)(2,1)S(1)} %pad_maximum_fusion.2), channel_id=1, source_target_pairs={{0,1},{1,0},{2,3},{3,2},{4,5},{5,4},{6,7},{7,6},{8,9},{9,8},{10,11... | collective-permute-start | bytes 297224 | tf_op jit(solution)/shard_map/ppermute | solution.py:37
  88.6 11.7 %copy-start.6 = (f32[1,1,16,1,512]{4,3,2,1,0:T(1,128)S(1)}, f32[1,1,16,1,512]{4,3,2,1,0:T(1,128)}, u32[]{:S(2)}) copy-start(f32[1,1,16,1,512]{4,3,2,1,0:T(1,128)} %get-tuple-element.59) | copy-start | bytes 98308
  88.6 11.7 %copy-start.7 = (f32[1,1,16,1,512]{4,3,2,1,0:T(1,128)S(1)}, f32[1,1,16,1,512]{4,3,2,1,0:T(1,128)}, u32[]{:S(2)}) copy-start(f32[1,1,16,1,512]{4,3,2,1,0:T(1,128)} %get-tuple-element.60) | copy-start | bytes 98308
  88.6 14.2 %copy-start.1 = (bf16[1,5,512,512]{3,2,1,0:T(8,128)(2,1)S(1)}, bf16[1,5,512,512]{3,2,1,0:T(8,128)(2,1)}, u32[]{:S(2)}) copy-start(bf16[1,5,512,512]{3,2,1,0:T(8,128)(2,1)} %param.29) | copy-start | bytes 7864324
  88.6 45.7 %collective-permute-start.6 = (bf16[1024,512]{1,0:T(8,128)(2,1)}, bf16[1024,512]{1,0:T(8,128)(2,1)S(1)}, u32[]{:S(2)}, u32[]{:S(2)}) collective-permute-start(bf16[1024,512]{1,0:T(8,128)(2,1)} %fusion.2), channel_id=1, source_target_pairs={{0,58},{2,8},{4,62},{6,12},{8,2},{10,16},{12,6},{14,20},{16,10},{1... | collective-permute-start | bytes 3145736 | tf_op jit(solution)/shard_map/ppermute | solution.py:94
  90.7 43.6 %collective-permute-start.5 = (bf16[1024,512]{1,0:T(8,128)(2,1)}, bf16[1024,512]{1,0:T(8,128)(2,1)S(1)}, u32[]{:S(2)}, u32[]{:S(2)}) collective-permute-start(bf16[1024,512]{1,0:T(8,128)(2,1)} %fusion.2), channel_id=1, source_target_pairs={{0,2},{2,0},{4,6},{6,4},{8,10},{10,8},{12,14},{14,12},{16,18},{18,... | collective-permute-start | bytes 3145736 | tf_op jit(solution)/shard_map/ppermute | solution.py:93
  94.0 81.7 %collective-permute-start.7 = (bf16[2048,512]{1,0:T(8,128)(2,1)S(1)}, bf16[2048,512]{1,0:T(8,128)(2,1)S(1)}, u32[]{:S(2)}, u32[]{:S(2)}) collective-permute-start(bf16[2048,512]{1,0:T(8,128)(2,1)S(1)} %pad_maximum_fusion), channel_id=1, source_target_pairs={{0,2},{2,0},{4,6},{6,4},{8,10},{10,8},{12,14},{14,12},{16,18},{18,... | collective-permute-start | bytes 6291464 | tf_op jit(solution)/shard_map/ppermute | solution.py:95
  96.7 6.1 %collective-permute-start.18 = (bf16[16,512]{1,0:T(8,128)(2,1)S(1)}, bf16[16,512]{1,0:T(8,128)(2,1)S(1)}, u32[]{:S(2)}, u32[]{:S(2)}) collective-permute-start(bf16[16,512]{1,0:T(8,128)(2,1)S(1)} %fusion.58), channel_id=1, source_target_pairs={{64,0},{128,64},{192,128},{256,192},{320,256},{384,320},{448,384},... | collective-permute-start | bytes 49160 | tf_op jit(solution)/shard_map/ppermute | solution.py:17
  100.4 78.7 %collective-permute-start.17 = (bf16[16,512]{1,0:T(8,128)(2,1)S(1)}, bf16[16,512]{1,0:T(8,128)(2,1)S(1)}, u32[]{:S(2)}, u32[]{:S(2)}) collective-permute-start(bf16[16,512]{1,0:T(8,128)(2,1)S(1)} %fusion.66), channel_id=1, source_target_pairs={{0,64},{64,128},{128,192},{192,256},{256,320},{320,384},{384,448},... | collective-permute-start | bytes 49160 | tf_op jit(solution)/shard_map/ppermute | solution.py:17
  134.3 4.7 %collective-permute-start.11 = (f32[2]{0:T(128)S(1)}, f32[2]{0:T(128)S(1)}, u32[]{:S(2)}, u32[]{:S(2)}) collective-permute-start(f32[2]{0:T(128)S(1)} %add.245), channel_id=1, source_target_pairs={{0,2},{2,0},{4,6},{6,4},{8,10},{10,8},{12,14},{14,12},{16,18},{18,... | collective-permute-start | bytes 32 | tf_op jit(solution)/shard_map/ppermute | solution.py:25
  137.5 36.8 %copy-start.15 = (f32[1,16,1,512]{3,2,1,0:T(1,128)S(1)}, f32[1,16,1,512]{3,2,1,0:T(1,128)}, u32[]{:S(2)}) copy-start(f32[1,16,1,512]{3,2,1,0:T(1,128)} %param.15) | copy-start | bytes 98308
  137.5 37.5 %copy-start.9 = (f32[1,16,1,512]{3,2,1,0:T(1,128)S(1)}, f32[1,16,1,512]{3,2,1,0:T(1,128)}, u32[]{:S(2)}) copy-start(f32[1,16,1,512]{3,2,1,0:T(1,128)} %param.20) | copy-start | bytes 98308
  137.6 37.4 %copy-start.14 = (f32[1,16,1,512]{3,2,1,0:T(1,128)S(1)}, f32[1,16,1,512]{3,2,1,0:T(1,128)}, u32[]{:S(2)}) copy-start(f32[1,16,1,512]{3,2,1,0:T(1,128)} %param.26) | copy-start | bytes 98308
  139.0 5.4 %collective-permute-start.12 = (f32[2]{0:T(128)S(1)}, f32[2]{0:T(128)S(1)}, u32[]{:S(2)}, u32[]{:S(2)}) collective-permute-start(f32[2]{0:T(128)S(1)} %add.246), channel_id=1, source_target_pairs={{0,4},{2,6},{4,0},{6,2},{8,12},{10,14},{12,8},{14,10},{16,20},{18,... | collective-permute-start | bytes 32 | tf_op jit(solution)/shard_map/ppermute | solution.py:25
  144.4 6.3 %collective-permute-start.13 = (f32[2]{0:T(128)S(1)}, f32[2]{0:T(128)S(1)}, u32[]{:S(2)}, u32[]{:S(2)}) collective-permute-start(f32[2]{0:T(128)S(1)} %add.247), channel_id=1, source_target_pairs={{0,8},{2,10},{4,12},{6,14},{8,0},{10,2},{12,4},{14,6},{16,24},{18,... | collective-permute-start | bytes 32 | tf_op jit(solution)/shard_map/ppermute | solution.py:25
  150.7 5.4 %collective-permute-start.14 = (f32[2]{0:T(128)S(1)}, f32[2]{0:T(128)S(1)}, u32[]{:S(2)}, u32[]{:S(2)}) collective-permute-start(f32[2]{0:T(128)S(1)} %add.248), channel_id=1, source_target_pairs={{0,16},{2,18},{4,20},{6,22},{8,24},{10,26},{12,28},{14,30},{16,0},... | collective-permute-start | bytes 32 | tf_op jit(solution)/shard_map/ppermute | solution.py:25
  156.2 6.9 %collective-permute-start.15 = (f32[2]{0:T(128)S(1)}, f32[2]{0:T(128)S(1)}, u32[]{:S(2)}, u32[]{:S(2)}) collective-permute-start(f32[2]{0:T(128)S(1)} %add.249), channel_id=1, source_target_pairs={{0,32},{2,34},{4,36},{6,38},{8,40},{10,42},{12,44},{14,46},{16,48}... | collective-permute-start | bytes 32 | tf_op jit(solution)/shard_map/ppermute | solution.py:25
  163.1 9.3 %collective-permute-start.16 = (f32[2]{0:T(128)S(1)}, f32[2]{0:T(128)S(1)}, u32[]{:S(2)}, u32[]{:S(2)}) collective-permute-start(f32[2]{0:T(128)S(1)} %add.250), channel_id=1, source_target_pairs={{0,1},{1,0},{2,3},{3,2},{4,5},{5,4},{6,7},{7,6},{8,9},{9,8},{10,11... | collective-permute-start | bytes 32 | tf_op jit(solution)/shard_map/ppermute | solution.py:25
  178.7 0.8 copy-start.11
  178.7 0.8 copy-start.13
  178.7 0.8 copy-start.17
  178.7 0.8 copy-start.18
  178.7 0.8 copy-start.19
